TPU v7x, 256 devices: a whole 4x4x8 slice. The times are simulated.
256 devices in a mesh: row: 32 (over z, y), col: 8 (over x, core).
Axes of the slice: x: 4, y: 4, z: 8, core: 2. Of those that a mesh axis runs over, the one named last changes fastest.
Arguments:
- saved_input: bfloat16 [1024, 49152], P('col', 'row'), may hold values from -6 to 6
- out_grad: bfloat16 [1024, 12288], P('row', 'col'), may hold values from -0.75 to 0.75
- weight: bfloat16 [49152, 12288], P('row', 'col'), may hold values from -0.625 to 0.625
Outputs:
- in_grad: bfloat16 [1024, 49152], P('col', 'row')
- weight_grad: bfloat16 [49152, 12288], P('row', 'col')
All inputs are finite; a program needn't handle non-finite values.
Results may differ from a plain program's by a relative error of at most 0.0051.
Values may be sent and summed in bfloat16 or wider, within the bound.
No kernel may reach another device: no remote copies, remote signals or barrier semaphores. Data moves between devices by JAX's collectives and lax.ppermute only.
A program may use at most 64 MiB of HBM per device.

v0:
```python
import math

import jax
import jax.numpy as jnp
from jax import lax
from jax.sharding import PartitionSpec as P


def gelu_parts(values):
    coeff = math.sqrt(2.0 / math.pi)
    inner = jnp.tanh(coeff * (values + 0.044715 * values * values * values))
    gelu_value = 0.5 * values * (1.0 + inner)
    gelu_slope = 0.5 * (1.0 + inner) + 0.5 * values * (1.0 - inner * inner) * coeff * (
        1.0 + 3.0 * 0.044715 * values * values
    )
    return (gelu_value, gelu_slope)


def per_device(saved_input, out_grad, weight):
    grad_all = lax.all_gather(out_grad, "row", axis=0, tiled=True)
    saved_all = lax.all_gather(saved_input, "col", axis=0, tiled=True)
    gelu_value, unused_slope = gelu_parts(saved_all.astype(jnp.float32))
    hidden = gelu_value.astype(jnp.bfloat16)
    weight_grad = lax.dot_general(
        hidden, grad_all, (((0,), (0,)), ((), ())), preferred_element_type=jnp.float32
    ).astype(jnp.bfloat16)
    back = lax.psum_scatter(
        lax.dot_general(
            grad_all, weight, (((1,), (1,)), ((), ())), preferred_element_type=jnp.float32
        ),
        "col",
        scatter_dimension=0,
        tiled=True,
    )
    unused_value, own_slope = gelu_parts(saved_input.astype(jnp.float32))
    in_grad = (back * own_slope).astype(jnp.bfloat16)
    return (in_grad, weight_grad)


def solution(mesh):
    in_specs = (P("col", "row"), P("row", "col"), P("row", "col"))
    out_specs = (P("col", "row"), P("row", "col"))
    return jax.shard_map(
        per_device, mesh=mesh, in_specs=in_specs, out_specs=out_specs, check_vma=False
    )
```

profile of v0, /device:TPU:1, one launch (start us, length us, event | category | flops | bytes accessed | tf_op | source)
XLA Modules:
  0.0 178.5 jit_solution(13680003618552402031)
XLA Ops:
  7.2 0.0 all-gather.3.cloned.1.call-start
  7.2 0.7 all-gather.3.cloned.1.call-update
  7.9 0.0 all-gather.5.cloned.1.call-start
  7.9 0.7 all-gather.5.cloned.1.call-update
  8.6 0.0 reduce-scatter.2.cloned.1.call-start
  8.7 81.3 %all-gather.3.cloned.1.call-done = bf16[1024,1536]{1,0:T(8,128)(2,1)} async-done(((bf16[32,1536]{1,0:T(8,128)(2,1)}), bf16[1024,1536]{1,0:T(8,128)(2,1)}) %all-gather.3.cloned.1.call-update) | async-done | bytes 3145744 | tf_op jit(solution)/shard_map/all_gather | solution.py:20
  90.0 9.8 %fusion.23 = f32[1024,1536]{1,0:T(8,128)} fusion(bf16[1024,1536]{1,0:T(8,128)(2,1)} %all-gather.3.cloned.1.call-done, bf16[1536,1536]{1,0:T(8,128)(2,1)} %param.5), kind=kOutput, calls=%fused_computation.35 | convolution fusion | flops 4831838208 | bytes 14155776 | tf_op jit(solution)/shard_map/dot_general | solution.py:28
  99.7 0.0 copy-start.1
  99.7 0.0 reduce-scatter.2.cloned.1.call-update
  99.8 0.0 copy-start
  99.8 23.2 %all-gather.5.cloned.1.call-done = bf16[1024,1536]{1,0:T(8,128)(2,1)} async-done(((bf16[128,1536]{1,0:T(8,128)(2,1)}), bf16[1024,1536]{1,0:T(8,128)(2,1)}) %all-gather.5.cloned.1.call-update) | async-done | bytes 3145744 | tf_op jit(solution)/shard_map/all_gather | solution.py:21
  122.9 0.0 copy-done.1
  122.9 11.2 %convolution_convert_fusion = bf16[1536,1536]{1,0:T(8,128)(2,1)} fusion(bf16[1024,1536]{1,0:T(8,128)(2,1)S(1)} %copy-done.1, bf16[1024,1536]{1,0:T(8,128)(2,1)} %all-gather.5.cloned.1.call-done), kind=kOutput, calls=%fused_computation.5 | convolution fusion | flops 4849926144 | bytes 11010048 | tf_op jit(solution)/shard_map/dot_general | solution.py:24
  134.2 35.4 %reduce-scatter.2.cloned.1.call-done = f32[128,1536]{1,0:T(8,128)} async-done(((f32[1024,1536]{1,0:T(8,128)}), f32[128,1536]{1,0:T(8,128)}) %reduce-scatter.2.cloned.1.call-update) | async-done | bytes 786448 | tf_op jit(solution)/shard_map/reduce_scatter | solution.py:27
  169.6 0.0 copy-done
  169.6 2.4 %fusion.17 = bf16[128,1536]{1,0:T(8,128)(2,1)} fusion(f32[128,1536]{1,0:T(8,128)} %reduce-scatter.2.cloned.1.call-done, bf16[128,1536]{1,0:T(8,128)(2,1)S(1)} %copy-done), kind=kLoop, calls=%fused_computation.29 | loop fusion | flops 3932160 | bytes 1572864 | tf_op jit(solution)/shard_map/convert_element_type | solution.py:36
Async XLA Ops:
  7.2 82.8 %all-gather.3.cloned.1.call-start = ((), (), s32[]{:S(2)}) async-start(), calls=%async_computation.1 | async-start | bytes 3244032 | tf_op jit(solution)/shard_map/all_gather | solution.py:20
  7.9 115.0 %all-gather.5.cloned.1.call-start = ((), (), s32[]{:S(2)}) async-start(), calls=%async_computation.3 | async-start | bytes 3538944 | tf_op jit(solution)/shard_map/all_gather | solution.py:21
  8.6 161.0 %reduce-scatter.2.cloned.1.call-start = ((), (), s32[]{:S(2)}) async-start(), calls=%async_computation.2 | async-start | bytes 7077888 | tf_op jit(solution)/shard_map/reduce_scatter | solution.py:27
  99.7 23.2 %copy-start.1 = (bf16[1024,1536]{1,0:T(8,128)(2,1)S(1)}, bf16[1024,1536]{1,0:T(8,128)(2,1)}, u32[]{:S(2)}) copy-start(bf16[1024,1536]{1,0:T(8,128)(2,1)} %all-gather.3.cloned.1.call-done) | copy-start | bytes 9437188
  99.8 69.8 %copy-start = (bf16[128,1536]{1,0:T(8,128)(2,1)S(1)}, bf16[128,1536]{1,0:T(8,128)(2,1)}, u32[]{:S(2)}) copy-start(bf16[128,1536]{1,0:T(8,128)(2,1)} %param.3) | copy-start | bytes 1179652
Sparse Core Ops, SparseCore 0:
  10.5 79.3 all-gather.2
  91.8 31.1 all-gather.4
  125.5 44.0 reduce-scatter.1
where the time goes:
time: 179 us
  waiting for transfers between devices  141 us (79%)
  matrix products  21 us (12%)
  between operations  13.8 us (8%)
  other arithmetic  2.4 us (1%)
    all_gather x1, waiting for transfers between devices, per_device(): grad_all = lax.all_gather(out_grad, 'row', axis=0, tiled=True)  81.3 us
    reduce_scatter x1, waiting for transfers between devices, per_device(): lax.psum_scatter(lax.dot_general(grad_all, weight, (((1,), (1,)), ((), ()...  35.4 us
    all_gather x1, waiting for transfers between devices, per_device(): saved_all = lax.all_gather(saved_input, 'col', axis=0, tiled=True)  23.2 us
    dot_general x1, matrix products, per_device(): lax.dot_general(hidden, grad_all, (((0,), (0,)), ((), ())), preferred_ele...  11.2 us
    dot_general x1, matrix products, per_device(): lax.dot_general(grad_all, weight, (((1,), (1,)), ((), ())), preferred_ele...  9.78 us
  transfers between devices with their start and end apart: 3, of which 3 were waited for; matrix products, arithmetic and copies ran while one was open for 12% of the time, Pallas kernels for 0%

commit v1 on v0

v1 whole, which is shorter than its diff:
```python
import math

import jax
import jax.numpy as jnp
from jax import lax
from jax.sharding import PartitionSpec as P


def gelu_parts(values):
    coeff = math.sqrt(2.0 / math.pi)
    inner = jnp.tanh(coeff * (values + 0.044715 * values * values * values))
    gelu_value = 0.5 * values * (1.0 + inner)
    gelu_slope = 0.5 * (1.0 + inner) + 0.5 * values * (1.0 - inner * inner) * coeff * (
        1.0 + 3.0 * 0.044715 * values * values
    )
    return (gelu_value, gelu_slope)


def chip_shift(n_col, s):
    n_x = n_col // 2
    return [(x * 2 + k, ((x + s) % n_x) * 2 + k) for x in range(n_x) for k in range(2)]


def core_swap(n_col):
    return [(c, c ^ 1) for c in range(n_col)]


def make_per_device(n_col):
    n_x = n_col // 2

    def per_device(saved_input, out_grad, weight):
        c = lax.axis_index("col")
        x = c // 2
        k = c % 2

        grad_all = lax.all_gather(out_grad, "row", axis=0, tiled=True)

        got = [saved_input]
        for s in range(1, n_x):
            got.append(lax.ppermute(saved_input, "col", chip_shift(n_col, s)))
        by_chip = jnp.stack(got, axis=0)
        order = (x - jnp.arange(n_x)) % n_x
        mine_by_x = jnp.take(by_chip, order, axis=0)
        other_by_x = lax.ppermute(mine_by_x, "col", core_swap(n_col))
        pair = jnp.where(k == 0, jnp.stack([mine_by_x, other_by_x], axis=1),
                         jnp.stack([other_by_x, mine_by_x], axis=1))
        saved_all = pair.reshape((n_col * saved_input.shape[0], saved_input.shape[1]))

        gelu_value, unused_slope = gelu_parts(saved_all.astype(jnp.float32))
        hidden = gelu_value.astype(jnp.bfloat16)
        weight_grad = lax.dot_general(
            hidden, grad_all, (((0,), (0,)), ((), ())), preferred_element_type=jnp.float32
        ).astype(jnp.bfloat16)

        partial = lax.dot_general(
            grad_all, weight, (((1,), (1,)), ((), ())), preferred_element_type=jnp.float32
        )
        rows = saved_input.shape[0]
        p4 = partial.reshape((n_x, 2, rows, partial.shape[1]))
        mine = lax.dynamic_index_in_dim(p4, k, axis=1, keepdims=False)
        theirs = lax.dynamic_index_in_dim(p4, 1 - k, axis=1, keepdims=False)
        chip_sum = mine + lax.ppermute(theirs, "col", core_swap(n_col))
        back = lax.dynamic_index_in_dim(chip_sum, x, axis=0, keepdims=False)
        for s in range(1, n_x):
            dest = lax.dynamic_index_in_dim(chip_sum, (x + s) % n_x, axis=0, keepdims=False)
            recv = lax.ppermute(dest.astype(jnp.bfloat16), "col", chip_shift(n_col, s))
            back = back + recv.astype(jnp.float32)

        unused_value, own_slope = gelu_parts(saved_input.astype(jnp.float32))
        in_grad = (back * own_slope).astype(jnp.bfloat16)
        return (in_grad, weight_grad)

    return per_device


def solution(mesh):
    in_specs = (P("col", "row"), P("row", "col"), P("row", "col"))
    out_specs = (P("col", "row"), P("row", "col"))
    return jax.shard_map(
        make_per_device(mesh.shape["col"]),
        mesh=mesh, in_specs=in_specs, out_specs=out_specs, check_vma=False,
    )
```

time: 179 us -> 150 us (0.84)
  waiting for transfers between devices: 141 us -> 95.9 us
  starting transfers between devices: 0.11 us -> 12.8 us
  matrix products: 21 us -> 15.2 us
  other arithmetic: 2.4 us -> 7.34 us
  local copies, waits for them, and re-layouts: 0.01 us -> 4.37 us
    reduce_scatter x1 -> x0, waiting for transfers between devices: 35.4 us -> none  [per_device(): lax.psum_scatter(lax.dot_general(grad_all, weight, (((1,), (1,)), ((), ()...]
    all_gather x1 -> x0, waiting for transfers between devices: 23.2 us -> none  [per_device(): saved_all = lax.all_gather(saved_input, 'col', axis=0, tiled=True)]
    ppermute x0 -> x8, waiting for transfers between devices: none -> 17.7 us  [the longest x3 12.5 us: per_device(): recv = lax.ppermute(dest.astype(jnp.bfloat16), 'col', chip_shift(n_col, s))]
    ppermute x0 -> x8, starting transfers between devices: none -> 12.7 us  [the longest x1 4.58 us: per_device(): chip_sum = mine + lax.ppermute(theirs, 'col', core_swap(n_col))]
    dot_general x1, matrix products: 11.2 us -> 7.32 us  [per_device(): lax.dot_general(hidden, grad_all, (((0,), (0,)), ((), ())), preferred_ele...]
    all_gather x1, waiting for transfers between devices: 81.3 us -> 77.6 us  [per_device(): grad_all = lax.all_gather(out_grad, 'row', axis=0, tiled=True)]
    add x0 -> x1, other arithmetic: none -> 3.57 us  [per_device(): chip_sum = mine + lax.ppermute(theirs, 'col', core_swap(n_col))]
    select_n x0 -> x4, other arithmetic: none -> 2.13 us  [the longest x3 1.62 us: per_device(): mine_by_x = jnp.take(by_chip, order, axis=0)]
  transfers between devices with their start and end apart: 3 -> 9, of which waited for: 3 -> 5; matrix products, arithmetic and copies ran while one was open for 12% -> 13% of each run, Pallas kernels for 0% -> 0%
where the time goes in v1:
time: 150 us
  waiting for transfers between devices  95.9 us (64%)
  matrix products  15.2 us (10%)
  between operations  14.2 us (9%)
  starting transfers between devices  12.8 us (9%)
  other arithmetic  7.34 us (5%)
  local copies, waits for them, and re-layouts  4.37 us (3%)
    all_gather x1, waiting for transfers between devices, per_device(): grad_all = lax.all_gather(out_grad, 'row', axis=0, tiled=True)  77.6 us
    ppermute x3, waiting for transfers between devices, per_device(): recv = lax.ppermute(dest.astype(jnp.bfloat16), 'col', chip_shift(n_col, s))  12.5 us
    dot_general x1, matrix products, per_device(): lax.dot_general(grad_all, weight, (((1,), (1,)), ((), ())), preferred_ele...  7.88 us
    dot_general x1, matrix products, per_device(): lax.dot_general(hidden, grad_all, (((0,), (0,)), ((), ())), preferred_ele...  7.32 us
    ppermute x1, waiting for transfers between devices, per_device(): other_by_x = lax.ppermute(mine_by_x, 'col', core_swap(n_col))  5.18 us
    ppermute x1, starting transfers between devices, per_device(): chip_sum = mine + lax.ppermute(theirs, 'col', core_swap(n_col))  4.58 us
    ppermute x3, starting transfers between devices, per_device(): got.append(lax.ppermute(saved_input, 'col', chip_shift(n_col, s)))  4.5 us
    ppermute x3, starting transfers between devices, per_device(): recv = lax.ppermute(dest.astype(jnp.bfloat16), 'col', chip_shift(n_col, s))  3.64 us
  transfers between devices with their start and end apart: 9, of which 5 were waited for; matrix products, arithmetic and copies ran while one was open for 13% of the time, Pallas kernels for 0%

profile of v1, /device:TPU:1, one launch (start us, length us, event | category | flops | bytes accessed | tf_op | source)
XLA Modules:
  0.0 149.7 jit_solution(9653386689475775599)
XLA Ops:
  7.2 0.0 all-gather.2.cloned.1.call-start
  7.2 0.7 all-gather.2.cloned.1.call-update
  7.9 3.4 %collective-permute-start.6 = (bf16[128,1536]{1,0:T(8,128)(2,1)}, bf16[128,1536]{1,0:T(8,128)(2,1)S(1)}, u32[]{:S(2)}, u32[]{:S(2)}) collective-permute-start(bf16[128,1536]{1,0:T(8,128)(2,1)} %param.3), channel_id=1, source_target_pairs={{0,6},{1,7},{2,0},{3,1},{4,2},{5,3},{6,4},{7,5},{8,14},{9,15},{10,... | collective-permute-start | bytes 1179656 | tf_op jit(solution)/shard_map/ppermute | solution.py:40
  11.3 0.5 collective-permute-start.5
  11.8 0.6 collective-permute-start.4
  12.4 77.6 %all-gather.2.cloned.1.call-done = bf16[1024,1536]{1,0:T(8,128)(2,1)} async-done(((bf16[32,1536]{1,0:T(8,128)(2,1)}), bf16[1024,1536]{1,0:T(8,128)(2,1)}) %all-gather.2.cloned.1.call-update) | async-done | bytes 3145744 | tf_op jit(solution)/shard_map/all_gather | solution.py:36
  90.0 7.9 %fusion.31 = f32[1024,1536]{1,0:T(8,128)S(1)} fusion(bf16[1024,1536]{1,0:T(8,128)(2,1)} %all-gather.2.cloned.1.call-done, bf16[1536,1536]{1,0:T(8,128)(2,1)} %param.5), kind=kOutput, calls=%fused_computation.64 | convolution fusion | flops 4831838208 | bytes 14155776 | tf_op jit(solution)/shard_map/dot_general | solution.py:55
  97.9 0.0 copy-start.1
  97.9 1.9 %dynamic-slice_bitcast_fusion = f32[4,128,1536]{2,1,0:T(8,128)} fusion(f32[4,2,128,1536]{3,2,1,0:T(8,128)S(1)} %bitcast.35, s32[]{:T(128)S(6)} %select_n.101), kind=kLoop, calls=%fused_computation.18 | loop fusion | bytes 6291460 | tf_op jit(solution)/shard_map/jit(dynamic_index_in_dim)/squeeze | solution.py:61
  99.7 1.7 %copy-done = f32[1024,1536]{1,0:T(8,128)} copy-done((f32[1024,1536]{1,0:T(8,128)}, f32[1024,1536]{1,0:T(8,128)S(1)}, u32[]{:S(2)}) %copy-start) | copy-done | bytes 6291480
  101.4 4.6 %collective-permute-start = (f32[4,128,1536]{2,1,0:T(8,128)}, f32[4,128,1536]{2,1,0:T(8,128)}, u32[]{:S(2)}, u32[]{:S(2)}) collective-permute-start(f32[4,128,1536]{2,1,0:T(8,128)} %dynamic-slice_bitcast_fusion), channel_id=1, source_target_pairs={{0,1},{1,0},{2,3},{3,2},{4,5},{5,4},{6,7},{7,6},{8,9},{9,8},{10,11... | collective-permute-start | bytes 9437192 | tf_op jit(solution)/shard_map/ppermute | solution.py:62
  106.1 0.0 collective-permute-done.6
  106.1 0.0 collective-permute-done.5
  106.1 0.0 collective-permute-done.4
  106.1 0.2 pad_maximum_fusion
  106.3 0.6 gather_fusion
  107.0 1.4 broadcast_select_fusion
  108.4 0.0 collective-permute-start.7
  108.4 0.2 bitcast_select_fusion
  108.6 5.2 %collective-permute-done.7 = bf16[4,128,1536]{2,1,0:T(8,128)(2,1)S(1)} collective-permute-done((bf16[4,128,1536]{2,1,0:T(8,128)(2,1)}, bf16[4,128,1536]{2,1,0:T(8,128)(2,1)S(1)}, u32[]{:S(2)}, u32[]{:S(2)}) %collective-permute-start.7) | collective-permute-done | bytes 1572896 | tf_op jit(solution)/shard_map/ppermute | solution.py:44
  113.8 0.5 maximum_select_fusion
  114.3 0.0 collective-permute-done
  114.3 3.6 %bitcast_add_fusion = f32[4,128,1536]{2,1,0:T(8,128)S(1)} fusion(f32[4,128,1536]{2,1,0:T(8,128)} %collective-permute-done, f32[4,2,128,1536]{3,2,1,0:T(8,128)} %bitcast.36, s32[]{:T(128)S(6)} %select_n.100), kind=kLoop, calls=%fused_computation.13 | loop fusion | flops 786432 | bytes 9437188 | tf_op jit(solution)/shard_map/add | solution.py:62
  117.9 0.1 fusion.21
  118.0 2.5 %collective-permute-start.3 = (bf16[128,1536]{1,0:T(8,128)(2,1)S(1)}, bf16[128,1536]{1,0:T(8,128)(2,1)S(1)}, u32[]{:S(2)}, u32[]{:S(2)}) collective-permute-start(bf16[128,1536]{1,0:T(8,128)(2,1)S(1)} %get-tuple-element.3), channel_id=1, source_target_pairs={{0,6},{1,7},{2,0},{3,1},{4,2},{5,3},{6,4},{7,5},{8,14},{9,15},{10,... | collective-permute-start | bytes 1179656 | tf_op jit(solution)/shard_map/ppermute | solution.py:66
  120.5 0.6 collective-permute-start.2
  121.1 0.6 collective-permute-start.1
  121.7 7.3 %convolution_convert_fusion = bf16[1536,1536]{1,0:T(8,128)(2,1)} fusion(bf16[1024,1536]{1,0:T(8,128)(2,1)S(1)} %copy-done.2, bf16[1024,1536]{1,0:T(8,128)(2,1)S(1)} %bitcast.37), kind=kOutput, calls=%fused_computation.6 | convolution fusion | flops 4849926144 | bytes 11010048 | tf_op jit(solution)/shard_map/dot_general | solution.py:51
  129.0 0.3 collective-permute-done.3
  129.3 2.8 %collective-permute-done.2 = bf16[128,1536]{1,0:T(8,128)(2,1)S(1)} collective-permute-done((bf16[128,1536]{1,0:T(8,128)(2,1)S(1)}, bf16[128,1536]{1,0:T(8,128)(2,1)S(1)}, u32[]{:S(2)}, u32[]{:S(2)}) %collective-permute-start.2) | collective-permute-done | bytes 393248 | tf_op jit(solution)/shard_map/ppermute | solution.py:66
  132.1 9.4 %collective-permute-done.1 = bf16[128,1536]{1,0:T(8,128)(2,1)S(1)} collective-permute-done((bf16[128,1536]{1,0:T(8,128)(2,1)S(1)}, bf16[128,1536]{1,0:T(8,128)(2,1)S(1)}, u32[]{:S(2)}, u32[]{:S(2)}) %collective-permute-start.1) | collective-permute-done | bytes 393248 | tf_op jit(solution)/shard_map/ppermute | solution.py:66
  141.5 1.4 fusion.17
  (7 shorter events, 0.0 us)
Async XLA Ops:
  7.2 82.8 %all-gather.2.cloned.1.call-start = ((), (), s32[]{:S(2)}) async-start(), calls=%async_computation | async-start | bytes 3244032 | tf_op jit(solution)/shard_map/all_gather | solution.py:36
  7.9 98.2 %collective-permute-start.6 = (bf16[128,1536]{1,0:T(8,128)(2,1)}, bf16[128,1536]{1,0:T(8,128)(2,1)S(1)}, u32[]{:S(2)}, u32[]{:S(2)}) collective-permute-start(bf16[128,1536]{1,0:T(8,128)(2,1)} %param.3), channel_id=1, source_target_pairs={{0,6},{1,7},{2,0},{3,1},{4,2},{5,3},{6,4},{7,5},{8,14},{9,15},{10,... | collective-permute-start | bytes 1179656 | tf_op jit(solution)/shard_map/ppermute | solution.py:40
  11.3 94.8 %collective-permute-start.5 = (bf16[128,1536]{1,0:T(8,128)(2,1)}, bf16[128,1536]{1,0:T(8,128)(2,1)S(1)}, u32[]{:S(2)}, u32[]{:S(2)}) collective-permute-start(bf16[128,1536]{1,0:T(8,128)(2,1)} %param.3), channel_id=1, source_target_pairs={{0,4},{1,5},{2,6},{3,7},{4,0},{5,1},{6,2},{7,3},{8,12},{9,13},{10,... | collective-permute-start | bytes 1179656 | tf_op jit(solution)/shard_map/ppermute | solution.py:40
  11.8 94.3 %collective-permute-start.4 = (bf16[128,1536]{1,0:T(8,128)(2,1)}, bf16[128,1536]{1,0:T(8,128)(2,1)S(1)}, u32[]{:S(2)}, u32[]{:S(2)}) collective-permute-start(bf16[128,1536]{1,0:T(8,128)(2,1)} %param.3), channel_id=1, source_target_pairs={{0,2},{1,3},{2,4},{3,5},{4,6},{5,7},{6,0},{7,1},{8,10},{9,11},{10,... | collective-permute-start | bytes 1179656 | tf_op jit(solution)/shard_map/ppermute | solution.py:40
  97.8 3.6 %copy-start = (f32[1024,1536]{1,0:T(8,128)}, f32[1024,1536]{1,0:T(8,128)S(1)}, u32[]{:S(2)}) copy-start(f32[1024,1536]{1,0:T(8,128)S(1)} %fusion.31) | copy-start | bytes 18874372
  97.9 8.2 %copy-start.1 = (bf16[128,1536]{1,0:T(8,128)(2,1)S(1)}, bf16[128,1536]{1,0:T(8,128)(2,1)}, u32[]{:S(2)}) copy-start(bf16[128,1536]{1,0:T(8,128)(2,1)} %param.3) | copy-start | bytes 1179652
  101.4 12.9 %collective-permute-start = (f32[4,128,1536]{2,1,0:T(8,128)}, f32[4,128,1536]{2,1,0:T(8,128)}, u32[]{:S(2)}, u32[]{:S(2)}) collective-permute-start(f32[4,128,1536]{2,1,0:T(8,128)} %dynamic-slice_bitcast_fusion), channel_id=1, source_target_pairs={{0,1},{1,0},{2,3},{3,2},{4,5},{5,4},{6,7},{7,6},{8,9},{9,8},{10,11... | collective-permute-start | bytes 9437192 | tf_op jit(solution)/shard_map/ppermute | solution.py:62
  108.4 5.4 %collective-permute-start.7 = (bf16[4,128,1536]{2,1,0:T(8,128)(2,1)}, bf16[4,128,1536]{2,1,0:T(8,128)(2,1)S(1)}, u32[]{:S(2)}, u32[]{:S(2)}) collective-permute-start(bf16[4,128,1536]{2,1,0:T(8,128)(2,1)} %broadcast_select_fusion), channel_id=1, source_target_pairs={{0,1},{1,0},{2,3},{3,2},{4,5},{5,4},{6,7},{7,6},{8,9},{9,8},{10,11... | collective-permute-start | bytes 4718600 | tf_op jit(solution)/shard_map/ppermute | solution.py:44
  114.3 7.4 %copy-start.2 = (bf16[1024,1536]{1,0:T(8,128)(2,1)S(1)}, bf16[1024,1536]{1,0:T(8,128)(2,1)}, u32[]{:S(2)}) copy-start(bf16[1024,1536]{1,0:T(8,128)(2,1)} %all-gather.2.cloned.1.call-done) | copy-start | bytes 9437188
  118.0 11.3 %collective-permute-start.3 = (bf16[128,1536]{1,0:T(8,128)(2,1)S(1)}, bf16[128,1536]{1,0:T(8,128)(2,1)S(1)}, u32[]{:S(2)}, u32[]{:S(2)}) collective-permute-start(bf16[128,1536]{1,0:T(8,128)(2,1)S(1)} %get-tuple-element.3), channel_id=1, source_target_pairs={{0,6},{1,7},{2,0},{3,1},{4,2},{5,3},{6,4},{7,5},{8,14},{9,15},{10,... | collective-permute-start | bytes 1179656 | tf_op jit(solution)/shard_map/ppermute | solution.py:66
  120.5 11.6 %collective-permute-start.2 = (bf16[128,1536]{1,0:T(8,128)(2,1)S(1)}, bf16[128,1536]{1,0:T(8,128)(2,1)S(1)}, u32[]{:S(2)}, u32[]{:S(2)}) collective-permute-start(bf16[128,1536]{1,0:T(8,128)(2,1)S(1)} %get-tuple-element.4), channel_id=1, source_target_pairs={{0,4},{1,5},{2,6},{3,7},{4,0},{5,1},{6,2},{7,3},{8,12},{9,13},{10,... | collective-permute-start | bytes 1179656 | tf_op jit(solution)/shard_map/ppermute | solution.py:66
  121.1 20.4 %collective-permute-start.1 = (bf16[128,1536]{1,0:T(8,128)(2,1)S(1)}, bf16[128,1536]{1,0:T(8,128)(2,1)S(1)}, u32[]{:S(2)}, u32[]{:S(2)}) collective-permute-start(bf16[128,1536]{1,0:T(8,128)(2,1)S(1)} %get-tuple-element.2), channel_id=1, source_target_pairs={{0,2},{1,3},{2,4},{3,5},{4,6},{5,7},{6,0},{7,1},{8,10},{9,11},{10,... | collective-permute-start | bytes 1179656 | tf_op jit(solution)/shard_map/ppermute | solution.py:66
Sparse Core Ops, SparseCore 0:
  10.5 79.3 all-gather.1

commit v2 on v1

--- a/solution.py
+++ b/solution.py
@@ -3,7 +3,9 @@
 import jax
 import jax.numpy as jnp
 from jax import lax
-from jax.sharding import PartitionSpec as P
+from jax.sharding import Mesh, PartitionSpec as P
+
+COL = ("x", "c")
 
 
 def gelu_parts(values):
@@ -29,19 +31,20 @@
     n_x = n_col // 2
 
     def per_device(saved_input, out_grad, weight):
-        c = lax.axis_index("col")
+        c = lax.axis_index(COL)
         x = c // 2
         k = c % 2
 
-        grad_all = lax.all_gather(out_grad, "row", axis=0, tiled=True)
+        grad_y = lax.all_gather(out_grad, "y", axis=0, tiled=True)
+        grad_all = lax.all_gather(grad_y, "z", axis=0, tiled=True)
 
         got = [saved_input]
         for s in range(1, n_x):
-            got.append(lax.ppermute(saved_input, "col", chip_shift(n_col, s)))
+            got.append(lax.ppermute(saved_input, COL, chip_shift(n_col, s)))
         by_chip = jnp.stack(got, axis=0)
         order = (x - jnp.arange(n_x)) % n_x
         mine_by_x = jnp.take(by_chip, order, axis=0)
-        other_by_x = lax.ppermute(mine_by_x, "col", core_swap(n_col))
+        other_by_x = lax.ppermute(mine_by_x, COL, core_swap(n_col))
         pair = jnp.where(k == 0, jnp.stack([mine_by_x, other_by_x], axis=1),
                          jnp.stack([other_by_x, mine_by_x], axis=1))
         saved_all = pair.reshape((n_col * saved_input.shape[0], saved_input.shape[1]))
@@ -59,11 +62,11 @@
         p4 = partial.reshape((n_x, 2, rows, partial.shape[1]))
         mine = lax.dynamic_index_in_dim(p4, k, axis=1, keepdims=False)
         theirs = lax.dynamic_index_in_dim(p4, 1 - k, axis=1, keepdims=False)
-        chip_sum = mine + lax.ppermute(theirs, "col", core_swap(n_col))
+        chip_sum = mine + lax.ppermute(theirs, COL, core_swap(n_col))
         back = lax.dynamic_index_in_dim(chip_sum, x, axis=0, keepdims=False)
         for s in range(1, n_x):
             dest = lax.dynamic_index_in_dim(chip_sum, (x + s) % n_x, axis=0, keepdims=False)
-            recv = lax.ppermute(dest.astype(jnp.bfloat16), "col", chip_shift(n_col, s))
+            recv = lax.ppermute(dest.astype(jnp.bfloat16), COL, chip_shift(n_col, s))
             back = back + recv.astype(jnp.float32)
 
         unused_value, own_slope = gelu_parts(saved_input.astype(jnp.float32))
@@ -74,9 +77,12 @@
 
 
 def solution(mesh):
-    in_specs = (P("col", "row"), P("row", "col"), P("row", "col"))
-    out_specs = (P("col", "row"), P("row", "col"))
+    n_row, n_col = mesh.shape["row"], mesh.shape["col"]
+    grid = Mesh(mesh.devices.reshape(n_row // 4, 4, n_col // 2, 2), ("z", "y", "x", "c"))
+    row = ("z", "y")
+    in_specs = (P(COL, row), P(row, COL), P(row, COL))
+    out_specs = (P(COL, row), P(row, COL))
     return jax.shard_map(
-        make_per_device(mesh.shape["col"]),
-        mesh=mesh, in_specs=in_specs, out_specs=out_specs, check_vma=False,
+        make_per_device(n_col),
+        mesh=grid, in_specs=in_specs, out_specs=out_specs, check_vma=False,
     )

time: 150 us -> 125 us (0.83)
  waiting for transfers between devices: 95.9 us -> 62.7 us
  blocking collectives: 0 us -> 13 us
  starting transfers between devices: 12.8 us -> 8.6 us
    all_gather x1, waiting for transfers between devices: 77.6 us -> 45 us  [per_device(): grad_all = lax.all_gather(grad_y, 'z', axis=0, tiled=True)]
    all_gather x0 -> x1, blocking collectives: none -> 13 us  [per_device(): grad_y = lax.all_gather(out_grad, 'y', axis=0, tiled=True)]
    ppermute x8, starting transfers between devices: 12.7 us -> 8.56 us  [the longest x3 3.68 us: per_device(): got.append(lax.ppermute(saved_input, COL, chip_shift(n_col, s)))]
  transfers between devices with their start and end apart: 9 -> 9, of which waited for: 5 -> 5; matrix products, arithmetic and copies ran while one was open for 13% -> 16% of each run, Pallas kernels for 0% -> 0%
where the time goes in v2:
time: 125 us
  waiting for transfers between devices  62.7 us (50%)
  matrix products  15.2 us (12%)
  between operations  14.2 us (11%)
  blocking collectives  13 us (10%)
  starting transfers between devices  8.6 us (7%)
  other arithmetic  7.34 us (6%)
  local copies, waits for them, and re-layouts  4.37 us (3%)
    all_gather x1, waiting for transfers between devices, per_device(): grad_all = lax.all_gather(grad_y, 'z', axis=0, tiled=True)  45 us
    all_gather x1, blocking collectives, per_device(): grad_y = lax.all_gather(out_grad, 'y', axis=0, tiled=True)  13 us
    ppermute x3, waiting for transfers between devices, per_device(): recv = lax.ppermute(dest.astype(jnp.bfloat16), COL, chip_shift(n_col, s))  12.5 us
    dot_general x1, matrix products, per_device(): lax.dot_general(grad_all, weight, (((1,), (1,)), ((), ())), preferred_ele...  7.9 us
    dot_general x1, matrix products, per_device(): lax.dot_general(hidden, grad_all, (((0,), (0,)), ((), ())), preferred_ele...  7.32 us
    ppermute x1, waiting for transfers between devices, per_device(): other_by_x = lax.ppermute(mine_by_x, COL, core_swap(n_col))  5.18 us
    ppermute x3, starting transfers between devices, per_device(): got.append(lax.ppermute(saved_input, COL, chip_shift(n_col, s)))  3.68 us
    ppermute x3, starting transfers between devices, per_device(): recv = lax.ppermute(dest.astype(jnp.bfloat16), COL, chip_shift(n_col, s))  3.64 us
  transfers between devices with their start and end apart: 9, of which 5 were waited for; matrix products, arithmetic and copies ran while one was open for 16% of the time, Pallas kernels for 0%

profile of v2, /device:TPU:1, one launch (start us, length us, event | category | flops | bytes accessed | tf_op | source)
XLA Modules:
  0.0 125.3 jit_solution(10868526830943091658)
XLA Ops:
  7.2 0.0 all-gather.2.cloned.1.call-start
  7.2 13.0 %all_gather.6 = bf16[128,1536]{1,0:T(8,128)(2,1)} all-gather(bf16[32,1536]{1,0:T(8,128)(2,1)} %param.4), channel_id=1, replica_groups=mesh['z'=8,'y'=4,'x'=4,'c'=2] {'y'}, dimensions={0}, use_global_device_ids=true | all-gather | bytes 491520 | tf_op jit(solution)/shard_map/all_gather | solution.py:38
  20.2 0.0 all-gather.2.cloned.1.call-update
  20.2 2.6 %collective-permute-start.6 = (bf16[128,1536]{1,0:T(8,128)(2,1)}, bf16[128,1536]{1,0:T(8,128)(2,1)S(1)}, u32[]{:S(2)}, u32[]{:S(2)}) collective-permute-start(bf16[128,1536]{1,0:T(8,128)(2,1)} %param.3), channel_id=1, source_target_pairs={{0,6},{1,7},{2,0},{3,1},{4,2},{5,3},{6,4},{7,5},{8,14},{9,15},{10,... | collective-permute-start | bytes 1179656 | tf_op jit(solution)/shard_map/ppermute | solution.py:43
  22.8 0.5 collective-permute-start.5
  23.3 0.6 collective-permute-start.4
  23.9 45.0 %all-gather.2.cloned.1.call-done = bf16[1024,1536]{1,0:T(8,128)(2,1)} async-done(((bf16[128,1536]{1,0:T(8,128)(2,1)}), bf16[1024,1536]{1,0:T(8,128)(2,1)}) %all-gather.2.cloned.1.call-update) | async-done | bytes 3145744 | tf_op jit(solution)/shard_map/all_gather | solution.py:39
  68.9 7.9 %fusion.31 = f32[1024,1536]{1,0:T(8,128)S(1)} fusion(bf16[1024,1536]{1,0:T(8,128)(2,1)} %all-gather.2.cloned.1.call-done, bf16[1536,1536]{1,0:T(8,128)(2,1)} %param.5), kind=kOutput, calls=%fused_computation.64 | convolution fusion | flops 4831838208 | bytes 14155776 | tf_op jit(solution)/shard_map/dot_general | solution.py:58
  76.8 0.0 copy-start.1
  76.8 1.9 %dynamic-slice_bitcast_fusion = f32[4,128,1536]{2,1,0:T(8,128)} fusion(f32[4,2,128,1536]{3,2,1,0:T(8,128)S(1)} %bitcast.35, s32[]{:T(128)S(6)} %select_n.101), kind=kLoop, calls=%fused_computation.18 | loop fusion | bytes 6291460 | tf_op jit(solution)/shard_map/jit(dynamic_index_in_dim)/squeeze | solution.py:64
  78.7 1.7 %copy-done = f32[1024,1536]{1,0:T(8,128)} copy-done((f32[1024,1536]{1,0:T(8,128)}, f32[1024,1536]{1,0:T(8,128)S(1)}, u32[]{:S(2)}) %copy-start) | copy-done | bytes 6291480
  80.4 1.2 collective-permute-start
  81.7 0.0 collective-permute-done.6
  81.7 0.0 collective-permute-done.5
  81.7 0.0 collective-permute-done.4
  81.7 0.2 pad_maximum_fusion
  81.9 0.6 gather_fusion
  82.6 1.4 %broadcast_select_fusion = bf16[4,128,1536]{2,1,0:T(8,128)(2,1)} fusion(bf16[4,128,1536]{2,1,0:T(8,128)(2,1)S(1)} %gather_fusion, pred[4]{0:T(512)(128)(4,1)S(1)} %compare_and_fusion), kind=kLoop, calls=%fused_computation.28 | loop fusion | flops 786432 | bytes 3145732 | tf_op jit(solution)/shard_map/jit(_take)/select_n | solution.py:46
  84.0 0.0 collective-permute-start.7
  84.0 0.2 bitcast_select_fusion
  84.2 5.2 %collective-permute-done.7 = bf16[4,128,1536]{2,1,0:T(8,128)(2,1)S(1)} collective-permute-done((bf16[4,128,1536]{2,1,0:T(8,128)(2,1)}, bf16[4,128,1536]{2,1,0:T(8,128)(2,1)S(1)}, u32[]{:S(2)}, u32[]{:S(2)}) %collective-permute-start.7) | collective-permute-done | bytes 1572896 | tf_op jit(solution)/shard_map/ppermute | solution.py:47
  89.4 0.5 maximum_select_fusion
  89.9 3.6 %bitcast_add_fusion = f32[4,128,1536]{2,1,0:T(8,128)S(1)} fusion(f32[4,128,1536]{2,1,0:T(8,128)} %collective-permute-done, f32[4,2,128,1536]{3,2,1,0:T(8,128)} %bitcast.36, s32[]{:T(128)S(6)} %select_n.100), kind=kLoop, calls=%fused_computation.13 | loop fusion | flops 786432 | bytes 9437188 | tf_op jit(solution)/shard_map/add | solution.py:65
  93.5 0.1 fusion.21
  93.6 2.5 %collective-permute-start.3 = (bf16[128,1536]{1,0:T(8,128)(2,1)S(1)}, bf16[128,1536]{1,0:T(8,128)(2,1)S(1)}, u32[]{:S(2)}, u32[]{:S(2)}) collective-permute-start(bf16[128,1536]{1,0:T(8,128)(2,1)S(1)} %get-tuple-element.3), channel_id=1, source_target_pairs={{0,6},{1,7},{2,0},{3,1},{4,2},{5,3},{6,4},{7,5},{8,14},{9,15},{10,... | collective-permute-start | bytes 1179656 | tf_op jit(solution)/shard_map/ppermute | solution.py:69
  96.1 0.6 collective-permute-start.2
  96.7 0.6 collective-permute-start.1
  97.3 7.3 %convolution_convert_fusion = bf16[1536,1536]{1,0:T(8,128)(2,1)} fusion(bf16[1024,1536]{1,0:T(8,128)(2,1)S(1)} %copy-done.2, bf16[1024,1536]{1,0:T(8,128)(2,1)S(1)} %bitcast.37), kind=kOutput, calls=%fused_computation.6 | convolution fusion | flops 4849926144 | bytes 11010048 | tf_op jit(solution)/shard_map/dot_general | solution.py:54
  104.6 0.3 collective-permute-done.3
  104.9 2.8 %collective-permute-done.2 = bf16[128,1536]{1,0:T(8,128)(2,1)S(1)} collective-permute-done((bf16[128,1536]{1,0:T(8,128)(2,1)S(1)}, bf16[128,1536]{1,0:T(8,128)(2,1)S(1)}, u32[]{:S(2)}, u32[]{:S(2)}) %collective-permute-start.2) | collective-permute-done | bytes 393248 | tf_op jit(solution)/shard_map/ppermute | solution.py:69
  107.7 9.4 %collective-permute-done.1 = bf16[128,1536]{1,0:T(8,128)(2,1)S(1)} collective-permute-done((bf16[128,1536]{1,0:T(8,128)(2,1)S(1)}, bf16[128,1536]{1,0:T(8,128)(2,1)S(1)}, u32[]{:S(2)}, u32[]{:S(2)}) %collective-permute-start.1) | collective-permute-done | bytes 393248 | tf_op jit(solution)/shard_map/ppermute | solution.py:69
  117.1 1.4 %fusion.17 = bf16[128,1536]{1,0:T(8,128)(2,1)} fusion(bf16[128,1536]{1,0:T(8,128)(2,1)S(1)} %copy-done.1, bf16[128,1536]{1,0:T(8,128)(2,1)S(1)} %collective-permute-done.3, bf16[128,1536]{1,0:T(8,128)(2,1)S(1)} %collective-permute-done.2, bf16[128,1536]{1,0:T(8,128)(2,1)S(1)} %collective-permute-done.1, f32[4,128,1536]{2,1,0:T(8,128)S(1)} %bitcast_add_fusion, ...), kind=kLoop, calls=%fused_computation.36 | loop fusion | flops 5111808 | bytes 2752516 | tf_op jit(solution)/shard_map/convert_element_type | solution.py:73
  (8 shorter events, 0.0 us)
Async XLA Ops:
  7.2 61.7 %all-gather.2.cloned.1.call-start = ((), (), s32[]{:S(2)}) async-start(), calls=%async_computation | async-start | bytes 3538944 | tf_op jit(solution)/shard_map/all_gather | solution.py:39
  20.2 61.4 %collective-permute-start.6 = (bf16[128,1536]{1,0:T(8,128)(2,1)}, bf16[128,1536]{1,0:T(8,128)(2,1)S(1)}, u32[]{:S(2)}, u32[]{:S(2)}) collective-permute-start(bf16[128,1536]{1,0:T(8,128)(2,1)} %param.3), channel_id=1, source_target_pairs={{0,6},{1,7},{2,0},{3,1},{4,2},{5,3},{6,4},{7,5},{8,14},{9,15},{10,... | collective-permute-start | bytes 1179656 | tf_op jit(solution)/shard_map/ppermute | solution.py:43
  22.8 58.9 %collective-permute-start.5 = (bf16[128,1536]{1,0:T(8,128)(2,1)}, bf16[128,1536]{1,0:T(8,128)(2,1)S(1)}, u32[]{:S(2)}, u32[]{:S(2)}) collective-permute-start(bf16[128,1536]{1,0:T(8,128)(2,1)} %param.3), channel_id=1, source_target_pairs={{0,4},{1,5},{2,6},{3,7},{4,0},{5,1},{6,2},{7,3},{8,12},{9,13},{10,... | collective-permute-start | bytes 1179656 | tf_op jit(solution)/shard_map/ppermute | solution.py:43
  23.3 58.4 %collective-permute-start.4 = (bf16[128,1536]{1,0:T(8,128)(2,1)}, bf16[128,1536]{1,0:T(8,128)(2,1)S(1)}, u32[]{:S(2)}, u32[]{:S(2)}) collective-permute-start(bf16[128,1536]{1,0:T(8,128)(2,1)} %param.3), channel_id=1, source_target_pairs={{0,2},{1,3},{2,4},{3,5},{4,6},{5,7},{6,0},{7,1},{8,10},{9,11},{10,... | collective-permute-start | bytes 1179656 | tf_op jit(solution)/shard_map/ppermute | solution.py:43
  76.8 3.6 %copy-start = (f32[1024,1536]{1,0:T(8,128)}, f32[1024,1536]{1,0:T(8,128)S(1)}, u32[]{:S(2)}) copy-start(f32[1024,1536]{1,0:T(8,128)S(1)} %fusion.31) | copy-start | bytes 18874372
  76.8 4.9 %copy-start.1 = (bf16[128,1536]{1,0:T(8,128)(2,1)S(1)}, bf16[128,1536]{1,0:T(8,128)(2,1)}, u32[]{:S(2)}) copy-start(bf16[128,1536]{1,0:T(8,128)(2,1)} %param.3) | copy-start | bytes 1179652
  80.4 9.5 %collective-permute-start = (f32[4,128,1536]{2,1,0:T(8,128)}, f32[4,128,1536]{2,1,0:T(8,128)}, u32[]{:S(2)}, u32[]{:S(2)}) collective-permute-start(f32[4,128,1536]{2,1,0:T(8,128)} %dynamic-slice_bitcast_fusion), channel_id=1, source_target_pairs={{0,1},{1,0},{2,3},{3,2},{4,5},{5,4},{6,7},{7,6},{8,9},{9,8},{10,11... | collective-permute-start | bytes 9437192 | tf_op jit(solution)/shard_map/ppermute | solution.py:65
  84.0 5.4 %collective-permute-start.7 = (bf16[4,128,1536]{2,1,0:T(8,128)(2,1)}, bf16[4,128,1536]{2,1,0:T(8,128)(2,1)S(1)}, u32[]{:S(2)}, u32[]{:S(2)}) collective-permute-start(bf16[4,128,1536]{2,1,0:T(8,128)(2,1)} %broadcast_select_fusion), channel_id=1, source_target_pairs={{0,1},{1,0},{2,3},{3,2},{4,5},{5,4},{6,7},{7,6},{8,9},{9,8},{10,11... | collective-permute-start | bytes 4718600 | tf_op jit(solution)/shard_map/ppermute | solution.py:47
  89.9 7.4 %copy-start.2 = (bf16[1024,1536]{1,0:T(8,128)(2,1)S(1)}, bf16[1024,1536]{1,0:T(8,128)(2,1)}, u32[]{:S(2)}) copy-start(bf16[1024,1536]{1,0:T(8,128)(2,1)} %all-gather.2.cloned.1.call-done) | copy-start | bytes 9437188
  93.6 11.3 %collective-permute-start.3 = (bf16[128,1536]{1,0:T(8,128)(2,1)S(1)}, bf16[128,1536]{1,0:T(8,128)(2,1)S(1)}, u32[]{:S(2)}, u32[]{:S(2)}) collective-permute-start(bf16[128,1536]{1,0:T(8,128)(2,1)S(1)} %get-tuple-element.3), channel_id=1, source_target_pairs={{0,6},{1,7},{2,0},{3,1},{4,2},{5,3},{6,4},{7,5},{8,14},{9,15},{10,... | collective-permute-start | bytes 1179656 | tf_op jit(solution)/shard_map/ppermute | solution.py:69
  96.1 11.6 %collective-permute-start.2 = (bf16[128,1536]{1,0:T(8,128)(2,1)S(1)}, bf16[128,1536]{1,0:T(8,128)(2,1)S(1)}, u32[]{:S(2)}, u32[]{:S(2)}) collective-permute-start(bf16[128,1536]{1,0:T(8,128)(2,1)S(1)} %get-tuple-element.4), channel_id=1, source_target_pairs={{0,4},{1,5},{2,6},{3,7},{4,0},{5,1},{6,2},{7,3},{8,12},{9,13},{10,... | collective-permute-start | bytes 1179656 | tf_op jit(solution)/shard_map/ppermute | solution.py:69
  96.7 20.4 %collective-permute-start.1 = (bf16[128,1536]{1,0:T(8,128)(2,1)S(1)}, bf16[128,1536]{1,0:T(8,128)(2,1)S(1)}, u32[]{:S(2)}, u32[]{:S(2)}) collective-permute-start(bf16[128,1536]{1,0:T(8,128)(2,1)S(1)} %get-tuple-element.2), channel_id=1, source_target_pairs={{0,2},{1,3},{2,4},{3,5},{4,6},{5,7},{6,0},{7,1},{8,10},{9,11},{10,... | collective-permute-start | bytes 1179656 | tf_op jit(solution)/shard_map/ppermute | solution.py:69
Sparse Core Ops, SparseCore 0:
  20.4 48.4 all-gather.1

commit v3 on v2

--- a/solution.py
+++ b/solution.py
@@ -27,7 +27,28 @@
     return [(c, c ^ 1) for c in range(n_col)]
 
 
-def make_per_device(n_col):
+def ring_gather(block, axis, n):
+    i = lax.axis_index(axis)
+    fwd = bwd = block
+    by_off = {0: block}
+    for step in range(1, n // 2 + 1):
+        ahead = [(j, (j + 1) % n) for j in range(n)]
+        behind = [(j, (j - 1) % n) for j in range(n)]
+        if 2 * step == n:
+            half = block.shape[-1] // 2
+            from_behind = lax.ppermute(fwd[..., :half], axis, ahead)
+            from_ahead = lax.ppermute(bwd[..., half:], axis, behind)
+            by_off[step] = jnp.concatenate([from_behind, from_ahead], axis=-1)
+        else:
+            fwd = lax.ppermute(fwd, axis, ahead)
+            bwd = lax.ppermute(bwd, axis, behind)
+            by_off[-step % n] = fwd
+            by_off[step] = bwd
+    stacked = jnp.stack([by_off[d] for d in range(n)], axis=0)
+    return jnp.roll(stacked, i, axis=0)
+
+
+def make_per_device(n_col, n_z, n_y):
     n_x = n_col // 2
 
     def per_device(saved_input, out_grad, weight):
@@ -35,8 +56,13 @@
         x = c // 2
         k = c % 2
 
-        grad_y = lax.all_gather(out_grad, "y", axis=0, tiled=True)
-        grad_all = lax.all_gather(grad_y, "z", axis=0, tiled=True)
+        tokens = out_grad.shape[0] * n_z * n_y
+        half = out_grad.shape[1] // 2
+        part_a = ring_gather(ring_gather(out_grad[:, :half], "z", n_z), "y", n_y)
+        part_b = ring_gather(ring_gather(out_grad[:, half:], "y", n_y), "z", n_z)
+        part_a = jnp.swapaxes(part_a, 0, 1).reshape((tokens, half))
+        part_b = part_b.reshape((tokens, out_grad.shape[1] - half))
+        grad_all = jnp.concatenate([part_a, part_b], axis=1)
 
         got = [saved_input]
         for s in range(1, n_x):
@@ -83,6 +109,6 @@
     in_specs = (P(COL, row), P(row, COL), P(row, COL))
     out_specs = (P(COL, row), P(row, COL))
     return jax.shard_map(
-        make_per_device(n_col),
+        make_per_device(n_col, n_row // 4, 4),
         mesh=grid, in_specs=in_specs, out_specs=out_specs, check_vma=False,
     )

time: 125 us -> 122 us (0.976)
  starting transfers between devices: 8.6 us -> 55.4 us
  waiting for transfers between devices: 62.7 us -> 26.6 us
  between operations: 14.2 us -> 1.11 us
  local copies, waits for them, and re-layouts: 4.37 us -> 17.4 us
  blocking collectives: 13 us -> 0 us
  matrix products: 15.2 us -> 12.5 us
  other arithmetic: 7.34 us -> 8.96 us
    all_gather x1 -> x0, waiting for transfers between devices: 45 us -> none  [per_device(): grad_all = lax.all_gather(grad_y, 'z', axis=0, tiled=True)]
    ppermute x0 -> x24, starting transfers between devices: none -> 34.2 us  [the longest x8 21 us: ring_gather(): bwd = lax.ppermute(bwd, axis, behind)]
    all_gather x1 -> x0, blocking collectives: 13 us -> none  [per_device(): grad_y = lax.all_gather(out_grad, 'y', axis=0, tiled=True)]
    ppermute x1, starting transfers between devices: 1.24 us -> 10.9 us  [per_device(): chip_sum = mine + lax.ppermute(theirs, COL, core_swap(n_col))]
    unnamed x6 -> x51, local copies, waits for them, and re-layouts: 1.7 us -> 11.1 us
    ppermute x0 -> x24, waiting for transfers between devices: none -> 9.15 us  [the longest x4 4.05 us: ring_gather(): from_behind = lax.ppermute(fwd[..., :half], axis, ahead)]
    ppermute x3, starting transfers between devices: 3.68 us -> 7.07 us  [per_device(): got.append(lax.ppermute(saved_input, COL, chip_shift(n_col, s)))]
    dot_general x1, matrix products: 7.9 us -> 5.06 us  [per_device(): lax.dot_general(grad_all, weight, (((1,), (1,)), ((), ())), preferred_ele...]
  transfers between devices with their start and end apart: 9 -> 32, of which waited for: 5 -> 13; matrix products, arithmetic and copies ran while one was open for 16% -> 24% of each run, Pallas kernels for 0% -> 0%
where the time goes in v3:
time: 122 us
  starting transfers between devices  55.4 us (45%)
  waiting for transfers between devices  26.6 us (22%)
  local copies, waits for them, and re-layouts  17.4 us (14%)
  matrix products  12.5 us (10%)
  other arithmetic  8.96 us (7%)
    ppermute x8, starting transfers between devices, ring_gather(): bwd = lax.ppermute(bwd, axis, behind)  21 us
    ppermute x3, waiting for transfers between devices, per_device(): recv = lax.ppermute(dest.astype(jnp.bfloat16), COL, chip_shift(n_col, s))  12.2 us
    ppermute x4, starting transfers between devices, ring_gather(): from_ahead = lax.ppermute(bwd[..., half:], axis, behind)  11.7 us
    unnamed x51, local copies, waits for them, and re-layouts  11.1 us
    ppermute x1, starting transfers between devices, per_device(): chip_sum = mine + lax.ppermute(theirs, COL, core_swap(n_col))  10.9 us
    dot_general x1, matrix products, per_device(): lax.dot_general(hidden, grad_all, (((0,), (0,)), ((), ())), preferred_ele...  7.4 us
    ppermute x3, starting transfers between devices, per_device(): got.append(lax.ppermute(saved_input, COL, chip_shift(n_col, s)))  7.07 us
    ppermute x1, waiting for transfers between devices, per_device(): other_by_x = lax.ppermute(mine_by_x, COL, core_swap(n_col))  5.22 us
  transfers between devices with their start and end apart: 32, of which 13 were waited for; matrix products, arithmetic and copies ran while one was open for 24% of the time, Pallas kernels for 0%

profile of v3, /device:TPU:1, one launch (start us, length us, event | category | flops | bytes accessed | tf_op | source)
XLA Modules:
  0.0 121.9 jit_solution(13545131967628503203)
XLA Ops:
  0.6 0.9 fusion.38
  1.5 6.5 %collective-permute-start = (bf16[32,768]{1,0:T(8,128)(2,1)S(1)}, bf16[32,768]{1,0:T(8,128)(2,1)S(1)}, u32[]{:S(2)}, u32[]{:S(2)}) collective-permute-start(bf16[32,768]{1,0:T(8,128)(2,1)S(1)} %get-tuple-element.11), channel_id=1, source_target_pairs={{0,224},{32,0},{64,32},{96,64},{128,96},{160,128},{192,160},{224,1... | collective-permute-start | bytes 147464 | tf_op jit(solution)/shard_map/ppermute | solution.py:44
  8.0 2.7 %collective-permute-start.12 = (bf16[32,768]{1,0:T(8,128)(2,1)S(1)}, bf16[32,768]{1,0:T(8,128)(2,1)S(1)}, u32[]{:S(2)}, u32[]{:S(2)}) collective-permute-start(bf16[32,768]{1,0:T(8,128)(2,1)S(1)} %get-tuple-element.12), channel_id=1, source_target_pairs={{0,24},{8,0},{16,8},{24,16},{1,25},{9,1},{17,9},{25,17},{2,26},{10... | collective-permute-start | bytes 147464 | tf_op jit(solution)/shard_map/ppermute | solution.py:44
  11.9 3.0 %collective-permute-start.15 = (bf16[32,384]{1,0:T(8,128)(2,1)S(1)}, bf16[32,384]{1,0:T(8,128)(2,1)S(1)}, u32[]{:S(2)}, u32[]{:S(2)}) collective-permute-start(bf16[32,384]{1,0:T(8,128)(2,1)S(1)} %slice.47), channel_id=1, source_target_pairs={{0,24},{8,0},{16,8},{24,16},{1,25},{9,1},{17,9},{25,17},{2,26},{10... | collective-permute-start | bytes 73736 | tf_op jit(solution)/shard_map/ppermute | solution.py:40
  14.9 2.8 %collective-permute-start.1 = (bf16[32,768]{1,0:T(8,128)(2,1)S(1)}, bf16[32,768]{1,0:T(8,128)(2,1)S(1)}, u32[]{:S(2)}, u32[]{:S(2)}) collective-permute-start(bf16[32,768]{1,0:T(8,128)(2,1)S(1)} %collective-permute-done), channel_id=1, source_target_pairs={{0,224},{32,0},{64,32},{96,64},{128,96},{160,128},{192,160},{224,1... | collective-permute-start | bytes 147464 | tf_op jit(solution)/shard_map/ppermute | solution.py:44
  17.8 1.0 collective-permute-done.14
  18.8 3.0 %collective-permute-start.2 = (bf16[32,768]{1,0:T(8,128)(2,1)S(1)}, bf16[32,768]{1,0:T(8,128)(2,1)S(1)}, u32[]{:S(2)}, u32[]{:S(2)}) collective-permute-start(bf16[32,768]{1,0:T(8,128)(2,1)S(1)} %collective-permute-done.1), channel_id=1, source_target_pairs={{0,224},{32,0},{64,32},{96,64},{128,96},{160,128},{192,160},{224,1... | collective-permute-start | bytes 147464 | tf_op jit(solution)/shard_map/ppermute | solution.py:44
  21.9 1.1 collective-permute-done.2
  23.0 3.0 %collective-permute-start.7 = (bf16[32,384]{1,0:T(8,128)(2,1)S(1)}, bf16[32,384]{1,0:T(8,128)(2,1)S(1)}, u32[]{:S(2)}, u32[]{:S(2)}) collective-permute-start(bf16[32,384]{1,0:T(8,128)(2,1)S(1)} %slice.43), channel_id=1, source_target_pairs={{0,224},{32,0},{64,32},{96,64},{128,96},{160,128},{192,160},{224,1... | collective-permute-start | bytes 73736 | tf_op jit(solution)/shard_map/ppermute | solution.py:40
  26.9 3.0 %collective-permute-done.6 = bf16[32,384]{1,0:T(8,128)(2,1)S(1)} collective-permute-done((bf16[32,384]{1,0:T(8,128)(2,1)S(1)}, bf16[32,384]{1,0:T(8,128)(2,1)S(1)}, u32[]{:S(2)}, u32[]{:S(2)}) %collective-permute-start.6) | collective-permute-done | bytes 24608 | tf_op jit(solution)/shard_map/ppermute | solution.py:39
  31.9 1.1 collective-permute-start.19
  34.0 2.7 %collective-permute-start.8 = (bf16[8,32,768]{2,1,0:T(8,128)(2,1)S(1)}, bf16[8,32,768]{2,1,0:T(8,128)(2,1)S(1)}, u32[]{:S(2)}, u32[]{:S(2)}) collective-permute-start(bf16[8,32,768]{2,1,0:T(8,128)(2,1)S(1)} %get-tuple-element.3), channel_id=1, source_target_pairs={{0,24},{8,0},{16,8},{24,16},{1,25},{9,1},{17,9},{25,17},{2,26},{10... | collective-permute-start | bytes 1179656 | tf_op jit(solution)/shard_map/ppermute | solution.py:44
  36.6 2.5 %collective-permute-start.30 = (bf16[128,1536]{1,0:T(8,128)(2,1)S(1)}, bf16[128,1536]{1,0:T(8,128)(2,1)S(1)}, u32[]{:S(2)}, u32[]{:S(2)}) collective-permute-start(bf16[128,1536]{1,0:T(8,128)(2,1)S(1)} %copy-done.5), channel_id=1, source_target_pairs={{0,6},{1,7},{2,0},{3,1},{4,2},{5,3},{6,4},{7,5},{8,14},{9,15},{10,... | collective-permute-start | bytes 1179656 | tf_op jit(solution)/shard_map/ppermute | solution.py:69
  39.1 1.6 %collective-permute-start.17 = (bf16[4,32,768]{2,1,0:T(8,128)(2,1)S(1)}, bf16[4,32,768]{2,1,0:T(8,128)(2,1)S(1)}, u32[]{:S(2)}, u32[]{:S(2)}) collective-permute-start(bf16[4,32,768]{2,1,0:T(8,128)(2,1)S(1)} %collective-permute-done.16), channel_id=1, source_target_pairs={{0,224},{32,0},{64,32},{96,64},{128,96},{160,128},{192,160},{224,1... | collective-permute-start | bytes 589832 | tf_op jit(solution)/shard_map/ppermute | solution.py:44
  41.4 3.2 %collective-permute-start.11 = (bf16[8,32,384]{2,1,0:T(8,128)(2,1)S(1)}, bf16[8,32,384]{2,1,0:T(8,128)(2,1)S(1)}, u32[]{:S(2)}, u32[]{:S(2)}) collective-permute-start(bf16[8,32,384]{2,1,0:T(8,128)(2,1)S(1)} %slice.45), channel_id=1, source_target_pairs={{0,24},{8,0},{16,8},{24,16},{1,25},{9,1},{17,9},{25,17},{2,26},{10... | collective-permute-start | bytes 589832 | tf_op jit(solution)/shard_map/ppermute | solution.py:40
  45.5 1.5 %collective-permute-start.18 = (bf16[4,32,768]{2,1,0:T(8,128)(2,1)S(1)}, bf16[4,32,768]{2,1,0:T(8,128)(2,1)S(1)}, u32[]{:S(2)}, u32[]{:S(2)}) collective-permute-start(bf16[4,32,768]{2,1,0:T(8,128)(2,1)S(1)} %collective-permute-done.17), channel_id=1, source_target_pairs={{0,224},{32,0},{64,32},{96,64},{128,96},{160,128},{192,160},{224,1... | collective-permute-start | bytes 589832 | tf_op jit(solution)/shard_map/ppermute | solution.py:44
  48.8 1.7 %collective-permute-done.18 = bf16[4,32,768]{2,1,0:T(8,128)(2,1)S(1)} collective-permute-done((bf16[4,32,768]{2,1,0:T(8,128)(2,1)S(1)}, bf16[4,32,768]{2,1,0:T(8,128)(2,1)S(1)}, u32[]{:S(2)}, u32[]{:S(2)}) %collective-permute-start.18) | collective-permute-done | bytes 196640 | tf_op jit(solution)/shard_map/ppermute | solution.py:44
  50.5 3.8 %collective-permute-start.29 = (bf16[128,1536]{1,0:T(8,128)(2,1)S(1)}, bf16[128,1536]{1,0:T(8,128)(2,1)S(1)}, u32[]{:S(2)}, u32[]{:S(2)}) collective-permute-start(bf16[128,1536]{1,0:T(8,128)(2,1)S(1)} %copy-done.5), channel_id=1, source_target_pairs={{0,4},{1,5},{2,6},{3,7},{4,0},{5,1},{6,2},{7,3},{8,12},{9,13},{10,... | collective-permute-start | bytes 1179656 | tf_op jit(solution)/shard_map/ppermute | solution.py:69
  55.1 2.6 %collective-permute-start.23 = (bf16[4,32,384]{2,1,0:T(8,128)(2,1)S(1)}, bf16[4,32,384]{2,1,0:T(8,128)(2,1)S(1)}, u32[]{:S(2)}, u32[]{:S(2)}) collective-permute-start(bf16[4,32,384]{2,1,0:T(8,128)(2,1)S(1)} %slice.49), channel_id=1, source_target_pairs={{0,224},{32,0},{64,32},{96,64},{128,96},{160,128},{192,160},{224,1... | collective-permute-start | bytes 294920 | tf_op jit(solution)/shard_map/ppermute | solution.py:40
  63.2 1.6 %constant_dynamic-slice_fusion.2 = bf16[4,8,32,768]{3,2,0,1:T(8,128)(2,1)S(1)} fusion(bf16[8,8,32,768]{3,2,0,1:T(8,128)(2,1)} %bitcast_dynamic-update-slice_fusion.3, s32[]{:T(128)S(6)} %select_n.136), kind=kLoop, calls=%fused_computation.106 | loop fusion | bytes 3145732 | tf_op jit(solution)/shard_map/jit(_roll_dynamic)/dynamic_slice | solution.py:48
  66.1 5.1 %fusion.10 = f32[1024,1536]{1,0:T(8,128)S(1)} fusion(bf16[1536,1536]{1,0:T(8,128)(2,1)S(1)} %bitcast.140, bf16[1024,768]{1,0:T(8,128)(2,1)S(1)} %bitcast.132, bf16[1024,768]{1,0:T(8,128)(2,1)S(1)} %bitcast.130), kind=kOutput, calls=%fused_computation.20 | convolution fusion | flops 4838129664 | bytes 14155776 | tf_op jit(solution)/shard_map/dot_general | solution.py:84
  71.2 2.0 %dynamic-slice_bitcast_fusion = f32[4,128,1536]{2,1,0:T(8,128)} fusion(f32[4,2,128,1536]{3,2,1,0:T(8,128)S(1)} %bitcast.127, s32[]{:T(128)S(6)} %select_n.139), kind=kLoop, calls=%fused_computation.19 | loop fusion | bytes 6291460 | tf_op jit(solution)/shard_map/jit(dynamic_index_in_dim)/squeeze | solution.py:90
  73.2 1.6 %copy-done = f32[1024,1536]{1,0:T(8,128)} copy-done((f32[1024,1536]{1,0:T(8,128)}, f32[1024,1536]{1,0:T(8,128)S(1)}, u32[]{:S(2)}) %copy-start) | copy-done | bytes 6291480
  74.8 10.9 %collective-permute-start.24 = (f32[4,128,1536]{2,1,0:T(8,128)}, f32[4,128,1536]{2,1,0:T(8,128)}, u32[]{:S(2)}, u32[]{:S(2)}) collective-permute-start(f32[4,128,1536]{2,1,0:T(8,128)} %dynamic-slice_bitcast_fusion), channel_id=1, source_target_pairs={{0,1},{1,0},{2,3},{3,2},{4,5},{5,4},{6,7},{7,6},{8,9},{9,8},{10,11... | collective-permute-start | bytes 9437192 | tf_op jit(solution)/shard_map/ppermute | solution.py:91
  86.7 1.4 %broadcast_select_fusion = bf16[4,128,1536]{2,1,0:T(8,128)(2,1)} fusion(bf16[4,128,1536]{2,1,0:T(8,128)(2,1)S(1)} %gather_fusion, pred[4]{0:T(512)(128)(4,1)S(1)} %compare_and_fusion), kind=kLoop, calls=%fused_computation.30 | loop fusion | flops 786432 | bytes 3145732 | tf_op jit(solution)/shard_map/jit(_take)/select_n | solution.py:72
  88.3 5.2 %collective-permute-done.31 = bf16[4,128,1536]{2,1,0:T(8,128)(2,1)S(1)} collective-permute-done((bf16[4,128,1536]{2,1,0:T(8,128)(2,1)}, bf16[4,128,1536]{2,1,0:T(8,128)(2,1)S(1)}, u32[]{:S(2)}, u32[]{:S(2)}) %collective-permute-start.31) | collective-permute-done | bytes 1572896 | tf_op jit(solution)/shard_map/ppermute | solution.py:73
  94.0 3.6 %bitcast_add_fusion = f32[4,128,1536]{2,1,0:T(8,128)S(1)} fusion(f32[4,128,1536]{2,1,0:T(8,128)} %collective-permute-done.24, f32[4,2,128,1536]{3,2,1,0:T(8,128)} %bitcast.128, s32[]{:T(128)S(6)} %select_n.138), kind=kLoop, calls=%fused_computation.14 | loop fusion | flops 786432 | bytes 9437188 | tf_op jit(solution)/shard_map/add | solution.py:91
  97.7 1.8 %collective-permute-start.27 = (bf16[128,1536]{1,0:T(8,128)(2,1)S(1)}, bf16[128,1536]{1,0:T(8,128)(2,1)S(1)}, u32[]{:S(2)}, u32[]{:S(2)}) collective-permute-start(bf16[128,1536]{1,0:T(8,128)(2,1)S(1)} %get-tuple-element.7), channel_id=1, source_target_pairs={{0,6},{1,7},{2,0},{3,1},{4,2},{5,3},{6,4},{7,5},{8,14},{9,15},{10,... | collective-permute-start | bytes 1179656 | tf_op jit(solution)/shard_map/ppermute | solution.py:95
  100.9 7.4 %convolution_convert_fusion = bf16[1536,1536]{1,0:T(8,128)(2,1)} fusion(bf16[1024,1536]{1,0:T(8,128)(2,1)S(1)} %bitcast.129, bf16[1024,768]{1,0:T(8,128)(2,1)S(1)} %bitcast.133, bf16[1024,768]{1,0:T(8,128)(2,1)S(1)} %bitcast.131), kind=kOutput, calls=%fused_computation.6 | convolution fusion | flops 4856217600 | bytes 11010048 | tf_op jit(solution)/shard_map/dot_general | solution.py:80
  108.3 2.8 %collective-permute-done.26 = bf16[128,1536]{1,0:T(8,128)(2,1)S(1)} collective-permute-done((bf16[128,1536]{1,0:T(8,128)(2,1)S(1)}, bf16[128,1536]{1,0:T(8,128)(2,1)S(1)}, u32[]{:S(2)}, u32[]{:S(2)}) %collective-permute-start.26) | collective-permute-done | bytes 393248 | tf_op jit(solution)/shard_map/ppermute | solution.py:95
  111.1 9.4 %collective-permute-done.25 = bf16[128,1536]{1,0:T(8,128)(2,1)S(1)} collective-permute-done((bf16[128,1536]{1,0:T(8,128)(2,1)S(1)}, bf16[128,1536]{1,0:T(8,128)(2,1)S(1)}, u32[]{:S(2)}, u32[]{:S(2)}) %collective-permute-start.25) | collective-permute-done | bytes 393248 | tf_op jit(solution)/shard_map/ppermute | solution.py:95
  120.5 1.4 %fusion.18 = bf16[128,1536]{1,0:T(8,128)(2,1)} fusion(bf16[128,1536]{1,0:T(8,128)(2,1)S(1)} %copy-done.5, bf16[128,1536]{1,0:T(8,128)(2,1)S(1)} %collective-permute-done.27, bf16[128,1536]{1,0:T(8,128)(2,1)S(1)} %collective-permute-done.26, bf16[128,1536]{1,0:T(8,128)(2,1)S(1)} %collective-permute-done.25, f32[4,128,1536]{2,1,0:T(8,128)S(1)} %bitcast_add_fusion, ...), kind=kLoop, calls=%fused_computation.38 | loop fusion | flops 5111808 | bytes 2752516 | tf_op jit(solution)/shard_map/convert_element_type | solution.py:99
  (121 shorter events, 19.2 us)
Async XLA Ops:
  1.5 13.4 %collective-permute-start = (bf16[32,768]{1,0:T(8,128)(2,1)S(1)}, bf16[32,768]{1,0:T(8,128)(2,1)S(1)}, u32[]{:S(2)}, u32[]{:S(2)}) collective-permute-start(bf16[32,768]{1,0:T(8,128)(2,1)S(1)} %get-tuple-element.11), channel_id=1, source_target_pairs={{0,224},{32,0},{64,32},{96,64},{128,96},{160,128},{192,160},{224,1... | collective-permute-start | bytes 147464 | tf_op jit(solution)/shard_map/ppermute | solution.py:44
  8.0 9.7 %collective-permute-start.3 = (bf16[32,768]{1,0:T(8,128)(2,1)S(1)}, bf16[32,768]{1,0:T(8,128)(2,1)S(1)}, u32[]{:S(2)}, u32[]{:S(2)}) collective-permute-start(bf16[32,768]{1,0:T(8,128)(2,1)S(1)} %get-tuple-element.11), channel_id=1, source_target_pairs={{0,32},{32,64},{64,96},{96,128},{128,160},{160,192},{192,224},{224... | collective-permute-start | bytes 147464 | tf_op jit(solution)/shard_map/ppermute | solution.py:43
  8.0 3.9 %collective-permute-start.12 = (bf16[32,768]{1,0:T(8,128)(2,1)S(1)}, bf16[32,768]{1,0:T(8,128)(2,1)S(1)}, u32[]{:S(2)}, u32[]{:S(2)}) collective-permute-start(bf16[32,768]{1,0:T(8,128)(2,1)S(1)} %get-tuple-element.12), channel_id=1, source_target_pairs={{0,24},{8,0},{16,8},{24,16},{1,25},{9,1},{17,9},{25,17},{2,26},{10... | collective-permute-start | bytes 147464 | tf_op jit(solution)/shard_map/ppermute | solution.py:44
  10.7 4.2 %collective-permute-start.13 = (bf16[32,768]{1,0:T(8,128)(2,1)S(1)}, bf16[32,768]{1,0:T(8,128)(2,1)S(1)}, u32[]{:S(2)}, u32[]{:S(2)}) collective-permute-start(bf16[32,768]{1,0:T(8,128)(2,1)S(1)} %get-tuple-element.12), channel_id=1, source_target_pairs={{0,8},{8,16},{16,24},{24,0},{1,9},{9,17},{17,25},{25,1},{2,10},{10... | collective-permute-start | bytes 147464 | tf_op jit(solution)/shard_map/ppermute | solution.py:43
  11.9 5.9 %collective-permute-start.15 = (bf16[32,384]{1,0:T(8,128)(2,1)S(1)}, bf16[32,384]{1,0:T(8,128)(2,1)S(1)}, u32[]{:S(2)}, u32[]{:S(2)}) collective-permute-start(bf16[32,384]{1,0:T(8,128)(2,1)S(1)} %slice.47), channel_id=1, source_target_pairs={{0,24},{8,0},{16,8},{24,16},{1,25},{9,1},{17,9},{25,17},{2,26},{10... | collective-permute-start | bytes 73736 | tf_op jit(solution)/shard_map/ppermute | solution.py:40
  14.9 3.9 %collective-permute-start.14 = (bf16[32,384]{1,0:T(8,128)(2,1)S(1)}, bf16[32,384]{1,0:T(8,128)(2,1)S(1)}, u32[]{:S(2)}, u32[]{:S(2)}) collective-permute-start(bf16[32,384]{1,0:T(8,128)(2,1)S(1)} %slice.46), channel_id=1, source_target_pairs={{0,8},{8,16},{16,24},{24,0},{1,9},{9,17},{17,25},{25,1},{2,10},{10... | collective-permute-start | bytes 73736 | tf_op jit(solution)/shard_map/ppermute | solution.py:39
  14.9 3.9 %collective-permute-start.1 = (bf16[32,768]{1,0:T(8,128)(2,1)S(1)}, bf16[32,768]{1,0:T(8,128)(2,1)S(1)}, u32[]{:S(2)}, u32[]{:S(2)}) collective-permute-start(bf16[32,768]{1,0:T(8,128)(2,1)S(1)} %collective-permute-done), channel_id=1, source_target_pairs={{0,224},{32,0},{64,32},{96,64},{128,96},{160,128},{192,160},{224,1... | collective-permute-start | bytes 147464 | tf_op jit(solution)/shard_map/ppermute | solution.py:44
  17.7 4.2 %collective-permute-start.4 = (bf16[32,768]{1,0:T(8,128)(2,1)S(1)}, bf16[32,768]{1,0:T(8,128)(2,1)S(1)}, u32[]{:S(2)}, u32[]{:S(2)}) collective-permute-start(bf16[32,768]{1,0:T(8,128)(2,1)S(1)} %collective-permute-done.3), channel_id=1, source_target_pairs={{0,32},{32,64},{64,96},{96,128},{128,160},{160,192},{192,224},{224... | collective-permute-start | bytes 147464 | tf_op jit(solution)/shard_map/ppermute | solution.py:43
  18.8 4.2 %collective-permute-start.2 = (bf16[32,768]{1,0:T(8,128)(2,1)S(1)}, bf16[32,768]{1,0:T(8,128)(2,1)S(1)}, u32[]{:S(2)}, u32[]{:S(2)}) collective-permute-start(bf16[32,768]{1,0:T(8,128)(2,1)S(1)} %collective-permute-done.1), channel_id=1, source_target_pairs={{0,224},{32,0},{64,32},{96,64},{128,96},{160,128},{192,160},{224,1... | collective-permute-start | bytes 147464 | tf_op jit(solution)/shard_map/ppermute | solution.py:44
  21.9 4.2 %collective-permute-start.5 = (bf16[32,768]{1,0:T(8,128)(2,1)S(1)}, bf16[32,768]{1,0:T(8,128)(2,1)S(1)}, u32[]{:S(2)}, u32[]{:S(2)}) collective-permute-start(bf16[32,768]{1,0:T(8,128)(2,1)S(1)} %collective-permute-done.4), channel_id=1, source_target_pairs={{0,32},{32,64},{64,96},{96,128},{128,160},{160,192},{192,224},{224... | collective-permute-start | bytes 147464 | tf_op jit(solution)/shard_map/ppermute | solution.py:43
  23.0 3.9 %collective-permute-start.7 = (bf16[32,384]{1,0:T(8,128)(2,1)S(1)}, bf16[32,384]{1,0:T(8,128)(2,1)S(1)}, u32[]{:S(2)}, u32[]{:S(2)}) collective-permute-start(bf16[32,384]{1,0:T(8,128)(2,1)S(1)} %slice.43), channel_id=1, source_target_pairs={{0,224},{32,0},{64,32},{96,64},{128,96},{160,128},{192,160},{224,1... | collective-permute-start | bytes 73736 | tf_op jit(solution)/shard_map/ppermute | solution.py:40
  26.1 3.9 %collective-permute-start.6 = (bf16[32,384]{1,0:T(8,128)(2,1)S(1)}, bf16[32,384]{1,0:T(8,128)(2,1)S(1)}, u32[]{:S(2)}, u32[]{:S(2)}) collective-permute-start(bf16[32,384]{1,0:T(8,128)(2,1)S(1)} %slice.42), channel_id=1, source_target_pairs={{0,32},{32,64},{64,96},{96,128},{128,160},{160,192},{192,224},{224... | collective-permute-start | bytes 73736 | tf_op jit(solution)/shard_map/ppermute | solution.py:39
  31.6 7.5 %collective-permute-start.16 = (bf16[4,32,768]{2,1,0:T(8,128)(2,1)S(1)}, bf16[4,32,768]{2,1,0:T(8,128)(2,1)S(1)}, u32[]{:S(2)}, u32[]{:S(2)}) collective-permute-start(bf16[4,32,768]{2,1,0:T(8,128)(2,1)S(1)} %get-tuple-element.5), channel_id=1, source_target_pairs={{0,224},{32,0},{64,32},{96,64},{128,96},{160,128},{192,160},{224,1... | collective-permute-start | bytes 589832 | tf_op jit(solution)/shard_map/ppermute | solution.py:44
  31.9 8.8 %collective-permute-start.19 = (bf16[4,32,768]{2,1,0:T(8,128)(2,1)S(1)}, bf16[4,32,768]{2,1,0:T(8,128)(2,1)S(1)}, u32[]{:S(2)}, u32[]{:S(2)}) collective-permute-start(bf16[4,32,768]{2,1,0:T(8,128)(2,1)S(1)} %get-tuple-element.5), channel_id=1, source_target_pairs={{0,32},{32,64},{64,96},{96,128},{128,160},{160,192},{192,224},{224... | collective-permute-start | bytes 589832 | tf_op jit(solution)/shard_map/ppermute | solution.py:43
  34.0 7.4 %collective-permute-start.8 = (bf16[8,32,768]{2,1,0:T(8,128)(2,1)S(1)}, bf16[8,32,768]{2,1,0:T(8,128)(2,1)S(1)}, u32[]{:S(2)}, u32[]{:S(2)}) collective-permute-start(bf16[8,32,768]{2,1,0:T(8,128)(2,1)S(1)} %get-tuple-element.3), channel_id=1, source_target_pairs={{0,24},{8,0},{16,8},{24,16},{1,25},{9,1},{17,9},{25,17},{2,26},{10... | collective-permute-start | bytes 1179656 | tf_op jit(solution)/shard_map/ppermute | solution.py:44
  36.6 8.1 %collective-permute-start.9 = (bf16[8,32,768]{2,1,0:T(8,128)(2,1)S(1)}, bf16[8,32,768]{2,1,0:T(8,128)(2,1)S(1)}, u32[]{:S(2)}, u32[]{:S(2)}) collective-permute-start(bf16[8,32,768]{2,1,0:T(8,128)(2,1)S(1)} %get-tuple-element.3), channel_id=1, source_target_pairs={{0,8},{8,16},{16,24},{24,0},{1,9},{9,17},{17,25},{25,1},{2,10},{10... | collective-permute-start | bytes 1179656 | tf_op jit(solution)/shard_map/ppermute | solution.py:43
  36.6 49.1 %collective-permute-start.30 = (bf16[128,1536]{1,0:T(8,128)(2,1)S(1)}, bf16[128,1536]{1,0:T(8,128)(2,1)S(1)}, u32[]{:S(2)}, u32[]{:S(2)}) collective-permute-start(bf16[128,1536]{1,0:T(8,128)(2,1)S(1)} %copy-done.5), channel_id=1, source_target_pairs={{0,6},{1,7},{2,0},{3,1},{4,2},{5,3},{6,4},{7,5},{8,14},{9,15},{10,... | collective-permute-start | bytes 1179656 | tf_op jit(solution)/shard_map/ppermute | solution.py:69
  39.1 6.4 %collective-permute-start.17 = (bf16[4,32,768]{2,1,0:T(8,128)(2,1)S(1)}, bf16[4,32,768]{2,1,0:T(8,128)(2,1)S(1)}, u32[]{:S(2)}, u32[]{:S(2)}) collective-permute-start(bf16[4,32,768]{2,1,0:T(8,128)(2,1)S(1)} %collective-permute-done.16), channel_id=1, source_target_pairs={{0,224},{32,0},{64,32},{96,64},{128,96},{160,128},{192,160},{224,1... | collective-permute-start | bytes 589832 | tf_op jit(solution)/shard_map/ppermute | solution.py:44
  40.7 6.4 %collective-permute-start.20 = (bf16[4,32,768]{2,1,0:T(8,128)(2,1)S(1)}, bf16[4,32,768]{2,1,0:T(8,128)(2,1)S(1)}, u32[]{:S(2)}, u32[]{:S(2)}) collective-permute-start(bf16[4,32,768]{2,1,0:T(8,128)(2,1)S(1)} %collective-permute-done.19), channel_id=1, source_target_pairs={{0,32},{32,64},{64,96},{96,128},{128,160},{160,192},{192,224},{224... | collective-permute-start | bytes 589832 | tf_op jit(solution)/shard_map/ppermute | solution.py:43
  41.4 13.7 %collective-permute-start.11 = (bf16[8,32,384]{2,1,0:T(8,128)(2,1)S(1)}, bf16[8,32,384]{2,1,0:T(8,128)(2,1)S(1)}, u32[]{:S(2)}, u32[]{:S(2)}) collective-permute-start(bf16[8,32,384]{2,1,0:T(8,128)(2,1)S(1)} %slice.45), channel_id=1, source_target_pairs={{0,24},{8,0},{16,8},{24,16},{1,25},{9,1},{17,9},{25,17},{2,26},{10... | collective-permute-start | bytes 589832 | tf_op jit(solution)/shard_map/ppermute | solution.py:40
  44.7 13.0 %collective-permute-start.10 = (bf16[8,32,384]{2,1,0:T(8,128)(2,1)S(1)}, bf16[8,32,384]{2,1,0:T(8,128)(2,1)S(1)}, u32[]{:S(2)}, u32[]{:S(2)}) collective-permute-start(bf16[8,32,384]{2,1,0:T(8,128)(2,1)S(1)} %slice.44), channel_id=1, source_target_pairs={{0,8},{8,16},{16,24},{24,0},{1,9},{9,17},{17,25},{25,1},{2,10},{10... | collective-permute-start | bytes 589832 | tf_op jit(solution)/shard_map/ppermute | solution.py:39
  45.5 4.9 %collective-permute-start.18 = (bf16[4,32,768]{2,1,0:T(8,128)(2,1)S(1)}, bf16[4,32,768]{2,1,0:T(8,128)(2,1)S(1)}, u32[]{:S(2)}, u32[]{:S(2)}) collective-permute-start(bf16[4,32,768]{2,1,0:T(8,128)(2,1)S(1)} %collective-permute-done.17), channel_id=1, source_target_pairs={{0,224},{32,0},{64,32},{96,64},{128,96},{160,128},{192,160},{224,1... | collective-permute-start | bytes 589832 | tf_op jit(solution)/shard_map/ppermute | solution.py:44
  47.0 7.3 %collective-permute-start.21 = (bf16[4,32,768]{2,1,0:T(8,128)(2,1)S(1)}, bf16[4,32,768]{2,1,0:T(8,128)(2,1)S(1)}, u32[]{:S(2)}, u32[]{:S(2)}) collective-permute-start(bf16[4,32,768]{2,1,0:T(8,128)(2,1)S(1)} %collective-permute-done.20), channel_id=1, source_target_pairs={{0,32},{32,64},{64,96},{96,128},{128,160},{160,192},{192,224},{224... | collective-permute-start | bytes 589832 | tf_op jit(solution)/shard_map/ppermute | solution.py:43
  50.5 35.3 %collective-permute-start.29 = (bf16[128,1536]{1,0:T(8,128)(2,1)S(1)}, bf16[128,1536]{1,0:T(8,128)(2,1)S(1)}, u32[]{:S(2)}, u32[]{:S(2)}) collective-permute-start(bf16[128,1536]{1,0:T(8,128)(2,1)S(1)} %copy-done.5), channel_id=1, source_target_pairs={{0,4},{1,5},{2,6},{3,7},{4,0},{5,1},{6,2},{7,3},{8,12},{9,13},{10,... | collective-permute-start | bytes 1179656 | tf_op jit(solution)/shard_map/ppermute | solution.py:69
  54.3 31.5 %collective-permute-start.28 = (bf16[128,1536]{1,0:T(8,128)(2,1)S(1)}, bf16[128,1536]{1,0:T(8,128)(2,1)S(1)}, u32[]{:S(2)}, u32[]{:S(2)}) collective-permute-start(bf16[128,1536]{1,0:T(8,128)(2,1)S(1)} %copy-done.5), channel_id=1, source_target_pairs={{0,2},{1,3},{2,4},{3,5},{4,6},{5,7},{6,0},{7,1},{8,10},{9,11},{10,... | collective-permute-start | bytes 1179656 | tf_op jit(solution)/shard_map/ppermute | solution.py:69
  55.1 9.7 %collective-permute-start.23 = (bf16[4,32,384]{2,1,0:T(8,128)(2,1)S(1)}, bf16[4,32,384]{2,1,0:T(8,128)(2,1)S(1)}, u32[]{:S(2)}, u32[]{:S(2)}) collective-permute-start(bf16[4,32,384]{2,1,0:T(8,128)(2,1)S(1)} %slice.49), channel_id=1, source_target_pairs={{0,224},{32,0},{64,32},{96,64},{128,96},{160,128},{192,160},{224,1... | collective-permute-start | bytes 294920 | tf_op jit(solution)/shard_map/ppermute | solution.py:40
  57.7 7.1 %collective-permute-start.22 = (bf16[4,32,384]{2,1,0:T(8,128)(2,1)S(1)}, bf16[4,32,384]{2,1,0:T(8,128)(2,1)S(1)}, u32[]{:S(2)}, u32[]{:S(2)}) collective-permute-start(bf16[4,32,384]{2,1,0:T(8,128)(2,1)S(1)} %slice.48), channel_id=1, source_target_pairs={{0,32},{32,64},{64,96},{96,128},{128,160},{160,192},{192,224},{224... | collective-permute-start | bytes 294920 | tf_op jit(solution)/shard_map/ppermute | solution.py:39
  74.8 19.2 %collective-permute-start.24 = (f32[4,128,1536]{2,1,0:T(8,128)}, f32[4,128,1536]{2,1,0:T(8,128)}, u32[]{:S(2)}, u32[]{:S(2)}) collective-permute-start(f32[4,128,1536]{2,1,0:T(8,128)} %dynamic-slice_bitcast_fusion), channel_id=1, source_target_pairs={{0,1},{1,0},{2,3},{3,2},{4,5},{5,4},{6,7},{7,6},{8,9},{9,8},{10,11... | collective-permute-start | bytes 9437192 | tf_op jit(solution)/shard_map/ppermute | solution.py:91
  88.0 5.4 %collective-permute-start.31 = (bf16[4,128,1536]{2,1,0:T(8,128)(2,1)}, bf16[4,128,1536]{2,1,0:T(8,128)(2,1)S(1)}, u32[]{:S(2)}, u32[]{:S(2)}) collective-permute-start(bf16[4,128,1536]{2,1,0:T(8,128)(2,1)} %broadcast_select_fusion), channel_id=1, source_target_pairs={{0,1},{1,0},{2,3},{3,2},{4,5},{5,4},{6,7},{7,6},{8,9},{9,8},{10,11... | collective-permute-start | bytes 4718600 | tf_op jit(solution)/shard_map/ppermute | solution.py:73
  97.7 10.6 %collective-permute-start.27 = (bf16[128,1536]{1,0:T(8,128)(2,1)S(1)}, bf16[128,1536]{1,0:T(8,128)(2,1)S(1)}, u32[]{:S(2)}, u32[]{:S(2)}) collective-permute-start(bf16[128,1536]{1,0:T(8,128)(2,1)S(1)} %get-tuple-element.7), channel_id=1, source_target_pairs={{0,6},{1,7},{2,0},{3,1},{4,2},{5,3},{6,4},{7,5},{8,14},{9,15},{10,... | collective-permute-start | bytes 1179656 | tf_op jit(solution)/shard_map/ppermute | solution.py:95
  99.5 11.6 %collective-permute-start.26 = (bf16[128,1536]{1,0:T(8,128)(2,1)S(1)}, bf16[128,1536]{1,0:T(8,128)(2,1)S(1)}, u32[]{:S(2)}, u32[]{:S(2)}) collective-permute-start(bf16[128,1536]{1,0:T(8,128)(2,1)S(1)} %get-tuple-element.8), channel_id=1, source_target_pairs={{0,4},{1,5},{2,6},{3,7},{4,0},{5,1},{6,2},{7,3},{8,12},{9,13},{10,... | collective-permute-start | bytes 1179656 | tf_op jit(solution)/shard_map/ppermute | solution.py:95
  100.1 20.4 %collective-permute-start.25 = (bf16[128,1536]{1,0:T(8,128)(2,1)S(1)}, bf16[128,1536]{1,0:T(8,128)(2,1)S(1)}, u32[]{:S(2)}, u32[]{:S(2)}) collective-permute-start(bf16[128,1536]{1,0:T(8,128)(2,1)S(1)} %get-tuple-element.6), channel_id=1, source_target_pairs={{0,2},{1,3},{2,4},{3,5},{4,6},{5,7},{6,0},{7,1},{8,10},{9,11},{10,... | collective-permute-start | bytes 1179656 | tf_op jit(solution)/shard_map/ppermute | solution.py:95
  (9 other events, 92.7 us)

commit v4 on v3

--- a/solution.py
+++ b/solution.py
@@ -58,8 +58,9 @@
 
         tokens = out_grad.shape[0] * n_z * n_y
         half = out_grad.shape[1] // 2
-        part_a = ring_gather(ring_gather(out_grad[:, :half], "z", n_z), "y", n_y)
-        part_b = ring_gather(ring_gather(out_grad[:, half:], "y", n_y), "z", n_z)
+        gather_z = lambda a: lax.all_gather(a, "z", axis=0, tiled=False)
+        part_a = ring_gather(gather_z(out_grad[:, :half]), "y", n_y)
+        part_b = gather_z(ring_gather(out_grad[:, half:], "y", n_y))
         part_a = jnp.swapaxes(part_a, 0, 1).reshape((tokens, half))
         part_b = part_b.reshape((tokens, out_grad.shape[1] - half))
         grad_all = jnp.concatenate([part_a, part_b], axis=1)

time: 122 us -> 127 us (1.041)
  starting transfers between devices: 55.4 us -> 27.8 us
  blocking collectives: 0 us -> 23.7 us
  between operations: 1.11 us -> 14.3 us
  local copies, waits for them, and re-layouts: 17.4 us -> 7.99 us
  waiting for transfers between devices: 26.6 us -> 30.6 us
  matrix products: 12.5 us -> 15.4 us
  other arithmetic: 8.96 us -> 7.41 us
    all_gather x0 -> x1, blocking collectives: none -> 23.7 us  [per_device(): gather_z = lambda a: lax.all_gather(a, 'z', axis=0, tiled=False)]
    ppermute x8 -> x2, starting transfers between devices: 21 us -> 3.61 us  [ring_gather(): bwd = lax.ppermute(bwd, axis, behind)]
    unnamed x51 -> x20, local copies, waits for them, and re-layouts: 11.1 us -> 3.49 us
    ppermute x4 -> x2, starting transfers between devices: 11.7 us -> 4.11 us  [ring_gather(): from_ahead = lax.ppermute(bwd[..., half:], axis, behind)]
    ppermute x4 -> x2, waiting for transfers between devices: 0.84 us -> 4.34 us  [ring_gather(): from_ahead = lax.ppermute(bwd[..., half:], axis, behind)]
    ppermute x3, starting transfers between devices: 7.07 us -> 3.7 us  [per_device(): got.append(lax.ppermute(saved_input, COL, chip_shift(n_col, s)))]
    dot_general x1, matrix products: 5.06 us -> 7.97 us  [per_device(): lax.dot_general(grad_all, weight, (((1,), (1,)), ((), ())), preferred_ele...]
    ppermute x4 -> x2, waiting for transfers between devices: 4.05 us -> 6.29 us  [ring_gather(): from_behind = lax.ppermute(fwd[..., :half], axis, ahead)]
  transfers between devices with their start and end apart: 32 -> 17, of which waited for: 13 -> 9; matrix products, arithmetic and copies ran while one was open for 24% -> 17% of each run, Pallas kernels for 0% -> 0%
where the time goes in v4:
time: 127 us
  waiting for transfers between devices  30.6 us (24%)
  starting transfers between devices  27.8 us (22%)
  blocking collectives  23.7 us (19%)
  matrix products  15.4 us (12%)
  between operations  14.3 us (11%)
  local copies, waits for them, and re-layouts  7.99 us (6%)
  other arithmetic  7.41 us (6%)
    all_gather x1, blocking collectives, per_device(): gather_z = lambda a: lax.all_gather(a, 'z', axis=0, tiled=False)  23.7 us
    ppermute x3, waiting for transfers between devices, per_device(): recv = lax.ppermute(dest.astype(jnp.bfloat16), COL, chip_shift(n_col, s))  12.6 us
    ppermute x1, starting transfers between devices, per_device(): chip_sum = mine + lax.ppermute(theirs, COL, core_swap(n_col))  10.7 us
    dot_general x1, matrix products, per_device(): lax.dot_general(grad_all, weight, (((1,), (1,)), ((), ())), preferred_ele...  7.97 us
    dot_general x1, matrix products, per_device(): lax.dot_general(hidden, grad_all, (((0,), (0,)), ((), ())), preferred_ele...  7.39 us
    ppermute x2, waiting for transfers between devices, ring_gather(): from_behind = lax.ppermute(fwd[..., :half], axis, ahead)  6.29 us
    ppermute x1, waiting for transfers between devices, per_device(): other_by_x = lax.ppermute(mine_by_x, COL, core_swap(n_col))  5.19 us
    ppermute x2, waiting for transfers between devices, ring_gather(): from_ahead = lax.ppermute(bwd[..., half:], axis, behind)  4.34 us
  transfers between devices with their start and end apart: 17, of which 9 were waited for; matrix products, arithmetic and copies ran while one was open for 17% of the time, Pallas kernels for 0%

profile of v4, /device:TPU:1, one launch (start us, length us, event | category | flops | bytes accessed | tf_op | source)
XLA Modules:
  0.0 127.1 jit_solution(13769232388588300520)
XLA Ops:
  7.2 0.8 fusion.36
  8.0 3.6 %collective-permute-start.4 = (bf16[32,768]{1,0:T(8,128)(2,1)S(1)}, bf16[32,768]{1,0:T(8,128)(2,1)S(1)}, u32[]{:S(2)}, u32[]{:S(2)}) collective-permute-start(bf16[32,768]{1,0:T(8,128)(2,1)S(1)} %get-tuple-element.6), channel_id=1, source_target_pairs={{0,24},{8,0},{16,8},{24,16},{1,25},{9,1},{17,9},{25,17},{2,26},{10... | collective-permute-start | bytes 147464 | tf_op jit(solution)/shard_map/ppermute | solution.py:44
  11.7 0.8 bitcast_dynamic-update-slice_fusion.8
  12.8 3.0 %collective-permute-start.7 = (bf16[32,384]{1,0:T(8,128)(2,1)S(1)}, bf16[32,384]{1,0:T(8,128)(2,1)S(1)}, u32[]{:S(2)}, u32[]{:S(2)}) collective-permute-start(bf16[32,384]{1,0:T(8,128)(2,1)S(1)} %slice.29), channel_id=1, source_target_pairs={{0,24},{8,0},{16,8},{24,16},{1,25},{9,1},{17,9},{25,17},{2,26},{10... | collective-permute-start | bytes 73736 | tf_op jit(solution)/shard_map/ppermute | solution.py:40
  15.8 0.9 collective-permute-done.7
  16.8 2.9 %collective-permute-done.6 = bf16[32,384]{1,0:T(8,128)(2,1)S(1)} collective-permute-done((bf16[32,384]{1,0:T(8,128)(2,1)S(1)}, bf16[32,384]{1,0:T(8,128)(2,1)S(1)}, u32[]{:S(2)}, u32[]{:S(2)}) %collective-permute-start.6) | collective-permute-done | bytes 24608 | tf_op jit(solution)/shard_map/ppermute | solution.py:39
  19.7 0.8 bitcast_dynamic-update-slice_fusion.9
  20.6 0.7 constant_dynamic-slice_fusion
  21.3 23.7 %all-gather = bf16[256,768]{1,0:T(8,128)(2,1)S(1)} all-gather(bf16[32,768]{1,0:T(8,128)(2,1)S(1)} %get-tuple-element.5), channel_id=2, replica_groups=mesh['z'=8,'y'=4,'x'=4,'c'=2] {'z'}, dimensions={0}, use_global_device_ids=true | all-gather | bytes 442368 | tf_op jit(solution)/shard_map/all_gather | solution.py:61
  44.9 1.5 %collective-permute-start.1 = (bf16[8,32,768]{2,1,0:T(8,128)(2,1)S(1)}, bf16[8,32,768]{2,1,0:T(8,128)(2,1)S(1)}, u32[]{:S(2)}, u32[]{:S(2)}) collective-permute-start(bf16[8,32,768]{2,1,0:T(8,128)(2,1)S(1)} %bitcast.69), channel_id=1, source_target_pairs={{0,8},{8,16},{16,24},{24,0},{1,9},{9,17},{17,25},{25,1},{2,10},{10... | collective-permute-start | bytes 1179656 | tf_op jit(solution)/shard_map/ppermute | solution.py:43
  46.4 2.8 %collective-permute-start.14 = (bf16[128,1536]{1,0:T(8,128)(2,1)}, bf16[128,1536]{1,0:T(8,128)(2,1)S(1)}, u32[]{:S(2)}, u32[]{:S(2)}) collective-permute-start(bf16[128,1536]{1,0:T(8,128)(2,1)} %param.3), channel_id=1, source_target_pairs={{0,6},{1,7},{2,0},{3,1},{4,2},{5,3},{6,4},{7,5},{8,14},{9,15},{10,... | collective-permute-start | bytes 1179656 | tf_op jit(solution)/shard_map/ppermute | solution.py:70
  49.4 0.7 collective-permute-start.12
  50.1 1.8 %collective-permute-done = bf16[8,32,768]{2,1,0:T(8,128)(2,1)S(1)} collective-permute-done((bf16[8,32,768]{2,1,0:T(8,128)(2,1)S(1)}, bf16[8,32,768]{2,1,0:T(8,128)(2,1)S(1)}, u32[]{:S(2)}, u32[]{:S(2)}) %collective-permute-start) | collective-permute-done | bytes 393248 | tf_op jit(solution)/shard_map/ppermute | solution.py:44
  52.0 1.1 collective-permute-start.3
  53.2 0.5 collective-permute-start.2
  53.7 3.4 %collective-permute-done.3 = bf16[8,32,384]{2,1,0:T(8,128)(2,1)S(1)} collective-permute-done((bf16[8,32,384]{2,1,0:T(8,128)(2,1)S(1)}, bf16[8,32,384]{2,1,0:T(8,128)(2,1)S(1)}, u32[]{:S(2)}, u32[]{:S(2)}) %collective-permute-start.3) | collective-permute-done | bytes 196640 | tf_op jit(solution)/shard_map/ppermute | solution.py:40
  57.1 3.3 %collective-permute-done.2 = bf16[8,32,384]{2,1,0:T(8,128)(2,1)S(1)} collective-permute-done((bf16[8,32,384]{2,1,0:T(8,128)(2,1)S(1)}, bf16[8,32,384]{2,1,0:T(8,128)(2,1)S(1)}, u32[]{:S(2)}, u32[]{:S(2)}) %collective-permute-start.2) | collective-permute-done | bytes 196640 | tf_op jit(solution)/shard_map/ppermute | solution.py:39
  60.9 8.0 %fusion.10 = f32[1024,1536]{1,0:T(8,128)S(1)} fusion(bf16[1536,1536]{1,0:T(8,128)(2,1)} %param.5, bf16[1024,768]{1,0:T(8,128)(2,1)} %bitcast.80, bf16[1024,768]{1,0:T(8,128)(2,1)S(1)} %bitcast.73), kind=kOutput, calls=%fused_computation.20 | convolution fusion | flops 4838129664 | bytes 14155776 | tf_op jit(solution)/shard_map/dot_general | solution.py:85
  68.9 1.9 %dynamic-slice_bitcast_fusion = f32[4,128,1536]{2,1,0:T(8,128)} fusion(f32[4,2,128,1536]{3,2,1,0:T(8,128)S(1)} %bitcast.66, s32[]{:T(128)S(6)} %select_n.121), kind=kLoop, calls=%fused_computation.19 | loop fusion | bytes 6291460 | tf_op jit(solution)/shard_map/jit(dynamic_index_in_dim)/squeeze | solution.py:91
  70.8 1.7 %copy-done = f32[1024,1536]{1,0:T(8,128)} copy-done((f32[1024,1536]{1,0:T(8,128)}, f32[1024,1536]{1,0:T(8,128)S(1)}, u32[]{:S(2)}) %copy-start) | copy-done | bytes 6291480
  72.5 10.7 %collective-permute-start.8 = (f32[4,128,1536]{2,1,0:T(8,128)}, f32[4,128,1536]{2,1,0:T(8,128)}, u32[]{:S(2)}, u32[]{:S(2)}) collective-permute-start(f32[4,128,1536]{2,1,0:T(8,128)} %dynamic-slice_bitcast_fusion), channel_id=1, source_target_pairs={{0,1},{1,0},{2,3},{3,2},{4,5},{5,4},{6,7},{7,6},{8,9},{9,8},{10,11... | collective-permute-start | bytes 9437192 | tf_op jit(solution)/shard_map/ppermute | solution.py:92
  83.5 0.6 gather_fusion
  84.2 1.4 %broadcast_select_fusion = bf16[4,128,1536]{2,1,0:T(8,128)(2,1)} fusion(bf16[4,128,1536]{2,1,0:T(8,128)(2,1)S(1)} %gather_fusion, pred[4]{0:T(512)(128)(4,1)S(1)} %compare_and_fusion), kind=kLoop, calls=%fused_computation.31 | loop fusion | flops 786432 | bytes 3145732 | tf_op jit(solution)/shard_map/jit(_take)/select_n | solution.py:73
  85.8 5.2 %collective-permute-done.15 = bf16[4,128,1536]{2,1,0:T(8,128)(2,1)S(1)} collective-permute-done((bf16[4,128,1536]{2,1,0:T(8,128)(2,1)}, bf16[4,128,1536]{2,1,0:T(8,128)(2,1)S(1)}, u32[]{:S(2)}, u32[]{:S(2)}) %collective-permute-start.15) | collective-permute-done | bytes 1572896 | tf_op jit(solution)/shard_map/ppermute | solution.py:74
  91.0 0.5 maximum_select_fusion
  91.5 3.6 %bitcast_add_fusion = f32[4,128,1536]{2,1,0:T(8,128)S(1)} fusion(f32[4,128,1536]{2,1,0:T(8,128)} %collective-permute-done.8, f32[4,2,128,1536]{3,2,1,0:T(8,128)} %bitcast.67, s32[]{:T(128)S(6)} %select_n.120), kind=kLoop, calls=%fused_computation.14 | loop fusion | flops 786432 | bytes 9437188 | tf_op jit(solution)/shard_map/add | solution.py:92
  95.2 2.6 %collective-permute-start.11 = (bf16[128,1536]{1,0:T(8,128)(2,1)S(1)}, bf16[128,1536]{1,0:T(8,128)(2,1)S(1)}, u32[]{:S(2)}, u32[]{:S(2)}) collective-permute-start(bf16[128,1536]{1,0:T(8,128)(2,1)S(1)} %get-tuple-element.3), channel_id=1, source_target_pairs={{0,6},{1,7},{2,0},{3,1},{4,2},{5,3},{6,4},{7,5},{8,14},{9,15},{10,... | collective-permute-start | bytes 1179656 | tf_op jit(solution)/shard_map/ppermute | solution.py:96
  98.3 0.6 collective-permute-start.9
  98.9 7.4 %convolution_convert_fusion = bf16[1536,1536]{1,0:T(8,128)(2,1)} fusion(bf16[1024,1536]{1,0:T(8,128)(2,1)S(1)} %bitcast.72, bf16[1024,768]{1,0:T(8,128)(2,1)S(1)} %bitcast.81, bf16[1024,768]{1,0:T(8,128)(2,1)S(1)} %bitcast.74), kind=kOutput, calls=%fused_computation.6 | convolution fusion | flops 4856217600 | bytes 11010048 | tf_op jit(solution)/shard_map/dot_general | solution.py:81
  106.3 8.0 %collective-permute-done.11 = bf16[128,1536]{1,0:T(8,128)(2,1)S(1)} collective-permute-done((bf16[128,1536]{1,0:T(8,128)(2,1)S(1)}, bf16[128,1536]{1,0:T(8,128)(2,1)S(1)}, u32[]{:S(2)}, u32[]{:S(2)}) %collective-permute-start.11) | collective-permute-done | bytes 393248 | tf_op jit(solution)/shard_map/ppermute | solution.py:96
  114.3 4.6 %collective-permute-done.9 = bf16[128,1536]{1,0:T(8,128)(2,1)S(1)} collective-permute-done((bf16[128,1536]{1,0:T(8,128)(2,1)S(1)}, bf16[128,1536]{1,0:T(8,128)(2,1)S(1)}, u32[]{:S(2)}, u32[]{:S(2)}) %collective-permute-start.9) | collective-permute-done | bytes 393248 | tf_op jit(solution)/shard_map/ppermute | solution.py:96
  118.8 1.4 %fusion.18 = bf16[128,1536]{1,0:T(8,128)(2,1)} fusion(bf16[128,1536]{1,0:T(8,128)(2,1)S(1)} %copy-done.3, bf16[128,1536]{1,0:T(8,128)(2,1)S(1)} %collective-permute-done.11, bf16[128,1536]{1,0:T(8,128)(2,1)S(1)} %collective-permute-done.10, bf16[128,1536]{1,0:T(8,128)(2,1)S(1)} %collective-permute-done.9, f32[4,128,1536]{2,1,0:T(8,128)S(1)} %bitcast_add_fusion, ...), kind=kLoop, calls=%fused_computation.39 | loop fusion | flops 5111808 | bytes 2752516 | tf_op jit(solution)/shard_map/convert_element_type | solution.py:100
  (52 shorter events, 2.3 us)
Async XLA Ops:
  7.2 53.8 %all-gather.4.cloned.1.call-start = ((), (), s32[]{:S(2)}) async-start(), calls=%async_computation | async-start | bytes 1769472 | tf_op jit(solution)/shard_map/all_gather | solution.py:61
  8.0 4.8 %collective-permute-start.4 = (bf16[32,768]{1,0:T(8,128)(2,1)S(1)}, bf16[32,768]{1,0:T(8,128)(2,1)S(1)}, u32[]{:S(2)}, u32[]{:S(2)}) collective-permute-start(bf16[32,768]{1,0:T(8,128)(2,1)S(1)} %get-tuple-element.6), channel_id=1, source_target_pairs={{0,24},{8,0},{16,8},{24,16},{1,25},{9,1},{17,9},{25,17},{2,26},{10... | collective-permute-start | bytes 147464 | tf_op jit(solution)/shard_map/ppermute | solution.py:44
  11.7 4.2 %collective-permute-start.5 = (bf16[32,768]{1,0:T(8,128)(2,1)S(1)}, bf16[32,768]{1,0:T(8,128)(2,1)S(1)}, u32[]{:S(2)}, u32[]{:S(2)}) collective-permute-start(bf16[32,768]{1,0:T(8,128)(2,1)S(1)} %get-tuple-element.6), channel_id=1, source_target_pairs={{0,8},{8,16},{16,24},{24,0},{1,9},{9,17},{17,25},{25,1},{2,10},{10... | collective-permute-start | bytes 147464 | tf_op jit(solution)/shard_map/ppermute | solution.py:43
  12.8 3.9 %collective-permute-start.7 = (bf16[32,384]{1,0:T(8,128)(2,1)S(1)}, bf16[32,384]{1,0:T(8,128)(2,1)S(1)}, u32[]{:S(2)}, u32[]{:S(2)}) collective-permute-start(bf16[32,384]{1,0:T(8,128)(2,1)S(1)} %slice.29), channel_id=1, source_target_pairs={{0,24},{8,0},{16,8},{24,16},{1,25},{9,1},{17,9},{25,17},{2,26},{10... | collective-permute-start | bytes 73736 | tf_op jit(solution)/shard_map/ppermute | solution.py:40
  15.8 3.9 %collective-permute-start.6 = (bf16[32,384]{1,0:T(8,128)(2,1)S(1)}, bf16[32,384]{1,0:T(8,128)(2,1)S(1)}, u32[]{:S(2)}, u32[]{:S(2)}) collective-permute-start(bf16[32,384]{1,0:T(8,128)(2,1)S(1)} %slice.28), channel_id=1, source_target_pairs={{0,8},{8,16},{16,24},{24,0},{1,9},{9,17},{17,25},{25,1},{2,10},{10... | collective-permute-start | bytes 73736 | tf_op jit(solution)/shard_map/ppermute | solution.py:39
  44.9 7.0 %collective-permute-start = (bf16[8,32,768]{2,1,0:T(8,128)(2,1)S(1)}, bf16[8,32,768]{2,1,0:T(8,128)(2,1)S(1)}, u32[]{:S(2)}, u32[]{:S(2)}) collective-permute-start(bf16[8,32,768]{2,1,0:T(8,128)(2,1)S(1)} %bitcast.68), channel_id=1, source_target_pairs={{0,24},{8,0},{16,8},{24,16},{1,25},{9,1},{17,9},{25,17},{2,26},{10... | collective-permute-start | bytes 1179656 | tf_op jit(solution)/shard_map/ppermute | solution.py:44
  44.9 8.2 %collective-permute-start.1 = (bf16[8,32,768]{2,1,0:T(8,128)(2,1)S(1)}, bf16[8,32,768]{2,1,0:T(8,128)(2,1)S(1)}, u32[]{:S(2)}, u32[]{:S(2)}) collective-permute-start(bf16[8,32,768]{2,1,0:T(8,128)(2,1)S(1)} %bitcast.69), channel_id=1, source_target_pairs={{0,8},{8,16},{16,24},{24,0},{1,9},{9,17},{17,25},{25,1},{2,10},{10... | collective-permute-start | bytes 1179656 | tf_op jit(solution)/shard_map/ppermute | solution.py:43
  46.4 36.9 %collective-permute-start.14 = (bf16[128,1536]{1,0:T(8,128)(2,1)}, bf16[128,1536]{1,0:T(8,128)(2,1)S(1)}, u32[]{:S(2)}, u32[]{:S(2)}) collective-permute-start(bf16[128,1536]{1,0:T(8,128)(2,1)} %param.3), channel_id=1, source_target_pairs={{0,6},{1,7},{2,0},{3,1},{4,2},{5,3},{6,4},{7,5},{8,14},{9,15},{10,... | collective-permute-start | bytes 1179656 | tf_op jit(solution)/shard_map/ppermute | solution.py:70
  49.2 34.1 %collective-permute-start.13 = (bf16[128,1536]{1,0:T(8,128)(2,1)}, bf16[128,1536]{1,0:T(8,128)(2,1)S(1)}, u32[]{:S(2)}, u32[]{:S(2)}) collective-permute-start(bf16[128,1536]{1,0:T(8,128)(2,1)} %param.3), channel_id=1, source_target_pairs={{0,4},{1,5},{2,6},{3,7},{4,0},{5,1},{6,2},{7,3},{8,12},{9,13},{10,... | collective-permute-start | bytes 1179656 | tf_op jit(solution)/shard_map/ppermute | solution.py:70
  49.4 33.9 %collective-permute-start.12 = (bf16[128,1536]{1,0:T(8,128)(2,1)}, bf16[128,1536]{1,0:T(8,128)(2,1)S(1)}, u32[]{:S(2)}, u32[]{:S(2)}) collective-permute-start(bf16[128,1536]{1,0:T(8,128)(2,1)} %param.3), channel_id=1, source_target_pairs={{0,2},{1,3},{2,4},{3,5},{4,6},{5,7},{6,0},{7,1},{8,10},{9,11},{10,... | collective-permute-start | bytes 1179656 | tf_op jit(solution)/shard_map/ppermute | solution.py:70
  52.0 5.1 %collective-permute-start.3 = (bf16[8,32,384]{2,1,0:T(8,128)(2,1)S(1)}, bf16[8,32,384]{2,1,0:T(8,128)(2,1)S(1)}, u32[]{:S(2)}, u32[]{:S(2)}) collective-permute-start(bf16[8,32,384]{2,1,0:T(8,128)(2,1)S(1)} %slice.27), channel_id=1, source_target_pairs={{0,24},{8,0},{16,8},{24,16},{1,25},{9,1},{17,9},{25,17},{2,26},{10... | collective-permute-start | bytes 589832 | tf_op jit(solution)/shard_map/ppermute | solution.py:40
  53.2 7.3 %collective-permute-start.2 = (bf16[8,32,384]{2,1,0:T(8,128)(2,1)S(1)}, bf16[8,32,384]{2,1,0:T(8,128)(2,1)S(1)}, u32[]{:S(2)}, u32[]{:S(2)}) collective-permute-start(bf16[8,32,384]{2,1,0:T(8,128)(2,1)S(1)} %slice.26), channel_id=1, source_target_pairs={{0,8},{8,16},{16,24},{24,0},{1,9},{9,17},{17,25},{25,1},{2,10},{10... | collective-permute-start | bytes 589832 | tf_op jit(solution)/shard_map/ppermute | solution.py:39
  60.9 8.0 %copy-start.1 = (bf16[8,4,32,768]{3,2,1,0:T(8,128)(2,1)}, bf16[8,4,32,768]{3,2,1,0:T(8,128)(2,1)S(1)}, u32[]{:S(2)}) copy-start(bf16[8,4,32,768]{3,2,1,0:T(8,128)(2,1)S(1)} %copy.8) | copy-start | bytes 4718596
  68.9 3.6 %copy-start = (f32[1024,1536]{1,0:T(8,128)}, f32[1024,1536]{1,0:T(8,128)S(1)}, u32[]{:S(2)}) copy-start(f32[1024,1536]{1,0:T(8,128)S(1)} %fusion.10) | copy-start | bytes 18874372
  68.9 14.4 %copy-start.3 = (bf16[128,1536]{1,0:T(8,128)(2,1)S(1)}, bf16[128,1536]{1,0:T(8,128)(2,1)}, u32[]{:S(2)}) copy-start(bf16[128,1536]{1,0:T(8,128)(2,1)} %param.3) | copy-start | bytes 1179652
  72.5 19.0 %collective-permute-start.8 = (f32[4,128,1536]{2,1,0:T(8,128)}, f32[4,128,1536]{2,1,0:T(8,128)}, u32[]{:S(2)}, u32[]{:S(2)}) collective-permute-start(f32[4,128,1536]{2,1,0:T(8,128)} %dynamic-slice_bitcast_fusion), channel_id=1, source_target_pairs={{0,1},{1,0},{2,3},{3,2},{4,5},{5,4},{6,7},{7,6},{8,9},{9,8},{10,11... | collective-permute-start | bytes 9437192 | tf_op jit(solution)/shard_map/ppermute | solution.py:92
  85.6 5.4 %collective-permute-start.15 = (bf16[4,128,1536]{2,1,0:T(8,128)(2,1)}, bf16[4,128,1536]{2,1,0:T(8,128)(2,1)S(1)}, u32[]{:S(2)}, u32[]{:S(2)}) collective-permute-start(bf16[4,128,1536]{2,1,0:T(8,128)(2,1)} %broadcast_select_fusion), channel_id=1, source_target_pairs={{0,1},{1,0},{2,3},{3,2},{4,5},{5,4},{6,7},{7,6},{8,9},{9,8},{10,11... | collective-permute-start | bytes 4718600 | tf_op jit(solution)/shard_map/ppermute | solution.py:74
  91.5 7.4 %copy-start.2 = (bf16[8,4,32,768]{3,2,1,0:T(8,128)(2,1)S(1)}, bf16[8,4,32,768]{3,2,1,0:T(8,128)(2,1)}, u32[]{:S(2)}) copy-start(bf16[8,4,32,768]{3,2,1,0:T(8,128)(2,1)} %copy-done.1) | copy-start | bytes 4718596
  91.5 7.4 %copy-start.4 = (bf16[32,32,768]{2,1,0:T(8,128)(2,1)S(1)}, bf16[32,32,768]{2,1,0:T(8,128)(2,1)}, u32[]{:S(2)}) copy-start(bf16[32,32,768]{2,1,0:T(8,128)(2,1)} %all-gather.4.cloned.1.call-done) | copy-start | bytes 4718596
  95.2 19.0 %collective-permute-start.11 = (bf16[128,1536]{1,0:T(8,128)(2,1)S(1)}, bf16[128,1536]{1,0:T(8,128)(2,1)S(1)}, u32[]{:S(2)}, u32[]{:S(2)}) collective-permute-start(bf16[128,1536]{1,0:T(8,128)(2,1)S(1)} %get-tuple-element.3), channel_id=1, source_target_pairs={{0,6},{1,7},{2,0},{3,1},{4,2},{5,3},{6,4},{7,5},{8,14},{9,15},{10,... | collective-permute-start | bytes 1179656 | tf_op jit(solution)/shard_map/ppermute | solution.py:96
  97.9 16.4 %collective-permute-start.10 = (bf16[128,1536]{1,0:T(8,128)(2,1)S(1)}, bf16[128,1536]{1,0:T(8,128)(2,1)S(1)}, u32[]{:S(2)}, u32[]{:S(2)}) collective-permute-start(bf16[128,1536]{1,0:T(8,128)(2,1)S(1)} %get-tuple-element.4), channel_id=1, source_target_pairs={{0,4},{1,5},{2,6},{3,7},{4,0},{5,1},{6,2},{7,3},{8,12},{9,13},{10,... | collective-permute-start | bytes 1179656 | tf_op jit(solution)/shard_map/ppermute | solution.py:96
  98.3 20.5 %collective-permute-start.9 = (bf16[128,1536]{1,0:T(8,128)(2,1)S(1)}, bf16[128,1536]{1,0:T(8,128)(2,1)S(1)}, u32[]{:S(2)}, u32[]{:S(2)}) collective-permute-start(bf16[128,1536]{1,0:T(8,128)(2,1)S(1)} %get-tuple-element.2), channel_id=1, source_target_pairs={{0,2},{1,3},{2,4},{3,5},{4,6},{5,7},{6,0},{7,1},{8,10},{9,11},{10,... | collective-permute-start | bytes 1179656 | tf_op jit(solution)/shard_map/ppermute | solution.py:96
Sparse Core Ops, SparseCore 0:
  21.4 39.2 all-gather.3

commit v5 on v3

--- a/solution.py
+++ b/solution.py
@@ -59,21 +59,13 @@
         tokens = out_grad.shape[0] * n_z * n_y
         half = out_grad.shape[1] // 2
         part_a = ring_gather(ring_gather(out_grad[:, :half], "z", n_z), "y", n_y)
-        part_b = ring_gather(ring_gather(out_grad[:, half:], "y", n_y), "z", n_z)
+        part_b = lax.all_gather(ring_gather(out_grad[:, half:], "y", n_y), "z", axis=0)
         part_a = jnp.swapaxes(part_a, 0, 1).reshape((tokens, half))
         part_b = part_b.reshape((tokens, out_grad.shape[1] - half))
         grad_all = jnp.concatenate([part_a, part_b], axis=1)
 
-        got = [saved_input]
-        for s in range(1, n_x):
-            got.append(lax.ppermute(saved_input, COL, chip_shift(n_col, s)))
-        by_chip = jnp.stack(got, axis=0)
-        order = (x - jnp.arange(n_x)) % n_x
-        mine_by_x = jnp.take(by_chip, order, axis=0)
-        other_by_x = lax.ppermute(mine_by_x, COL, core_swap(n_col))
-        pair = jnp.where(k == 0, jnp.stack([mine_by_x, other_by_x], axis=1),
-                         jnp.stack([other_by_x, mine_by_x], axis=1))
-        saved_all = pair.reshape((n_col * saved_input.shape[0], saved_input.shape[1]))
+        saved_after, part_b = lax.optimization_barrier((saved_input, part_b))
+        saved_all = lax.all_gather(saved_after, COL, axis=0, tiled=True)
 
         gelu_value, unused_slope = gelu_parts(saved_all.astype(jnp.float32))
         hidden = gelu_value.astype(jnp.bfloat16)

time: 122 us -> 146 us (1.20)
  waiting for transfers between devices: 26.6 us -> 58 us
  starting transfers between devices: 55.4 us -> 35.6 us
  between operations: 1.11 us -> 14.3 us
  matrix products: 12.5 us -> 17.1 us
  local copies, waits for them, and re-layouts: 17.4 us -> 13.3 us
    all_gather x0 -> x2, waiting for transfers between devices: none -> 12.1 us  [the longest x1 12.1 us: per_device(): lax.all_gather(ring_gather(out_grad[:, half:], 'y', n_y), 'z', axis=0)]
    ppermute x3, waiting for transfers between devices: 12.2 us -> 21.2 us  [per_device(): recv = lax.ppermute(dest.astype(jnp.bfloat16), COL, chip_shift(n_col, s))]
    ppermute x4 -> x0, starting transfers between devices: 7.08 us -> none  [the longest x3 7.07 us: per_device(): got.append(lax.ppermute(saved_input, COL, chip_shift(n_col, s)))]
    ppermute x1, starting transfers between devices: 10.9 us -> 4.85 us  [per_device(): chip_sum = mine + lax.ppermute(theirs, COL, core_swap(n_col))]
    ppermute x1, waiting for transfers between devices: 0.01 us -> 5.98 us  [per_device(): chip_sum = mine + lax.ppermute(theirs, COL, core_swap(n_col))]
    ppermute x4 -> x0, waiting for transfers between devices: 5.23 us -> none  [the longest x1 5.22 us: per_device(): other_by_x = lax.ppermute(mine_by_x, COL, core_swap(n_col))]
    ppermute x4 -> x3, waiting for transfers between devices: 4.05 us -> 7.85 us  [ring_gather(): from_behind = lax.ppermute(fwd[..., :half], axis, ahead)]
    ppermute x4 -> x3, waiting for transfers between devices: 0.84 us -> 4.48 us  [ring_gather(): from_ahead = lax.ppermute(bwd[..., half:], axis, behind)]
  transfers between devices with their start and end apart: 32 -> 22, of which waited for: 13 -> 15; matrix products, arithmetic and copies ran while one was open for 24% -> 16% of each run, Pallas kernels for 0% -> 0%
where the time goes in v5:
time: 146 us
  waiting for transfers between devices  58 us (40%)
  starting transfers between devices  35.6 us (24%)
  matrix products  17.1 us (12%)
  between operations  14.3 us (10%)
  local copies, waits for them, and re-layouts  13.3 us (9%)
  other arithmetic  7.74 us (5%)
    ppermute x3, waiting for transfers between devices, per_device(): recv = lax.ppermute(dest.astype(jnp.bfloat16), COL, chip_shift(n_col, s))  21.2 us
    ppermute x5, starting transfers between devices, ring_gather(): bwd = lax.ppermute(bwd, axis, behind)  17.6 us
    all_gather x1, waiting for transfers between devices, per_device(): lax.all_gather(ring_gather(out_grad[:, half:], 'y', n_y), 'z', axis=0)  12.1 us
    dot_general x1, matrix products, per_device(): lax.dot_general(hidden, grad_all, (((0,), (0,)), ((), ())), preferred_ele...  9.68 us
    ppermute x3, starting transfers between devices, ring_gather(): from_ahead = lax.ppermute(bwd[..., half:], axis, behind)  9.14 us
    unnamed x26, local copies, waits for them, and re-layouts  8.07 us
    ppermute x3, waiting for transfers between devices, ring_gather(): from_behind = lax.ppermute(fwd[..., :half], axis, ahead)  7.85 us
    dot_general x1, matrix products, per_device(): lax.dot_general(grad_all, weight, (((1,), (1,)), ((), ())), preferred_ele...  7.44 us
  transfers between devices with their start and end apart: 22, of which 15 were waited for; matrix products, arithmetic and copies ran while one was open for 16% of the time, Pallas kernels for 0%

profile of v5, /device:TPU:1, one launch (start us, length us, event | category | flops | bytes accessed | tf_op | source)
XLA Modules:
  0.0 146.0 jit_solution(15176601878363299801)
XLA Ops:
  7.2 0.8 fusion.33
  8.0 6.5 %collective-permute-start = (bf16[32,768]{1,0:T(8,128)(2,1)S(1)}, bf16[32,768]{1,0:T(8,128)(2,1)S(1)}, u32[]{:S(2)}, u32[]{:S(2)}) collective-permute-start(bf16[32,768]{1,0:T(8,128)(2,1)S(1)} %get-tuple-element.11), channel_id=1, source_target_pairs={{0,224},{32,0},{64,32},{96,64},{128,96},{160,128},{192,160},{224,1... | collective-permute-start | bytes 147464 | tf_op jit(solution)/shard_map/ppermute | solution.py:44
  14.5 2.7 %collective-permute-start.12 = (bf16[32,768]{1,0:T(8,128)(2,1)S(1)}, bf16[32,768]{1,0:T(8,128)(2,1)S(1)}, u32[]{:S(2)}, u32[]{:S(2)}) collective-permute-start(bf16[32,768]{1,0:T(8,128)(2,1)S(1)} %get-tuple-element.12), channel_id=1, source_target_pairs={{0,24},{8,0},{16,8},{24,16},{1,25},{9,1},{17,9},{25,17},{2,26},{10... | collective-permute-start | bytes 147464 | tf_op jit(solution)/shard_map/ppermute | solution.py:44
  17.2 0.8 constant_dynamic-update-slice_fusion.15
  18.4 3.0 %collective-permute-start.15 = (bf16[32,384]{1,0:T(8,128)(2,1)S(1)}, bf16[32,384]{1,0:T(8,128)(2,1)S(1)}, u32[]{:S(2)}, u32[]{:S(2)}) collective-permute-start(bf16[32,384]{1,0:T(8,128)(2,1)S(1)} %slice.37), channel_id=1, source_target_pairs={{0,24},{8,0},{16,8},{24,16},{1,25},{9,1},{17,9},{25,17},{2,26},{10... | collective-permute-start | bytes 73736 | tf_op jit(solution)/shard_map/ppermute | solution.py:40
  21.4 2.8 %collective-permute-start.1 = (bf16[32,768]{1,0:T(8,128)(2,1)S(1)}, bf16[32,768]{1,0:T(8,128)(2,1)S(1)}, u32[]{:S(2)}, u32[]{:S(2)}) collective-permute-start(bf16[32,768]{1,0:T(8,128)(2,1)S(1)} %collective-permute-done), channel_id=1, source_target_pairs={{0,224},{32,0},{64,32},{96,64},{128,96},{160,128},{192,160},{224,1... | collective-permute-start | bytes 147464 | tf_op jit(solution)/shard_map/ppermute | solution.py:44
  24.3 1.0 collective-permute-done.14
  25.3 3.0 %collective-permute-start.2 = (bf16[32,768]{1,0:T(8,128)(2,1)S(1)}, bf16[32,768]{1,0:T(8,128)(2,1)S(1)}, u32[]{:S(2)}, u32[]{:S(2)}) collective-permute-start(bf16[32,768]{1,0:T(8,128)(2,1)S(1)} %collective-permute-done.1), channel_id=1, source_target_pairs={{0,224},{32,0},{64,32},{96,64},{128,96},{160,128},{192,160},{224,1... | collective-permute-start | bytes 147464 | tf_op jit(solution)/shard_map/ppermute | solution.py:44
  28.4 1.1 collective-permute-done.2
  29.5 3.0 %collective-permute-start.7 = (bf16[32,384]{1,0:T(8,128)(2,1)S(1)}, bf16[32,384]{1,0:T(8,128)(2,1)S(1)}, u32[]{:S(2)}, u32[]{:S(2)}) collective-permute-start(bf16[32,384]{1,0:T(8,128)(2,1)S(1)} %slice.33), channel_id=1, source_target_pairs={{0,224},{32,0},{64,32},{96,64},{128,96},{160,128},{192,160},{224,1... | collective-permute-start | bytes 73736 | tf_op jit(solution)/shard_map/ppermute | solution.py:40
  33.4 3.0 %collective-permute-done.6 = bf16[32,384]{1,0:T(8,128)(2,1)S(1)} collective-permute-done((bf16[32,384]{1,0:T(8,128)(2,1)S(1)}, bf16[32,384]{1,0:T(8,128)(2,1)S(1)}, u32[]{:S(2)}, u32[]{:S(2)}) %collective-permute-start.6) | collective-permute-done | bytes 24608 | tf_op jit(solution)/shard_map/ppermute | solution.py:39
  36.5 0.8 constant_dynamic-update-slice_fusion.7
  38.2 0.8 bitcast_dynamic-update-slice_fusion.4
  39.1 2.7 %collective-permute-start.8 = (bf16[8,32,768]{2,1,0:T(8,128)(2,1)S(1)}, bf16[8,32,768]{2,1,0:T(8,128)(2,1)S(1)}, u32[]{:S(2)}, u32[]{:S(2)}) collective-permute-start(bf16[8,32,768]{2,1,0:T(8,128)(2,1)S(1)} %get-tuple-element.5), channel_id=1, source_target_pairs={{0,24},{8,0},{16,8},{24,16},{1,25},{9,1},{17,9},{25,17},{2,26},{10... | collective-permute-start | bytes 1179656 | tf_op jit(solution)/shard_map/ppermute | solution.py:44
  41.8 4.7 %collective-permute-done.8 = bf16[8,32,768]{2,1,0:T(8,128)(2,1)S(1)} collective-permute-done((bf16[8,32,768]{2,1,0:T(8,128)(2,1)S(1)}, bf16[8,32,768]{2,1,0:T(8,128)(2,1)S(1)}, u32[]{:S(2)}, u32[]{:S(2)}) %collective-permute-start.8) | collective-permute-done | bytes 393248 | tf_op jit(solution)/shard_map/ppermute | solution.py:44
  46.5 3.2 %collective-permute-start.11 = (bf16[8,32,384]{2,1,0:T(8,128)(2,1)S(1)}, bf16[8,32,384]{2,1,0:T(8,128)(2,1)S(1)}, u32[]{:S(2)}, u32[]{:S(2)}) collective-permute-start(bf16[8,32,384]{2,1,0:T(8,128)(2,1)S(1)} %slice.35), channel_id=1, source_target_pairs={{0,24},{8,0},{16,8},{24,16},{1,25},{9,1},{17,9},{25,17},{2,26},{10... | collective-permute-start | bytes 589832 | tf_op jit(solution)/shard_map/ppermute | solution.py:40
  50.8 3.6 %collective-permute-done.11 = bf16[8,32,384]{2,1,0:T(8,128)(2,1)S(1)} collective-permute-done((bf16[8,32,384]{2,1,0:T(8,128)(2,1)S(1)}, bf16[8,32,384]{2,1,0:T(8,128)(2,1)S(1)}, u32[]{:S(2)}, u32[]{:S(2)}) %collective-permute-start.11) | collective-permute-done | bytes 196640 | tf_op jit(solution)/shard_map/ppermute | solution.py:40
  54.4 3.8 %collective-permute-done.10 = bf16[8,32,384]{2,1,0:T(8,128)(2,1)S(1)} collective-permute-done((bf16[8,32,384]{2,1,0:T(8,128)(2,1)S(1)}, bf16[8,32,384]{2,1,0:T(8,128)(2,1)S(1)}, u32[]{:S(2)}, u32[]{:S(2)}) %collective-permute-start.10) | collective-permute-done | bytes 196640 | tf_op jit(solution)/shard_map/ppermute | solution.py:39
  62.9 1.6 %constant_dynamic-slice_fusion.1 = bf16[4,8,32,768]{3,2,0,1:T(8,128)(2,1)S(1)} fusion(bf16[8,8,32,768]{3,2,0,1:T(8,128)(2,1)} %bitcast_dynamic-update-slice_fusion.3, s32[]{:T(128)S(6)} %select_n.74), kind=kLoop, calls=%fused_computation.80 | loop fusion | bytes 3145732 | tf_op jit(solution)/shard_map/jit(_roll_dynamic)/dynamic_slice | solution.py:48
  64.5 12.1 %all-gather.6.cloned.1.call-done = bf16[32,32,768]{2,1,0:T(8,128)(2,1)} async-done(((bf16[4,32,768]{2,1,0:T(8,128)(2,1)}), bf16[32,32,768]{2,1,0:T(8,128)(2,1)}) %all-gather.6.cloned.1.call-update) | async-done | bytes 1572880 | tf_op jit(solution)/shard_map/all_gather | solution.py:62
  76.6 7.4 %fusion.10 = f32[1024,1536]{1,0:T(8,128)S(1)} fusion(bf16[1536,1536]{1,0:T(8,128)(2,1)} %param.5, bf16[1024,768]{1,0:T(8,128)(2,1)} %bitcast.91, bf16[1024,768]{1,0:T(8,128)(2,1)S(1)} %bitcast.89), kind=kOutput, calls=%fused_computation.18 | convolution fusion | flops 4838129664 | bytes 14155776 | tf_op jit(solution)/shard_map/dot_general | solution.py:76
  84.3 2.4 %copy-done = f32[1024,1536]{1,0:T(8,128)} copy-done((f32[1024,1536]{1,0:T(8,128)}, f32[1024,1536]{1,0:T(8,128)S(1)}, u32[]{:S(2)}) %copy-start) | copy-done | bytes 6291480
  86.7 4.9 %collective-permute-start.16 = (f32[4,128,1536]{2,1,0:T(8,128)S(1)}, f32[4,128,1536]{2,1,0:T(8,128)}, u32[]{:S(2)}, u32[]{:S(2)}) collective-permute-start(f32[4,128,1536]{2,1,0:T(8,128)S(1)} %dynamic-slice_bitcast_fusion), channel_id=1, source_target_pairs={{0,1},{1,0},{2,3},{3,2},{4,5},{5,4},{6,7},{7,6},{8,9},{9,8},{10,11... | collective-permute-start | bytes 9437192 | tf_op jit(solution)/shard_map/ppermute | solution.py:83
  91.5 6.0 %collective-permute-done.16 = f32[4,128,1536]{2,1,0:T(8,128)} collective-permute-done((f32[4,128,1536]{2,1,0:T(8,128)S(1)}, f32[4,128,1536]{2,1,0:T(8,128)}, u32[]{:S(2)}, u32[]{:S(2)}) %collective-permute-start.16) | collective-permute-done | bytes 3145760 | tf_op jit(solution)/shard_map/ppermute | solution.py:83
  97.5 3.5 %bitcast_add_fusion = f32[4,128,1536]{2,1,0:T(8,128)S(1)} fusion(f32[4,128,1536]{2,1,0:T(8,128)} %collective-permute-done.16, f32[4,2,128,1536]{3,2,1,0:T(8,128)} %bitcast.88, s32[]{:T(128)S(6)} %select_n.76), kind=kLoop, calls=%fused_computation.12 | loop fusion | flops 786432 | bytes 9437188 | tf_op jit(solution)/shard_map/add | solution.py:83
  101.0 1.1 fusion.22
  102.0 2.3 %collective-permute-start.19 = (bf16[128,1536]{1,0:T(8,128)(2,1)}, bf16[128,1536]{1,0:T(8,128)(2,1)}, u32[]{:S(2)}, u32[]{:S(2)}) collective-permute-start(bf16[128,1536]{1,0:T(8,128)(2,1)} %get-tuple-element.7), channel_id=1, source_target_pairs={{0,6},{1,7},{2,0},{3,1},{4,2},{5,3},{6,4},{7,5},{8,14},{9,15},{10,... | collective-permute-start | bytes 1179656 | tf_op jit(solution)/shard_map/ppermute | solution.py:87
  105.6 11.8 %collective-permute-done.19 = bf16[128,1536]{1,0:T(8,128)(2,1)} collective-permute-done((bf16[128,1536]{1,0:T(8,128)(2,1)}, bf16[128,1536]{1,0:T(8,128)(2,1)}, u32[]{:S(2)}, u32[]{:S(2)}) %collective-permute-start.19) | collective-permute-done | bytes 393248 | tf_op jit(solution)/shard_map/ppermute | solution.py:87
  117.4 1.2 collective-permute-done.18
  118.6 8.2 %collective-permute-done.17 = bf16[128,1536]{1,0:T(8,128)(2,1)} collective-permute-done((bf16[128,1536]{1,0:T(8,128)(2,1)}, bf16[128,1536]{1,0:T(8,128)(2,1)}, u32[]{:S(2)}, u32[]{:S(2)}) %collective-permute-start.17) | collective-permute-done | bytes 393248 | tf_op jit(solution)/shard_map/ppermute | solution.py:87
  126.8 2.7 %fusion.18 = bf16[128,1536]{1,0:T(8,128)(2,1)} fusion(bf16[128,1536]{1,0:T(8,128)(2,1)S(1)} %copy-done.2, bf16[128,1536]{1,0:T(8,128)(2,1)} %collective-permute-done.19, bf16[128,1536]{1,0:T(8,128)(2,1)} %collective-permute-done.18, bf16[128,1536]{1,0:T(8,128)(2,1)} %collective-permute-done.17, f32[4,128,1536]{2,1,0:T(8,128)S(1)} %bitcast_add_fusion, ...), kind=kLoop, calls=%fused_computation.33 | loop fusion | flops 5111808 | bytes 2752516 | tf_op jit(solution)/shard_map/convert_element_type | solution.py:91
  129.5 9.7 %convolution_convert_fusion = bf16[1536,1536]{1,0:T(8,128)(2,1)} fusion(bf16[1024,1536]{1,0:T(8,128)(2,1)} %all-gather.4.cloned.1.call-done, bf16[1024,768]{1,0:T(8,128)(2,1)} %bitcast.92, bf16[1024,768]{1,0:T(8,128)(2,1)} %bitcast.90), kind=kOutput, calls=%fused_computation.5 | convolution fusion | flops 4856217600 | bytes 11010048 | tf_op jit(solution)/shard_map/dot_general | solution.py:72
  (64 shorter events, 9.6 us)
Async XLA Ops:
  7.2 69.4 %all-gather.6.cloned.1.call-start = ((), (), s32[]{:S(2)}) async-start(), calls=%async_computation.1 | async-start | bytes 1769472 | tf_op jit(solution)/shard_map/all_gather | solution.py:62
  8.0 13.4 %collective-permute-start = (bf16[32,768]{1,0:T(8,128)(2,1)S(1)}, bf16[32,768]{1,0:T(8,128)(2,1)S(1)}, u32[]{:S(2)}, u32[]{:S(2)}) collective-permute-start(bf16[32,768]{1,0:T(8,128)(2,1)S(1)} %get-tuple-element.11), channel_id=1, source_target_pairs={{0,224},{32,0},{64,32},{96,64},{128,96},{160,128},{192,160},{224,1... | collective-permute-start | bytes 147464 | tf_op jit(solution)/shard_map/ppermute | solution.py:44
  14.5 9.7 %collective-permute-start.3 = (bf16[32,768]{1,0:T(8,128)(2,1)S(1)}, bf16[32,768]{1,0:T(8,128)(2,1)S(1)}, u32[]{:S(2)}, u32[]{:S(2)}) collective-permute-start(bf16[32,768]{1,0:T(8,128)(2,1)S(1)} %get-tuple-element.11), channel_id=1, source_target_pairs={{0,32},{32,64},{64,96},{96,128},{128,160},{160,192},{192,224},{224... | collective-permute-start | bytes 147464 | tf_op jit(solution)/shard_map/ppermute | solution.py:43
  14.5 3.9 %collective-permute-start.12 = (bf16[32,768]{1,0:T(8,128)(2,1)S(1)}, bf16[32,768]{1,0:T(8,128)(2,1)S(1)}, u32[]{:S(2)}, u32[]{:S(2)}) collective-permute-start(bf16[32,768]{1,0:T(8,128)(2,1)S(1)} %get-tuple-element.12), channel_id=1, source_target_pairs={{0,24},{8,0},{16,8},{24,16},{1,25},{9,1},{17,9},{25,17},{2,26},{10... | collective-permute-start | bytes 147464 | tf_op jit(solution)/shard_map/ppermute | solution.py:44
  17.2 4.2 %collective-permute-start.13 = (bf16[32,768]{1,0:T(8,128)(2,1)S(1)}, bf16[32,768]{1,0:T(8,128)(2,1)S(1)}, u32[]{:S(2)}, u32[]{:S(2)}) collective-permute-start(bf16[32,768]{1,0:T(8,128)(2,1)S(1)} %get-tuple-element.12), channel_id=1, source_target_pairs={{0,8},{8,16},{16,24},{24,0},{1,9},{9,17},{17,25},{25,1},{2,10},{10... | collective-permute-start | bytes 147464 | tf_op jit(solution)/shard_map/ppermute | solution.py:43
  18.4 5.9 %collective-permute-start.15 = (bf16[32,384]{1,0:T(8,128)(2,1)S(1)}, bf16[32,384]{1,0:T(8,128)(2,1)S(1)}, u32[]{:S(2)}, u32[]{:S(2)}) collective-permute-start(bf16[32,384]{1,0:T(8,128)(2,1)S(1)} %slice.37), channel_id=1, source_target_pairs={{0,24},{8,0},{16,8},{24,16},{1,25},{9,1},{17,9},{25,17},{2,26},{10... | collective-permute-start | bytes 73736 | tf_op jit(solution)/shard_map/ppermute | solution.py:40
  21.4 3.9 %collective-permute-start.14 = (bf16[32,384]{1,0:T(8,128)(2,1)S(1)}, bf16[32,384]{1,0:T(8,128)(2,1)S(1)}, u32[]{:S(2)}, u32[]{:S(2)}) collective-permute-start(bf16[32,384]{1,0:T(8,128)(2,1)S(1)} %slice.36), channel_id=1, source_target_pairs={{0,8},{8,16},{16,24},{24,0},{1,9},{9,17},{17,25},{25,1},{2,10},{10... | collective-permute-start | bytes 73736 | tf_op jit(solution)/shard_map/ppermute | solution.py:39
  21.4 3.9 %collective-permute-start.1 = (bf16[32,768]{1,0:T(8,128)(2,1)S(1)}, bf16[32,768]{1,0:T(8,128)(2,1)S(1)}, u32[]{:S(2)}, u32[]{:S(2)}) collective-permute-start(bf16[32,768]{1,0:T(8,128)(2,1)S(1)} %collective-permute-done), channel_id=1, source_target_pairs={{0,224},{32,0},{64,32},{96,64},{128,96},{160,128},{192,160},{224,1... | collective-permute-start | bytes 147464 | tf_op jit(solution)/shard_map/ppermute | solution.py:44
  24.2 4.2 %collective-permute-start.4 = (bf16[32,768]{1,0:T(8,128)(2,1)S(1)}, bf16[32,768]{1,0:T(8,128)(2,1)S(1)}, u32[]{:S(2)}, u32[]{:S(2)}) collective-permute-start(bf16[32,768]{1,0:T(8,128)(2,1)S(1)} %collective-permute-done.3), channel_id=1, source_target_pairs={{0,32},{32,64},{64,96},{96,128},{128,160},{160,192},{192,224},{224... | collective-permute-start | bytes 147464 | tf_op jit(solution)/shard_map/ppermute | solution.py:43
  25.3 4.2 %collective-permute-start.2 = (bf16[32,768]{1,0:T(8,128)(2,1)S(1)}, bf16[32,768]{1,0:T(8,128)(2,1)S(1)}, u32[]{:S(2)}, u32[]{:S(2)}) collective-permute-start(bf16[32,768]{1,0:T(8,128)(2,1)S(1)} %collective-permute-done.1), channel_id=1, source_target_pairs={{0,224},{32,0},{64,32},{96,64},{128,96},{160,128},{192,160},{224,1... | collective-permute-start | bytes 147464 | tf_op jit(solution)/shard_map/ppermute | solution.py:44
  28.4 4.2 %collective-permute-start.5 = (bf16[32,768]{1,0:T(8,128)(2,1)S(1)}, bf16[32,768]{1,0:T(8,128)(2,1)S(1)}, u32[]{:S(2)}, u32[]{:S(2)}) collective-permute-start(bf16[32,768]{1,0:T(8,128)(2,1)S(1)} %collective-permute-done.4), channel_id=1, source_target_pairs={{0,32},{32,64},{64,96},{96,128},{128,160},{160,192},{192,224},{224... | collective-permute-start | bytes 147464 | tf_op jit(solution)/shard_map/ppermute | solution.py:43
  29.5 3.9 %collective-permute-start.7 = (bf16[32,384]{1,0:T(8,128)(2,1)S(1)}, bf16[32,384]{1,0:T(8,128)(2,1)S(1)}, u32[]{:S(2)}, u32[]{:S(2)}) collective-permute-start(bf16[32,384]{1,0:T(8,128)(2,1)S(1)} %slice.33), channel_id=1, source_target_pairs={{0,224},{32,0},{64,32},{96,64},{128,96},{160,128},{192,160},{224,1... | collective-permute-start | bytes 73736 | tf_op jit(solution)/shard_map/ppermute | solution.py:40
  32.6 3.9 %collective-permute-start.6 = (bf16[32,384]{1,0:T(8,128)(2,1)S(1)}, bf16[32,384]{1,0:T(8,128)(2,1)S(1)}, u32[]{:S(2)}, u32[]{:S(2)}) collective-permute-start(bf16[32,384]{1,0:T(8,128)(2,1)S(1)} %slice.32), channel_id=1, source_target_pairs={{0,32},{32,64},{64,96},{96,128},{128,160},{160,192},{192,224},{224... | collective-permute-start | bytes 73736 | tf_op jit(solution)/shard_map/ppermute | solution.py:39
  38.1 91.4 %all-gather.4.cloned.1.call-start = ((), (), s32[]{:S(2)}) async-start(), calls=%async_computation | async-start | bytes 3538944 | tf_op jit(solution)/shard_map/all_gather | solution.py:68
  39.1 7.4 %collective-permute-start.8 = (bf16[8,32,768]{2,1,0:T(8,128)(2,1)S(1)}, bf16[8,32,768]{2,1,0:T(8,128)(2,1)S(1)}, u32[]{:S(2)}, u32[]{:S(2)}) collective-permute-start(bf16[8,32,768]{2,1,0:T(8,128)(2,1)S(1)} %get-tuple-element.5), channel_id=1, source_target_pairs={{0,24},{8,0},{16,8},{24,16},{1,25},{9,1},{17,9},{25,17},{2,26},{10... | collective-permute-start | bytes 1179656 | tf_op jit(solution)/shard_map/ppermute | solution.py:44
  41.8 7.9 %collective-permute-start.9 = (bf16[8,32,768]{2,1,0:T(8,128)(2,1)S(1)}, bf16[8,32,768]{2,1,0:T(8,128)(2,1)S(1)}, u32[]{:S(2)}, u32[]{:S(2)}) collective-permute-start(bf16[8,32,768]{2,1,0:T(8,128)(2,1)S(1)} %get-tuple-element.5), channel_id=1, source_target_pairs={{0,8},{8,16},{16,24},{24,0},{1,9},{9,17},{17,25},{25,1},{2,10},{10... | collective-permute-start | bytes 1179656 | tf_op jit(solution)/shard_map/ppermute | solution.py:43
  46.5 7.9 %collective-permute-start.11 = (bf16[8,32,384]{2,1,0:T(8,128)(2,1)S(1)}, bf16[8,32,384]{2,1,0:T(8,128)(2,1)S(1)}, u32[]{:S(2)}, u32[]{:S(2)}) collective-permute-start(bf16[8,32,384]{2,1,0:T(8,128)(2,1)S(1)} %slice.35), channel_id=1, source_target_pairs={{0,24},{8,0},{16,8},{24,16},{1,25},{9,1},{17,9},{25,17},{2,26},{10... | collective-permute-start | bytes 589832 | tf_op jit(solution)/shard_map/ppermute | solution.py:40
  49.7 8.5 %collective-permute-start.10 = (bf16[8,32,384]{2,1,0:T(8,128)(2,1)S(1)}, bf16[8,32,384]{2,1,0:T(8,128)(2,1)S(1)}, u32[]{:S(2)}, u32[]{:S(2)}) collective-permute-start(bf16[8,32,384]{2,1,0:T(8,128)(2,1)S(1)} %slice.34), channel_id=1, source_target_pairs={{0,8},{8,16},{16,24},{24,0},{1,9},{9,17},{17,25},{25,1},{2,10},{10... | collective-permute-start | bytes 589832 | tf_op jit(solution)/shard_map/ppermute | solution.py:39
  64.5 19.6 %copy-start.1 = (bf16[4,8,32,768]{3,2,0,1:T(8,128)(2,1)}, bf16[4,8,32,768]{3,2,0,1:T(8,128)(2,1)S(1)}, u32[]{:S(2)}) copy-start(bf16[4,8,32,768]{3,2,0,1:T(8,128)(2,1)S(1)} %constant_dynamic-slice_fusion.1) | copy-start | bytes 4718596
  84.0 2.6 %copy-start = (f32[1024,1536]{1,0:T(8,128)}, f32[1024,1536]{1,0:T(8,128)S(1)}, u32[]{:S(2)}) copy-start(f32[1024,1536]{1,0:T(8,128)S(1)} %fusion.10) | copy-start | bytes 18874372
  86.7 10.8 %collective-permute-start.16 = (f32[4,128,1536]{2,1,0:T(8,128)S(1)}, f32[4,128,1536]{2,1,0:T(8,128)}, u32[]{:S(2)}, u32[]{:S(2)}) collective-permute-start(f32[4,128,1536]{2,1,0:T(8,128)S(1)} %dynamic-slice_bitcast_fusion), channel_id=1, source_target_pairs={{0,1},{1,0},{2,3},{3,2},{4,5},{5,4},{6,7},{7,6},{8,9},{9,8},{10,11... | collective-permute-start | bytes 9437192 | tf_op jit(solution)/shard_map/ppermute | solution.py:83
  91.5 35.3 %copy-start.2 = (bf16[128,1536]{1,0:T(8,128)(2,1)S(1)}, bf16[128,1536]{1,0:T(8,128)(2,1)}, u32[]{:S(2)}) copy-start(bf16[128,1536]{1,0:T(8,128)(2,1)} %param.3) | copy-start | bytes 1179652
  102.0 15.3 %collective-permute-start.19 = (bf16[128,1536]{1,0:T(8,128)(2,1)}, bf16[128,1536]{1,0:T(8,128)(2,1)}, u32[]{:S(2)}, u32[]{:S(2)}) collective-permute-start(bf16[128,1536]{1,0:T(8,128)(2,1)} %get-tuple-element.7), channel_id=1, source_target_pairs={{0,6},{1,7},{2,0},{3,1},{4,2},{5,3},{6,4},{7,5},{8,14},{9,15},{10,... | collective-permute-start | bytes 1179656 | tf_op jit(solution)/shard_map/ppermute | solution.py:87
  104.4 14.2 %collective-permute-start.18 = (bf16[128,1536]{1,0:T(8,128)(2,1)}, bf16[128,1536]{1,0:T(8,128)(2,1)}, u32[]{:S(2)}, u32[]{:S(2)}) collective-permute-start(bf16[128,1536]{1,0:T(8,128)(2,1)} %get-tuple-element.8), channel_id=1, source_target_pairs={{0,4},{1,5},{2,6},{3,7},{4,0},{5,1},{6,2},{7,3},{8,12},{9,13},{10,... | collective-permute-start | bytes 1179656 | tf_op jit(solution)/shard_map/ppermute | solution.py:87
  105.0 21.8 %collective-permute-start.17 = (bf16[128,1536]{1,0:T(8,128)(2,1)}, bf16[128,1536]{1,0:T(8,128)(2,1)}, u32[]{:S(2)}, u32[]{:S(2)}) collective-permute-start(bf16[128,1536]{1,0:T(8,128)(2,1)} %get-tuple-element.6), channel_id=1, source_target_pairs={{0,2},{1,3},{2,4},{3,5},{4,6},{5,7},{6,0},{7,1},{8,10},{9,11},{10,... | collective-permute-start | bytes 1179656 | tf_op jit(solution)/shard_map/ppermute | solution.py:87
Sparse Core Ops, SparseCore 0:
  38.2 38.2 all-gather.5
  78.4 42.7 all-gather.3

commit v6 on v3

--- a/solution.py
+++ b/solution.py
@@ -57,12 +57,8 @@
         k = c % 2
 
         tokens = out_grad.shape[0] * n_z * n_y
-        half = out_grad.shape[1] // 2
-        part_a = ring_gather(ring_gather(out_grad[:, :half], "z", n_z), "y", n_y)
-        part_b = ring_gather(ring_gather(out_grad[:, half:], "y", n_y), "z", n_z)
-        part_a = jnp.swapaxes(part_a, 0, 1).reshape((tokens, half))
-        part_b = part_b.reshape((tokens, out_grad.shape[1] - half))
-        grad_all = jnp.concatenate([part_a, part_b], axis=1)
+        gathered = ring_gather(ring_gather(out_grad, "z", n_z), "y", n_y)
+        grad_all = jnp.swapaxes(gathered, 0, 1).reshape((tokens, out_grad.shape[1]))
 
         got = [saved_input]
         for s in range(1, n_x):

time: 122 us -> 118 us (0.967)
  starting transfers between devices: 55.4 us -> 37.5 us
  waiting for transfers between devices: 26.6 us -> 41.6 us
  local copies, waits for them, and re-layouts: 17.4 us -> 13.7 us
  other arithmetic: 8.96 us -> 12.4 us
    ppermute x8 -> x4, waiting for transfers between devices: 3.91 us -> 11.9 us  [ring_gather(): bwd = lax.ppermute(bwd, axis, behind)]
    ppermute x8 -> x4, starting transfers between devices: 21 us -> 15.2 us  [ring_gather(): bwd = lax.ppermute(bwd, axis, behind)]
    ppermute x4 -> x2, waiting for transfers between devices: 0.84 us -> 6.46 us  [ring_gather(): from_ahead = lax.ppermute(bwd[..., half:], axis, behind)]
    ppermute x4 -> x2, starting transfers between devices: 11.7 us -> 6.53 us  [ring_gather(): from_ahead = lax.ppermute(bwd[..., half:], axis, behind)]
    unnamed x51 -> x32, local copies, waits for them, and re-layouts: 11.1 us -> 7.64 us
    ppermute x3, starting transfers between devices: 7.07 us -> 3.6 us  [per_device(): got.append(lax.ppermute(saved_input, COL, chip_shift(n_col, s)))]
    ppermute x1, starting transfers between devices: 10.9 us -> 8.12 us  [per_device(): chip_sum = mine + lax.ppermute(theirs, COL, core_swap(n_col))]
    convert_element_type x0 -> x1, other arithmetic: none -> 2.39 us  [per_device(): hidden = gelu_value.astype(jnp.bfloat16)]
  transfers between devices with their start and end apart: 32 -> 20, of which waited for: 13 -> 12; matrix products, arithmetic and copies ran while one was open for 24% -> 25% of each run, Pallas kernels for 0% -> 0%
where the time goes in v6:
time: 118 us
  waiting for transfers between devices  41.6 us (35%)
  starting transfers between devices  37.5 us (32%)
  local copies, waits for them, and re-layouts  13.7 us (12%)
  other arithmetic  12.4 us (11%)
  matrix products  11.8 us (10%)
    ppermute x4, starting transfers between devices, ring_gather(): bwd = lax.ppermute(bwd, axis, behind)  15.2 us
    ppermute x3, waiting for transfers between devices, per_device(): recv = lax.ppermute(dest.astype(jnp.bfloat16), COL, chip_shift(n_col, s))  12.9 us
    ppermute x4, waiting for transfers between devices, ring_gather(): bwd = lax.ppermute(bwd, axis, behind)  11.9 us
    ppermute x1, starting transfers between devices, per_device(): chip_sum = mine + lax.ppermute(theirs, COL, core_swap(n_col))  8.12 us
    unnamed x32, local copies, waits for them, and re-layouts  7.64 us
    dot_general x1, matrix products, per_device(): lax.dot_general(hidden, grad_all, (((0,), (0,)), ((), ())), preferred_ele...  6.78 us
    ppermute x2, starting transfers between devices, ring_gather(): from_ahead = lax.ppermute(bwd[..., half:], axis, behind)  6.53 us
    ppermute x2, waiting for transfers between devices, ring_gather(): from_ahead = lax.ppermute(bwd[..., half:], axis, behind)  6.46 us
  transfers between devices with their start and end apart: 20, of which 12 were waited for; matrix products, arithmetic and copies ran while one was open for 25% of the time, Pallas kernels for 0%

profile of v6, /device:TPU:1, one launch (start us, length us, event | category | flops | bytes accessed | tf_op | source)
XLA Modules:
  0.0 118.0 jit_solution(16064869187616714405)
XLA Ops:
  0.6 6.5 %collective-permute-start = (bf16[32,1536]{1,0:T(8,128)(2,1)}, bf16[32,1536]{1,0:T(8,128)(2,1)S(1)}, u32[]{:S(2)}, u32[]{:S(2)}) collective-permute-start(bf16[32,1536]{1,0:T(8,128)(2,1)} %param.4), channel_id=1, source_target_pairs={{0,224},{32,0},{64,32},{96,64},{128,96},{160,128},{192,160},{224,1... | collective-permute-start | bytes 294920 | tf_op jit(solution)/shard_map/ppermute | solution.py:44
  9.1 2.9 %collective-permute-start.1 = (bf16[32,1536]{1,0:T(8,128)(2,1)S(1)}, bf16[32,1536]{1,0:T(8,128)(2,1)S(1)}, u32[]{:S(2)}, u32[]{:S(2)}) collective-permute-start(bf16[32,1536]{1,0:T(8,128)(2,1)S(1)} %collective-permute-done), channel_id=1, source_target_pairs={{0,224},{32,0},{64,32},{96,64},{128,96},{160,128},{192,160},{224,1... | collective-permute-start | bytes 294920 | tf_op jit(solution)/shard_map/ppermute | solution.py:44
  12.0 1.6 %collective-permute-done.1 = bf16[32,1536]{1,0:T(8,128)(2,1)S(1)} collective-permute-done((bf16[32,1536]{1,0:T(8,128)(2,1)S(1)}, bf16[32,1536]{1,0:T(8,128)(2,1)S(1)}, u32[]{:S(2)}, u32[]{:S(2)}) %collective-permute-start.1) | collective-permute-done | bytes 98336 | tf_op jit(solution)/shard_map/ppermute | solution.py:44
  13.6 3.0 %collective-permute-start.2 = (bf16[32,1536]{1,0:T(8,128)(2,1)S(1)}, bf16[32,1536]{1,0:T(8,128)(2,1)S(1)}, u32[]{:S(2)}, u32[]{:S(2)}) collective-permute-start(bf16[32,1536]{1,0:T(8,128)(2,1)S(1)} %collective-permute-done.1), channel_id=1, source_target_pairs={{0,224},{32,0},{64,32},{96,64},{128,96},{160,128},{192,160},{224,1... | collective-permute-start | bytes 294920 | tf_op jit(solution)/shard_map/ppermute | solution.py:44
  16.7 1.6 %collective-permute-done.2 = bf16[32,1536]{1,0:T(8,128)(2,1)S(1)} collective-permute-done((bf16[32,1536]{1,0:T(8,128)(2,1)S(1)}, bf16[32,1536]{1,0:T(8,128)(2,1)S(1)}, u32[]{:S(2)}, u32[]{:S(2)}) %collective-permute-start.2) | collective-permute-done | bytes 98336 | tf_op jit(solution)/shard_map/ppermute | solution.py:44
  18.3 3.0 %collective-permute-start.7 = (bf16[32,768]{1,0:T(8,128)(2,1)S(1)}, bf16[32,768]{1,0:T(8,128)(2,1)S(1)}, u32[]{:S(2)}, u32[]{:S(2)}) collective-permute-start(bf16[32,768]{1,0:T(8,128)(2,1)S(1)} %slice.19), channel_id=1, source_target_pairs={{0,224},{32,0},{64,32},{96,64},{128,96},{160,128},{192,160},{224,1... | collective-permute-start | bytes 147464 | tf_op jit(solution)/shard_map/ppermute | solution.py:40
  21.5 1.1 collective-permute-done.7
  22.5 3.1 %collective-permute-done.6 = bf16[32,768]{1,0:T(8,128)(2,1)S(1)} collective-permute-done((bf16[32,768]{1,0:T(8,128)(2,1)S(1)}, bf16[32,768]{1,0:T(8,128)(2,1)S(1)}, u32[]{:S(2)}, u32[]{:S(2)}) %collective-permute-start.6) | collective-permute-done | bytes 49184 | tf_op jit(solution)/shard_map/ppermute | solution.py:39
  25.8 1.1 bitcast_dynamic-update-slice_fusion.4
  26.9 2.7 %collective-permute-start.8 = (bf16[8,32,1536]{2,1,0:T(8,128)(2,1)S(1)}, bf16[8,32,1536]{2,1,0:T(8,128)(2,1)S(1)}, u32[]{:S(2)}, u32[]{:S(2)}) collective-permute-start(bf16[8,32,1536]{2,1,0:T(8,128)(2,1)S(1)} %get-tuple-element.3), channel_id=1, source_target_pairs={{0,24},{8,0},{16,8},{24,16},{1,25},{9,1},{17,9},{25,17},{2,26},{10... | collective-permute-start | bytes 2359304 | tf_op jit(solution)/shard_map/ppermute | solution.py:44
  29.6 2.5 %collective-permute-start.18 = (bf16[128,1536]{1,0:T(8,128)(2,1)S(1)}, bf16[128,1536]{1,0:T(8,128)(2,1)}, u32[]{:S(2)}, u32[]{:S(2)}) collective-permute-start(bf16[128,1536]{1,0:T(8,128)(2,1)S(1)} %copy-done.3), channel_id=1, source_target_pairs={{0,6},{1,7},{2,0},{3,1},{4,2},{5,3},{6,4},{7,5},{8,14},{9,15},{10,... | collective-permute-start | bytes 1179656 | tf_op jit(solution)/shard_map/ppermute | solution.py:65
  33.3 7.7 %collective-permute-done.8 = bf16[8,32,1536]{2,1,0:T(8,128)(2,1)S(1)} collective-permute-done((bf16[8,32,1536]{2,1,0:T(8,128)(2,1)S(1)}, bf16[8,32,1536]{2,1,0:T(8,128)(2,1)S(1)}, u32[]{:S(2)}, u32[]{:S(2)}) %collective-permute-start.8) | collective-permute-done | bytes 786464 | tf_op jit(solution)/shard_map/ppermute | solution.py:44
  41.0 3.5 %collective-permute-start.11 = (bf16[8,32,768]{2,1,0:T(8,128)(2,1)S(1)}, bf16[8,32,768]{2,1,0:T(8,128)(2,1)S(1)}, u32[]{:S(2)}, u32[]{:S(2)}) collective-permute-start(bf16[8,32,768]{2,1,0:T(8,128)(2,1)S(1)} %slice.21), channel_id=1, source_target_pairs={{0,24},{8,0},{16,8},{24,16},{1,25},{9,1},{17,9},{25,17},{2,26},{10... | collective-permute-start | bytes 1179656 | tf_op jit(solution)/shard_map/ppermute | solution.py:40
  44.8 1.0 bitcast_dynamic-update-slice_fusion
  45.8 5.4 %collective-permute-done.11 = bf16[8,32,768]{2,1,0:T(8,128)(2,1)S(1)} collective-permute-done((bf16[8,32,768]{2,1,0:T(8,128)(2,1)S(1)}, bf16[8,32,768]{2,1,0:T(8,128)(2,1)S(1)}, u32[]{:S(2)}, u32[]{:S(2)}) %collective-permute-start.11) | collective-permute-done | bytes 393248 | tf_op jit(solution)/shard_map/ppermute | solution.py:40
  51.2 3.1 %collective-permute-done.10 = bf16[8,32,768]{2,1,0:T(8,128)(2,1)S(1)} collective-permute-done((bf16[8,32,768]{2,1,0:T(8,128)(2,1)S(1)}, bf16[8,32,768]{2,1,0:T(8,128)(2,1)S(1)}, u32[]{:S(2)}, u32[]{:S(2)}) %collective-permute-start.10) | collective-permute-done | bytes 393248 | tf_op jit(solution)/shard_map/ppermute | solution.py:39
  59.2 1.0 bitcast_dynamic-update-slice_fusion.3
  60.2 2.2 %constant_dynamic-slice_fusion = bf16[4,8,32,1536]{3,2,0,1:T(8,128)(2,1)S(1)} fusion(bf16[8,8,32,1536]{3,2,0,1:T(8,128)(2,1)} %bitcast_dynamic-update-slice_fusion.3, s32[]{:T(128)S(6)} %select_n.130), kind=kLoop, calls=%fused_computation.78 | loop fusion | bytes 6291460 | tf_op jit(solution)/shard_map/jit(_roll_dynamic)/dynamic_slice | solution.py:48
  62.4 5.1 %fusion.5 = f32[4,2,128,1536]{3,2,1,0:T(8,128)S(1)} fusion(bf16[4,2,128,1536]{3,2,1,0:T(8,128)(2,1)S(1)} %bitcast.91, bf16[1536,1536]{1,0:T(8,128)(2,1)S(1)} %bitcast.97), kind=kOutput, calls=%fused_computation.12 | convolution fusion | flops 4831838208 | bytes 14155776 | tf_op jit(solution)/shard_map/dot_general | solution.py:80
  67.5 2.0 %dynamic-slice_bitcast_fusion = f32[4,128,1536]{2,1,0:T(8,128)} fusion(f32[4,2,128,1536]{3,2,1,0:T(8,128)S(1)} %fusion.5, s32[]{:T(128)S(6)} %select_n.133), kind=kLoop, calls=%fused_computation.16 | loop fusion | bytes 6291460 | tf_op jit(solution)/shard_map/jit(dynamic_index_in_dim)/squeeze | solution.py:86
  69.5 1.5 %copy-done = f32[4,2,128,1536]{3,2,1,0:T(8,128)} copy-done((f32[4,2,128,1536]{3,2,1,0:T(8,128)}, f32[4,2,128,1536]{3,2,1,0:T(8,128)S(1)}, u32[]{:S(2)}) %copy-start) | copy-done | bytes 6291480
  71.1 8.1 %collective-permute-start.12 = (f32[4,128,1536]{2,1,0:T(8,128)}, f32[4,128,1536]{2,1,0:T(8,128)}, u32[]{:S(2)}, u32[]{:S(2)}) collective-permute-start(f32[4,128,1536]{2,1,0:T(8,128)} %dynamic-slice_bitcast_fusion), channel_id=1, source_target_pairs={{0,1},{1,0},{2,3},{3,2},{4,5},{5,4},{6,7},{7,6},{8,9},{9,8},{10,11... | collective-permute-start | bytes 9437192 | tf_op jit(solution)/shard_map/ppermute | solution.py:87
  79.2 1.4 %pad_maximum_fusion = bf16[4,128,1536]{2,1,0:T(8,128)(2,1)S(1)} fusion(bf16[1,128,1536]{2,1,0:T(8,128)(2,1)} %bitcast.29, bf16[1,128,1536]{2,1,0:T(8,128)(2,1)} %bitcast.28, bf16[1,128,1536]{2,1,0:T(8,128)(2,1)} %bitcast.27, bf16[1,128,1536]{2,1,0:T(8,128)(2,1)S(1)} %bitcast.95), kind=kLoop, calls=%fused_computation.24 | loop fusion | flops 2359296 | bytes 3145728 | tf_op jit(solution)/shard_map/stack | solution.py:66
  81.3 1.4 %broadcast_select_fusion = bf16[4,128,1536]{2,1,0:T(8,128)(2,1)} fusion(bf16[4,128,1536]{2,1,0:T(8,128)(2,1)S(1)} %gather_fusion, pred[4]{0:T(512)(128)(4,1)S(1)} %compare_and_fusion), kind=kLoop, calls=%fused_computation.26 | loop fusion | flops 786432 | bytes 3145732 | tf_op jit(solution)/shard_map/jit(_take)/select_n | solution.py:68
  82.9 4.0 %collective-permute-done.19 = bf16[4,128,1536]{2,1,0:T(8,128)(2,1)S(1)} collective-permute-done((bf16[4,128,1536]{2,1,0:T(8,128)(2,1)}, bf16[4,128,1536]{2,1,0:T(8,128)(2,1)S(1)}, u32[]{:S(2)}, u32[]{:S(2)}) %collective-permute-start.19) | collective-permute-done | bytes 1572896 | tf_op jit(solution)/shard_map/ppermute | solution.py:69
  87.0 2.4 %fusion.1 = bf16[4,2,128,1536]{3,2,1,0:T(8,128)(2,1)S(1)} fusion(bf16[4,1,128,1536]{3,2,1,0:T(8,128)(2,1)S(1)} %bitcast.94, bf16[4,1,128,1536]{3,2,1,0:T(8,128)(2,1)S(1)} %bitcast_select_fusion, pred[]{:T(512)S(6)} %eq.15), kind=kLoop, calls=%fused_computation.8 | loop fusion | flops 20447232 | bytes 6291457 | tf_op jit(solution)/shard_map/convert_element_type | solution.py:75
  89.4 3.6 %bitcast_add_fusion = f32[4,128,1536]{2,1,0:T(8,128)S(1)} fusion(f32[4,128,1536]{2,1,0:T(8,128)} %collective-permute-done.12, f32[4,2,128,1536]{3,2,1,0:T(8,128)} %copy-done, s32[]{:T(128)S(6)} %select_n.132), kind=kLoop, calls=%fused_computation.15 | loop fusion | flops 786432 | bytes 9437188 | tf_op jit(solution)/shard_map/add | solution.py:87
  93.1 2.5 %collective-permute-start.15 = (bf16[128,1536]{1,0:T(8,128)(2,1)S(1)}, bf16[128,1536]{1,0:T(8,128)(2,1)S(1)}, u32[]{:S(2)}, u32[]{:S(2)}) collective-permute-start(bf16[128,1536]{1,0:T(8,128)(2,1)S(1)} %get-tuple-element.5), channel_id=1, source_target_pairs={{0,6},{1,7},{2,0},{3,1},{4,2},{5,3},{6,4},{7,5},{8,14},{9,15},{10,... | collective-permute-start | bytes 1179656 | tf_op jit(solution)/shard_map/ppermute | solution.py:91
  96.8 6.8 %convolution_convert_fusion = bf16[1536,1536]{1,0:T(8,128)(2,1)} fusion(bf16[1024,1536]{1,0:T(8,128)(2,1)S(1)} %bitcast.93, bf16[1024,1536]{1,0:T(8,128)(2,1)S(1)} %bitcast.92), kind=kOutput, calls=%fused_computation.6 | convolution fusion | flops 4834197504 | bytes 11010048 | tf_op jit(solution)/shard_map/dot_general | solution.py:76
  104.4 2.8 %collective-permute-done.14 = bf16[128,1536]{1,0:T(8,128)(2,1)S(1)} collective-permute-done((bf16[128,1536]{1,0:T(8,128)(2,1)S(1)}, bf16[128,1536]{1,0:T(8,128)(2,1)S(1)}, u32[]{:S(2)}, u32[]{:S(2)}) %collective-permute-start.14) | collective-permute-done | bytes 393248 | tf_op jit(solution)/shard_map/ppermute | solution.py:91
  107.1 9.4 %collective-permute-done.13 = bf16[128,1536]{1,0:T(8,128)(2,1)S(1)} collective-permute-done((bf16[128,1536]{1,0:T(8,128)(2,1)S(1)}, bf16[128,1536]{1,0:T(8,128)(2,1)S(1)}, u32[]{:S(2)}, u32[]{:S(2)}) %collective-permute-start.13) | collective-permute-done | bytes 393248 | tf_op jit(solution)/shard_map/ppermute | solution.py:91
  116.5 1.4 %fusion.14 = bf16[128,1536]{1,0:T(8,128)(2,1)} fusion(bf16[128,1536]{1,0:T(8,128)(2,1)S(1)} %copy-done.3, bf16[128,1536]{1,0:T(8,128)(2,1)S(1)} %collective-permute-done.15, bf16[128,1536]{1,0:T(8,128)(2,1)S(1)} %collective-permute-done.14, bf16[128,1536]{1,0:T(8,128)(2,1)S(1)} %collective-permute-done.13, f32[4,128,1536]{2,1,0:T(8,128)S(1)} %bitcast_add_fusion, ...), kind=kLoop, calls=%fused_computation.34 | loop fusion | flops 5111808 | bytes 2752516 | tf_op jit(solution)/shard_map/convert_element_type | solution.py:95
  (66 shorter events, 11.6 us)
Async XLA Ops:
  0.6 25.0 %copy-start.4 = (bf16[32,1536]{1,0:T(8,128)(2,1)S(1)}, bf16[32,1536]{1,0:T(8,128)(2,1)}, u32[]{:S(2)}) copy-start(bf16[32,1536]{1,0:T(8,128)(2,1)} %param.4) | copy-start | bytes 294916
  0.6 8.4 %collective-permute-start = (bf16[32,1536]{1,0:T(8,128)(2,1)}, bf16[32,1536]{1,0:T(8,128)(2,1)S(1)}, u32[]{:S(2)}, u32[]{:S(2)}) collective-permute-start(bf16[32,1536]{1,0:T(8,128)(2,1)} %param.4), channel_id=1, source_target_pairs={{0,224},{32,0},{64,32},{96,64},{128,96},{160,128},{192,160},{224,1... | collective-permute-start | bytes 294920 | tf_op jit(solution)/shard_map/ppermute | solution.py:44
  7.1 4.9 %collective-permute-start.3 = (bf16[32,1536]{1,0:T(8,128)(2,1)}, bf16[32,1536]{1,0:T(8,128)(2,1)S(1)}, u32[]{:S(2)}, u32[]{:S(2)}) collective-permute-start(bf16[32,1536]{1,0:T(8,128)(2,1)} %param.4), channel_id=1, source_target_pairs={{0,32},{32,64},{64,96},{96,128},{128,160},{160,192},{192,224},{224... | collective-permute-start | bytes 294920 | tf_op jit(solution)/shard_map/ppermute | solution.py:43
  9.1 4.6 %collective-permute-start.1 = (bf16[32,1536]{1,0:T(8,128)(2,1)S(1)}, bf16[32,1536]{1,0:T(8,128)(2,1)S(1)}, u32[]{:S(2)}, u32[]{:S(2)}) collective-permute-start(bf16[32,1536]{1,0:T(8,128)(2,1)S(1)} %collective-permute-done), channel_id=1, source_target_pairs={{0,224},{32,0},{64,32},{96,64},{128,96},{160,128},{192,160},{224,1... | collective-permute-start | bytes 294920 | tf_op jit(solution)/shard_map/ppermute | solution.py:44
  12.0 4.7 %collective-permute-start.4 = (bf16[32,1536]{1,0:T(8,128)(2,1)S(1)}, bf16[32,1536]{1,0:T(8,128)(2,1)S(1)}, u32[]{:S(2)}, u32[]{:S(2)}) collective-permute-start(bf16[32,1536]{1,0:T(8,128)(2,1)S(1)} %collective-permute-done.3), channel_id=1, source_target_pairs={{0,32},{32,64},{64,96},{96,128},{128,160},{160,192},{192,224},{224... | collective-permute-start | bytes 294920 | tf_op jit(solution)/shard_map/ppermute | solution.py:43
  13.6 4.7 %collective-permute-start.2 = (bf16[32,1536]{1,0:T(8,128)(2,1)S(1)}, bf16[32,1536]{1,0:T(8,128)(2,1)S(1)}, u32[]{:S(2)}, u32[]{:S(2)}) collective-permute-start(bf16[32,1536]{1,0:T(8,128)(2,1)S(1)} %collective-permute-done.1), channel_id=1, source_target_pairs={{0,224},{32,0},{64,32},{96,64},{128,96},{160,128},{192,160},{224,1... | collective-permute-start | bytes 294920 | tf_op jit(solution)/shard_map/ppermute | solution.py:44
  16.7 4.7 %collective-permute-start.5 = (bf16[32,1536]{1,0:T(8,128)(2,1)S(1)}, bf16[32,1536]{1,0:T(8,128)(2,1)S(1)}, u32[]{:S(2)}, u32[]{:S(2)}) collective-permute-start(bf16[32,1536]{1,0:T(8,128)(2,1)S(1)} %collective-permute-done.4), channel_id=1, source_target_pairs={{0,32},{32,64},{64,96},{96,128},{128,160},{160,192},{192,224},{224... | collective-permute-start | bytes 294920 | tf_op jit(solution)/shard_map/ppermute | solution.py:43
  18.3 4.2 %collective-permute-start.7 = (bf16[32,768]{1,0:T(8,128)(2,1)S(1)}, bf16[32,768]{1,0:T(8,128)(2,1)S(1)}, u32[]{:S(2)}, u32[]{:S(2)}) collective-permute-start(bf16[32,768]{1,0:T(8,128)(2,1)S(1)} %slice.19), channel_id=1, source_target_pairs={{0,224},{32,0},{64,32},{96,64},{128,96},{160,128},{192,160},{224,1... | collective-permute-start | bytes 147464 | tf_op jit(solution)/shard_map/ppermute | solution.py:40
  21.4 4.2 %collective-permute-start.6 = (bf16[32,768]{1,0:T(8,128)(2,1)S(1)}, bf16[32,768]{1,0:T(8,128)(2,1)S(1)}, u32[]{:S(2)}, u32[]{:S(2)}) collective-permute-start(bf16[32,768]{1,0:T(8,128)(2,1)S(1)} %slice.18), channel_id=1, source_target_pairs={{0,32},{32,64},{64,96},{96,128},{128,160},{160,192},{192,224},{224... | collective-permute-start | bytes 147464 | tf_op jit(solution)/shard_map/ppermute | solution.py:39
  25.7 3.9 %copy-start.3 = (bf16[128,1536]{1,0:T(8,128)(2,1)S(1)}, bf16[128,1536]{1,0:T(8,128)(2,1)}, u32[]{:S(2)}) copy-start(bf16[128,1536]{1,0:T(8,128)(2,1)} %param.3) | copy-start | bytes 1179652
  26.9 14.1 %collective-permute-start.8 = (bf16[8,32,1536]{2,1,0:T(8,128)(2,1)S(1)}, bf16[8,32,1536]{2,1,0:T(8,128)(2,1)S(1)}, u32[]{:S(2)}, u32[]{:S(2)}) collective-permute-start(bf16[8,32,1536]{2,1,0:T(8,128)(2,1)S(1)} %get-tuple-element.3), channel_id=1, source_target_pairs={{0,24},{8,0},{16,8},{24,16},{1,25},{9,1},{17,9},{25,17},{2,26},{10... | collective-permute-start | bytes 2359304 | tf_op jit(solution)/shard_map/ppermute | solution.py:44
  29.6 14.9 %collective-permute-start.9 = (bf16[8,32,1536]{2,1,0:T(8,128)(2,1)S(1)}, bf16[8,32,1536]{2,1,0:T(8,128)(2,1)S(1)}, u32[]{:S(2)}, u32[]{:S(2)}) collective-permute-start(bf16[8,32,1536]{2,1,0:T(8,128)(2,1)S(1)} %get-tuple-element.3), channel_id=1, source_target_pairs={{0,8},{8,16},{16,24},{24,0},{1,9},{9,17},{17,25},{25,1},{2,10},{10... | collective-permute-start | bytes 2359304 | tf_op jit(solution)/shard_map/ppermute | solution.py:43
  29.6 49.6 %collective-permute-start.18 = (bf16[128,1536]{1,0:T(8,128)(2,1)S(1)}, bf16[128,1536]{1,0:T(8,128)(2,1)}, u32[]{:S(2)}, u32[]{:S(2)}) collective-permute-start(bf16[128,1536]{1,0:T(8,128)(2,1)S(1)} %copy-done.3), channel_id=1, source_target_pairs={{0,6},{1,7},{2,0},{3,1},{4,2},{5,3},{6,4},{7,5},{8,14},{9,15},{10,... | collective-permute-start | bytes 1179656 | tf_op jit(solution)/shard_map/ppermute | solution.py:65
  32.1 47.1 %collective-permute-start.17 = (bf16[128,1536]{1,0:T(8,128)(2,1)S(1)}, bf16[128,1536]{1,0:T(8,128)(2,1)}, u32[]{:S(2)}, u32[]{:S(2)}) collective-permute-start(bf16[128,1536]{1,0:T(8,128)(2,1)S(1)} %copy-done.3), channel_id=1, source_target_pairs={{0,4},{1,5},{2,6},{3,7},{4,0},{5,1},{6,2},{7,3},{8,12},{9,13},{10,... | collective-permute-start | bytes 1179656 | tf_op jit(solution)/shard_map/ppermute | solution.py:65
  32.6 46.6 %collective-permute-start.16 = (bf16[128,1536]{1,0:T(8,128)(2,1)S(1)}, bf16[128,1536]{1,0:T(8,128)(2,1)}, u32[]{:S(2)}, u32[]{:S(2)}) collective-permute-start(bf16[128,1536]{1,0:T(8,128)(2,1)S(1)} %copy-done.3), channel_id=1, source_target_pairs={{0,2},{1,3},{2,4},{3,5},{4,6},{5,7},{6,0},{7,1},{8,10},{9,11},{10,... | collective-permute-start | bytes 1179656 | tf_op jit(solution)/shard_map/ppermute | solution.py:65
  41.0 10.2 %collective-permute-start.11 = (bf16[8,32,768]{2,1,0:T(8,128)(2,1)S(1)}, bf16[8,32,768]{2,1,0:T(8,128)(2,1)S(1)}, u32[]{:S(2)}, u32[]{:S(2)}) collective-permute-start(bf16[8,32,768]{2,1,0:T(8,128)(2,1)S(1)} %slice.21), channel_id=1, source_target_pairs={{0,24},{8,0},{16,8},{24,16},{1,25},{9,1},{17,9},{25,17},{2,26},{10... | collective-permute-start | bytes 1179656 | tf_op jit(solution)/shard_map/ppermute | solution.py:40
  44.5 9.8 %collective-permute-start.10 = (bf16[8,32,768]{2,1,0:T(8,128)(2,1)S(1)}, bf16[8,32,768]{2,1,0:T(8,128)(2,1)S(1)}, u32[]{:S(2)}, u32[]{:S(2)}) collective-permute-start(bf16[8,32,768]{2,1,0:T(8,128)(2,1)S(1)} %slice.20), channel_id=1, source_target_pairs={{0,8},{8,16},{16,24},{24,0},{1,9},{9,17},{17,25},{25,1},{2,10},{10... | collective-permute-start | bytes 1179656 | tf_op jit(solution)/shard_map/ppermute | solution.py:39
  55.3 7.1 %slice-start = ((s8[4718592]{0:T(1024)(128)(4,1)}), s8[4194304]{0:T(1024)(128)(4,1)S(1)}, s32[]{:S(2)}) async-start(s8[4718592]{0:T(1024)(128)(4,1)} %bitcast.96), calls=%async_computation | async-start | bytes 8388608
  59.2 3.2 %slice-start.1 = ((s8[4718592]{0:T(1024)(128)(4,1)}), s8[524288]{0:T(1024)(128)(4,1)S(1)}, s32[]{:S(2)}) async-start(s8[4718592]{0:T(1024)(128)(4,1)} %bitcast.96), calls=%async_computation.1 | async-start | bytes 1048576
  62.4 5.1 %copy-start.1 = (bf16[4,8,32,1536]{3,2,0,1:T(8,128)(2,1)}, bf16[4,8,32,1536]{3,2,0,1:T(8,128)(2,1)S(1)}, u32[]{:S(2)}) copy-start(bf16[4,8,32,1536]{3,2,0,1:T(8,128)(2,1)S(1)} %constant_dynamic-slice_fusion) | copy-start | bytes 9437188
  67.5 3.6 %copy-start = (f32[4,2,128,1536]{3,2,1,0:T(8,128)}, f32[4,2,128,1536]{3,2,1,0:T(8,128)S(1)}, u32[]{:S(2)}) copy-start(f32[4,2,128,1536]{3,2,1,0:T(8,128)S(1)} %fusion.5) | copy-start | bytes 18874372
  71.1 18.3 %collective-permute-start.12 = (f32[4,128,1536]{2,1,0:T(8,128)}, f32[4,128,1536]{2,1,0:T(8,128)}, u32[]{:S(2)}, u32[]{:S(2)}) collective-permute-start(f32[4,128,1536]{2,1,0:T(8,128)} %dynamic-slice_bitcast_fusion), channel_id=1, source_target_pairs={{0,1},{1,0},{2,3},{3,2},{4,5},{5,4},{6,7},{7,6},{8,9},{9,8},{10,11... | collective-permute-start | bytes 9437192 | tf_op jit(solution)/shard_map/ppermute | solution.py:87
  82.7 4.3 %collective-permute-start.19 = (bf16[4,128,1536]{2,1,0:T(8,128)(2,1)}, bf16[4,128,1536]{2,1,0:T(8,128)(2,1)S(1)}, u32[]{:S(2)}, u32[]{:S(2)}) collective-permute-start(bf16[4,128,1536]{2,1,0:T(8,128)(2,1)} %broadcast_select_fusion), channel_id=1, source_target_pairs={{0,1},{1,0},{2,3},{3,2},{4,5},{5,4},{6,7},{7,6},{8,9},{9,8},{10,11... | collective-permute-start | bytes 4718600 | tf_op jit(solution)/shard_map/ppermute | solution.py:69
  89.4 7.4 %copy-start.2 = (bf16[4,8,32,1536]{3,2,0,1:T(8,128)(2,1)S(1)}, bf16[4,8,32,1536]{3,2,0,1:T(8,128)(2,1)}, u32[]{:S(2)}) copy-start(bf16[4,8,32,1536]{3,2,0,1:T(8,128)(2,1)} %copy-done.1) | copy-start | bytes 9437188
  93.1 11.3 %collective-permute-start.15 = (bf16[128,1536]{1,0:T(8,128)(2,1)S(1)}, bf16[128,1536]{1,0:T(8,128)(2,1)S(1)}, u32[]{:S(2)}, u32[]{:S(2)}) collective-permute-start(bf16[128,1536]{1,0:T(8,128)(2,1)S(1)} %get-tuple-element.5), channel_id=1, source_target_pairs={{0,6},{1,7},{2,0},{3,1},{4,2},{5,3},{6,4},{7,5},{8,14},{9,15},{10,... | collective-permute-start | bytes 1179656 | tf_op jit(solution)/shard_map/ppermute | solution.py:91
  95.6 11.6 %collective-permute-start.14 = (bf16[128,1536]{1,0:T(8,128)(2,1)S(1)}, bf16[128,1536]{1,0:T(8,128)(2,1)S(1)}, u32[]{:S(2)}, u32[]{:S(2)}) collective-permute-start(bf16[128,1536]{1,0:T(8,128)(2,1)S(1)} %get-tuple-element.6), channel_id=1, source_target_pairs={{0,4},{1,5},{2,6},{3,7},{4,0},{5,1},{6,2},{7,3},{8,12},{9,13},{10,... | collective-permute-start | bytes 1179656 | tf_op jit(solution)/shard_map/ppermute | solution.py:91
  96.2 20.3 %collective-permute-start.13 = (bf16[128,1536]{1,0:T(8,128)(2,1)S(1)}, bf16[128,1536]{1,0:T(8,128)(2,1)S(1)}, u32[]{:S(2)}, u32[]{:S(2)}) collective-permute-start(bf16[128,1536]{1,0:T(8,128)(2,1)S(1)} %get-tuple-element.4), channel_id=1, source_target_pairs={{0,2},{1,3},{2,4},{3,5},{4,6},{5,7},{6,0},{7,1},{8,10},{9,11},{10,... | collective-permute-start | bytes 1179656 | tf_op jit(solution)/shard_map/ppermute | solution.py:91

commit v7 on v6

--- a/solution.py
+++ b/solution.py
@@ -58,7 +58,8 @@
 
         tokens = out_grad.shape[0] * n_z * n_y
         gathered = ring_gather(ring_gather(out_grad, "z", n_z), "y", n_y)
-        grad_all = jnp.swapaxes(gathered, 0, 1).reshape((tokens, out_grad.shape[1]))
+        grad_all = gathered.reshape((tokens, out_grad.shape[1]))
+        rows_r = out_grad.shape[0]
 
         got = [saved_input]
         for s in range(1, n_x):
@@ -72,7 +73,8 @@
         saved_all = pair.reshape((n_col * saved_input.shape[0], saved_input.shape[1]))
 
         gelu_value, unused_slope = gelu_parts(saved_all.astype(jnp.float32))
-        hidden = gelu_value.astype(jnp.bfloat16)
+        hidden = gelu_value.astype(jnp.bfloat16).reshape((n_z, n_y, rows_r, -1))
+        hidden = jnp.swapaxes(hidden, 0, 1).reshape((tokens, -1))
         weight_grad = lax.dot_general(
             hidden, grad_all, (((0,), (0,)), ((), ())), preferred_element_type=jnp.float32
         ).astype(jnp.bfloat16)
@@ -81,15 +83,28 @@
             grad_all, weight, (((1,), (1,)), ((), ())), preferred_element_type=jnp.float32
         )
         rows = saved_input.shape[0]
-        p4 = partial.reshape((n_x, 2, rows, partial.shape[1]))
+        p_nat = jnp.swapaxes(partial.reshape((n_y, n_z, rows_r, -1)), 0, 1)
+        p4 = p_nat.reshape((n_x, 2, rows, partial.shape[1]))
         mine = lax.dynamic_index_in_dim(p4, k, axis=1, keepdims=False)
         theirs = lax.dynamic_index_in_dim(p4, 1 - k, axis=1, keepdims=False)
         chip_sum = mine + lax.ppermute(theirs, COL, core_swap(n_col))
         back = lax.dynamic_index_in_dim(chip_sum, x, axis=0, keepdims=False)
-        for s in range(1, n_x):
-            dest = lax.dynamic_index_in_dim(chip_sum, (x + s) % n_x, axis=0, keepdims=False)
-            recv = lax.ppermute(dest.astype(jnp.bfloat16), COL, chip_shift(n_col, s))
-            back = back + recv.astype(jnp.float32)
+        dest = lambda s: lax.dynamic_index_in_dim(
+            chip_sum, (x + s) % n_x, axis=0, keepdims=False).astype(jnp.bfloat16)
+        if n_x == 4:
+            cut = chip_sum.shape[-1] // 2
+            far = dest(2)
+            up, up_relay = lax.ppermute((dest(1), far[:, :cut]), COL, chip_shift(n_col, 1))
+            dn, dn_relay = lax.ppermute((dest(-1), far[:, cut:]), COL, chip_shift(n_col, -1))
+            far_lo = lax.ppermute(up_relay, COL, chip_shift(n_col, 1))
+            far_hi = lax.ppermute(dn_relay, COL, chip_shift(n_col, -1))
+            far_got = jnp.concatenate([far_lo, far_hi], axis=-1)
+            for recv in (up, dn, far_got):
+                back = back + recv.astype(jnp.float32)
+        else:
+            for s in range(1, n_x):
+                recv = lax.ppermute(dest(s), COL, chip_shift(n_col, s))
+                back = back + recv.astype(jnp.float32)
 
         unused_value, own_slope = gelu_parts(saved_input.astype(jnp.float32))
         in_grad = (back * own_slope).astype(jnp.bfloat16)

time: 118 us -> 124 us (1.051)
  other arithmetic: 12.4 us -> 7.18 us
  waiting for transfers between devices: 41.6 us -> 46.3 us
  matrix products: 11.8 us -> 14.4 us
  starting transfers between devices: 37.5 us -> 39.7 us
    ppermute x4, waiting for transfers between devices: 0.01 us -> 18.7 us  [ring_gather(): fwd = lax.ppermute(fwd, axis, ahead)]
    ppermute x3, waiting for transfers between devices: 0.01 us -> 17 us  [per_device(): got.append(lax.ppermute(saved_input, COL, chip_shift(n_col, s)))]
    ppermute x4, waiting for transfers between devices: 11.9 us -> 0.01 us  [ring_gather(): bwd = lax.ppermute(bwd, axis, behind)]
    ppermute x3 -> x6, waiting for transfers between devices: 12.9 us -> 4.2 us  [the longest x1 2.13 us: per_device(): far_lo = lax.ppermute(up_relay, COL, chip_shift(n_col, 1))]
    ppermute x2, waiting for transfers between devices: 6.46 us -> 0.03 us  [ring_gather(): from_ahead = lax.ppermute(bwd[..., half:], axis, behind)]
    ppermute x4, starting transfers between devices: 15.2 us -> 10.8 us  [ring_gather(): bwd = lax.ppermute(bwd, axis, behind)]
    ppermute x1, waiting for transfers between devices: 4.04 us -> 0.01 us  [per_device(): other_by_x = lax.ppermute(mine_by_x, COL, core_swap(n_col))]
    ppermute x4, starting transfers between devices: 0.01 us -> 3.83 us  [ring_gather(): fwd = lax.ppermute(fwd, axis, ahead)]
  transfers between devices with their start and end apart: 20 -> 23, of which waited for: 12 -> 10; matrix products, arithmetic and copies ran while one was open for 25% -> 11% of each run, Pallas kernels for 0% -> 0%
where the time goes in v7:
time: 124 us; the launch traced here: 123 us
  waiting for transfers between devices  46.3 us (37%)
  starting transfers between devices  39.7 us (32%)
  local copies, waits for them, and re-layouts  14.4 us (12%)
  matrix products  14.4 us (12%)
  other arithmetic  7.18 us (6%)
    ppermute x4, waiting for transfers between devices, ring_gather(): fwd = lax.ppermute(fwd, axis, ahead)  18.7 us
    ppermute x3, waiting for transfers between devices, per_device(): got.append(lax.ppermute(saved_input, COL, chip_shift(n_col, s)))  17 us
    ppermute x4, starting transfers between devices, ring_gather(): bwd = lax.ppermute(bwd, axis, behind)  10.8 us
    unnamed x32, local copies, waits for them, and re-layouts  9.9 us
    dot_general x1, matrix products, per_device(): lax.dot_general(hidden, grad_all, (((0,), (0,)), ((), ())), preferred_ele...  7.43 us
    ppermute x1, starting transfers between devices, per_device(): chip_sum = mine + lax.ppermute(theirs, COL, core_swap(n_col))  7.24 us
    dot_general x1, matrix products, per_device(): lax.dot_general(grad_all, weight, (((1,), (1,)), ((), ())), preferred_ele...  6.94 us
    ppermute x2, waiting for transfers between devices, ring_gather(): from_behind = lax.ppermute(fwd[..., :half], axis, ahead)  6.36 us
  transfers between devices with their start and end apart: 23, of which 10 were waited for; matrix products, arithmetic and copies ran while one was open for 11% of the time, Pallas kernels for 0%

profile of v7, /device:TPU:1, one launch (start us, length us, event | category | flops | bytes accessed | tf_op | source)
XLA Modules:
  0.0 122.9 jit_solution(9865791449554705938)
XLA Ops:
  0.6 2.5 %collective-permute-start.3 = (bf16[32,1536]{1,0:T(8,128)(2,1)}, bf16[32,1536]{1,0:T(8,128)(2,1)S(1)}, u32[]{:S(2)}, u32[]{:S(2)}) collective-permute-start(bf16[32,1536]{1,0:T(8,128)(2,1)} %param.4), channel_id=1, source_target_pairs={{0,32},{32,64},{64,96},{96,128},{128,160},{160,192},{192,224},{224... | collective-permute-start | bytes 294920 | tf_op jit(solution)/shard_map/ppermute | solution.py:43
  3.2 4.0 %collective-permute-start = (bf16[32,1536]{1,0:T(8,128)(2,1)}, bf16[32,1536]{1,0:T(8,128)(2,1)S(1)}, u32[]{:S(2)}, u32[]{:S(2)}) collective-permute-start(bf16[32,1536]{1,0:T(8,128)(2,1)} %param.4), channel_id=1, source_target_pairs={{0,224},{32,0},{64,32},{96,64},{128,96},{160,128},{192,160},{224,1... | collective-permute-start | bytes 294920 | tf_op jit(solution)/shard_map/ppermute | solution.py:44
  8.1 1.7 %collective-permute-done.3 = bf16[32,1536]{1,0:T(8,128)(2,1)S(1)} collective-permute-done((bf16[32,1536]{1,0:T(8,128)(2,1)}, bf16[32,1536]{1,0:T(8,128)(2,1)S(1)}, u32[]{:S(2)}, u32[]{:S(2)}) %collective-permute-start.3) | collective-permute-done | bytes 98336 | tf_op jit(solution)/shard_map/ppermute | solution.py:43
  9.8 2.7 %collective-permute-start.1 = (bf16[32,1536]{1,0:T(8,128)(2,1)S(1)}, bf16[32,1536]{1,0:T(8,128)(2,1)S(1)}, u32[]{:S(2)}, u32[]{:S(2)}) collective-permute-start(bf16[32,1536]{1,0:T(8,128)(2,1)S(1)} %collective-permute-done), channel_id=1, source_target_pairs={{0,224},{32,0},{64,32},{96,64},{128,96},{160,128},{192,160},{224,1... | collective-permute-start | bytes 294920 | tf_op jit(solution)/shard_map/ppermute | solution.py:44
  12.5 2.0 %collective-permute-done.4 = bf16[32,1536]{1,0:T(8,128)(2,1)S(1)} collective-permute-done((bf16[32,1536]{1,0:T(8,128)(2,1)S(1)}, bf16[32,1536]{1,0:T(8,128)(2,1)S(1)}, u32[]{:S(2)}, u32[]{:S(2)}) %collective-permute-start.4) | collective-permute-done | bytes 98336 | tf_op jit(solution)/shard_map/ppermute | solution.py:43
  14.5 2.7 %collective-permute-start.2 = (bf16[32,1536]{1,0:T(8,128)(2,1)S(1)}, bf16[32,1536]{1,0:T(8,128)(2,1)S(1)}, u32[]{:S(2)}, u32[]{:S(2)}) collective-permute-start(bf16[32,1536]{1,0:T(8,128)(2,1)S(1)} %collective-permute-done.1), channel_id=1, source_target_pairs={{0,224},{32,0},{64,32},{96,64},{128,96},{160,128},{192,160},{224,1... | collective-permute-start | bytes 294920 | tf_op jit(solution)/shard_map/ppermute | solution.py:44
  17.2 2.0 %collective-permute-done.5 = bf16[32,1536]{1,0:T(8,128)(2,1)S(1)} collective-permute-done((bf16[32,1536]{1,0:T(8,128)(2,1)S(1)}, bf16[32,1536]{1,0:T(8,128)(2,1)S(1)}, u32[]{:S(2)}, u32[]{:S(2)}) %collective-permute-start.5) | collective-permute-done | bytes 98336 | tf_op jit(solution)/shard_map/ppermute | solution.py:43
  19.2 2.7 %collective-permute-start.7 = (bf16[32,768]{1,0:T(8,128)(2,1)S(1)}, bf16[32,768]{1,0:T(8,128)(2,1)S(1)}, u32[]{:S(2)}, u32[]{:S(2)}) collective-permute-start(bf16[32,768]{1,0:T(8,128)(2,1)S(1)} %slice.27), channel_id=1, source_target_pairs={{0,224},{32,0},{64,32},{96,64},{128,96},{160,128},{192,160},{224,1... | collective-permute-start | bytes 147464 | tf_op jit(solution)/shard_map/ppermute | solution.py:40
  21.9 1.4 %collective-permute-done.6 = bf16[32,768]{1,0:T(8,128)(2,1)S(1)} collective-permute-done((bf16[32,768]{1,0:T(8,128)(2,1)S(1)}, bf16[32,768]{1,0:T(8,128)(2,1)S(1)}, u32[]{:S(2)}, u32[]{:S(2)}) %collective-permute-start.6) | collective-permute-done | bytes 49184 | tf_op jit(solution)/shard_map/ppermute | solution.py:39
  25.5 1.3 %collective-permute-start.9 = (bf16[8,32,1536]{2,1,0:T(8,128)(2,1)S(1)}, bf16[8,32,1536]{2,1,0:T(8,128)(2,1)S(1)}, u32[]{:S(2)}, u32[]{:S(2)}) collective-permute-start(bf16[8,32,1536]{2,1,0:T(8,128)(2,1)S(1)} %get-tuple-element.3), channel_id=1, source_target_pairs={{0,8},{8,16},{16,24},{24,0},{1,9},{9,17},{17,25},{25,1},{2,10},{10... | collective-permute-start | bytes 2359304 | tf_op jit(solution)/shard_map/ppermute | solution.py:43
  26.8 1.4 %collective-permute-start.8 = (bf16[8,32,1536]{2,1,0:T(8,128)(2,1)S(1)}, bf16[8,32,1536]{2,1,0:T(8,128)(2,1)S(1)}, u32[]{:S(2)}, u32[]{:S(2)}) collective-permute-start(bf16[8,32,1536]{2,1,0:T(8,128)(2,1)S(1)} %get-tuple-element.3), channel_id=1, source_target_pairs={{0,24},{8,0},{16,8},{24,16},{1,25},{9,1},{17,9},{25,17},{2,26},{10... | collective-permute-start | bytes 2359304 | tf_op jit(solution)/shard_map/ppermute | solution.py:44
  28.2 13.0 %collective-permute-done.9 = bf16[8,32,1536]{2,1,0:T(8,128)(2,1)S(1)} collective-permute-done((bf16[8,32,1536]{2,1,0:T(8,128)(2,1)S(1)}, bf16[8,32,1536]{2,1,0:T(8,128)(2,1)S(1)}, u32[]{:S(2)}, u32[]{:S(2)}) %collective-permute-start.9) | collective-permute-done | bytes 786464 | tf_op jit(solution)/shard_map/ppermute | solution.py:43
  41.4 2.9 %collective-permute-start.11 = (bf16[8,32,768]{2,1,0:T(8,128)(2,1)S(1)}, bf16[8,32,768]{2,1,0:T(8,128)(2,1)S(1)}, u32[]{:S(2)}, u32[]{:S(2)}) collective-permute-start(bf16[8,32,768]{2,1,0:T(8,128)(2,1)S(1)} %slice.29), channel_id=1, source_target_pairs={{0,24},{8,0},{16,8},{24,16},{1,25},{9,1},{17,9},{25,17},{2,26},{10... | collective-permute-start | bytes 1179656 | tf_op jit(solution)/shard_map/ppermute | solution.py:40
  45.2 5.0 %collective-permute-done.10 = bf16[8,32,768]{2,1,0:T(8,128)(2,1)S(1)} collective-permute-done((bf16[8,32,768]{2,1,0:T(8,128)(2,1)S(1)}, bf16[8,32,768]{2,1,0:T(8,128)(2,1)S(1)}, u32[]{:S(2)}, u32[]{:S(2)}) %collective-permute-start.10) | collective-permute-done | bytes 393248 | tf_op jit(solution)/shard_map/ppermute | solution.py:39
  56.0 6.9 %fusion.7 = f32[8,4,32,1536]{3,2,0,1:T(8,128)S(1)} fusion(bf16[1536,1536]{1,0:T(8,128)(2,1)S(1)} %bitcast.102, bf16[8,8,32,1536]{3,2,1,0:T(8,128)(2,1)} %bitcast_dynamic-update-slice_fusion.1, s32[]{:T(128)S(6)} %select_n.125), kind=kOutput, calls=%fused_computation.14 | convolution fusion | flops 4831838208 | bytes 14155780 | tf_op jit(solution)/shard_map/dot_general | solution.py:82
  63.7 1.9 %dynamic-slice_bitcast_fusion = f32[4,128,1536]{2,1,0:T(8,128)} fusion(f32[4,2,128,1536]{3,2,1,0:T(8,128)S(1)} %bitcast.91, s32[]{:T(128)S(6)} %select_n.128), kind=kLoop, calls=%fused_computation.19 | loop fusion | bytes 6291460 | tf_op jit(solution)/shard_map/jit(dynamic_index_in_dim)/squeeze | solution.py:89
  65.6 1.7 %copy-done = f32[8,4,32,1536]{3,2,1,0:T(8,128)} copy-done((f32[8,4,32,1536]{3,2,1,0:T(8,128)}, f32[8,4,32,1536]{3,2,1,0:T(8,128)S(1)}, u32[]{:S(2)}) %copy-start) | copy-done | bytes 6291480
  67.3 7.2 %collective-permute-start.12 = (f32[4,128,1536]{2,1,0:T(8,128)}, f32[4,128,1536]{2,1,0:T(8,128)}, u32[]{:S(2)}, u32[]{:S(2)}) collective-permute-start(f32[4,128,1536]{2,1,0:T(8,128)} %dynamic-slice_bitcast_fusion), channel_id=1, source_target_pairs={{0,1},{1,0},{2,3},{3,2},{4,5},{5,4},{6,7},{7,6},{8,9},{9,8},{10,11... | collective-permute-start | bytes 9437192 | tf_op jit(solution)/shard_map/ppermute | solution.py:90
  74.5 1.2 collective-permute-start.19
  75.7 1.5 %collective-permute-start.21 = (bf16[128,1536]{1,0:T(8,128)(2,1)S(1)}, bf16[128,1536]{1,0:T(8,128)(2,1)S(1)}, u32[]{:S(2)}, u32[]{:S(2)}) collective-permute-start(bf16[128,1536]{1,0:T(8,128)(2,1)S(1)} %copy-done.2), channel_id=1, source_target_pairs={{0,6},{1,7},{2,0},{3,1},{4,2},{5,3},{6,4},{7,5},{8,14},{9,15},{10,... | collective-permute-start | bytes 1179656 | tf_op jit(solution)/shard_map/ppermute | solution.py:66
  77.2 1.5 %collective-permute-start.20 = (bf16[128,1536]{1,0:T(8,128)(2,1)S(1)}, bf16[128,1536]{1,0:T(8,128)(2,1)S(1)}, u32[]{:S(2)}, u32[]{:S(2)}) collective-permute-start(bf16[128,1536]{1,0:T(8,128)(2,1)S(1)} %copy-done.2), channel_id=1, source_target_pairs={{0,4},{1,5},{2,6},{3,7},{4,0},{5,1},{6,2},{7,3},{8,12},{9,13},{10,... | collective-permute-start | bytes 1179656 | tf_op jit(solution)/shard_map/ppermute | solution.py:66
  78.8 7.6 %collective-permute-done.19 = bf16[128,1536]{1,0:T(8,128)(2,1)S(1)} collective-permute-done((bf16[128,1536]{1,0:T(8,128)(2,1)S(1)}, bf16[128,1536]{1,0:T(8,128)(2,1)S(1)}, u32[]{:S(2)}, u32[]{:S(2)}) %collective-permute-start.19) | collective-permute-done | bytes 393248 | tf_op jit(solution)/shard_map/ppermute | solution.py:66
  86.4 9.4 %collective-permute-done.20 = bf16[128,1536]{1,0:T(8,128)(2,1)S(1)} collective-permute-done((bf16[128,1536]{1,0:T(8,128)(2,1)S(1)}, bf16[128,1536]{1,0:T(8,128)(2,1)S(1)}, u32[]{:S(2)}, u32[]{:S(2)}) %collective-permute-start.20) | collective-permute-done | bytes 393248 | tf_op jit(solution)/shard_map/ppermute | solution.py:66
  98.1 1.4 %copy-done.1 = f32[8,4,32,1536]{3,2,1,0:T(8,128)S(1)} copy-done((f32[8,4,32,1536]{3,2,1,0:T(8,128)S(1)}, f32[8,4,32,1536]{3,2,1,0:T(8,128)}, u32[]{:S(2)}) %copy-start.1) | copy-done | bytes 6291480
  99.5 2.6 %bitcast_add_fusion = f32[4,128,1536]{2,1,0:T(8,128)S(1)} fusion(f32[4,128,1536]{2,1,0:T(8,128)} %collective-permute-done.12, f32[4,2,128,1536]{3,2,1,0:T(8,128)S(1)} %bitcast.92, s32[]{:T(128)S(6)} %select_n.127), kind=kLoop, calls=%fused_computation.17 | loop fusion | flops 786432 | bytes 9437188 | tf_op jit(solution)/shard_map/add | solution.py:90
  102.9 2.1 %collective-permute-start.17 = (bf16[128,768]{1,0:T(8,128)(2,1)S(1)}, bf16[128,768]{1,0:T(8,128)(2,1)S(1)}, u32[]{:S(2)}, u32[]{:S(2)}) collective-permute-start(bf16[128,768]{1,0:T(8,128)(2,1)S(1)} %get-tuple-element.8), channel_id=1, source_target_pairs={{0,6},{1,7},{2,0},{3,1},{4,2},{5,3},{6,4},{7,5},{8,14},{9,15},{10,... | collective-permute-start | bytes 589832 | tf_op jit(solution)/shard_map/ppermute | solution.py:98
  105.7 1.5 %collective-permute-start.13 = (bf16[128,1536]{1,0:T(8,128)(2,1)S(1)}, bf16[128,1536]{1,0:T(8,128)(2,1)S(1)}, u32[]{:S(2)}, u32[]{:S(2)}) collective-permute-start(bf16[128,1536]{1,0:T(8,128)(2,1)S(1)} %get-tuple-element.6), channel_id=1, source_target_pairs={{0,2},{1,3},{2,4},{3,5},{4,6},{5,7},{6,0},{7,1},{8,10},{9,11},{10,... | collective-permute-start | bytes 1179656 | tf_op jit(solution)/shard_map/ppermute | solution.py:97
  107.1 2.1 %collective-permute-done.15 = bf16[128,768]{1,0:T(8,128)(2,1)S(1)} collective-permute-done((bf16[128,768]{1,0:T(8,128)(2,1)S(1)}, bf16[128,768]{1,0:T(8,128)(2,1)S(1)}, u32[]{:S(2)}, u32[]{:S(2)}) %collective-permute-start.15) | collective-permute-done | bytes 196640 | tf_op jit(solution)/shard_map/ppermute | solution.py:97
  109.2 2.7 %collective-permute-start.18 = (bf16[128,768]{1,0:T(8,128)(2,1)S(1)}, bf16[128,768]{1,0:T(8,128)(2,1)S(1)}, u32[]{:S(2)}, u32[]{:S(2)}) collective-permute-start(bf16[128,768]{1,0:T(8,128)(2,1)S(1)} %collective-permute-done.17), channel_id=1, source_target_pairs={{0,6},{1,7},{2,0},{3,1},{4,2},{5,3},{6,4},{7,5},{8,14},{9,15},{10,... | collective-permute-start | bytes 589832 | tf_op jit(solution)/shard_map/ppermute | solution.py:100
  111.9 7.4 %bitcast_convert_fusion = bf16[1536,1536]{1,0:T(8,128)(2,1)} fusion(bf16[8,8,32,1536]{3,2,1,0:T(8,128)(2,1)S(1)} %bitcast.100, s32[]{:T(128)S(6)} %select_n.125, bf16[8,4,32,1536]{3,2,1,0:T(8,128)(2,1)S(1)} %bitcast.93), kind=kOutput, calls=%fused_computation.6 | convolution fusion | flops 4849926144 | bytes 11010052 | tf_op jit(solution)/shard_map/dot_general | solution.py:78
  119.3 2.1 %collective-permute-done.16 = bf16[128,768]{1,0:T(8,128)(2,1)S(1)} collective-permute-done((bf16[128,768]{1,0:T(8,128)(2,1)S(1)}, bf16[128,768]{1,0:T(8,128)(2,1)S(1)}, u32[]{:S(2)}, u32[]{:S(2)}) %collective-permute-start.16) | collective-permute-done | bytes 196640 | tf_op jit(solution)/shard_map/ppermute | solution.py:99
  121.4 1.4 %fusion.21 = bf16[128,1536]{1,0:T(8,128)(2,1)} fusion(bf16[128,1536]{1,0:T(8,128)(2,1)S(1)} %copy-done.2, bf16[128,1536]{1,0:T(8,128)(2,1)S(1)} %collective-permute-done.14, bf16[128,1536]{1,0:T(8,128)(2,1)S(1)} %collective-permute-done.13, f32[4,128,1536]{2,1,0:T(8,128)S(1)} %bitcast_add_fusion, s32[]{:T(128)S(6)} %select_n.130, ...), kind=kLoop, calls=%fused_computation.39 | loop fusion | flops 5701632 | bytes 2752516 | tf_op jit(solution)/shard_map/convert_element_type | solution.py:110
  (74 shorter events, 14.4 us)
Async XLA Ops:
  0.6 9.2 %collective-permute-start.3 = (bf16[32,1536]{1,0:T(8,128)(2,1)}, bf16[32,1536]{1,0:T(8,128)(2,1)S(1)}, u32[]{:S(2)}, u32[]{:S(2)}) collective-permute-start(bf16[32,1536]{1,0:T(8,128)(2,1)} %param.4), channel_id=1, source_target_pairs={{0,32},{32,64},{64,96},{96,128},{128,160},{160,192},{192,224},{224... | collective-permute-start | bytes 294920 | tf_op jit(solution)/shard_map/ppermute | solution.py:43
  3.2 6.7 %collective-permute-start = (bf16[32,1536]{1,0:T(8,128)(2,1)}, bf16[32,1536]{1,0:T(8,128)(2,1)S(1)}, u32[]{:S(2)}, u32[]{:S(2)}) collective-permute-start(bf16[32,1536]{1,0:T(8,128)(2,1)} %param.4), channel_id=1, source_target_pairs={{0,224},{32,0},{64,32},{96,64},{128,96},{160,128},{192,160},{224,1... | collective-permute-start | bytes 294920 | tf_op jit(solution)/shard_map/ppermute | solution.py:44
  9.8 4.7 %collective-permute-start.4 = (bf16[32,1536]{1,0:T(8,128)(2,1)S(1)}, bf16[32,1536]{1,0:T(8,128)(2,1)S(1)}, u32[]{:S(2)}, u32[]{:S(2)}) collective-permute-start(bf16[32,1536]{1,0:T(8,128)(2,1)S(1)} %collective-permute-done.3), channel_id=1, source_target_pairs={{0,32},{32,64},{64,96},{96,128},{128,160},{160,192},{192,224},{224... | collective-permute-start | bytes 294920 | tf_op jit(solution)/shard_map/ppermute | solution.py:43
  9.8 4.7 %collective-permute-start.1 = (bf16[32,1536]{1,0:T(8,128)(2,1)S(1)}, bf16[32,1536]{1,0:T(8,128)(2,1)S(1)}, u32[]{:S(2)}, u32[]{:S(2)}) collective-permute-start(bf16[32,1536]{1,0:T(8,128)(2,1)S(1)} %collective-permute-done), channel_id=1, source_target_pairs={{0,224},{32,0},{64,32},{96,64},{128,96},{160,128},{192,160},{224,1... | collective-permute-start | bytes 294920 | tf_op jit(solution)/shard_map/ppermute | solution.py:44
  14.5 4.7 %collective-permute-start.5 = (bf16[32,1536]{1,0:T(8,128)(2,1)S(1)}, bf16[32,1536]{1,0:T(8,128)(2,1)S(1)}, u32[]{:S(2)}, u32[]{:S(2)}) collective-permute-start(bf16[32,1536]{1,0:T(8,128)(2,1)S(1)} %collective-permute-done.4), channel_id=1, source_target_pairs={{0,32},{32,64},{64,96},{96,128},{128,160},{160,192},{192,224},{224... | collective-permute-start | bytes 294920 | tf_op jit(solution)/shard_map/ppermute | solution.py:43
  14.5 4.7 %collective-permute-start.2 = (bf16[32,1536]{1,0:T(8,128)(2,1)S(1)}, bf16[32,1536]{1,0:T(8,128)(2,1)S(1)}, u32[]{:S(2)}, u32[]{:S(2)}) collective-permute-start(bf16[32,1536]{1,0:T(8,128)(2,1)S(1)} %collective-permute-done.1), channel_id=1, source_target_pairs={{0,224},{32,0},{64,32},{96,64},{128,96},{160,128},{192,160},{224,1... | collective-permute-start | bytes 294920 | tf_op jit(solution)/shard_map/ppermute | solution.py:44
  19.2 4.2 %collective-permute-start.6 = (bf16[32,768]{1,0:T(8,128)(2,1)S(1)}, bf16[32,768]{1,0:T(8,128)(2,1)S(1)}, u32[]{:S(2)}, u32[]{:S(2)}) collective-permute-start(bf16[32,768]{1,0:T(8,128)(2,1)S(1)} %slice.26), channel_id=1, source_target_pairs={{0,32},{32,64},{64,96},{96,128},{128,160},{160,192},{192,224},{224... | collective-permute-start | bytes 147464 | tf_op jit(solution)/shard_map/ppermute | solution.py:39
  19.2 4.1 %collective-permute-start.7 = (bf16[32,768]{1,0:T(8,128)(2,1)S(1)}, bf16[32,768]{1,0:T(8,128)(2,1)S(1)}, u32[]{:S(2)}, u32[]{:S(2)}) collective-permute-start(bf16[32,768]{1,0:T(8,128)(2,1)S(1)} %slice.27), channel_id=1, source_target_pairs={{0,224},{32,0},{64,32},{96,64},{128,96},{160,128},{192,160},{224,1... | collective-permute-start | bytes 147464 | tf_op jit(solution)/shard_map/ppermute | solution.py:40
  25.5 15.7 %collective-permute-start.9 = (bf16[8,32,1536]{2,1,0:T(8,128)(2,1)S(1)}, bf16[8,32,1536]{2,1,0:T(8,128)(2,1)S(1)}, u32[]{:S(2)}, u32[]{:S(2)}) collective-permute-start(bf16[8,32,1536]{2,1,0:T(8,128)(2,1)S(1)} %get-tuple-element.3), channel_id=1, source_target_pairs={{0,8},{8,16},{16,24},{24,0},{1,9},{9,17},{17,25},{25,1},{2,10},{10... | collective-permute-start | bytes 2359304 | tf_op jit(solution)/shard_map/ppermute | solution.py:43
  26.8 14.6 %collective-permute-start.8 = (bf16[8,32,1536]{2,1,0:T(8,128)(2,1)S(1)}, bf16[8,32,1536]{2,1,0:T(8,128)(2,1)S(1)}, u32[]{:S(2)}, u32[]{:S(2)}) collective-permute-start(bf16[8,32,1536]{2,1,0:T(8,128)(2,1)S(1)} %get-tuple-element.3), channel_id=1, source_target_pairs={{0,24},{8,0},{16,8},{24,16},{1,25},{9,1},{17,9},{25,17},{2,26},{10... | collective-permute-start | bytes 2359304 | tf_op jit(solution)/shard_map/ppermute | solution.py:44
  41.2 14.8 %slice-start.2 = ((s8[4718592]{0:T(1024)(128)(4,1)}), s8[4194304]{0:T(1024)(128)(4,1)S(1)}, s32[]{:S(2)}) async-start(s8[4718592]{0:T(1024)(128)(4,1)} %bitcast.101), calls=%async_computation.2 | async-start | bytes 8388608
  41.2 9.0 %collective-permute-start.10 = (bf16[8,32,768]{2,1,0:T(8,128)(2,1)S(1)}, bf16[8,32,768]{2,1,0:T(8,128)(2,1)S(1)}, u32[]{:S(2)}, u32[]{:S(2)}) collective-permute-start(bf16[8,32,768]{2,1,0:T(8,128)(2,1)S(1)} %slice.28), channel_id=1, source_target_pairs={{0,8},{8,16},{16,24},{24,0},{1,9},{9,17},{17,25},{25,1},{2,10},{10... | collective-permute-start | bytes 1179656 | tf_op jit(solution)/shard_map/ppermute | solution.py:39
  41.4 8.9 %collective-permute-start.11 = (bf16[8,32,768]{2,1,0:T(8,128)(2,1)S(1)}, bf16[8,32,768]{2,1,0:T(8,128)(2,1)S(1)}, u32[]{:S(2)}, u32[]{:S(2)}) collective-permute-start(bf16[8,32,768]{2,1,0:T(8,128)(2,1)S(1)} %slice.29), channel_id=1, source_target_pairs={{0,24},{8,0},{16,8},{24,16},{1,25},{9,1},{17,9},{25,17},{2,26},{10... | collective-permute-start | bytes 1179656 | tf_op jit(solution)/shard_map/ppermute | solution.py:40
  51.2 4.8 %slice-start.3 = ((s8[4718592]{0:T(1024)(128)(4,1)}), s8[524288]{0:T(1024)(128)(4,1)S(1)}, s32[]{:S(2)}) async-start(s8[4718592]{0:T(1024)(128)(4,1)} %bitcast.101), calls=%async_computation.3 | async-start | bytes 1048576
  63.7 3.6 %copy-start = (f32[8,4,32,1536]{3,2,1,0:T(8,128)}, f32[8,4,32,1536]{3,2,1,0:T(8,128)S(1)}, u32[]{:S(2)}) copy-start(f32[8,4,32,1536]{3,2,1,0:T(8,128)S(1)} %copy.5) | copy-start | bytes 18874372
  63.7 10.8 %copy-start.2 = (bf16[128,1536]{1,0:T(8,128)(2,1)S(1)}, bf16[128,1536]{1,0:T(8,128)(2,1)}, u32[]{:S(2)}) copy-start(bf16[128,1536]{1,0:T(8,128)(2,1)} %param.3) | copy-start | bytes 1179652
  67.3 30.8 %collective-permute-start.12 = (f32[4,128,1536]{2,1,0:T(8,128)}, f32[4,128,1536]{2,1,0:T(8,128)}, u32[]{:S(2)}, u32[]{:S(2)}) collective-permute-start(f32[4,128,1536]{2,1,0:T(8,128)} %dynamic-slice_bitcast_fusion), channel_id=1, source_target_pairs={{0,1},{1,0},{2,3},{3,2},{4,5},{5,4},{6,7},{7,6},{8,9},{9,8},{10,11... | collective-permute-start | bytes 9437192 | tf_op jit(solution)/shard_map/ppermute | solution.py:90
  74.5 11.9 %collective-permute-start.19 = (bf16[128,1536]{1,0:T(8,128)(2,1)S(1)}, bf16[128,1536]{1,0:T(8,128)(2,1)S(1)}, u32[]{:S(2)}, u32[]{:S(2)}) collective-permute-start(bf16[128,1536]{1,0:T(8,128)(2,1)S(1)} %copy-done.2), channel_id=1, source_target_pairs={{0,2},{1,3},{2,4},{3,5},{4,6},{5,7},{6,0},{7,1},{8,10},{9,11},{10,... | collective-permute-start | bytes 1179656 | tf_op jit(solution)/shard_map/ppermute | solution.py:66
  75.7 10.7 %collective-permute-start.21 = (bf16[128,1536]{1,0:T(8,128)(2,1)S(1)}, bf16[128,1536]{1,0:T(8,128)(2,1)S(1)}, u32[]{:S(2)}, u32[]{:S(2)}) collective-permute-start(bf16[128,1536]{1,0:T(8,128)(2,1)S(1)} %copy-done.2), channel_id=1, source_target_pairs={{0,6},{1,7},{2,0},{3,1},{4,2},{5,3},{6,4},{7,5},{8,14},{9,15},{10,... | collective-permute-start | bytes 1179656 | tf_op jit(solution)/shard_map/ppermute | solution.py:66
  77.2 18.6 %collective-permute-start.20 = (bf16[128,1536]{1,0:T(8,128)(2,1)S(1)}, bf16[128,1536]{1,0:T(8,128)(2,1)S(1)}, u32[]{:S(2)}, u32[]{:S(2)}) collective-permute-start(bf16[128,1536]{1,0:T(8,128)(2,1)S(1)} %copy-done.2), channel_id=1, source_target_pairs={{0,4},{1,5},{2,6},{3,7},{4,0},{5,1},{6,2},{7,3},{8,12},{9,13},{10,... | collective-permute-start | bytes 1179656 | tf_op jit(solution)/shard_map/ppermute | solution.py:66
  96.7 2.8 %copy-start.1 = (f32[8,4,32,1536]{3,2,1,0:T(8,128)S(1)}, f32[8,4,32,1536]{3,2,1,0:T(8,128)}, u32[]{:S(2)}) copy-start(f32[8,4,32,1536]{3,2,1,0:T(8,128)} %copy-done) | copy-start | bytes 18874372
  96.9 8.1 %collective-permute-start.22 = (bf16[4,128,1536]{2,1,0:T(8,128)(2,1)S(1)}, bf16[4,128,1536]{2,1,0:T(8,128)(2,1)S(1)}, u32[]{:S(2)}, u32[]{:S(2)}) collective-permute-start(bf16[4,128,1536]{2,1,0:T(8,128)(2,1)S(1)} %broadcast_select_fusion), channel_id=1, source_target_pairs={{0,1},{1,0},{2,3},{3,2},{4,5},{5,4},{6,7},{7,6},{8,9},{9,8},{10,11... | collective-permute-start | bytes 4718600 | tf_op jit(solution)/shard_map/ppermute | solution.py:70
  99.5 12.4 %slice-start = ((s8[6291456]{0:T(1024)(128)(4,1)}), s8[2097152]{0:T(1024)(128)(4,1)S(1)}, s32[]{:S(2)}) async-start(s8[6291456]{0:T(1024)(128)(4,1)} %bitcast.99), calls=%async_computation | async-start | bytes 4194304
  102.1 9.8 %slice-start.1 = ((s8[6291456]{0:T(1024)(128)(4,1)}), s8[4194304]{0:T(1024)(128)(4,1)S(1)}, s32[]{:S(2)}) async-start(s8[6291456]{0:T(1024)(128)(4,1)} %bitcast.99), calls=%async_computation.1 | async-start | bytes 8388608
  102.3 6.9 %collective-permute-start.15 = (bf16[128,768]{1,0:T(8,128)(2,1)S(1)}, bf16[128,768]{1,0:T(8,128)(2,1)S(1)}, u32[]{:S(2)}, u32[]{:S(2)}) collective-permute-start(bf16[128,768]{1,0:T(8,128)(2,1)S(1)} %get-tuple-element.7), channel_id=1, source_target_pairs={{0,2},{1,3},{2,4},{3,5},{4,6},{5,7},{6,0},{7,1},{8,10},{9,11},{10,... | collective-permute-start | bytes 589832 | tf_op jit(solution)/shard_map/ppermute | solution.py:97
  102.9 6.2 %collective-permute-start.17 = (bf16[128,768]{1,0:T(8,128)(2,1)S(1)}, bf16[128,768]{1,0:T(8,128)(2,1)S(1)}, u32[]{:S(2)}, u32[]{:S(2)}) collective-permute-start(bf16[128,768]{1,0:T(8,128)(2,1)S(1)} %get-tuple-element.8), channel_id=1, source_target_pairs={{0,6},{1,7},{2,0},{3,1},{4,2},{5,3},{6,4},{7,5},{8,14},{9,15},{10,... | collective-permute-start | bytes 589832 | tf_op jit(solution)/shard_map/ppermute | solution.py:98
  105.6 15.9 %collective-permute-start.14 = (bf16[128,1536]{1,0:T(8,128)(2,1)S(1)}, bf16[128,1536]{1,0:T(8,128)(2,1)S(1)}, u32[]{:S(2)}, u32[]{:S(2)}) collective-permute-start(bf16[128,1536]{1,0:T(8,128)(2,1)S(1)} %get-tuple-element.5), channel_id=1, source_target_pairs={{0,6},{1,7},{2,0},{3,1},{4,2},{5,3},{6,4},{7,5},{8,14},{9,15},{10,... | collective-permute-start | bytes 1179656 | tf_op jit(solution)/shard_map/ppermute | solution.py:98
  105.7 15.8 %collective-permute-start.13 = (bf16[128,1536]{1,0:T(8,128)(2,1)S(1)}, bf16[128,1536]{1,0:T(8,128)(2,1)S(1)}, u32[]{:S(2)}, u32[]{:S(2)}) collective-permute-start(bf16[128,1536]{1,0:T(8,128)(2,1)S(1)} %get-tuple-element.6), channel_id=1, source_target_pairs={{0,2},{1,3},{2,4},{3,5},{4,6},{5,7},{6,0},{7,1},{8,10},{9,11},{10,... | collective-permute-start | bytes 1179656 | tf_op jit(solution)/shard_map/ppermute | solution.py:97
  109.2 12.2 %collective-permute-start.16 = (bf16[128,768]{1,0:T(8,128)(2,1)S(1)}, bf16[128,768]{1,0:T(8,128)(2,1)S(1)}, u32[]{:S(2)}, u32[]{:S(2)}) collective-permute-start(bf16[128,768]{1,0:T(8,128)(2,1)S(1)} %collective-permute-done.15), channel_id=1, source_target_pairs={{0,2},{1,3},{2,4},{3,5},{4,6},{5,7},{6,0},{7,1},{8,10},{9,11},{10,... | collective-permute-start | bytes 589832 | tf_op jit(solution)/shard_map/ppermute | solution.py:99
  109.2 12.2 %collective-permute-start.18 = (bf16[128,768]{1,0:T(8,128)(2,1)S(1)}, bf16[128,768]{1,0:T(8,128)(2,1)S(1)}, u32[]{:S(2)}, u32[]{:S(2)}) collective-permute-start(bf16[128,768]{1,0:T(8,128)(2,1)S(1)} %collective-permute-done.17), channel_id=1, source_target_pairs={{0,6},{1,7},{2,0},{3,1},{4,2},{5,3},{6,4},{7,5},{8,14},{9,15},{10,... | collective-permute-start | bytes 589832 | tf_op jit(solution)/shard_map/ppermute | solution.py:100

commit v8 on v7

--- a/solution.py
+++ b/solution.py
@@ -72,6 +72,7 @@
                          jnp.stack([other_by_x, mine_by_x], axis=1))
         saved_all = pair.reshape((n_col * saved_input.shape[0], saved_input.shape[1]))
 
+        saved_all, grad_all = lax.optimization_barrier((saved_all, grad_all))
         gelu_value, unused_slope = gelu_parts(saved_all.astype(jnp.float32))
         hidden = gelu_value.astype(jnp.bfloat16).reshape((n_z, n_y, rows_r, -1))
         hidden = jnp.swapaxes(hidden, 0, 1).reshape((tokens, -1))

time: 124 us -> 117 us (0.944)
  waiting for transfers between devices: 46.3 us -> 26.2 us
  starting transfers between devices: 39.7 us -> 47.7 us
  local copies, waits for them, and re-layouts: 14.4 us -> 19 us
  matrix products: 14.4 us -> 11.8 us
  other arithmetic: 7.18 us -> 9.57 us
    ppermute x3, waiting for transfers between devices: 17 us -> 0.01 us  [per_device(): got.append(lax.ppermute(saved_input, COL, chip_shift(n_col, s)))]
    ppermute x4, waiting for transfers between devices: 18.7 us -> 11 us  [ring_gather(): fwd = lax.ppermute(fwd, axis, ahead)]
    ppermute x1, waiting for transfers between devices: 0.01 us -> 5.63 us  [per_device(): chip_sum = mine + lax.ppermute(theirs, COL, core_swap(n_col))]
    ppermute x1, starting transfers between devices: 0.95 us -> 5.58 us  [per_device(): other_by_x = lax.ppermute(mine_by_x, COL, core_swap(n_col))]
    ppermute x4, starting transfers between devices: 10.8 us -> 15.3 us  [ring_gather(): bwd = lax.ppermute(bwd, axis, behind)]
    ppermute x4, starting transfers between devices: 3.83 us -> 0.01 us  [ring_gather(): fwd = lax.ppermute(fwd, axis, ahead)]
    ppermute x2, starting transfers between devices: 2.18 us -> 4.84 us  [per_device(): lax.ppermute((dest(-1), far[:, cut:]), COL, chip_shift(n_col, -1))]
    convert_element_type x0 -> x1, other arithmetic: none -> 2.16 us  [per_device(): hidden = gelu_value.astype(jnp.bfloat16).reshape((n_z, n_y, rows_r, -1))]
  transfers between devices with their start and end apart: 23 -> 23, of which waited for: 10 -> 7; matrix products, arithmetic and copies ran while one was open for 11% -> 20% of each run, Pallas kernels for 0% -> 0%
where the time goes in v8:
time: 117 us; the launch traced here: 115 us
  starting transfers between devices  47.7 us (41%)
  waiting for transfers between devices  26.2 us (22%)
  local copies, waits for them, and re-layouts  19 us (16%)
  matrix products  11.8 us (10%)
  other arithmetic  9.57 us (8%)
    ppermute x4, starting transfers between devices, ring_gather(): bwd = lax.ppermute(bwd, axis, behind)  15.3 us
    unnamed x38, local copies, waits for them, and re-layouts  11.6 us
    ppermute x4, waiting for transfers between devices, ring_gather(): fwd = lax.ppermute(fwd, axis, ahead)  11 us
    ppermute x1, starting transfers between devices, per_device(): chip_sum = mine + lax.ppermute(theirs, COL, core_swap(n_col))  8.13 us
    dot_general x1, matrix products, per_device(): lax.dot_general(hidden, grad_all, (((0,), (0,)), ((), ())), preferred_ele...  6.79 us
    ppermute x1, waiting for transfers between devices, per_device(): chip_sum = mine + lax.ppermute(theirs, COL, core_swap(n_col))  5.63 us
    ppermute x1, starting transfers between devices, per_device(): other_by_x = lax.ppermute(mine_by_x, COL, core_swap(n_col))  5.58 us
    ppermute x2, starting transfers between devices, ring_gather(): from_ahead = lax.ppermute(bwd[..., half:], axis, behind)  5.46 us
  transfers between devices with their start and end apart: 23, of which 7 were waited for; matrix products, arithmetic and copies ran while one was open for 20% of the time, Pallas kernels for 0%

profile of v8, /device:TPU:1, one launch (start us, length us, event | category | flops | bytes accessed | tf_op | source)
XLA Modules:
  0.0 115.3 jit_solution(2829574252017212452)
XLA Ops:
  0.6 6.5 %collective-permute-start.4 = (bf16[32,1536]{1,0:T(8,128)(2,1)}, bf16[32,1536]{1,0:T(8,128)(2,1)S(1)}, u32[]{:S(2)}, u32[]{:S(2)}) collective-permute-start(bf16[32,1536]{1,0:T(8,128)(2,1)} %param.4), channel_id=1, source_target_pairs={{0,224},{32,0},{64,32},{96,64},{128,96},{160,128},{192,160},{224,1... | collective-permute-start | bytes 294920 | tf_op jit(solution)/shard_map/ppermute | solution.py:44
  7.1 1.2 %collective-permute-start = (bf16[128,1536]{1,0:T(8,128)(2,1)}, bf16[128,1536]{1,0:T(8,128)(2,1)S(1)}, u32[]{:S(2)}, u32[]{:S(2)}) collective-permute-start(bf16[128,1536]{1,0:T(8,128)(2,1)} %param.3), channel_id=1, source_target_pairs={{0,2},{1,3},{2,4},{3,5},{4,6},{5,7},{6,0},{7,1},{8,10},{9,11},{10,... | collective-permute-start | bytes 1179656 | tf_op jit(solution)/shard_map/ppermute | solution.py:66
  8.3 2.5 %collective-permute-start.1 = (bf16[128,1536]{1,0:T(8,128)(2,1)}, bf16[128,1536]{1,0:T(8,128)(2,1)S(1)}, u32[]{:S(2)}, u32[]{:S(2)}) collective-permute-start(bf16[128,1536]{1,0:T(8,128)(2,1)} %param.3), channel_id=1, source_target_pairs={{0,4},{1,5},{2,6},{3,7},{4,0},{5,1},{6,2},{7,3},{8,12},{9,13},{10,... | collective-permute-start | bytes 1179656 | tf_op jit(solution)/shard_map/ppermute | solution.py:66
  12.9 2.8 %collective-permute-start.5 = (bf16[32,1536]{1,0:T(8,128)(2,1)S(1)}, bf16[32,1536]{1,0:T(8,128)(2,1)S(1)}, u32[]{:S(2)}, u32[]{:S(2)}) collective-permute-start(bf16[32,1536]{1,0:T(8,128)(2,1)S(1)} %collective-permute-done.4), channel_id=1, source_target_pairs={{0,224},{32,0},{64,32},{96,64},{128,96},{160,128},{192,160},{224,1... | collective-permute-start | bytes 294920 | tf_op jit(solution)/shard_map/ppermute | solution.py:44
  15.7 1.6 %collective-permute-done.5 = bf16[32,1536]{1,0:T(8,128)(2,1)S(1)} collective-permute-done((bf16[32,1536]{1,0:T(8,128)(2,1)S(1)}, bf16[32,1536]{1,0:T(8,128)(2,1)S(1)}, u32[]{:S(2)}, u32[]{:S(2)}) %collective-permute-start.5) | collective-permute-done | bytes 98336 | tf_op jit(solution)/shard_map/ppermute | solution.py:44
  17.3 3.3 %collective-permute-start.6 = (bf16[32,1536]{1,0:T(8,128)(2,1)S(1)}, bf16[32,1536]{1,0:T(8,128)(2,1)S(1)}, u32[]{:S(2)}, u32[]{:S(2)}) collective-permute-start(bf16[32,1536]{1,0:T(8,128)(2,1)S(1)} %collective-permute-done.5), channel_id=1, source_target_pairs={{0,224},{32,0},{64,32},{96,64},{128,96},{160,128},{192,160},{224,1... | collective-permute-start | bytes 294920 | tf_op jit(solution)/shard_map/ppermute | solution.py:44
  20.6 5.0 %collective-permute-done.9 = bf16[32,1536]{1,0:T(8,128)(2,1)S(1)} collective-permute-done((bf16[32,1536]{1,0:T(8,128)(2,1)S(1)}, bf16[32,1536]{1,0:T(8,128)(2,1)S(1)}, u32[]{:S(2)}, u32[]{:S(2)}) %collective-permute-start.9) | collective-permute-done | bytes 98336 | tf_op jit(solution)/shard_map/ppermute | solution.py:43
  25.6 2.7 %collective-permute-start.11 = (bf16[32,768]{1,0:T(8,128)(2,1)S(1)}, bf16[32,768]{1,0:T(8,128)(2,1)S(1)}, u32[]{:S(2)}, u32[]{:S(2)}) collective-permute-start(bf16[32,768]{1,0:T(8,128)(2,1)S(1)} %slice.27), channel_id=1, source_target_pairs={{0,224},{32,0},{64,32},{96,64},{128,96},{160,128},{192,160},{224,1... | collective-permute-start | bytes 147464 | tf_op jit(solution)/shard_map/ppermute | solution.py:40
  28.4 1.4 %collective-permute-done.10 = bf16[32,768]{1,0:T(8,128)(2,1)S(1)} collective-permute-done((bf16[32,768]{1,0:T(8,128)(2,1)S(1)}, bf16[32,768]{1,0:T(8,128)(2,1)S(1)}, u32[]{:S(2)}, u32[]{:S(2)}) %collective-permute-start.10) | collective-permute-done | bytes 49184 | tf_op jit(solution)/shard_map/ppermute | solution.py:39
  30.8 1.3 %bitcast_dynamic-update-slice_fusion.4 = (bf16[8,8,32,1536]{3,2,1,0:T(8,128)(2,1)}, bf16[8,32,1536]{2,1,0:T(8,128)(2,1)}) fusion(bf16[16,32,1536]{2,1,0:T(8,128)(2,1)S(1)} %bitcast_dynamic-update-slice_fusion.7, s32[]{:T(128)S(6)} %select_n.135), kind=kLoop, calls=%fused_computation.42 | loop fusion | bytes 2359300
  32.2 2.7 %collective-permute-start.12 = (bf16[8,32,1536]{2,1,0:T(8,128)(2,1)}, bf16[8,32,1536]{2,1,0:T(8,128)(2,1)}, u32[]{:S(2)}, u32[]{:S(2)}) collective-permute-start(bf16[8,32,1536]{2,1,0:T(8,128)(2,1)} %get-tuple-element.7), channel_id=1, source_target_pairs={{0,24},{8,0},{16,8},{24,16},{1,25},{9,1},{17,9},{25,17},{2,26},{10... | collective-permute-start | bytes 2359304 | tf_op jit(solution)/shard_map/ppermute | solution.py:44
  35.9 1.4 %pad_maximum_fusion = bf16[4,128,1536]{2,1,0:T(8,128)(2,1)S(1)} fusion(bf16[1,128,1536]{2,1,0:T(8,128)(2,1)} %bitcast.97, bf16[1,128,1536]{2,1,0:T(8,128)(2,1)} %bitcast.96, bf16[1,128,1536]{2,1,0:T(8,128)(2,1)} %bitcast.95, bf16[1,128,1536]{2,1,0:T(8,128)(2,1)S(1)} %bitcast.94), kind=kLoop, calls=%fused_computation.22 | loop fusion | flops 2359296 | bytes 3145728 | tf_op jit(solution)/shard_map/stack | solution.py:67
  38.2 5.6 %collective-permute-start.3 = (bf16[4,128,1536]{2,1,0:T(8,128)(2,1)S(1)}, bf16[4,128,1536]{2,1,0:T(8,128)(2,1)S(1)}, u32[]{:S(2)}, u32[]{:S(2)}) collective-permute-start(bf16[4,128,1536]{2,1,0:T(8,128)(2,1)S(1)} %broadcast_select_fusion), channel_id=1, source_target_pairs={{0,1},{1,0},{2,3},{3,2},{4,5},{5,4},{6,7},{7,6},{8,9},{9,8},{10,11... | collective-permute-start | bytes 4718600 | tf_op jit(solution)/shard_map/ppermute | solution.py:70
  44.0 6.0 %collective-permute-done.13 = bf16[8,32,1536]{2,1,0:T(8,128)(2,1)} collective-permute-done((bf16[8,32,1536]{2,1,0:T(8,128)(2,1)}, bf16[8,32,1536]{2,1,0:T(8,128)(2,1)}, u32[]{:S(2)}, u32[]{:S(2)}) %collective-permute-start.13) | collective-permute-done | bytes 786464 | tf_op jit(solution)/shard_map/ppermute | solution.py:43
  52.4 2.7 %collective-permute-start.15 = (bf16[8,32,768]{2,1,0:T(8,128)(2,1)S(1)}, bf16[8,32,768]{2,1,0:T(8,128)(2,1)S(1)}, u32[]{:S(2)}, u32[]{:S(2)}) collective-permute-start(bf16[8,32,768]{2,1,0:T(8,128)(2,1)S(1)} %slice.29), channel_id=1, source_target_pairs={{0,24},{8,0},{16,8},{24,16},{1,25},{9,1},{17,9},{25,17},{2,26},{10... | collective-permute-start | bytes 1179656 | tf_op jit(solution)/shard_map/ppermute | solution.py:40
  56.3 3.5 %collective-permute-done.14 = bf16[8,32,768]{2,1,0:T(8,128)(2,1)S(1)} collective-permute-done((bf16[8,32,768]{2,1,0:T(8,128)(2,1)S(1)}, bf16[8,32,768]{2,1,0:T(8,128)(2,1)S(1)}, u32[]{:S(2)}, u32[]{:S(2)}) %collective-permute-start.14) | collective-permute-done | bytes 393248 | tf_op jit(solution)/shard_map/ppermute | solution.py:39
  61.1 1.2 %bitcast_dynamic-update-slice_fusion.5 = bf16[8,8,32,1536]{3,2,1,0:T(8,128)(2,1)S(1)} fusion(bf16[8,8,32,1536]{3,2,1,0:T(8,128)(2,1)S(1)} %bitcast_dynamic-update-slice_fusion, bf16[8,32,1536]{2,1,0:T(8,128)(2,1)} %get-tuple-element.7), kind=kLoop, calls=%fused_computation.43 | loop fusion | bytes 1572864
  62.2 1.2 %bitcast_dynamic-update-slice_fusion.3 = bf16[8,8,32,1536]{3,2,1,0:T(8,128)(2,1)S(1)} fusion(bf16[8,8,32,1536]{3,2,1,0:T(8,128)(2,1)S(1)} %bitcast_dynamic-update-slice_fusion.5, bf16[8,32,1536]{2,1,0:T(8,128)(2,1)} %collective-permute-done.12), kind=kLoop, calls=%fused_computation.41 | loop fusion | bytes 1572864
  63.5 1.3 %bitcast_dynamic-update-slice_fusion.1 = bf16[8,8,32,1536]{3,2,1,0:T(8,128)(2,1)S(1)} fusion(bf16[8,8,32,1536]{3,2,1,0:T(8,128)(2,1)S(1)} %fusion.17, bf16[8,32,1536]{2,1,0:T(8,128)(2,1)} %collective-permute-done.13), kind=kLoop, calls=%fused_computation.39 | loop fusion | bytes 1572864 | tf_op jit(solution)/shard_map/jit(_roll_dynamic)/concatenate | solution.py:48
  66.9 5.1 %fusion.27 = f32[1024,1536]{1,0:T(8,128)S(1)} fusion(bf16[1024,1536]{1,0:T(8,128)(2,1)S(1)} %bitcast.90, bf16[1536,1536]{1,0:T(8,128)(2,1)S(1)} %bitcast.99), kind=kOutput, calls=%fused_computation.85 | convolution fusion | flops 4831838208 | bytes 14155776 | tf_op jit(solution)/shard_map/dot_general | solution.py:83
  72.4 2.0 %dynamic-slice_bitcast_fusion = f32[4,128,1536]{2,1,0:T(8,128)} fusion(f32[4,2,128,1536]{3,2,1,0:T(8,128)S(1)} %bitcast.85, s32[]{:T(128)S(6)} %select_n.139), kind=kLoop, calls=%fused_computation.14 | loop fusion | bytes 6291460 | tf_op jit(solution)/shard_map/jit(dynamic_index_in_dim)/squeeze | solution.py:90
  74.5 1.6 %copy-done = f32[4,8,32,1536]{3,2,0,1:T(8,128)} copy-done((f32[4,8,32,1536]{3,2,0,1:T(8,128)}, f32[4,8,32,1536]{3,2,0,1:T(8,128)S(1)}, u32[]{:S(2)}) %copy-start) | copy-done | bytes 6291480
  76.0 8.1 %collective-permute-start.16 = (f32[4,128,1536]{2,1,0:T(8,128)}, f32[4,128,1536]{2,1,0:T(8,128)}, u32[]{:S(2)}, u32[]{:S(2)}) collective-permute-start(f32[4,128,1536]{2,1,0:T(8,128)} %dynamic-slice_bitcast_fusion), channel_id=1, source_target_pairs={{0,1},{1,0},{2,3},{3,2},{4,5},{5,4},{6,7},{7,6},{8,9},{9,8},{10,11... | collective-permute-start | bytes 9437192 | tf_op jit(solution)/shard_map/ppermute | solution.py:91
  84.2 5.6 %collective-permute-done.16 = f32[4,128,1536]{2,1,0:T(8,128)} collective-permute-done((f32[4,128,1536]{2,1,0:T(8,128)}, f32[4,128,1536]{2,1,0:T(8,128)}, u32[]{:S(2)}, u32[]{:S(2)}) %collective-permute-start.16) | collective-permute-done | bytes 3145760 | tf_op jit(solution)/shard_map/ppermute | solution.py:91
  89.8 3.4 %bitcast_add_fusion = f32[4,128,1536]{2,1,0:T(8,128)S(1)} fusion(f32[4,128,1536]{2,1,0:T(8,128)} %collective-permute-done.16, f32[4,2,128,1536]{3,2,1,0:T(8,128)} %bitcast.86, s32[]{:T(128)S(6)} %select_n.138), kind=kLoop, calls=%fused_computation.13 | loop fusion | flops 786432 | bytes 9437188 | tf_op jit(solution)/shard_map/add | solution.py:91
  94.0 2.2 %collective-permute-start.21 = (bf16[128,768]{1,0:T(8,128)(2,1)S(1)}, bf16[128,768]{1,0:T(8,128)(2,1)S(1)}, u32[]{:S(2)}, u32[]{:S(2)}) collective-permute-start(bf16[128,768]{1,0:T(8,128)(2,1)S(1)} %get-tuple-element.12), channel_id=1, source_target_pairs={{0,6},{1,7},{2,0},{3,1},{4,2},{5,3},{6,4},{7,5},{8,14},{9,15},{10,... | collective-permute-start | bytes 589832 | tf_op jit(solution)/shard_map/ppermute | solution.py:99
  96.1 2.2 %fusion.1 = bf16[1024,1536]{1,0:T(8,128)(2,1)S(1)} fusion(bf16[1024,1536]{1,0:T(8,128)(2,1)S(1)} %bitcast.87), kind=kLoop, calls=%fused_computation.8 | loop fusion | flops 15728640 | bytes 6291456 | tf_op jit(solution)/shard_map/convert_element_type | solution.py:77
  98.7 2.7 %collective-permute-start.18 = (bf16[128,1536]{1,0:T(8,128)(2,1)S(1)}, bf16[128,1536]{1,0:T(8,128)(2,1)S(1)}, u32[]{:S(2)}, u32[]{:S(2)}) collective-permute-start(bf16[128,1536]{1,0:T(8,128)(2,1)S(1)} %get-tuple-element.9), channel_id=1, source_target_pairs={{0,6},{1,7},{2,0},{3,1},{4,2},{5,3},{6,4},{7,5},{8,14},{9,15},{10,... | collective-permute-start | bytes 1179656 | tf_op jit(solution)/shard_map/ppermute | solution.py:99
  101.4 2.7 %collective-permute-start.22 = (bf16[128,768]{1,0:T(8,128)(2,1)S(1)}, bf16[128,768]{1,0:T(8,128)(2,1)S(1)}, u32[]{:S(2)}, u32[]{:S(2)}) collective-permute-start(bf16[128,768]{1,0:T(8,128)(2,1)S(1)} %collective-permute-done.21), channel_id=1, source_target_pairs={{0,6},{1,7},{2,0},{3,1},{4,2},{5,3},{6,4},{7,5},{8,14},{9,15},{10,... | collective-permute-start | bytes 589832 | tf_op jit(solution)/shard_map/ppermute | solution.py:101
  104.1 6.8 %convolution_convert_fusion = bf16[1536,1536]{1,0:T(8,128)(2,1)} fusion(bf16[1024,1536]{1,0:T(8,128)(2,1)S(1)} %bitcast.92, bf16[1024,1536]{1,0:T(8,128)(2,1)S(1)} %bitcast.91), kind=kOutput, calls=%fused_computation.6 | convolution fusion | flops 4834197504 | bytes 11010048 | tf_op jit(solution)/shard_map/dot_general | solution.py:79
  110.9 3.0 %collective-permute-done.20 = bf16[128,768]{1,0:T(8,128)(2,1)S(1)} collective-permute-done((bf16[128,768]{1,0:T(8,128)(2,1)S(1)}, bf16[128,768]{1,0:T(8,128)(2,1)S(1)}, u32[]{:S(2)}, u32[]{:S(2)}) %collective-permute-start.20) | collective-permute-done | bytes 196640 | tf_op jit(solution)/shard_map/ppermute | solution.py:100
  113.9 1.4 %fusion.12 = bf16[128,1536]{1,0:T(8,128)(2,1)} fusion(bf16[128,1536]{1,0:T(8,128)(2,1)S(1)} %copy-done.4, bf16[128,1536]{1,0:T(8,128)(2,1)S(1)} %collective-permute-done.18, bf16[128,1536]{1,0:T(8,128)(2,1)S(1)} %collective-permute-done.17, f32[4,128,1536]{2,1,0:T(8,128)S(1)} %bitcast_add_fusion, s32[]{:T(128)S(6)} %select_n.140, ...), kind=kLoop, calls=%fused_computation.32 | loop fusion | flops 5701632 | bytes 2752516 | tf_op jit(solution)/shard_map/convert_element_type | solution.py:111
  (82 shorter events, 13.7 us)
Async XLA Ops:
  0.6 35.3 %copy-start.4 = (bf16[128,1536]{1,0:T(8,128)(2,1)S(1)}, bf16[128,1536]{1,0:T(8,128)(2,1)}, u32[]{:S(2)}) copy-start(bf16[128,1536]{1,0:T(8,128)(2,1)} %param.3) | copy-start | bytes 1179652
  0.6 12.3 %collective-permute-start.4 = (bf16[32,1536]{1,0:T(8,128)(2,1)}, bf16[32,1536]{1,0:T(8,128)(2,1)S(1)}, u32[]{:S(2)}, u32[]{:S(2)}) collective-permute-start(bf16[32,1536]{1,0:T(8,128)(2,1)} %param.4), channel_id=1, source_target_pairs={{0,224},{32,0},{64,32},{96,64},{128,96},{160,128},{192,160},{224,1... | collective-permute-start | bytes 294920 | tf_op jit(solution)/shard_map/ppermute | solution.py:44
  7.1 8.5 %collective-permute-start.7 = (bf16[32,1536]{1,0:T(8,128)(2,1)}, bf16[32,1536]{1,0:T(8,128)(2,1)S(1)}, u32[]{:S(2)}, u32[]{:S(2)}) collective-permute-start(bf16[32,1536]{1,0:T(8,128)(2,1)} %param.4), channel_id=1, source_target_pairs={{0,32},{32,64},{64,96},{96,128},{128,160},{160,192},{192,224},{224... | collective-permute-start | bytes 294920 | tf_op jit(solution)/shard_map/ppermute | solution.py:43
  7.1 27.8 %collective-permute-start = (bf16[128,1536]{1,0:T(8,128)(2,1)}, bf16[128,1536]{1,0:T(8,128)(2,1)S(1)}, u32[]{:S(2)}, u32[]{:S(2)}) collective-permute-start(bf16[128,1536]{1,0:T(8,128)(2,1)} %param.3), channel_id=1, source_target_pairs={{0,2},{1,3},{2,4},{3,5},{4,6},{5,7},{6,0},{7,1},{8,10},{9,11},{10,... | collective-permute-start | bytes 1179656 | tf_op jit(solution)/shard_map/ppermute | solution.py:66
  8.3 26.6 %collective-permute-start.1 = (bf16[128,1536]{1,0:T(8,128)(2,1)}, bf16[128,1536]{1,0:T(8,128)(2,1)S(1)}, u32[]{:S(2)}, u32[]{:S(2)}) collective-permute-start(bf16[128,1536]{1,0:T(8,128)(2,1)} %param.3), channel_id=1, source_target_pairs={{0,4},{1,5},{2,6},{3,7},{4,0},{5,1},{6,2},{7,3},{8,12},{9,13},{10,... | collective-permute-start | bytes 1179656 | tf_op jit(solution)/shard_map/ppermute | solution.py:66
  10.8 24.1 %collective-permute-start.2 = (bf16[128,1536]{1,0:T(8,128)(2,1)}, bf16[128,1536]{1,0:T(8,128)(2,1)S(1)}, u32[]{:S(2)}, u32[]{:S(2)}) collective-permute-start(bf16[128,1536]{1,0:T(8,128)(2,1)} %param.3), channel_id=1, source_target_pairs={{0,6},{1,7},{2,0},{3,1},{4,2},{5,3},{6,4},{7,5},{8,14},{9,15},{10,... | collective-permute-start | bytes 1179656 | tf_op jit(solution)/shard_map/ppermute | solution.py:66
  12.9 4.4 %collective-permute-start.5 = (bf16[32,1536]{1,0:T(8,128)(2,1)S(1)}, bf16[32,1536]{1,0:T(8,128)(2,1)S(1)}, u32[]{:S(2)}, u32[]{:S(2)}) collective-permute-start(bf16[32,1536]{1,0:T(8,128)(2,1)S(1)} %collective-permute-done.4), channel_id=1, source_target_pairs={{0,224},{32,0},{64,32},{96,64},{128,96},{160,128},{192,160},{224,1... | collective-permute-start | bytes 294920 | tf_op jit(solution)/shard_map/ppermute | solution.py:44
  15.7 5.0 %collective-permute-start.8 = (bf16[32,1536]{1,0:T(8,128)(2,1)S(1)}, bf16[32,1536]{1,0:T(8,128)(2,1)S(1)}, u32[]{:S(2)}, u32[]{:S(2)}) collective-permute-start(bf16[32,1536]{1,0:T(8,128)(2,1)S(1)} %collective-permute-done.7), channel_id=1, source_target_pairs={{0,32},{32,64},{64,96},{96,128},{128,160},{160,192},{192,224},{224... | collective-permute-start | bytes 294920 | tf_op jit(solution)/shard_map/ppermute | solution.py:43
  17.3 8.3 %collective-permute-start.6 = (bf16[32,1536]{1,0:T(8,128)(2,1)S(1)}, bf16[32,1536]{1,0:T(8,128)(2,1)S(1)}, u32[]{:S(2)}, u32[]{:S(2)}) collective-permute-start(bf16[32,1536]{1,0:T(8,128)(2,1)S(1)} %collective-permute-done.5), channel_id=1, source_target_pairs={{0,224},{32,0},{64,32},{96,64},{128,96},{160,128},{192,160},{224,1... | collective-permute-start | bytes 294920 | tf_op jit(solution)/shard_map/ppermute | solution.py:44
  20.6 5.0 %collective-permute-start.9 = (bf16[32,1536]{1,0:T(8,128)(2,1)S(1)}, bf16[32,1536]{1,0:T(8,128)(2,1)S(1)}, u32[]{:S(2)}, u32[]{:S(2)}) collective-permute-start(bf16[32,1536]{1,0:T(8,128)(2,1)S(1)} %collective-permute-done.8), channel_id=1, source_target_pairs={{0,32},{32,64},{64,96},{96,128},{128,160},{160,192},{192,224},{224... | collective-permute-start | bytes 294920 | tf_op jit(solution)/shard_map/ppermute | solution.py:43
  25.6 4.2 %collective-permute-start.10 = (bf16[32,768]{1,0:T(8,128)(2,1)S(1)}, bf16[32,768]{1,0:T(8,128)(2,1)S(1)}, u32[]{:S(2)}, u32[]{:S(2)}) collective-permute-start(bf16[32,768]{1,0:T(8,128)(2,1)S(1)} %slice.26), channel_id=1, source_target_pairs={{0,32},{32,64},{64,96},{96,128},{128,160},{160,192},{192,224},{224... | collective-permute-start | bytes 147464 | tf_op jit(solution)/shard_map/ppermute | solution.py:39
  25.6 4.1 %collective-permute-start.11 = (bf16[32,768]{1,0:T(8,128)(2,1)S(1)}, bf16[32,768]{1,0:T(8,128)(2,1)S(1)}, u32[]{:S(2)}, u32[]{:S(2)}) collective-permute-start(bf16[32,768]{1,0:T(8,128)(2,1)S(1)} %slice.27), channel_id=1, source_target_pairs={{0,224},{32,0},{64,32},{96,64},{128,96},{160,128},{192,160},{224,1... | collective-permute-start | bytes 147464 | tf_op jit(solution)/shard_map/ppermute | solution.py:40
  32.2 19.2 %collective-permute-start.12 = (bf16[8,32,1536]{2,1,0:T(8,128)(2,1)}, bf16[8,32,1536]{2,1,0:T(8,128)(2,1)}, u32[]{:S(2)}, u32[]{:S(2)}) collective-permute-start(bf16[8,32,1536]{2,1,0:T(8,128)(2,1)} %get-tuple-element.7), channel_id=1, source_target_pairs={{0,24},{8,0},{16,8},{24,16},{1,25},{9,1},{17,9},{25,17},{2,26},{10... | collective-permute-start | bytes 2359304 | tf_op jit(solution)/shard_map/ppermute | solution.py:44
  34.9 15.1 %collective-permute-start.13 = (bf16[8,32,1536]{2,1,0:T(8,128)(2,1)}, bf16[8,32,1536]{2,1,0:T(8,128)(2,1)}, u32[]{:S(2)}, u32[]{:S(2)}) collective-permute-start(bf16[8,32,1536]{2,1,0:T(8,128)(2,1)} %get-tuple-element.7), channel_id=1, source_target_pairs={{0,8},{8,16},{16,24},{24,0},{1,9},{9,17},{17,25},{25,1},{2,10},{10... | collective-permute-start | bytes 2359304 | tf_op jit(solution)/shard_map/ppermute | solution.py:43
  34.9 0.9 copy-start.6
  34.9 1.0 copy-start.7
  38.0 17.1 %copy-start.3 = (bf16[8,8,32,1536]{3,2,1,0:T(8,128)(2,1)S(1)}, bf16[8,8,32,1536]{3,2,1,0:T(8,128)(2,1)}, u32[]{:S(2)}) copy-start(bf16[8,8,32,1536]{3,2,1,0:T(8,128)(2,1)} %get-tuple-element.6) | copy-start | bytes 18874372
  38.2 27.0 %collective-permute-start.3 = (bf16[4,128,1536]{2,1,0:T(8,128)(2,1)S(1)}, bf16[4,128,1536]{2,1,0:T(8,128)(2,1)S(1)}, u32[]{:S(2)}, u32[]{:S(2)}) collective-permute-start(bf16[4,128,1536]{2,1,0:T(8,128)(2,1)S(1)} %broadcast_select_fusion), channel_id=1, source_target_pairs={{0,1},{1,0},{2,3},{3,2},{4,5},{5,4},{6,7},{7,6},{8,9},{9,8},{10,11... | collective-permute-start | bytes 4718600 | tf_op jit(solution)/shard_map/ppermute | solution.py:70
  51.0 8.7 %collective-permute-start.14 = (bf16[8,32,768]{2,1,0:T(8,128)(2,1)S(1)}, bf16[8,32,768]{2,1,0:T(8,128)(2,1)S(1)}, u32[]{:S(2)}, u32[]{:S(2)}) collective-permute-start(bf16[8,32,768]{2,1,0:T(8,128)(2,1)S(1)} %slice.28), channel_id=1, source_target_pairs={{0,8},{8,16},{16,24},{24,0},{1,9},{9,17},{17,25},{25,1},{2,10},{10... | collective-permute-start | bytes 1179656 | tf_op jit(solution)/shard_map/ppermute | solution.py:39
  52.4 7.5 %collective-permute-start.15 = (bf16[8,32,768]{2,1,0:T(8,128)(2,1)S(1)}, bf16[8,32,768]{2,1,0:T(8,128)(2,1)S(1)}, u32[]{:S(2)}, u32[]{:S(2)}) collective-permute-start(bf16[8,32,768]{2,1,0:T(8,128)(2,1)S(1)} %slice.29), channel_id=1, source_target_pairs={{0,24},{8,0},{16,8},{24,16},{1,25},{9,1},{17,9},{25,17},{2,26},{10... | collective-permute-start | bytes 1179656 | tf_op jit(solution)/shard_map/ppermute | solution.py:40
  63.5 3.4 %slice-start = ((s8[4718592]{0:T(1024)(128)(4,1)}), s8[4194304]{0:T(1024)(128)(4,1)S(1)}, s32[]{:S(2)}) async-start(s8[4718592]{0:T(1024)(128)(4,1)} %bitcast.98), calls=%async_computation | async-start | bytes 8388608
  64.8 2.1 %slice-start.1 = ((s8[4718592]{0:T(1024)(128)(4,1)}), s8[524288]{0:T(1024)(128)(4,1)S(1)}, s32[]{:S(2)}) async-start(s8[4718592]{0:T(1024)(128)(4,1)} %bitcast.98), calls=%async_computation.1 | async-start | bytes 1048576
  65.2 1.7 %copy-start.1 = (bf16[4,8,32,1536]{3,2,1,0:T(8,128)(2,1)}, bf16[4,8,32,1536]{3,2,1,0:T(8,128)(2,1)S(1)}, u32[]{:S(2)}) copy-start(bf16[4,8,32,1536]{3,2,1,0:T(8,128)(2,1)S(1)} %constant_dynamic-slice_fusion) | copy-start | bytes 9437188
  72.4 3.6 %copy-start = (f32[4,8,32,1536]{3,2,0,1:T(8,128)}, f32[4,8,32,1536]{3,2,0,1:T(8,128)S(1)}, u32[]{:S(2)}) copy-start(f32[4,8,32,1536]{3,2,0,1:T(8,128)S(1)} %copy.6) | copy-start | bytes 18874372
  76.0 13.8 %collective-permute-start.16 = (f32[4,128,1536]{2,1,0:T(8,128)}, f32[4,128,1536]{2,1,0:T(8,128)}, u32[]{:S(2)}, u32[]{:S(2)}) collective-permute-start(f32[4,128,1536]{2,1,0:T(8,128)} %dynamic-slice_bitcast_fusion), channel_id=1, source_target_pairs={{0,1},{1,0},{2,3},{3,2},{4,5},{5,4},{6,7},{7,6},{8,9},{9,8},{10,11... | collective-permute-start | bytes 9437192 | tf_op jit(solution)/shard_map/ppermute | solution.py:91
  93.4 8.0 %collective-permute-start.19 = (bf16[128,768]{1,0:T(8,128)(2,1)S(1)}, bf16[128,768]{1,0:T(8,128)(2,1)S(1)}, u32[]{:S(2)}, u32[]{:S(2)}) collective-permute-start(bf16[128,768]{1,0:T(8,128)(2,1)S(1)} %get-tuple-element.11), channel_id=1, source_target_pairs={{0,2},{1,3},{2,4},{3,5},{4,6},{5,7},{6,0},{7,1},{8,10},{9,11},{10,... | collective-permute-start | bytes 589832 | tf_op jit(solution)/shard_map/ppermute | solution.py:98
  94.0 7.4 %collective-permute-start.21 = (bf16[128,768]{1,0:T(8,128)(2,1)S(1)}, bf16[128,768]{1,0:T(8,128)(2,1)S(1)}, u32[]{:S(2)}, u32[]{:S(2)}) collective-permute-start(bf16[128,768]{1,0:T(8,128)(2,1)S(1)} %get-tuple-element.12), channel_id=1, source_target_pairs={{0,6},{1,7},{2,0},{3,1},{4,2},{5,3},{6,4},{7,5},{8,14},{9,15},{10,... | collective-permute-start | bytes 589832 | tf_op jit(solution)/shard_map/ppermute | solution.py:99
  98.3 5.8 %copy-start.2 = (bf16[4,8,32,1536]{3,2,1,0:T(8,128)(2,1)S(1)}, bf16[4,8,32,1536]{3,2,1,0:T(8,128)(2,1)}, u32[]{:S(2)}) copy-start(bf16[4,8,32,1536]{3,2,1,0:T(8,128)(2,1)} %copy-done.1) | copy-start | bytes 9437188
  98.6 15.2 %collective-permute-start.17 = (bf16[128,1536]{1,0:T(8,128)(2,1)S(1)}, bf16[128,1536]{1,0:T(8,128)(2,1)S(1)}, u32[]{:S(2)}, u32[]{:S(2)}) collective-permute-start(bf16[128,1536]{1,0:T(8,128)(2,1)S(1)} %get-tuple-element.10), channel_id=1, source_target_pairs={{0,2},{1,3},{2,4},{3,5},{4,6},{5,7},{6,0},{7,1},{8,10},{9,11},{10,... | collective-permute-start | bytes 1179656 | tf_op jit(solution)/shard_map/ppermute | solution.py:98
  98.7 15.2 %collective-permute-start.18 = (bf16[128,1536]{1,0:T(8,128)(2,1)S(1)}, bf16[128,1536]{1,0:T(8,128)(2,1)S(1)}, u32[]{:S(2)}, u32[]{:S(2)}) collective-permute-start(bf16[128,1536]{1,0:T(8,128)(2,1)S(1)} %get-tuple-element.9), channel_id=1, source_target_pairs={{0,6},{1,7},{2,0},{3,1},{4,2},{5,3},{6,4},{7,5},{8,14},{9,15},{10,... | collective-permute-start | bytes 1179656 | tf_op jit(solution)/shard_map/ppermute | solution.py:99
  101.4 12.5 %collective-permute-start.20 = (bf16[128,768]{1,0:T(8,128)(2,1)S(1)}, bf16[128,768]{1,0:T(8,128)(2,1)S(1)}, u32[]{:S(2)}, u32[]{:S(2)}) collective-permute-start(bf16[128,768]{1,0:T(8,128)(2,1)S(1)} %collective-permute-done.19), channel_id=1, source_target_pairs={{0,2},{1,3},{2,4},{3,5},{4,6},{5,7},{6,0},{7,1},{8,10},{9,11},{10,... | collective-permute-start | bytes 589832 | tf_op jit(solution)/shard_map/ppermute | solution.py:100
  101.4 12.5 %collective-permute-start.22 = (bf16[128,768]{1,0:T(8,128)(2,1)S(1)}, bf16[128,768]{1,0:T(8,128)(2,1)S(1)}, u32[]{:S(2)}, u32[]{:S(2)}) collective-permute-start(bf16[128,768]{1,0:T(8,128)(2,1)S(1)} %collective-permute-done.21), channel_id=1, source_target_pairs={{0,6},{1,7},{2,0},{3,1},{4,2},{5,3},{6,4},{7,5},{8,14},{9,15},{10,... | collective-permute-start | bytes 589832 | tf_op jit(solution)/shard_map/ppermute | solution.py:101
  (1 other events, 0.8 us)

commit v9 on v8

--- a/solution.py
+++ b/solution.py
@@ -80,20 +80,33 @@
             hidden, grad_all, (((0,), (0,)), ((), ())), preferred_element_type=jnp.float32
         ).astype(jnp.bfloat16)
 
-        partial = lax.dot_general(
-            grad_all, weight, (((1,), (1,)), ((), ())), preferred_element_type=jnp.float32
-        )
         rows = saved_input.shape[0]
-        p_nat = jnp.swapaxes(partial.reshape((n_y, n_z, rows_r, -1)), 0, 1)
-        p4 = p_nat.reshape((n_x, 2, rows, partial.shape[1]))
-        mine = lax.dynamic_index_in_dim(p4, k, axis=1, keepdims=False)
-        theirs = lax.dynamic_index_in_dim(p4, 1 - k, axis=1, keepdims=False)
-        chip_sum = mine + lax.ppermute(theirs, COL, core_swap(n_col))
-        back = lax.dynamic_index_in_dim(chip_sum, x, axis=0, keepdims=False)
-        dest = lambda s: lax.dynamic_index_in_dim(
-            chip_sum, (x + s) % n_x, axis=0, keepdims=False).astype(jnp.bfloat16)
+        if n_z == n_col:
+            g = grad_all.reshape((n_y, n_x, 2, rows_r, -1))
+            g_theirs = lax.dynamic_index_in_dim(g, 1 - k, axis=2, keepdims=False)
+            g_mine = lax.dynamic_index_in_dim(g, k, axis=2, keepdims=False)
+            p_theirs = lax.dot_general(g_theirs, weight, (((3,), (1,)), ((), ())),
+                                       preferred_element_type=jnp.float32)
+            got_theirs = lax.ppermute(p_theirs.astype(jnp.bfloat16), COL, core_swap(n_col))
+            p_mine = lax.dot_general(g_mine, weight, (((3,), (1,)), ((), ())),
+                                     preferred_element_type=jnp.float32)
+            chip_sum = p_mine + got_theirs.astype(jnp.float32)
+            pick = lambda c: lax.dynamic_index_in_dim(
+                chip_sum, c, axis=1, keepdims=False).reshape((rows, -1))
+        else:
+            partial = lax.dot_general(
+                grad_all, weight, (((1,), (1,)), ((), ())), preferred_element_type=jnp.float32
+            )
+            p_nat = jnp.swapaxes(partial.reshape((n_y, n_z, rows_r, -1)), 0, 1)
+            p4 = p_nat.reshape((n_x, 2, rows, partial.shape[1]))
+            mine = lax.dynamic_index_in_dim(p4, k, axis=1, keepdims=False)
+            theirs = lax.dynamic_index_in_dim(p4, 1 - k, axis=1, keepdims=False)
+            chip_sum = mine + lax.ppermute(theirs, COL, core_swap(n_col))
+            pick = lambda c: lax.dynamic_index_in_dim(chip_sum, c, axis=0, keepdims=False)
+        back = pick(x)
+        dest = lambda s: pick((x + s) % n_x).astype(jnp.bfloat16)
         if n_x == 4:
-            cut = chip_sum.shape[-1] // 2
+            cut = back.shape[-1] // 2
             far = dest(2)
             up, up_relay = lax.ppermute((dest(1), far[:, :cut]), COL, chip_shift(n_col, 1))
             dn, dn_relay = lax.ppermute((dest(-1), far[:, cut:]), COL, chip_shift(n_col, -1))

time: 117 us -> 110 us (0.940)
  local copies, waits for them, and re-layouts: 19 us -> 14.6 us
  matrix products: 11.8 us -> 16.2 us
  other arithmetic: 9.57 us -> 6.16 us
  waiting for transfers between devices: 26.2 us -> 23.1 us
    ppermute x1, waiting for transfers between devices: 5.63 us -> 0.99 us  [per_device(): lax.ppermute(p_theirs.astype(jnp.bfloat16), COL, core_swap(n_col))]
    dot_general x1 -> x2, matrix products: 5.06 us -> 9.26 us  [the longest x1 5.49 us: per_device(): lax.dot_general(g_mine, weight, (((3,), (1,)), ((), ())), preferred_eleme...]
    add x1 -> x0, other arithmetic: 3.42 us -> none  [per_device(): chip_sum = mine + lax.ppermute(theirs, COL, core_swap(n_col))]
    squeeze x1 -> x0, local copies, waits for them, and re-layouts: 2.02 us -> none  [per_device(): theirs = lax.dynamic_index_in_dim(p4, 1 - k, axis=1, keepdims=False)]
    unnamed x38, local copies, waits for them, and re-layouts: 11.6 us -> 9.84 us
    ppermute x1, waiting for transfers between devices: 3.01 us -> 4.54 us  [per_device(): far_lo = lax.ppermute(up_relay, COL, chip_shift(n_col, 1))]
  transfers between devices with their start and end apart: 23 -> 23, of which waited for: 7 -> 7; matrix products, arithmetic and copies ran while one was open for 20% -> 21% of each run, Pallas kernels for 0% -> 0%
where the time goes in v9:
time: 110 us; the launch traced here: 109 us
  starting transfers between devices  47.7 us (43%)
  waiting for transfers between devices  23.1 us (21%)
  matrix products  16.2 us (15%)
  local copies, waits for them, and re-layouts  14.6 us (13%)
  other arithmetic  6.16 us (6%)
    ppermute x4, starting transfers between devices, ring_gather(): bwd = lax.ppermute(bwd, axis, behind)  15.3 us
    ppermute x4, waiting for transfers between devices, ring_gather(): fwd = lax.ppermute(fwd, axis, ahead)  11 us
    unnamed x38, local copies, waits for them, and re-layouts  9.84 us
    ppermute x1, starting transfers between devices, per_device(): lax.ppermute(p_theirs.astype(jnp.bfloat16), COL, core_swap(n_col))  8.13 us
    dot_general x1, matrix products, per_device(): lax.dot_general(hidden, grad_all, (((0,), (0,)), ((), ())), preferred_ele...  6.92 us
    ppermute x1, starting transfers between devices, per_device(): other_by_x = lax.ppermute(mine_by_x, COL, core_swap(n_col))  5.58 us
    dot_general x1, matrix products, per_device(): lax.dot_general(g_mine, weight, (((3,), (1,)), ((), ())), preferred_eleme...  5.49 us
    ppermute x2, starting transfers between devices, ring_gather(): from_ahead = lax.ppermute(bwd[..., half:], axis, behind)  5.46 us
  transfers between devices with their start and end apart: 23, of which 7 were waited for; matrix products, arithmetic and copies ran while one was open for 21% of the time, Pallas kernels for 0%

profile of v9, /device:TPU:1, one launch (start us, length us, event | category | flops | bytes accessed | tf_op | source)
XLA Modules:
  0.0 108.7 jit_solution(16883752726753701587)
XLA Ops:
  0.6 6.5 %collective-permute-start.4 = (bf16[32,1536]{1,0:T(8,128)(2,1)}, bf16[32,1536]{1,0:T(8,128)(2,1)S(1)}, u32[]{:S(2)}, u32[]{:S(2)}) collective-permute-start(bf16[32,1536]{1,0:T(8,128)(2,1)} %param.4), channel_id=1, source_target_pairs={{0,224},{32,0},{64,32},{96,64},{128,96},{160,128},{192,160},{224,1... | collective-permute-start | bytes 294920 | tf_op jit(solution)/shard_map/ppermute | solution.py:44
  7.1 1.2 %collective-permute-start = (bf16[128,1536]{1,0:T(8,128)(2,1)}, bf16[128,1536]{1,0:T(8,128)(2,1)S(1)}, u32[]{:S(2)}, u32[]{:S(2)}) collective-permute-start(bf16[128,1536]{1,0:T(8,128)(2,1)} %param.3), channel_id=1, source_target_pairs={{0,2},{1,3},{2,4},{3,5},{4,6},{5,7},{6,0},{7,1},{8,10},{9,11},{10,... | collective-permute-start | bytes 1179656 | tf_op jit(solution)/shard_map/ppermute | solution.py:66
  8.3 2.5 %collective-permute-start.1 = (bf16[128,1536]{1,0:T(8,128)(2,1)}, bf16[128,1536]{1,0:T(8,128)(2,1)S(1)}, u32[]{:S(2)}, u32[]{:S(2)}) collective-permute-start(bf16[128,1536]{1,0:T(8,128)(2,1)} %param.3), channel_id=1, source_target_pairs={{0,4},{1,5},{2,6},{3,7},{4,0},{5,1},{6,2},{7,3},{8,12},{9,13},{10,... | collective-permute-start | bytes 1179656 | tf_op jit(solution)/shard_map/ppermute | solution.py:66
  10.8 1.2 %collective-permute-start.2 = (bf16[128,1536]{1,0:T(8,128)(2,1)}, bf16[128,1536]{1,0:T(8,128)(2,1)S(1)}, u32[]{:S(2)}, u32[]{:S(2)}) collective-permute-start(bf16[128,1536]{1,0:T(8,128)(2,1)} %param.3), channel_id=1, source_target_pairs={{0,6},{1,7},{2,0},{3,1},{4,2},{5,3},{6,4},{7,5},{8,14},{9,15},{10,... | collective-permute-start | bytes 1179656 | tf_op jit(solution)/shard_map/ppermute | solution.py:66
  12.9 2.8 %collective-permute-start.5 = (bf16[32,1536]{1,0:T(8,128)(2,1)S(1)}, bf16[32,1536]{1,0:T(8,128)(2,1)S(1)}, u32[]{:S(2)}, u32[]{:S(2)}) collective-permute-start(bf16[32,1536]{1,0:T(8,128)(2,1)S(1)} %collective-permute-done.4), channel_id=1, source_target_pairs={{0,224},{32,0},{64,32},{96,64},{128,96},{160,128},{192,160},{224,1... | collective-permute-start | bytes 294920 | tf_op jit(solution)/shard_map/ppermute | solution.py:44
  15.7 1.6 %collective-permute-done.5 = bf16[32,1536]{1,0:T(8,128)(2,1)S(1)} collective-permute-done((bf16[32,1536]{1,0:T(8,128)(2,1)S(1)}, bf16[32,1536]{1,0:T(8,128)(2,1)S(1)}, u32[]{:S(2)}, u32[]{:S(2)}) %collective-permute-start.5) | collective-permute-done | bytes 98336 | tf_op jit(solution)/shard_map/ppermute | solution.py:44
  17.3 3.3 %collective-permute-start.6 = (bf16[32,1536]{1,0:T(8,128)(2,1)S(1)}, bf16[32,1536]{1,0:T(8,128)(2,1)S(1)}, u32[]{:S(2)}, u32[]{:S(2)}) collective-permute-start(bf16[32,1536]{1,0:T(8,128)(2,1)S(1)} %collective-permute-done.5), channel_id=1, source_target_pairs={{0,224},{32,0},{64,32},{96,64},{128,96},{160,128},{192,160},{224,1... | collective-permute-start | bytes 294920 | tf_op jit(solution)/shard_map/ppermute | solution.py:44
  20.6 5.0 %collective-permute-done.9 = bf16[32,1536]{1,0:T(8,128)(2,1)S(1)} collective-permute-done((bf16[32,1536]{1,0:T(8,128)(2,1)S(1)}, bf16[32,1536]{1,0:T(8,128)(2,1)S(1)}, u32[]{:S(2)}, u32[]{:S(2)}) %collective-permute-start.9) | collective-permute-done | bytes 98336 | tf_op jit(solution)/shard_map/ppermute | solution.py:43
  25.6 2.7 %collective-permute-start.11 = (bf16[32,768]{1,0:T(8,128)(2,1)S(1)}, bf16[32,768]{1,0:T(8,128)(2,1)S(1)}, u32[]{:S(2)}, u32[]{:S(2)}) collective-permute-start(bf16[32,768]{1,0:T(8,128)(2,1)S(1)} %slice.27), channel_id=1, source_target_pairs={{0,224},{32,0},{64,32},{96,64},{128,96},{160,128},{192,160},{224,1... | collective-permute-start | bytes 147464 | tf_op jit(solution)/shard_map/ppermute | solution.py:40
  28.4 1.4 %collective-permute-done.10 = bf16[32,768]{1,0:T(8,128)(2,1)S(1)} collective-permute-done((bf16[32,768]{1,0:T(8,128)(2,1)S(1)}, bf16[32,768]{1,0:T(8,128)(2,1)S(1)}, u32[]{:S(2)}, u32[]{:S(2)}) %collective-permute-start.10) | collective-permute-done | bytes 49184 | tf_op jit(solution)/shard_map/ppermute | solution.py:39
  30.0 1.3 %bitcast_dynamic-update-slice_fusion.4 = (bf16[8,8,32,1536]{3,2,1,0:T(8,128)(2,1)}, bf16[8,32,1536]{2,1,0:T(8,128)(2,1)}) fusion(bf16[16,32,1536]{2,1,0:T(8,128)(2,1)S(1)} %bitcast_dynamic-update-slice_fusion.7, s32[]{:T(128)S(6)} %select_n.135), kind=kLoop, calls=%fused_computation.50 | loop fusion | bytes 2359300
  31.3 2.7 %collective-permute-start.12 = (bf16[8,32,1536]{2,1,0:T(8,128)(2,1)}, bf16[8,32,1536]{2,1,0:T(8,128)(2,1)}, u32[]{:S(2)}, u32[]{:S(2)}) collective-permute-start(bf16[8,32,1536]{2,1,0:T(8,128)(2,1)} %get-tuple-element.7), channel_id=1, source_target_pairs={{0,24},{8,0},{16,8},{24,16},{1,25},{9,1},{17,9},{25,17},{2,26},{10... | collective-permute-start | bytes 2359304 | tf_op jit(solution)/shard_map/ppermute | solution.py:44
  35.0 1.4 %pad_maximum_fusion = bf16[4,128,1536]{2,1,0:T(8,128)(2,1)S(1)} fusion(bf16[1,128,1536]{2,1,0:T(8,128)(2,1)} %bitcast.103, bf16[1,128,1536]{2,1,0:T(8,128)(2,1)} %bitcast.102, bf16[1,128,1536]{2,1,0:T(8,128)(2,1)} %bitcast.101, bf16[1,128,1536]{2,1,0:T(8,128)(2,1)S(1)} %bitcast.100), kind=kLoop, calls=%fused_computation.26 | loop fusion | flops 2359296 | bytes 3145728 | tf_op jit(solution)/shard_map/stack | solution.py:67
  37.4 5.6 %collective-permute-start.3 = (bf16[4,128,1536]{2,1,0:T(8,128)(2,1)S(1)}, bf16[4,128,1536]{2,1,0:T(8,128)(2,1)S(1)}, u32[]{:S(2)}, u32[]{:S(2)}) collective-permute-start(bf16[4,128,1536]{2,1,0:T(8,128)(2,1)S(1)} %broadcast_select_fusion), channel_id=1, source_target_pairs={{0,1},{1,0},{2,3},{3,2},{4,5},{5,4},{6,7},{7,6},{8,9},{9,8},{10,11... | collective-permute-start | bytes 4718600 | tf_op jit(solution)/shard_map/ppermute | solution.py:70
  43.2 6.0 %collective-permute-done.13 = bf16[8,32,1536]{2,1,0:T(8,128)(2,1)} collective-permute-done((bf16[8,32,1536]{2,1,0:T(8,128)(2,1)}, bf16[8,32,1536]{2,1,0:T(8,128)(2,1)}, u32[]{:S(2)}, u32[]{:S(2)}) %collective-permute-start.13) | collective-permute-done | bytes 786464 | tf_op jit(solution)/shard_map/ppermute | solution.py:43
  51.5 2.7 %collective-permute-start.15 = (bf16[8,32,768]{2,1,0:T(8,128)(2,1)S(1)}, bf16[8,32,768]{2,1,0:T(8,128)(2,1)S(1)}, u32[]{:S(2)}, u32[]{:S(2)}) collective-permute-start(bf16[8,32,768]{2,1,0:T(8,128)(2,1)S(1)} %slice.29), channel_id=1, source_target_pairs={{0,24},{8,0},{16,8},{24,16},{1,25},{9,1},{17,9},{25,17},{2,26},{10... | collective-permute-start | bytes 1179656 | tf_op jit(solution)/shard_map/ppermute | solution.py:40
  54.2 1.2 %bitcast_dynamic-update-slice_fusion.2 = bf16[8,8,32,1536]{3,2,1,0:T(8,128)(2,1)S(1)} fusion(bf16[8,8,32,1536]{3,2,1,0:T(8,128)(2,1)S(1)} %copy-done.2, bf16[8,32,1536]{2,1,0:T(8,128)(2,1)} %collective-permute-done.12), kind=kLoop, calls=%fused_computation.48 | loop fusion | bytes 1572864
  55.4 3.5 %collective-permute-done.14 = bf16[8,32,768]{2,1,0:T(8,128)(2,1)S(1)} collective-permute-done((bf16[8,32,768]{2,1,0:T(8,128)(2,1)S(1)}, bf16[8,32,768]{2,1,0:T(8,128)(2,1)S(1)}, u32[]{:S(2)}, u32[]{:S(2)}) %collective-permute-start.14) | collective-permute-done | bytes 393248 | tf_op jit(solution)/shard_map/ppermute | solution.py:39
  59.0 1.2 %bitcast_dynamic-update-slice_fusion = bf16[8,8,32,1536]{3,2,1,0:T(8,128)(2,1)S(1)} fusion(bf16[8,8,32,1536]{3,2,1,0:T(8,128)(2,1)S(1)} %fusion.31, bf16[8,32,1536]{2,1,0:T(8,128)(2,1)} %collective-permute-done.13), kind=kLoop, calls=%fused_computation.46 | loop fusion | bytes 1572864
  60.2 1.2 %bitcast_dynamic-update-slice_fusion.5 = bf16[8,8,32,1536]{3,2,1,0:T(8,128)(2,1)S(1)} fusion(bf16[8,8,32,1536]{3,2,1,0:T(8,128)(2,1)S(1)} %bitcast_dynamic-update-slice_fusion, bf16[8,32,1536]{2,1,0:T(8,128)(2,1)} %get-tuple-element.7), kind=kLoop, calls=%fused_computation.51 | loop fusion | bytes 1572864
  61.4 1.2 %bitcast_dynamic-update-slice_fusion.3 = bf16[8,8,32,1536]{3,2,1,0:T(8,128)(2,1)S(1)} fusion(bf16[8,8,32,1536]{3,2,1,0:T(8,128)(2,1)S(1)} %bitcast_dynamic-update-slice_fusion.5, bf16[8,32,1536]{2,1,0:T(8,128)(2,1)} %collective-permute-done.12), kind=kLoop, calls=%fused_computation.49 | loop fusion | bytes 1572864
  62.7 1.3 %bitcast_dynamic-update-slice_fusion.1 = bf16[8,8,32,1536]{3,2,1,0:T(8,128)(2,1)S(1)} fusion(bf16[8,8,32,1536]{3,2,1,0:T(8,128)(2,1)S(1)} %fusion.32, bf16[8,32,1536]{2,1,0:T(8,128)(2,1)} %collective-permute-done.13), kind=kLoop, calls=%fused_computation.47 | loop fusion | bytes 1572864 | tf_op jit(solution)/shard_map/jit(_roll_dynamic)/concatenate | solution.py:48
  66.0 3.8 %fusion.9 = bf16[4,4,32,1536]{3,2,1,0:T(8,128)(2,1)} fusion(bf16[1536,1536]{1,0:T(8,128)(2,1)S(1)} %bitcast.107, bf16[4,4,2,32,1536]{4,3,2,1,0:T(8,128)(2,1)S(1)} %bitcast.94, s32[]{:T(128)S(6)} %select_n.139), kind=kOutput, calls=%fused_computation.18 | convolution fusion | flops 2416705536 | bytes 7864324 | tf_op jit(solution)/shard_map/dot_general | solution.py:88
  69.8 8.1 %collective-permute-start.16 = (bf16[4,4,32,1536]{3,2,1,0:T(8,128)(2,1)}, bf16[4,4,32,1536]{3,2,1,0:T(8,128)(2,1)}, u32[]{:S(2)}, u32[]{:S(2)}) collective-permute-start(bf16[4,4,32,1536]{3,2,1,0:T(8,128)(2,1)} %fusion.9), channel_id=1, source_target_pairs={{0,1},{1,0},{2,3},{3,2},{4,5},{5,4},{6,7},{7,6},{8,9},{9,8},{10,11... | collective-permute-start | bytes 4718600 | tf_op jit(solution)/shard_map/ppermute | solution.py:90
  77.9 2.2 %fusion.1 = bf16[1024,1536]{1,0:T(8,128)(2,1)S(1)} fusion(bf16[1024,1536]{1,0:T(8,128)(2,1)S(1)} %bitcast.92), kind=kLoop, calls=%fused_computation.8 | loop fusion | flops 15728640 | bytes 6291456 | tf_op jit(solution)/shard_map/convert_element_type | solution.py:77
  82.0 5.5 %convert_add_fusion.1 = f32[4,4,32,1536]{3,2,1,0:T(8,128)S(1)} fusion(bf16[4,4,32,1536]{3,2,1,0:T(8,128)(2,1)} %collective-permute-done.16, bf16[1536,1536]{1,0:T(8,128)(2,1)} %param.5, bf16[4,4,2,32,1536]{4,3,2,1,0:T(8,128)(2,1)S(1)} %bitcast.95, s32[]{:T(128)S(6)} %select_n.138), kind=kOutput, calls=%fused_computation.17 | convolution fusion | flops 2417491968 | bytes 11010052 | tf_op jit(solution)/shard_map/dot_general | solution.py:91
  88.2 2.2 %collective-permute-start.21 = (bf16[128,768]{1,0:T(8,128)(2,1)S(1)}, bf16[128,768]{1,0:T(8,128)(2,1)S(1)}, u32[]{:S(2)}, u32[]{:S(2)}) collective-permute-start(bf16[128,768]{1,0:T(8,128)(2,1)S(1)} %get-tuple-element.12), channel_id=1, source_target_pairs={{0,6},{1,7},{2,0},{3,1},{4,2},{5,3},{6,4},{7,5},{8,14},{9,15},{10,... | collective-permute-start | bytes 589832 | tf_op jit(solution)/shard_map/ppermute | solution.py:112
  90.4 2.7 %collective-permute-start.18 = (bf16[128,1536]{1,0:T(8,128)(2,1)S(1)}, bf16[128,1536]{1,0:T(8,128)(2,1)S(1)}, u32[]{:S(2)}, u32[]{:S(2)}) collective-permute-start(bf16[128,1536]{1,0:T(8,128)(2,1)S(1)} %bitcast.104), channel_id=1, source_target_pairs={{0,6},{1,7},{2,0},{3,1},{4,2},{5,3},{6,4},{7,5},{8,14},{9,15},{10,... | collective-permute-start | bytes 1179656 | tf_op jit(solution)/shard_map/ppermute | solution.py:112
  93.1 6.9 %convolution_convert_fusion = bf16[1536,1536]{1,0:T(8,128)(2,1)} fusion(bf16[1024,1536]{1,0:T(8,128)(2,1)S(1)} %bitcast.97, bf16[1024,1536]{1,0:T(8,128)(2,1)S(1)} %bitcast.96), kind=kOutput, calls=%fused_computation.6 | convolution fusion | flops 4834197504 | bytes 11010048 | tf_op jit(solution)/shard_map/dot_general | solution.py:79
  100.0 2.7 %collective-permute-start.22 = (bf16[128,768]{1,0:T(8,128)(2,1)S(1)}, bf16[128,768]{1,0:T(8,128)(2,1)S(1)}, u32[]{:S(2)}, u32[]{:S(2)}) collective-permute-start(bf16[128,768]{1,0:T(8,128)(2,1)S(1)} %collective-permute-done.21), channel_id=1, source_target_pairs={{0,6},{1,7},{2,0},{3,1},{4,2},{5,3},{6,4},{7,5},{8,14},{9,15},{10,... | collective-permute-start | bytes 589832 | tf_op jit(solution)/shard_map/ppermute | solution.py:114
  102.8 4.5 %collective-permute-done.20 = bf16[128,768]{1,0:T(8,128)(2,1)S(1)} collective-permute-done((bf16[128,768]{1,0:T(8,128)(2,1)S(1)}, bf16[128,768]{1,0:T(8,128)(2,1)S(1)}, u32[]{:S(2)}, u32[]{:S(2)}) %collective-permute-start.20) | collective-permute-done | bytes 196640 | tf_op jit(solution)/shard_map/ppermute | solution.py:113
  107.3 1.4 %fusion.27 = bf16[128,1536]{1,0:T(8,128)(2,1)} fusion(bf16[128,1536]{1,0:T(8,128)(2,1)S(1)} %copy-done.3, f32[4,1,32,1536]{3,2,1,0:T(8,128)S(1)} %constant_dynamic-slice_fusion, bf16[128,1536]{1,0:T(8,128)(2,1)S(1)} %collective-permute-done.18, bf16[128,1536]{1,0:T(8,128)(2,1)S(1)} %collective-permute-done.17, ...), kind=kLoop, calls=%fused_computation.40 | loop fusion | flops 5701632 | bytes 2752512 | tf_op jit(solution)/shard_map/convert_element_type | solution.py:124
  (81 shorter events, 10.3 us)
Async XLA Ops:
  0.6 29.2 %copy-start.7 = (bf16[32,1536]{1,0:T(8,128)(2,1)S(1)}, bf16[32,1536]{1,0:T(8,128)(2,1)}, u32[]{:S(2)}) copy-start(bf16[32,1536]{1,0:T(8,128)(2,1)} %param.4) | copy-start | bytes 294916
  0.6 12.3 %collective-permute-start.4 = (bf16[32,1536]{1,0:T(8,128)(2,1)}, bf16[32,1536]{1,0:T(8,128)(2,1)S(1)}, u32[]{:S(2)}, u32[]{:S(2)}) collective-permute-start(bf16[32,1536]{1,0:T(8,128)(2,1)} %param.4), channel_id=1, source_target_pairs={{0,224},{32,0},{64,32},{96,64},{128,96},{160,128},{192,160},{224,1... | collective-permute-start | bytes 294920 | tf_op jit(solution)/shard_map/ppermute | solution.py:44
  7.1 8.5 %collective-permute-start.7 = (bf16[32,1536]{1,0:T(8,128)(2,1)}, bf16[32,1536]{1,0:T(8,128)(2,1)S(1)}, u32[]{:S(2)}, u32[]{:S(2)}) collective-permute-start(bf16[32,1536]{1,0:T(8,128)(2,1)} %param.4), channel_id=1, source_target_pairs={{0,32},{32,64},{64,96},{96,128},{128,160},{160,192},{192,224},{224... | collective-permute-start | bytes 294920 | tf_op jit(solution)/shard_map/ppermute | solution.py:43
  7.1 26.9 %collective-permute-start = (bf16[128,1536]{1,0:T(8,128)(2,1)}, bf16[128,1536]{1,0:T(8,128)(2,1)S(1)}, u32[]{:S(2)}, u32[]{:S(2)}) collective-permute-start(bf16[128,1536]{1,0:T(8,128)(2,1)} %param.3), channel_id=1, source_target_pairs={{0,2},{1,3},{2,4},{3,5},{4,6},{5,7},{6,0},{7,1},{8,10},{9,11},{10,... | collective-permute-start | bytes 1179656 | tf_op jit(solution)/shard_map/ppermute | solution.py:66
  8.3 25.7 %collective-permute-start.1 = (bf16[128,1536]{1,0:T(8,128)(2,1)}, bf16[128,1536]{1,0:T(8,128)(2,1)S(1)}, u32[]{:S(2)}, u32[]{:S(2)}) collective-permute-start(bf16[128,1536]{1,0:T(8,128)(2,1)} %param.3), channel_id=1, source_target_pairs={{0,4},{1,5},{2,6},{3,7},{4,0},{5,1},{6,2},{7,3},{8,12},{9,13},{10,... | collective-permute-start | bytes 1179656 | tf_op jit(solution)/shard_map/ppermute | solution.py:66
  10.8 23.3 %collective-permute-start.2 = (bf16[128,1536]{1,0:T(8,128)(2,1)}, bf16[128,1536]{1,0:T(8,128)(2,1)S(1)}, u32[]{:S(2)}, u32[]{:S(2)}) collective-permute-start(bf16[128,1536]{1,0:T(8,128)(2,1)} %param.3), channel_id=1, source_target_pairs={{0,6},{1,7},{2,0},{3,1},{4,2},{5,3},{6,4},{7,5},{8,14},{9,15},{10,... | collective-permute-start | bytes 1179656 | tf_op jit(solution)/shard_map/ppermute | solution.py:66
  12.9 4.4 %collective-permute-start.5 = (bf16[32,1536]{1,0:T(8,128)(2,1)S(1)}, bf16[32,1536]{1,0:T(8,128)(2,1)S(1)}, u32[]{:S(2)}, u32[]{:S(2)}) collective-permute-start(bf16[32,1536]{1,0:T(8,128)(2,1)S(1)} %collective-permute-done.4), channel_id=1, source_target_pairs={{0,224},{32,0},{64,32},{96,64},{128,96},{160,128},{192,160},{224,1... | collective-permute-start | bytes 294920 | tf_op jit(solution)/shard_map/ppermute | solution.py:44
  15.7 5.0 %collective-permute-start.8 = (bf16[32,1536]{1,0:T(8,128)(2,1)S(1)}, bf16[32,1536]{1,0:T(8,128)(2,1)S(1)}, u32[]{:S(2)}, u32[]{:S(2)}) collective-permute-start(bf16[32,1536]{1,0:T(8,128)(2,1)S(1)} %collective-permute-done.7), channel_id=1, source_target_pairs={{0,32},{32,64},{64,96},{96,128},{128,160},{160,192},{192,224},{224... | collective-permute-start | bytes 294920 | tf_op jit(solution)/shard_map/ppermute | solution.py:43
  17.3 8.3 %collective-permute-start.6 = (bf16[32,1536]{1,0:T(8,128)(2,1)S(1)}, bf16[32,1536]{1,0:T(8,128)(2,1)S(1)}, u32[]{:S(2)}, u32[]{:S(2)}) collective-permute-start(bf16[32,1536]{1,0:T(8,128)(2,1)S(1)} %collective-permute-done.5), channel_id=1, source_target_pairs={{0,224},{32,0},{64,32},{96,64},{128,96},{160,128},{192,160},{224,1... | collective-permute-start | bytes 294920 | tf_op jit(solution)/shard_map/ppermute | solution.py:44
  20.6 5.0 %collective-permute-start.9 = (bf16[32,1536]{1,0:T(8,128)(2,1)S(1)}, bf16[32,1536]{1,0:T(8,128)(2,1)S(1)}, u32[]{:S(2)}, u32[]{:S(2)}) collective-permute-start(bf16[32,1536]{1,0:T(8,128)(2,1)S(1)} %collective-permute-done.8), channel_id=1, source_target_pairs={{0,32},{32,64},{64,96},{96,128},{128,160},{160,192},{192,224},{224... | collective-permute-start | bytes 294920 | tf_op jit(solution)/shard_map/ppermute | solution.py:43
  25.6 4.2 %collective-permute-start.10 = (bf16[32,768]{1,0:T(8,128)(2,1)S(1)}, bf16[32,768]{1,0:T(8,128)(2,1)S(1)}, u32[]{:S(2)}, u32[]{:S(2)}) collective-permute-start(bf16[32,768]{1,0:T(8,128)(2,1)S(1)} %slice.26), channel_id=1, source_target_pairs={{0,32},{32,64},{64,96},{96,128},{128,160},{160,192},{192,224},{224... | collective-permute-start | bytes 147464 | tf_op jit(solution)/shard_map/ppermute | solution.py:39
  25.6 4.1 %collective-permute-start.11 = (bf16[32,768]{1,0:T(8,128)(2,1)S(1)}, bf16[32,768]{1,0:T(8,128)(2,1)S(1)}, u32[]{:S(2)}, u32[]{:S(2)}) collective-permute-start(bf16[32,768]{1,0:T(8,128)(2,1)S(1)} %slice.27), channel_id=1, source_target_pairs={{0,224},{32,0},{64,32},{96,64},{128,96},{160,128},{192,160},{224,1... | collective-permute-start | bytes 147464 | tf_op jit(solution)/shard_map/ppermute | solution.py:40
  29.9 5.1 %copy-start.3 = (bf16[128,1536]{1,0:T(8,128)(2,1)S(1)}, bf16[128,1536]{1,0:T(8,128)(2,1)}, u32[]{:S(2)}) copy-start(bf16[128,1536]{1,0:T(8,128)(2,1)} %param.3) | copy-start | bytes 1179652
  31.3 19.2 %collective-permute-start.12 = (bf16[8,32,1536]{2,1,0:T(8,128)(2,1)}, bf16[8,32,1536]{2,1,0:T(8,128)(2,1)}, u32[]{:S(2)}, u32[]{:S(2)}) collective-permute-start(bf16[8,32,1536]{2,1,0:T(8,128)(2,1)} %get-tuple-element.7), channel_id=1, source_target_pairs={{0,24},{8,0},{16,8},{24,16},{1,25},{9,1},{17,9},{25,17},{2,26},{10... | collective-permute-start | bytes 2359304 | tf_op jit(solution)/shard_map/ppermute | solution.py:44
  34.0 15.1 %collective-permute-start.13 = (bf16[8,32,1536]{2,1,0:T(8,128)(2,1)}, bf16[8,32,1536]{2,1,0:T(8,128)(2,1)}, u32[]{:S(2)}, u32[]{:S(2)}) collective-permute-start(bf16[8,32,1536]{2,1,0:T(8,128)(2,1)} %get-tuple-element.7), channel_id=1, source_target_pairs={{0,8},{8,16},{16,24},{24,0},{1,9},{9,17},{17,25},{25,1},{2,10},{10... | collective-permute-start | bytes 2359304 | tf_op jit(solution)/shard_map/ppermute | solution.py:43
  34.1 0.9 copy-start.5
  34.1 1.0 copy-start.6
  37.1 17.1 %copy-start.2 = (bf16[8,8,32,1536]{3,2,1,0:T(8,128)(2,1)S(1)}, bf16[8,8,32,1536]{3,2,1,0:T(8,128)(2,1)}, u32[]{:S(2)}) copy-start(bf16[8,8,32,1536]{3,2,1,0:T(8,128)(2,1)} %get-tuple-element.6) | copy-start | bytes 18874372
  37.4 27.0 %collective-permute-start.3 = (bf16[4,128,1536]{2,1,0:T(8,128)(2,1)S(1)}, bf16[4,128,1536]{2,1,0:T(8,128)(2,1)S(1)}, u32[]{:S(2)}, u32[]{:S(2)}) collective-permute-start(bf16[4,128,1536]{2,1,0:T(8,128)(2,1)S(1)} %broadcast_select_fusion), channel_id=1, source_target_pairs={{0,1},{1,0},{2,3},{3,2},{4,5},{5,4},{6,7},{7,6},{8,9},{9,8},{10,11... | collective-permute-start | bytes 4718600 | tf_op jit(solution)/shard_map/ppermute | solution.py:70
  50.2 8.7 %collective-permute-start.14 = (bf16[8,32,768]{2,1,0:T(8,128)(2,1)S(1)}, bf16[8,32,768]{2,1,0:T(8,128)(2,1)S(1)}, u32[]{:S(2)}, u32[]{:S(2)}) collective-permute-start(bf16[8,32,768]{2,1,0:T(8,128)(2,1)S(1)} %slice.28), channel_id=1, source_target_pairs={{0,8},{8,16},{16,24},{24,0},{1,9},{9,17},{17,25},{25,1},{2,10},{10... | collective-permute-start | bytes 1179656 | tf_op jit(solution)/shard_map/ppermute | solution.py:39
  51.5 7.5 %collective-permute-start.15 = (bf16[8,32,768]{2,1,0:T(8,128)(2,1)S(1)}, bf16[8,32,768]{2,1,0:T(8,128)(2,1)S(1)}, u32[]{:S(2)}, u32[]{:S(2)}) collective-permute-start(bf16[8,32,768]{2,1,0:T(8,128)(2,1)S(1)} %slice.29), channel_id=1, source_target_pairs={{0,24},{8,0},{16,8},{24,16},{1,25},{9,1},{17,9},{25,17},{2,26},{10... | collective-permute-start | bytes 1179656 | tf_op jit(solution)/shard_map/ppermute | solution.py:40
  62.6 3.4 %slice-start = ((s8[4718592]{0:T(1024)(128)(4,1)}), s8[4194304]{0:T(1024)(128)(4,1)S(1)}, s32[]{:S(2)}) async-start(s8[4718592]{0:T(1024)(128)(4,1)} %bitcast.106), calls=%async_computation | async-start | bytes 8388608
  64.0 2.0 %slice-start.1 = ((s8[4718592]{0:T(1024)(128)(4,1)}), s8[524288]{0:T(1024)(128)(4,1)S(1)}, s32[]{:S(2)}) async-start(s8[4718592]{0:T(1024)(128)(4,1)} %bitcast.106), calls=%async_computation.1 | async-start | bytes 1048576
  64.3 1.7 %copy-start = (bf16[4,8,32,1536]{3,2,1,0:T(8,128)(2,1)}, bf16[4,8,32,1536]{3,2,1,0:T(8,128)(2,1)S(1)}, u32[]{:S(2)}) copy-start(bf16[4,8,32,1536]{3,2,1,0:T(8,128)(2,1)S(1)} %constant_dynamic-slice_fusion.1) | copy-start | bytes 9437188
  69.8 11.5 %collective-permute-start.16 = (bf16[4,4,32,1536]{3,2,1,0:T(8,128)(2,1)}, bf16[4,4,32,1536]{3,2,1,0:T(8,128)(2,1)}, u32[]{:S(2)}, u32[]{:S(2)}) collective-permute-start(bf16[4,4,32,1536]{3,2,1,0:T(8,128)(2,1)} %fusion.9), channel_id=1, source_target_pairs={{0,1},{1,0},{2,3},{3,2},{4,5},{5,4},{6,7},{7,6},{8,9},{9,8},{10,11... | collective-permute-start | bytes 4718600 | tf_op jit(solution)/shard_map/ppermute | solution.py:90
  80.1 1.9 %copy-start.1 = (bf16[4,8,32,1536]{3,2,1,0:T(8,128)(2,1)S(1)}, bf16[4,8,32,1536]{3,2,1,0:T(8,128)(2,1)}, u32[]{:S(2)}) copy-start(bf16[4,8,32,1536]{3,2,1,0:T(8,128)(2,1)} %copy-done) | copy-start | bytes 9437188
  87.7 12.4 %collective-permute-start.19 = (bf16[128,768]{1,0:T(8,128)(2,1)S(1)}, bf16[128,768]{1,0:T(8,128)(2,1)S(1)}, u32[]{:S(2)}, u32[]{:S(2)}) collective-permute-start(bf16[128,768]{1,0:T(8,128)(2,1)S(1)} %get-tuple-element.11), channel_id=1, source_target_pairs={{0,2},{1,3},{2,4},{3,5},{4,6},{5,7},{6,0},{7,1},{8,10},{9,11},{10,... | collective-permute-start | bytes 589832 | tf_op jit(solution)/shard_map/ppermute | solution.py:111
  88.2 11.8 %collective-permute-start.21 = (bf16[128,768]{1,0:T(8,128)(2,1)S(1)}, bf16[128,768]{1,0:T(8,128)(2,1)S(1)}, u32[]{:S(2)}, u32[]{:S(2)}) collective-permute-start(bf16[128,768]{1,0:T(8,128)(2,1)S(1)} %get-tuple-element.12), channel_id=1, source_target_pairs={{0,6},{1,7},{2,0},{3,1},{4,2},{5,3},{6,4},{7,5},{8,14},{9,15},{10,... | collective-permute-start | bytes 589832 | tf_op jit(solution)/shard_map/ppermute | solution.py:112
  90.4 16.9 %collective-permute-start.17 = (bf16[128,1536]{1,0:T(8,128)(2,1)S(1)}, bf16[128,1536]{1,0:T(8,128)(2,1)S(1)}, u32[]{:S(2)}, u32[]{:S(2)}) collective-permute-start(bf16[128,1536]{1,0:T(8,128)(2,1)S(1)} %bitcast.105), channel_id=1, source_target_pairs={{0,2},{1,3},{2,4},{3,5},{4,6},{5,7},{6,0},{7,1},{8,10},{9,11},{10,... | collective-permute-start | bytes 1179656 | tf_op jit(solution)/shard_map/ppermute | solution.py:111
  90.4 16.9 %collective-permute-start.18 = (bf16[128,1536]{1,0:T(8,128)(2,1)S(1)}, bf16[128,1536]{1,0:T(8,128)(2,1)S(1)}, u32[]{:S(2)}, u32[]{:S(2)}) collective-permute-start(bf16[128,1536]{1,0:T(8,128)(2,1)S(1)} %bitcast.104), channel_id=1, source_target_pairs={{0,6},{1,7},{2,0},{3,1},{4,2},{5,3},{6,4},{7,5},{8,14},{9,15},{10,... | collective-permute-start | bytes 1179656 | tf_op jit(solution)/shard_map/ppermute | solution.py:112
  100.0 7.3 %collective-permute-start.20 = (bf16[128,768]{1,0:T(8,128)(2,1)S(1)}, bf16[128,768]{1,0:T(8,128)(2,1)S(1)}, u32[]{:S(2)}, u32[]{:S(2)}) collective-permute-start(bf16[128,768]{1,0:T(8,128)(2,1)S(1)} %collective-permute-done.19), channel_id=1, source_target_pairs={{0,2},{1,3},{2,4},{3,5},{4,6},{5,7},{6,0},{7,1},{8,10},{9,11},{10,... | collective-permute-start | bytes 589832 | tf_op jit(solution)/shard_map/ppermute | solution.py:113
  100.0 7.3 %collective-permute-start.22 = (bf16[128,768]{1,0:T(8,128)(2,1)S(1)}, bf16[128,768]{1,0:T(8,128)(2,1)S(1)}, u32[]{:S(2)}, u32[]{:S(2)}) collective-permute-start(bf16[128,768]{1,0:T(8,128)(2,1)S(1)} %collective-permute-done.21), channel_id=1, source_target_pairs={{0,6},{1,7},{2,0},{3,1},{4,2},{5,3},{6,4},{7,5},{8,14},{9,15},{10,... | collective-permute-start | bytes 589832 | tf_op jit(solution)/shard_map/ppermute | solution.py:114
  (1 other events, 0.8 us)

commit v10 on v9

--- a/solution.py
+++ b/solution.py
@@ -56,11 +56,6 @@
         x = c // 2
         k = c % 2
 
-        tokens = out_grad.shape[0] * n_z * n_y
-        gathered = ring_gather(ring_gather(out_grad, "z", n_z), "y", n_y)
-        grad_all = gathered.reshape((tokens, out_grad.shape[1]))
-        rows_r = out_grad.shape[0]
-
         got = [saved_input]
         for s in range(1, n_x):
             got.append(lax.ppermute(saved_input, COL, chip_shift(n_col, s)))
@@ -72,13 +67,34 @@
                          jnp.stack([other_by_x, mine_by_x], axis=1))
         saved_all = pair.reshape((n_col * saved_input.shape[0], saved_input.shape[1]))
 
-        saved_all, grad_all = lax.optimization_barrier((saved_all, grad_all))
+        tokens = out_grad.shape[0] * n_z * n_y
+        zg = ring_gather(out_grad, "z", n_z)
+        y = lax.axis_index("y")
+        ahead = [(j, (j + 1) % n_y) for j in range(n_y)]
+        behind = [(j, (j - 1) % n_y) for j in range(n_y)]
+        from_behind = lax.ppermute(zg, "y", ahead)
+        from_ahead = lax.ppermute(zg, "y", behind)
+        cut = zg.shape[-1] // 2
+        far = jnp.concatenate([lax.ppermute(from_behind[..., :cut], "y", ahead),
+                               lax.ppermute(from_ahead[..., cut:], "y", behind)], axis=-1)
+        saved_all, from_behind, from_ahead = lax.optimization_barrier(
+            (saved_all, from_behind, from_ahead))
+        by_off = {0: zg, 1: from_ahead, n_y - 1: from_behind, 2: far}
+        gathered = jnp.roll(jnp.stack([by_off[d] for d in range(n_y)], axis=0), y, axis=0)
+        grad_all = gathered.reshape((tokens, out_grad.shape[1]))
+        rows_r = out_grad.shape[0]
+
+
         gelu_value, unused_slope = gelu_parts(saved_all.astype(jnp.float32))
         hidden = gelu_value.astype(jnp.bfloat16).reshape((n_z, n_y, rows_r, -1))
-        hidden = jnp.swapaxes(hidden, 0, 1).reshape((tokens, -1))
-        weight_grad = lax.dot_general(
-            hidden, grad_all, (((0,), (0,)), ((), ())), preferred_element_type=jnp.float32
-        ).astype(jnp.bfloat16)
+        hidden = jnp.swapaxes(hidden, 0, 1)
+        weight_grad = None
+        for d in range(n_y):
+            term = lax.dot_general(
+                lax.dynamic_index_in_dim(hidden, (y + d) % n_y, axis=0, keepdims=False),
+                by_off[d], (((0, 1), (0, 1)), ((), ())), preferred_element_type=jnp.float32)
+            weight_grad = term if weight_grad is None else weight_grad + term
+        weight_grad = weight_grad.astype(jnp.bfloat16)
 
         rows = saved_input.shape[0]
         if n_z == n_col:

time: 110 us -> 125 us (1.14)
  matrix products: 16.2 us -> 35.3 us
  starting transfers between devices: 47.7 us -> 44.9 us
  local copies, waits for them, and re-layouts: 14.6 us -> 13 us
    dot_general x1 -> x4, matrix products: 6.92 us -> 30 us  [per_device(): lax.dot_general(lax.dynamic_index_in_dim(hidden, (y + d) % n_y, axis=0, k...]
    ppermute x0 -> x4, waiting for transfers between devices: none -> 13.6 us  [the longest x1 7.6 us: per_device(): lax.ppermute(from_behind[..., :cut], 'y', ahead)]
    ppermute x0 -> x4, starting transfers between devices: none -> 6.49 us  [the longest x1 3.49 us: per_device(): lax.ppermute(from_ahead[..., cut:], 'y', behind)]
    ppermute x4 -> x3, waiting for transfers between devices: 11 us -> 4.57 us  [ring_gather(): fwd = lax.ppermute(fwd, axis, ahead)]
    ppermute x4 -> x3, starting transfers between devices: 15.3 us -> 9.36 us  [ring_gather(): bwd = lax.ppermute(bwd, axis, behind)]
    ppermute x2 -> x1, waiting for transfers between devices: 4.9 us -> 1.68 us  [ring_gather(): from_behind = lax.ppermute(fwd[..., :half], axis, ahead)]
    dot_general x1, matrix products: 5.49 us -> 2.67 us  [per_device(): lax.dot_general(g_mine, weight, (((3,), (1,)), ((), ())), preferred_eleme...]
    ppermute x2 -> x1, starting transfers between devices: 5.46 us -> 2.73 us  [ring_gather(): from_ahead = lax.ppermute(bwd[..., half:], axis, behind)]
  transfers between devices with their start and end apart: 23 -> 23, of which waited for: 7 -> 6; matrix products, arithmetic and copies ran while one was open for 21% -> 31% of each run, Pallas kernels for 0% -> 0%
where the time goes in v10:
time: 125 us; the launch traced here: 124 us
  starting transfers between devices  44.9 us (36%)
  matrix products  35.3 us (28%)
  waiting for transfers between devices  23.6 us (19%)
  local copies, waits for them, and re-layouts  13 us (10%)
  other arithmetic  5.98 us (5%)
    dot_general x4, matrix products, per_device(): lax.dot_general(lax.dynamic_index_in_dim(hidden, (y + d) % n_y, axis=0, k...  30 us
    ppermute x3, starting transfers between devices, ring_gather(): bwd = lax.ppermute(bwd, axis, behind)  9.36 us
    unnamed x31, local copies, waits for them, and re-layouts  8.5 us
    ppermute x1, waiting for transfers between devices, per_device(): lax.ppermute(from_behind[..., :cut], 'y', ahead)  7.6 us
    ppermute x1, starting transfers between devices, per_device(): lax.ppermute(p_theirs.astype(jnp.bfloat16), COL, core_swap(n_col))  6.73 us
    ppermute x1, waiting for transfers between devices, per_device(): from_ahead = lax.ppermute(zg, 'y', behind)  5.96 us
    ppermute x3, starting transfers between devices, per_device(): got.append(lax.ppermute(saved_input, COL, chip_shift(n_col, s)))  5.42 us
    ppermute x1, starting transfers between devices, per_device(): other_by_x = lax.ppermute(mine_by_x, COL, core_swap(n_col))  4.64 us
  transfers between devices with their start and end apart: 23, of which 6 were waited for; matrix products, arithmetic and copies ran while one was open for 31% of the time, Pallas kernels for 0%

profile of v10, /device:TPU:1, one launch (start us, length us, event | category | flops | bytes accessed | tf_op | source)
XLA Modules:
  0.0 123.9 jit_solution(10521227031957333345)
XLA Ops:
  0.6 2.5 %collective-permute-start.3 = (bf16[32,1536]{1,0:T(8,128)(2,1)}, bf16[32,1536]{1,0:T(8,128)(2,1)S(1)}, u32[]{:S(2)}, u32[]{:S(2)}) collective-permute-start(bf16[32,1536]{1,0:T(8,128)(2,1)} %param.4), channel_id=1, source_target_pairs={{0,32},{32,64},{64,96},{96,128},{128,160},{160,192},{192,224},{224... | collective-permute-start | bytes 294920 | tf_op jit(solution)/shard_map/ppermute | solution.py:43
  3.2 4.0 %collective-permute-start = (bf16[32,1536]{1,0:T(8,128)(2,1)}, bf16[32,1536]{1,0:T(8,128)(2,1)S(1)}, u32[]{:S(2)}, u32[]{:S(2)}) collective-permute-start(bf16[32,1536]{1,0:T(8,128)(2,1)} %param.4), channel_id=1, source_target_pairs={{0,224},{32,0},{64,32},{96,64},{128,96},{160,128},{192,160},{224,1... | collective-permute-start | bytes 294920 | tf_op jit(solution)/shard_map/ppermute | solution.py:44
  7.2 2.7 %collective-permute-start.9 = (bf16[128,1536]{1,0:T(8,128)(2,1)}, bf16[128,1536]{1,0:T(8,128)(2,1)S(1)}, u32[]{:S(2)}, u32[]{:S(2)}) collective-permute-start(bf16[128,1536]{1,0:T(8,128)(2,1)} %param.3), channel_id=1, source_target_pairs={{0,4},{1,5},{2,6},{3,7},{4,0},{5,1},{6,2},{7,3},{8,12},{9,13},{10,... | collective-permute-start | bytes 1179656 | tf_op jit(solution)/shard_map/ppermute | solution.py:61
  10.3 2.4 %collective-permute-start.10 = (bf16[128,1536]{1,0:T(8,128)(2,1)}, bf16[128,1536]{1,0:T(8,128)(2,1)S(1)}, u32[]{:S(2)}, u32[]{:S(2)}) collective-permute-start(bf16[128,1536]{1,0:T(8,128)(2,1)} %param.3), channel_id=1, source_target_pairs={{0,6},{1,7},{2,0},{3,1},{4,2},{5,3},{6,4},{7,5},{8,14},{9,15},{10,... | collective-permute-start | bytes 1179656 | tf_op jit(solution)/shard_map/ppermute | solution.py:61
  13.7 2.7 %collective-permute-start.1 = (bf16[32,1536]{1,0:T(8,128)(2,1)S(1)}, bf16[32,1536]{1,0:T(8,128)(2,1)S(1)}, u32[]{:S(2)}, u32[]{:S(2)}) collective-permute-start(bf16[32,1536]{1,0:T(8,128)(2,1)S(1)} %collective-permute-done), channel_id=1, source_target_pairs={{0,224},{32,0},{64,32},{96,64},{128,96},{160,128},{192,160},{224,1... | collective-permute-start | bytes 294920 | tf_op jit(solution)/shard_map/ppermute | solution.py:44
  16.4 2.3 %collective-permute-done.4 = bf16[32,1536]{1,0:T(8,128)(2,1)S(1)} collective-permute-done((bf16[32,1536]{1,0:T(8,128)(2,1)S(1)}, bf16[32,1536]{1,0:T(8,128)(2,1)S(1)}, u32[]{:S(2)}, u32[]{:S(2)}) %collective-permute-start.4) | collective-permute-done | bytes 98336 | tf_op jit(solution)/shard_map/ppermute | solution.py:43
  18.6 2.7 %collective-permute-start.2 = (bf16[32,1536]{1,0:T(8,128)(2,1)S(1)}, bf16[32,1536]{1,0:T(8,128)(2,1)S(1)}, u32[]{:S(2)}, u32[]{:S(2)}) collective-permute-start(bf16[32,1536]{1,0:T(8,128)(2,1)S(1)} %collective-permute-done.1), channel_id=1, source_target_pairs={{0,224},{32,0},{64,32},{96,64},{128,96},{160,128},{192,160},{224,1... | collective-permute-start | bytes 294920 | tf_op jit(solution)/shard_map/ppermute | solution.py:44
  21.3 2.3 %collective-permute-done.5 = bf16[32,1536]{1,0:T(8,128)(2,1)S(1)} collective-permute-done((bf16[32,1536]{1,0:T(8,128)(2,1)S(1)}, bf16[32,1536]{1,0:T(8,128)(2,1)S(1)}, u32[]{:S(2)}, u32[]{:S(2)}) %collective-permute-start.5) | collective-permute-done | bytes 98336 | tf_op jit(solution)/shard_map/ppermute | solution.py:43
  23.6 2.7 %collective-permute-start.7 = (bf16[32,768]{1,0:T(8,128)(2,1)S(1)}, bf16[32,768]{1,0:T(8,128)(2,1)S(1)}, u32[]{:S(2)}, u32[]{:S(2)}) collective-permute-start(bf16[32,768]{1,0:T(8,128)(2,1)S(1)} %slice.27), channel_id=1, source_target_pairs={{0,224},{32,0},{64,32},{96,64},{128,96},{160,128},{192,160},{224,1... | collective-permute-start | bytes 147464 | tf_op jit(solution)/shard_map/ppermute | solution.py:40
  26.4 1.7 %collective-permute-done.6 = bf16[32,768]{1,0:T(8,128)(2,1)S(1)} collective-permute-done((bf16[32,768]{1,0:T(8,128)(2,1)S(1)}, bf16[32,768]{1,0:T(8,128)(2,1)S(1)}, u32[]{:S(2)}, u32[]{:S(2)}) %collective-permute-start.6) | collective-permute-done | bytes 49184 | tf_op jit(solution)/shard_map/ppermute | solution.py:39
  29.1 1.3 %bitcast_dynamic-update-slice_fusion.6 = (bf16[8,8,32,1536]{3,2,1,0:T(8,128)(2,1)}, bf16[8,32,1536]{2,1,0:T(8,128)(2,1)}) fusion(bf16[16,32,1536]{2,1,0:T(8,128)(2,1)S(1)} %bitcast_dynamic-update-slice_fusion.9, s32[]{:T(128)S(6)} %select_n.151), kind=kLoop, calls=%fused_computation.61 | loop fusion | bytes 2359300
  30.5 2.7 %collective-permute-start.13 = (bf16[8,32,1536]{2,1,0:T(8,128)(2,1)}, bf16[8,32,1536]{2,1,0:T(8,128)(2,1)}, u32[]{:S(2)}, u32[]{:S(2)}) collective-permute-start(bf16[8,32,1536]{2,1,0:T(8,128)(2,1)} %get-tuple-element.9), channel_id=1, source_target_pairs={{0,24},{8,0},{16,8},{24,16},{1,25},{9,1},{17,9},{25,17},{2,26},{10... | collective-permute-start | bytes 2359304 | tf_op jit(solution)/shard_map/ppermute | solution.py:76
  34.1 1.4 %broadcast_select_fusion = bf16[4,128,1536]{2,1,0:T(8,128)(2,1)} fusion(bf16[4,128,1536]{2,1,0:T(8,128)(2,1)S(1)} %gather_fusion, pred[4]{0:T(512)(128)(4,1)S(1)} %compare_and_fusion), kind=kLoop, calls=%fused_computation.35 | loop fusion | flops 786432 | bytes 3145732 | tf_op jit(solution)/shard_map/jit(_take)/select_n | solution.py:64
  35.5 4.6 %collective-permute-start.11 = (bf16[4,128,1536]{2,1,0:T(8,128)(2,1)}, bf16[4,128,1536]{2,1,0:T(8,128)(2,1)S(1)}, u32[]{:S(2)}, u32[]{:S(2)}) collective-permute-start(bf16[4,128,1536]{2,1,0:T(8,128)(2,1)} %broadcast_select_fusion), channel_id=1, source_target_pairs={{0,1},{1,0},{2,3},{3,2},{4,5},{5,4},{6,7},{7,6},{8,9},{9,8},{10,11... | collective-permute-start | bytes 4718600 | tf_op jit(solution)/shard_map/ppermute | solution.py:65
  40.1 6.0 %collective-permute-done.13 = bf16[8,32,1536]{2,1,0:T(8,128)(2,1)} collective-permute-done((bf16[8,32,1536]{2,1,0:T(8,128)(2,1)}, bf16[8,32,1536]{2,1,0:T(8,128)(2,1)}, u32[]{:S(2)}, u32[]{:S(2)}) %collective-permute-start.13) | collective-permute-done | bytes 786464 | tf_op jit(solution)/shard_map/ppermute | solution.py:76
  47.1 3.5 %collective-permute-start.15 = (bf16[8,32,768]{2,1,0:T(8,128)(2,1)S(1)}, bf16[8,32,768]{2,1,0:T(8,128)(2,1)S(1)}, u32[]{:S(2)}, u32[]{:S(2)}) collective-permute-start(bf16[8,32,768]{2,1,0:T(8,128)(2,1)S(1)} %slice.29), channel_id=1, source_target_pairs={{0,24},{8,0},{16,8},{24,16},{1,25},{9,1},{17,9},{25,17},{2,26},{10... | collective-permute-start | bytes 1179656 | tf_op jit(solution)/shard_map/ppermute | solution.py:79
  52.1 7.6 %collective-permute-done.14 = bf16[8,32,768]{2,1,0:T(8,128)(2,1)S(1)} collective-permute-done((bf16[8,32,768]{2,1,0:T(8,128)(2,1)S(1)}, bf16[8,32,768]{2,1,0:T(8,128)(2,1)S(1)}, u32[]{:S(2)}, u32[]{:S(2)}) %collective-permute-start.14) | collective-permute-done | bytes 393248 | tf_op jit(solution)/shard_map/ppermute | solution.py:78
  60.4 2.2 %fusion.2 = bf16[1024,1536]{1,0:T(8,128)(2,1)S(1)} fusion(bf16[1024,1536]{1,0:T(8,128)(2,1)S(1)} %bitcast.113), kind=kLoop, calls=%fused_computation.11 | loop fusion | flops 15728640 | bytes 6291456 | tf_op jit(solution)/shard_map/convert_element_type | solution.py:89
  63.9 1.3 %bitcast_dynamic-update-slice_fusion = bf16[8,8,32,1536]{3,2,1,0:T(8,128)(2,1)S(1)} fusion(bf16[8,8,32,1536]{3,2,1,0:T(8,128)(2,1)S(1)} %bitcast_dynamic-update-slice_fusion.2, bf16[8,32,1536]{2,1,0:T(8,128)(2,1)} %collective-permute-done.12), kind=kLoop, calls=%fused_computation.55 | loop fusion | bytes 1572864
  65.2 1.3 %bitcast_dynamic-update-slice_fusion.7 = bf16[8,8,32,1536]{3,2,1,0:T(8,128)(2,1)S(1)} fusion(bf16[8,8,32,1536]{3,2,1,0:T(8,128)(2,1)S(1)} %bitcast_dynamic-update-slice_fusion, bf16[8,32,1536]{2,1,0:T(8,128)(2,1)} %get-tuple-element.9), kind=kLoop, calls=%fused_computation.62 | loop fusion | bytes 1572864
  69.4 2.6 %fusion.10 = bf16[4,4,32,1536]{3,2,1,0:T(8,128)(2,1)S(1)} fusion(bf16[1536,1536]{1,0:T(8,128)(2,1)S(1)} %bitcast.131, bf16[4,4,2,32,1536]{4,3,2,1,0:T(8,128)(2,1)S(1)} %bitcast.118, s32[]{:T(128)S(6)} %select_n.166), kind=kOutput, calls=%fused_computation.21 | convolution fusion | flops 2416705536 | bytes 7864324 | tf_op jit(solution)/shard_map/dot_general | solution.py:104
  72.1 6.7 %collective-permute-start.16 = (bf16[4,4,32,1536]{3,2,1,0:T(8,128)(2,1)S(1)}, bf16[4,4,32,1536]{3,2,1,0:T(8,128)(2,1)S(1)}, u32[]{:S(2)}, u32[]{:S(2)}) collective-permute-start(bf16[4,4,32,1536]{3,2,1,0:T(8,128)(2,1)S(1)} %fusion.10), channel_id=1, source_target_pairs={{0,1},{1,0},{2,3},{3,2},{4,5},{5,4},{6,7},{7,6},{8,9},{9,8},{10,11... | collective-permute-start | bytes 4718600 | tf_op jit(solution)/shard_map/ppermute | solution.py:106
  78.8 5.1 %fusion.31 = f32[1536,1536,1]{1,0,2:T(8,128)} fusion(bf16[8,32,1536]{2,1,0:T(8,128)(2,1)S(1)} %constant_dynamic-update-slice_fusion, bf16[8,4,32,1536]{3,2,1,0:T(8,128)(2,1)S(1)} %bitcast.114, s32[]{:T(128)S(6)} %select_n.178), kind=kOutput, calls=%fused_computation.46 | convolution fusion | flops 1207959552 | bytes 11010052 | tf_op jit(solution)/shard_map/dot_general | solution.py:93
  83.9 6.2 %fusion.33 = f32[1536,1536,1]{1,0,2:T(8,128)} fusion(bf16[8,32,1536]{2,1,0:T(8,128)(2,1)} %collective-permute-done.13, bf16[8,4,32,1536]{3,2,1,0:T(8,128)(2,1)S(1)} %bitcast.115, s32[]{:T(128)S(6)} %select_n.176), kind=kOutput, calls=%fused_computation.48 | convolution fusion | flops 1207959552 | bytes 11010052 | tf_op jit(solution)/shard_map/dot_general | solution.py:93
  90.1 6.2 %fusion.35 = f32[1536,1536,1]{1,0,2:T(8,128)} fusion(bf16[8,32,1536]{2,1,0:T(8,128)(2,1)} %get-tuple-element.9, bf16[8,4,32,1536]{3,2,1,0:T(8,128)(2,1)S(1)} %bitcast.116, s32[]{:T(128)S(6)} %select_n.174), kind=kOutput, calls=%fused_computation.50 | convolution fusion | flops 1207959552 | bytes 11010052 | tf_op jit(solution)/shard_map/dot_general | solution.py:93
  96.3 2.7 %convert_add_fusion.1 = f32[4,4,32,1536]{3,2,1,0:T(8,128)S(1)} fusion(bf16[4,4,32,1536]{3,2,1,0:T(8,128)(2,1)S(1)} %collective-permute-done.16, bf16[1536,1536]{1,0:T(8,128)(2,1)S(1)} %bitcast.131, bf16[4,4,2,32,1536]{4,3,2,1,0:T(8,128)(2,1)S(1)} %bitcast.119, s32[]{:T(128)S(6)} %select_n.165), kind=kOutput, calls=%fused_computation.20 | convolution fusion | flops 2417491968 | bytes 11010052 | tf_op jit(solution)/shard_map/dot_general | solution.py:107
  99.3 2.7 %collective-permute-start.21 = (bf16[128,768]{1,0:T(8,128)(2,1)S(1)}, bf16[128,768]{1,0:T(8,128)(2,1)S(1)}, u32[]{:S(2)}, u32[]{:S(2)}) collective-permute-start(bf16[128,768]{1,0:T(8,128)(2,1)S(1)} %get-tuple-element.14), channel_id=1, source_target_pairs={{0,6},{1,7},{2,0},{3,1},{4,2},{5,3},{6,4},{7,5},{8,14},{9,15},{10,... | collective-permute-start | bytes 589832 | tf_op jit(solution)/shard_map/ppermute | solution.py:128
  102.0 1.4 %collective-permute-start.17 = (bf16[128,1536]{1,0:T(8,128)(2,1)S(1)}, bf16[128,1536]{1,0:T(8,128)(2,1)S(1)}, u32[]{:S(2)}, u32[]{:S(2)}) collective-permute-start(bf16[128,1536]{1,0:T(8,128)(2,1)S(1)} %bitcast.128), channel_id=1, source_target_pairs={{0,2},{1,3},{2,4},{3,5},{4,6},{5,7},{6,0},{7,1},{8,10},{9,11},{10,... | collective-permute-start | bytes 1179656 | tf_op jit(solution)/shard_map/ppermute | solution.py:127
  103.4 12.5 %fusion = bf16[1536,1536]{1,0:T(8,128)(2,1)} fusion(f32[1536,1536,1]{1,0,2:T(8,128)} %fusion.31, f32[1536,1536,1]{1,0,2:T(8,128)} %fusion.33, f32[1536,1536,1]{1,0,2:T(8,128)} %fusion.35, bf16[8,32,1536]{2,1,0:T(8,128)(2,1)} %collective-permute-done.12, bf16[8,4,32,1536]{3,2,1,0:T(8,128)(2,1)S(1)} %bitcast.117, s32[]{:T(128)S(6)} %select_n.180), kind=kOutput, calls=%fused_computation.7 | convolution fusion | flops 1217396736 | bytes 34603012 | tf_op jit(solution)/shard_map/dot_general | solution.py:93
  115.9 2.7 %collective-permute-start.22 = (bf16[128,768]{1,0:T(8,128)(2,1)S(1)}, bf16[128,768]{1,0:T(8,128)(2,1)S(1)}, u32[]{:S(2)}, u32[]{:S(2)}) collective-permute-start(bf16[128,768]{1,0:T(8,128)(2,1)S(1)} %collective-permute-done.21), channel_id=1, source_target_pairs={{0,6},{1,7},{2,0},{3,1},{4,2},{5,3},{6,4},{7,5},{8,14},{9,15},{10,... | collective-permute-start | bytes 589832 | tf_op jit(solution)/shard_map/ppermute | solution.py:130
  118.6 3.8 %collective-permute-done.20 = bf16[128,768]{1,0:T(8,128)(2,1)S(1)} collective-permute-done((bf16[128,768]{1,0:T(8,128)(2,1)S(1)}, bf16[128,768]{1,0:T(8,128)(2,1)S(1)}, u32[]{:S(2)}, u32[]{:S(2)}) %collective-permute-start.20) | collective-permute-done | bytes 196640 | tf_op jit(solution)/shard_map/ppermute | solution.py:129
  122.4 1.4 %fusion.28 = bf16[128,1536]{1,0:T(8,128)(2,1)} fusion(bf16[128,1536]{1,0:T(8,128)(2,1)S(1)} %copy-done, f32[4,1,32,1536]{3,2,1,0:T(8,128)S(1)} %constant_dynamic-slice_fusion, bf16[128,1536]{1,0:T(8,128)(2,1)S(1)} %collective-permute-done.18, bf16[128,1536]{1,0:T(8,128)(2,1)S(1)} %collective-permute-done.17, ...), kind=kLoop, calls=%fused_computation.43 | loop fusion | flops 5701632 | bytes 2752512 | tf_op jit(solution)/shard_map/convert_element_type | solution.py:140
  (76 shorter events, 10.9 us)
Async XLA Ops:
  0.6 32.6 %copy-start = (bf16[128,1536]{1,0:T(8,128)(2,1)S(1)}, bf16[128,1536]{1,0:T(8,128)(2,1)}, u32[]{:S(2)}) copy-start(bf16[128,1536]{1,0:T(8,128)(2,1)} %param.3) | copy-start | bytes 1179652
  0.6 12.9 %collective-permute-start.3 = (bf16[32,1536]{1,0:T(8,128)(2,1)}, bf16[32,1536]{1,0:T(8,128)(2,1)S(1)}, u32[]{:S(2)}, u32[]{:S(2)}) collective-permute-start(bf16[32,1536]{1,0:T(8,128)(2,1)} %param.4), channel_id=1, source_target_pairs={{0,32},{32,64},{64,96},{96,128},{128,160},{160,192},{192,224},{224... | collective-permute-start | bytes 294920 | tf_op jit(solution)/shard_map/ppermute | solution.py:43
  3.2 10.5 %collective-permute-start = (bf16[32,1536]{1,0:T(8,128)(2,1)}, bf16[32,1536]{1,0:T(8,128)(2,1)S(1)}, u32[]{:S(2)}, u32[]{:S(2)}) collective-permute-start(bf16[32,1536]{1,0:T(8,128)(2,1)} %param.4), channel_id=1, source_target_pairs={{0,224},{32,0},{64,32},{96,64},{128,96},{160,128},{192,160},{224,1... | collective-permute-start | bytes 294920 | tf_op jit(solution)/shard_map/ppermute | solution.py:44
  7.2 26.0 %collective-permute-start.9 = (bf16[128,1536]{1,0:T(8,128)(2,1)}, bf16[128,1536]{1,0:T(8,128)(2,1)S(1)}, u32[]{:S(2)}, u32[]{:S(2)}) collective-permute-start(bf16[128,1536]{1,0:T(8,128)(2,1)} %param.3), channel_id=1, source_target_pairs={{0,4},{1,5},{2,6},{3,7},{4,0},{5,1},{6,2},{7,3},{8,12},{9,13},{10,... | collective-permute-start | bytes 1179656 | tf_op jit(solution)/shard_map/ppermute | solution.py:61
  9.9 23.3 %collective-permute-start.8 = (bf16[128,1536]{1,0:T(8,128)(2,1)}, bf16[128,1536]{1,0:T(8,128)(2,1)S(1)}, u32[]{:S(2)}, u32[]{:S(2)}) collective-permute-start(bf16[128,1536]{1,0:T(8,128)(2,1)} %param.3), channel_id=1, source_target_pairs={{0,2},{1,3},{2,4},{3,5},{4,6},{5,7},{6,0},{7,1},{8,10},{9,11},{10,... | collective-permute-start | bytes 1179656 | tf_op jit(solution)/shard_map/ppermute | solution.py:61
  10.3 23.0 %collective-permute-start.10 = (bf16[128,1536]{1,0:T(8,128)(2,1)}, bf16[128,1536]{1,0:T(8,128)(2,1)S(1)}, u32[]{:S(2)}, u32[]{:S(2)}) collective-permute-start(bf16[128,1536]{1,0:T(8,128)(2,1)} %param.3), channel_id=1, source_target_pairs={{0,6},{1,7},{2,0},{3,1},{4,2},{5,3},{6,4},{7,5},{8,14},{9,15},{10,... | collective-permute-start | bytes 1179656 | tf_op jit(solution)/shard_map/ppermute | solution.py:61
  13.6 5.1 %collective-permute-start.4 = (bf16[32,1536]{1,0:T(8,128)(2,1)S(1)}, bf16[32,1536]{1,0:T(8,128)(2,1)S(1)}, u32[]{:S(2)}, u32[]{:S(2)}) collective-permute-start(bf16[32,1536]{1,0:T(8,128)(2,1)S(1)} %collective-permute-done.3), channel_id=1, source_target_pairs={{0,32},{32,64},{64,96},{96,128},{128,160},{160,192},{192,224},{224... | collective-permute-start | bytes 294920 | tf_op jit(solution)/shard_map/ppermute | solution.py:43
  13.7 5.0 %collective-permute-start.1 = (bf16[32,1536]{1,0:T(8,128)(2,1)S(1)}, bf16[32,1536]{1,0:T(8,128)(2,1)S(1)}, u32[]{:S(2)}, u32[]{:S(2)}) collective-permute-start(bf16[32,1536]{1,0:T(8,128)(2,1)S(1)} %collective-permute-done), channel_id=1, source_target_pairs={{0,224},{32,0},{64,32},{96,64},{128,96},{160,128},{192,160},{224,1... | collective-permute-start | bytes 294920 | tf_op jit(solution)/shard_map/ppermute | solution.py:44
  18.6 5.0 %collective-permute-start.5 = (bf16[32,1536]{1,0:T(8,128)(2,1)S(1)}, bf16[32,1536]{1,0:T(8,128)(2,1)S(1)}, u32[]{:S(2)}, u32[]{:S(2)}) collective-permute-start(bf16[32,1536]{1,0:T(8,128)(2,1)S(1)} %collective-permute-done.4), channel_id=1, source_target_pairs={{0,32},{32,64},{64,96},{96,128},{128,160},{160,192},{192,224},{224... | collective-permute-start | bytes 294920 | tf_op jit(solution)/shard_map/ppermute | solution.py:43
  18.6 5.0 %collective-permute-start.2 = (bf16[32,1536]{1,0:T(8,128)(2,1)S(1)}, bf16[32,1536]{1,0:T(8,128)(2,1)S(1)}, u32[]{:S(2)}, u32[]{:S(2)}) collective-permute-start(bf16[32,1536]{1,0:T(8,128)(2,1)S(1)} %collective-permute-done.1), channel_id=1, source_target_pairs={{0,224},{32,0},{64,32},{96,64},{128,96},{160,128},{192,160},{224,1... | collective-permute-start | bytes 294920 | tf_op jit(solution)/shard_map/ppermute | solution.py:44
  23.6 4.4 %collective-permute-start.6 = (bf16[32,768]{1,0:T(8,128)(2,1)S(1)}, bf16[32,768]{1,0:T(8,128)(2,1)S(1)}, u32[]{:S(2)}, u32[]{:S(2)}) collective-permute-start(bf16[32,768]{1,0:T(8,128)(2,1)S(1)} %slice.26), channel_id=1, source_target_pairs={{0,32},{32,64},{64,96},{96,128},{128,160},{160,192},{192,224},{224... | collective-permute-start | bytes 147464 | tf_op jit(solution)/shard_map/ppermute | solution.py:39
  23.6 4.4 %collective-permute-start.7 = (bf16[32,768]{1,0:T(8,128)(2,1)S(1)}, bf16[32,768]{1,0:T(8,128)(2,1)S(1)}, u32[]{:S(2)}, u32[]{:S(2)}) collective-permute-start(bf16[32,768]{1,0:T(8,128)(2,1)S(1)} %slice.27), channel_id=1, source_target_pairs={{0,224},{32,0},{64,32},{96,64},{128,96},{160,128},{192,160},{224,1... | collective-permute-start | bytes 147464 | tf_op jit(solution)/shard_map/ppermute | solution.py:40
  30.5 15.6 %collective-permute-start.13 = (bf16[8,32,1536]{2,1,0:T(8,128)(2,1)}, bf16[8,32,1536]{2,1,0:T(8,128)(2,1)}, u32[]{:S(2)}, u32[]{:S(2)}) collective-permute-start(bf16[8,32,1536]{2,1,0:T(8,128)(2,1)} %get-tuple-element.9), channel_id=1, source_target_pairs={{0,24},{8,0},{16,8},{24,16},{1,25},{9,1},{17,9},{25,17},{2,26},{10... | collective-permute-start | bytes 2359304 | tf_op jit(solution)/shard_map/ppermute | solution.py:76
  33.2 17.4 %collective-permute-start.12 = (bf16[8,32,1536]{2,1,0:T(8,128)(2,1)}, bf16[8,32,1536]{2,1,0:T(8,128)(2,1)}, u32[]{:S(2)}, u32[]{:S(2)}) collective-permute-start(bf16[8,32,1536]{2,1,0:T(8,128)(2,1)} %get-tuple-element.9), channel_id=1, source_target_pairs={{0,8},{8,16},{16,24},{24,0},{1,9},{9,17},{17,25},{25,1},{2,10},{10... | collective-permute-start | bytes 2359304 | tf_op jit(solution)/shard_map/ppermute | solution.py:75
  35.5 24.3 %collective-permute-start.11 = (bf16[4,128,1536]{2,1,0:T(8,128)(2,1)}, bf16[4,128,1536]{2,1,0:T(8,128)(2,1)S(1)}, u32[]{:S(2)}, u32[]{:S(2)}) collective-permute-start(bf16[4,128,1536]{2,1,0:T(8,128)(2,1)} %broadcast_select_fusion), channel_id=1, source_target_pairs={{0,1},{1,0},{2,3},{3,2},{4,5},{5,4},{6,7},{7,6},{8,9},{9,8},{10,11... | collective-permute-start | bytes 4718600 | tf_op jit(solution)/shard_map/ppermute | solution.py:65
  47.1 12.6 %collective-permute-start.15 = (bf16[8,32,768]{2,1,0:T(8,128)(2,1)S(1)}, bf16[8,32,768]{2,1,0:T(8,128)(2,1)S(1)}, u32[]{:S(2)}, u32[]{:S(2)}) collective-permute-start(bf16[8,32,768]{2,1,0:T(8,128)(2,1)S(1)} %slice.29), channel_id=1, source_target_pairs={{0,24},{8,0},{16,8},{24,16},{1,25},{9,1},{17,9},{25,17},{2,26},{10... | collective-permute-start | bytes 1179656 | tf_op jit(solution)/shard_map/ppermute | solution.py:79
  51.6 8.1 %collective-permute-start.14 = (bf16[8,32,768]{2,1,0:T(8,128)(2,1)S(1)}, bf16[8,32,768]{2,1,0:T(8,128)(2,1)S(1)}, u32[]{:S(2)}, u32[]{:S(2)}) collective-permute-start(bf16[8,32,768]{2,1,0:T(8,128)(2,1)S(1)} %slice.28), channel_id=1, source_target_pairs={{0,8},{8,16},{16,24},{24,0},{1,9},{9,17},{17,25},{25,1},{2,10},{10... | collective-permute-start | bytes 1179656 | tf_op jit(solution)/shard_map/ppermute | solution.py:78
  59.8 2.8 %slice-start = ((s8[6291456]{0:T(1024)(128)(4,1)}), s8[4194304]{0:T(1024)(128)(4,1)S(1)}, s32[]{:S(2)}) async-start(s8[6291456]{0:T(1024)(128)(4,1)} %bitcast.120), calls=%async_computation | async-start | bytes 8388608
  59.8 2.8 %slice-start.1 = ((s8[6291456]{0:T(1024)(128)(4,1)}), s8[2097152]{0:T(1024)(128)(4,1)S(1)}, s32[]{:S(2)}) async-start(s8[6291456]{0:T(1024)(128)(4,1)} %bitcast.120), calls=%async_computation.1 | async-start | bytes 4194304
  63.9 5.5 %slice-start.2 = ((s8[4718592]{0:T(1024)(128)(4,1)}), s8[4194304]{0:T(1024)(128)(4,1)S(1)}, s32[]{:S(2)}) async-start(s8[4718592]{0:T(1024)(128)(4,1)} %bitcast.130), calls=%async_computation.2 | async-start | bytes 8388608
  67.8 1.6 %slice-start.3 = ((s8[4718592]{0:T(1024)(128)(4,1)}), s8[524288]{0:T(1024)(128)(4,1)S(1)}, s32[]{:S(2)}) async-start(s8[4718592]{0:T(1024)(128)(4,1)} %bitcast.130), calls=%async_computation.3 | async-start | bytes 1048576
  72.1 24.2 %collective-permute-start.16 = (bf16[4,4,32,1536]{3,2,1,0:T(8,128)(2,1)S(1)}, bf16[4,4,32,1536]{3,2,1,0:T(8,128)(2,1)S(1)}, u32[]{:S(2)}, u32[]{:S(2)}) collective-permute-start(bf16[4,4,32,1536]{3,2,1,0:T(8,128)(2,1)S(1)} %fusion.10), channel_id=1, source_target_pairs={{0,1},{1,0},{2,3},{3,2},{4,5},{5,4},{6,7},{7,6},{8,9},{9,8},{10,11... | collective-permute-start | bytes 4718600 | tf_op jit(solution)/shard_map/ppermute | solution.py:106
  99.2 16.7 %collective-permute-start.19 = (bf16[128,768]{1,0:T(8,128)(2,1)S(1)}, bf16[128,768]{1,0:T(8,128)(2,1)S(1)}, u32[]{:S(2)}, u32[]{:S(2)}) collective-permute-start(bf16[128,768]{1,0:T(8,128)(2,1)S(1)} %get-tuple-element.13), channel_id=1, source_target_pairs={{0,2},{1,3},{2,4},{3,5},{4,6},{5,7},{6,0},{7,1},{8,10},{9,11},{10,... | collective-permute-start | bytes 589832 | tf_op jit(solution)/shard_map/ppermute | solution.py:127
  99.3 16.6 %collective-permute-start.21 = (bf16[128,768]{1,0:T(8,128)(2,1)S(1)}, bf16[128,768]{1,0:T(8,128)(2,1)S(1)}, u32[]{:S(2)}, u32[]{:S(2)}) collective-permute-start(bf16[128,768]{1,0:T(8,128)(2,1)S(1)} %get-tuple-element.14), channel_id=1, source_target_pairs={{0,6},{1,7},{2,0},{3,1},{4,2},{5,3},{6,4},{7,5},{8,14},{9,15},{10,... | collective-permute-start | bytes 589832 | tf_op jit(solution)/shard_map/ppermute | solution.py:128
  102.0 20.5 %collective-permute-start.18 = (bf16[128,1536]{1,0:T(8,128)(2,1)S(1)}, bf16[128,1536]{1,0:T(8,128)(2,1)S(1)}, u32[]{:S(2)}, u32[]{:S(2)}) collective-permute-start(bf16[128,1536]{1,0:T(8,128)(2,1)S(1)} %bitcast.129), channel_id=1, source_target_pairs={{0,6},{1,7},{2,0},{3,1},{4,2},{5,3},{6,4},{7,5},{8,14},{9,15},{10,... | collective-permute-start | bytes 1179656 | tf_op jit(solution)/shard_map/ppermute | solution.py:128
  102.0 20.5 %collective-permute-start.17 = (bf16[128,1536]{1,0:T(8,128)(2,1)S(1)}, bf16[128,1536]{1,0:T(8,128)(2,1)S(1)}, u32[]{:S(2)}, u32[]{:S(2)}) collective-permute-start(bf16[128,1536]{1,0:T(8,128)(2,1)S(1)} %bitcast.128), channel_id=1, source_target_pairs={{0,2},{1,3},{2,4},{3,5},{4,6},{5,7},{6,0},{7,1},{8,10},{9,11},{10,... | collective-permute-start | bytes 1179656 | tf_op jit(solution)/shard_map/ppermute | solution.py:127
  115.9 6.5 %collective-permute-start.20 = (bf16[128,768]{1,0:T(8,128)(2,1)S(1)}, bf16[128,768]{1,0:T(8,128)(2,1)S(1)}, u32[]{:S(2)}, u32[]{:S(2)}) collective-permute-start(bf16[128,768]{1,0:T(8,128)(2,1)S(1)} %collective-permute-done.19), channel_id=1, source_target_pairs={{0,2},{1,3},{2,4},{3,5},{4,6},{5,7},{6,0},{7,1},{8,10},{9,11},{10,... | collective-permute-start | bytes 589832 | tf_op jit(solution)/shard_map/ppermute | solution.py:129
  115.9 6.5 %collective-permute-start.22 = (bf16[128,768]{1,0:T(8,128)(2,1)S(1)}, bf16[128,768]{1,0:T(8,128)(2,1)S(1)}, u32[]{:S(2)}, u32[]{:S(2)}) collective-permute-start(bf16[128,768]{1,0:T(8,128)(2,1)S(1)} %collective-permute-done.21), channel_id=1, source_target_pairs={{0,6},{1,7},{2,0},{3,1},{4,2},{5,3},{6,4},{7,5},{8,14},{9,15},{10,... | collective-permute-start | bytes 589832 | tf_op jit(solution)/shard_map/ppermute | solution.py:130

commit v11 on v9

--- a/solution.py
+++ b/solution.py
@@ -48,6 +48,38 @@
     return jnp.roll(stacked, i, axis=0)
 
 
+def z_then_y(block, n_z, n_y):
+    z = lax.axis_index("z")
+    fwd = bwd = block
+    by_off = {0: block}
+    groups, taken = [], set()
+    mid = max(1, n_z // 4)
+    for step in range(1, n_z // 2 + 1):
+        ahead = [(j, (j + 1) % n_z) for j in range(n_z)]
+        behind = [(j, (j - 1) % n_z) for j in range(n_z)]
+        if 2 * step == n_z:
+            half = block.shape[-1] // 2
+            by_off[step] = jnp.concatenate([lax.ppermute(fwd[..., :half], "z", ahead),
+                                            lax.ppermute(bwd[..., half:], "z", behind)], axis=-1)
+        else:
+            fwd = lax.ppermute(fwd, "z", ahead)
+            bwd = lax.ppermute(bwd, "z", behind)
+            by_off[-step % n_z] = fwd
+            by_off[step] = bwd
+        if step == mid or step == n_z // 2:
+            new = [d for d in sorted(by_off) if d not in taken]
+            taken.update(new)
+            groups.append(new)
+    if not groups:
+        groups.append([0])
+    parts = [ring_gather(jnp.stack([by_off[d] for d in g], axis=0), "y", n_y) for g in groups]
+    offsets = [d for g in groups for d in g]
+    joined = jnp.concatenate(parts, axis=1)
+    where = jnp.array([offsets.index(d) for d in range(n_z)], dtype=jnp.int32)
+    pick = jnp.take(where, (jnp.arange(n_z) - z) % n_z)
+    return jnp.take(joined, pick, axis=1)
+
+
 def make_per_device(n_col, n_z, n_y):
     n_x = n_col // 2
 
@@ -57,7 +89,7 @@
         k = c % 2
 
         tokens = out_grad.shape[0] * n_z * n_y
-        gathered = ring_gather(ring_gather(out_grad, "z", n_z), "y", n_y)
+        gathered = z_then_y(out_grad, n_z, n_y)
         grad_all = gathered.reshape((tokens, out_grad.shape[1]))
         rows_r = out_grad.shape[0]
 

time: 110 us -> 121 us (1.10)
  waiting for transfers between devices: 23.1 us -> 11.6 us
  local copies, waits for them, and re-layouts: 14.6 us -> 25.1 us
  other arithmetic: 6.16 us -> 12.6 us
  starting transfers between devices: 47.7 us -> 52.6 us
    ppermute x0 -> x8, starting transfers between devices: none -> 15.3 us  [the longest x3 12.6 us: z_then_y(): bwd = lax.ppermute(bwd, 'z', behind)]
    ppermute x4 -> x2, starting transfers between devices: 15.3 us -> 5.4 us  [ring_gather(): bwd = lax.ppermute(bwd, axis, behind)]
    ppermute x4 -> x2, waiting for transfers between devices: 11 us -> 1.2 us  [ring_gather(): fwd = lax.ppermute(fwd, axis, ahead)]
    gather x0 -> x3, local copies, waits for them, and re-layouts: none -> 5.95 us  [the longest x2 4.65 us: z_then_y(): return jnp.take(joined, pick, axis=1)]
    ppermute x2, waiting for transfers between devices: 4.9 us -> 0.01 us  [ring_gather(): from_behind = lax.ppermute(fwd[..., :half], axis, ahead)]
    ppermute x0 -> x8, waiting for transfers between devices: none -> 4.69 us  [the longest x3 3.69 us: z_then_y(): fwd = lax.ppermute(fwd, 'z', ahead)]
    select_n x3, other arithmetic: 0.45 us -> 2.72 us  [per_device(): mine_by_x = jnp.take(by_chip, order, axis=0)]
    unnamed x38, local copies, waits for them, and re-layouts: 9.84 us -> 12 us
  transfers between devices with their start and end apart: 23 -> 27, of which waited for: 7 -> 6; matrix products, arithmetic and copies ran while one was open for 21% -> 33% of each run, Pallas kernels for 0% -> 0%
where the time goes in v11:
time: 121 us; the launch traced here: 119 us
  starting transfers between devices  52.6 us (43%)
  local copies, waits for them, and re-layouts  25.1 us (21%)
  matrix products  16.2 us (13%)
  other arithmetic  12.6 us (10%)
  waiting for transfers between devices  11.6 us (10%)
    ppermute x3, starting transfers between devices, z_then_y(): bwd = lax.ppermute(bwd, 'z', behind)  12.6 us
    unnamed x38, local copies, waits for them, and re-layouts  12 us
    ppermute x1, starting transfers between devices, per_device(): lax.ppermute(p_theirs.astype(jnp.bfloat16), COL, core_swap(n_col))  7.72 us
    dot_general x1, matrix products, per_device(): lax.dot_general(hidden, grad_all, (((0,), (0,)), ((), ())), preferred_ele...  6.92 us
    ppermute x1, starting transfers between devices, per_device(): other_by_x = lax.ppermute(mine_by_x, COL, core_swap(n_col))  5.6 us
    dot_general x1, matrix products, per_device(): lax.dot_general(g_mine, weight, (((3,), (1,)), ((), ())), preferred_eleme...  5.49 us
    ppermute x2, starting transfers between devices, ring_gather(): from_ahead = lax.ppermute(bwd[..., half:], axis, behind)  5.46 us
    ppermute x2, starting transfers between devices, ring_gather(): bwd = lax.ppermute(bwd, axis, behind)  5.4 us
  transfers between devices with their start and end apart: 27, of which 6 were waited for; matrix products, arithmetic and copies ran while one was open for 33% of the time, Pallas kernels for 0%

profile of v11, /device:TPU:1, one launch (start us, length us, event | category | flops | bytes accessed | tf_op | source)
XLA Modules:
  0.0 119.2 jit_solution(13540787240082470422)
XLA Ops:
  0.6 6.5 %collective-permute-start.4 = (bf16[32,1536]{1,0:T(8,128)(2,1)}, bf16[32,1536]{1,0:T(8,128)(2,1)S(1)}, u32[]{:S(2)}, u32[]{:S(2)}) collective-permute-start(bf16[32,1536]{1,0:T(8,128)(2,1)} %param.5), channel_id=1, source_target_pairs={{0,224},{32,0},{64,32},{96,64},{128,96},{160,128},{192,160},{224,1... | collective-permute-start | bytes 294920 | tf_op jit(solution)/shard_map/ppermute | solution.py:66
  7.1 1.2 %collective-permute-start = (bf16[128,1536]{1,0:T(8,128)(2,1)}, bf16[128,1536]{1,0:T(8,128)(2,1)S(1)}, u32[]{:S(2)}, u32[]{:S(2)}) collective-permute-start(bf16[128,1536]{1,0:T(8,128)(2,1)} %param.4), channel_id=1, source_target_pairs={{0,2},{1,3},{2,4},{3,5},{4,6},{5,7},{6,0},{7,1},{8,10},{9,11},{10,... | collective-permute-start | bytes 1179656 | tf_op jit(solution)/shard_map/ppermute | solution.py:98
  8.3 2.5 %collective-permute-start.1 = (bf16[128,1536]{1,0:T(8,128)(2,1)}, bf16[128,1536]{1,0:T(8,128)(2,1)S(1)}, u32[]{:S(2)}, u32[]{:S(2)}) collective-permute-start(bf16[128,1536]{1,0:T(8,128)(2,1)} %param.4), channel_id=1, source_target_pairs={{0,4},{1,5},{2,6},{3,7},{4,0},{5,1},{6,2},{7,3},{8,12},{9,13},{10,... | collective-permute-start | bytes 1179656 | tf_op jit(solution)/shard_map/ppermute | solution.py:98
  11.9 1.5 %bitcast_dynamic-update-slice_fusion.16 = bf16[5,32,1536]{2,1,0:T(8,128)(2,1)} fusion(bf16[32,1536]{1,0:T(8,128)(2,1)} %param.5), kind=kLoop, calls=%fused_computation.76 | loop fusion | bytes 196608
  13.5 1.3 %gather_fusion.1 = s32[8]{0:T(128)S(1)} fusion(s32[8]{0:T(128)} %constant.184.clone, s32[1024]{0:T(1024)S(1)} %pad_clamp_fusion.1), kind=kCustom, calls=%fused_computation.1 | custom fusion | bytes 96 | tf_op jit(solution)/shard_map/jit(_take)/gather | solution.py:79
  15.1 2.8 %collective-permute-start.5 = (bf16[32,1536]{1,0:T(8,128)(2,1)S(1)}, bf16[32,1536]{1,0:T(8,128)(2,1)S(1)}, u32[]{:S(2)}, u32[]{:S(2)}) collective-permute-start(bf16[32,1536]{1,0:T(8,128)(2,1)S(1)} %collective-permute-done.4), channel_id=1, source_target_pairs={{0,224},{32,0},{64,32},{96,64},{128,96},{160,128},{192,160},{224,1... | collective-permute-start | bytes 294920 | tf_op jit(solution)/shard_map/ppermute | solution.py:66
  19.5 3.3 %collective-permute-start.12 = (bf16[32,1536]{1,0:T(8,128)(2,1)S(1)}, bf16[32,1536]{1,0:T(8,128)(2,1)S(1)}, u32[]{:S(2)}, u32[]{:S(2)}) collective-permute-start(bf16[32,1536]{1,0:T(8,128)(2,1)S(1)} %collective-permute-done.5), channel_id=1, source_target_pairs={{0,224},{32,0},{64,32},{96,64},{128,96},{160,128},{192,160},{224,1... | collective-permute-start | bytes 294920 | tf_op jit(solution)/shard_map/ppermute | solution.py:66
  24.8 3.7 %collective-permute-done.13 = bf16[32,1536]{1,0:T(8,128)(2,1)S(1)} collective-permute-done((bf16[32,1536]{1,0:T(8,128)(2,1)S(1)}, bf16[32,1536]{1,0:T(8,128)(2,1)S(1)}, u32[]{:S(2)}, u32[]{:S(2)}) %collective-permute-start.13) | collective-permute-done | bytes 98336 | tf_op jit(solution)/shard_map/ppermute | solution.py:65
  28.5 2.7 %collective-permute-start.15 = (bf16[32,768]{1,0:T(8,128)(2,1)S(1)}, bf16[32,768]{1,0:T(8,128)(2,1)S(1)}, u32[]{:S(2)}, u32[]{:S(2)}) collective-permute-start(bf16[32,768]{1,0:T(8,128)(2,1)S(1)} %slice.41), channel_id=1, source_target_pairs={{0,224},{32,0},{64,32},{96,64},{128,96},{160,128},{192,160},{224,1... | collective-permute-start | bytes 147464 | tf_op jit(solution)/shard_map/ppermute | solution.py:63
  31.2 1.8 %bitcast_dynamic-update-slice_fusion.4 = bf16[8,5,32,1536]{3,2,1,0:T(8,128)(2,1)} fusion(bf16[5,32,1536]{2,1,0:T(8,128)(2,1)} %bitcast_dynamic-update-slice_fusion.12), kind=kLoop, calls=%fused_computation.57 | loop fusion | bytes 983040
  33.1 2.7 %collective-permute-start.8 = (bf16[5,32,1536]{2,1,0:T(8,128)(2,1)}, bf16[5,32,1536]{2,1,0:T(8,128)(2,1)}, u32[]{:S(2)}, u32[]{:S(2)}) collective-permute-start(bf16[5,32,1536]{2,1,0:T(8,128)(2,1)} %bitcast_dynamic-update-slice_fusion.12), channel_id=1, source_target_pairs={{0,24},{8,0},{16,8},{24,16},{1,25},{9,1},{17,9},{25,17},{2,26},{10... | collective-permute-start | bytes 1474568 | tf_op jit(solution)/shard_map/ppermute | solution.py:44
  37.3 2.7 %collective-permute-start.16 = (bf16[3,32,1536]{2,1,0:T(8,128)(2,1)}, bf16[3,32,1536]{2,1,0:T(8,128)(2,1)S(1)}, u32[]{:S(2)}, u32[]{:S(2)}) collective-permute-start(bf16[3,32,1536]{2,1,0:T(8,128)(2,1)} %pad_maximum_fusion.2), channel_id=1, source_target_pairs={{0,24},{8,0},{16,8},{24,16},{1,25},{9,1},{17,9},{25,17},{2,26},{10... | collective-permute-start | bytes 884744 | tf_op jit(solution)/shard_map/ppermute | solution.py:44
  40.0 1.2 %pad_maximum_fusion.1 = bf16[4,128,1536]{2,1,0:T(8,128)(2,1)S(1)} fusion(bf16[1,128,1536]{2,1,0:T(8,128)(2,1)} %bitcast.3, bf16[1,128,1536]{2,1,0:T(8,128)(2,1)S(1)} %bitcast.119, bf16[1,128,1536]{2,1,0:T(8,128)(2,1)S(1)} %bitcast.118, bf16[1,128,1536]{2,1,0:T(8,128)(2,1)S(1)} %bitcast.111), kind=kLoop, calls=%fused_computation.30 | loop fusion | flops 2359296 | bytes 3145728 | tf_op jit(solution)/shard_map/stack | solution.py:99
  41.9 1.4 %broadcast_select_fusion = bf16[4,128,1536]{2,1,0:T(8,128)(2,1)} fusion(bf16[4,128,1536]{2,1,0:T(8,128)(2,1)S(1)} %gather_fusion, pred[4]{0:T(512)(128)(4,1)S(1)} %compare_and_fusion.1), kind=kLoop, calls=%fused_computation.36 | loop fusion | flops 786432 | bytes 3145732 | tf_op jit(solution)/shard_map/jit(_take)/select_n | solution.py:101
  43.3 1.4 %bitcast_select_fusion.1 = bf16[4,1,128,1536]{3,2,1,0:T(8,128)(2,1)} fusion(bf16[4,128,1536]{2,1,0:T(8,128)(2,1)S(1)} %gather_fusion, pred[4]{0:T(512)(128)(4,1)S(1)} %compare_and_fusion.1), kind=kLoop, calls=%fused_computation.31 | loop fusion | flops 786432 | bytes 3145732 | tf_op jit(solution)/shard_map/jit(_take)/select_n | solution.py:101
  44.6 5.6 %collective-permute-start.3 = (bf16[4,128,1536]{2,1,0:T(8,128)(2,1)}, bf16[4,128,1536]{2,1,0:T(8,128)(2,1)}, u32[]{:S(2)}, u32[]{:S(2)}) collective-permute-start(bf16[4,128,1536]{2,1,0:T(8,128)(2,1)} %broadcast_select_fusion), channel_id=1, source_target_pairs={{0,1},{1,0},{2,3},{3,2},{4,5},{5,4},{6,7},{7,6},{8,9},{9,8},{10,11... | collective-permute-start | bytes 4718600 | tf_op jit(solution)/shard_map/ppermute | solution.py:102
  50.2 1.2 %collective-permute-done.17 = bf16[3,32,1536]{2,1,0:T(8,128)(2,1)} collective-permute-done((bf16[3,32,1536]{2,1,0:T(8,128)(2,1)}, bf16[3,32,1536]{2,1,0:T(8,128)(2,1)}, u32[]{:S(2)}, u32[]{:S(2)}) %collective-permute-start.17) | collective-permute-done | bytes 294944 | tf_op jit(solution)/shard_map/ppermute | solution.py:43
  52.5 2.7 %collective-permute-start.19 = (bf16[3,32,768]{2,1,0:T(8,128)(2,1)S(1)}, bf16[3,32,768]{2,1,0:T(8,128)(2,1)S(1)}, u32[]{:S(2)}, u32[]{:S(2)}) collective-permute-start(bf16[3,32,768]{2,1,0:T(8,128)(2,1)S(1)} %slice.43), channel_id=1, source_target_pairs={{0,24},{8,0},{16,8},{24,16},{1,25},{9,1},{17,9},{25,17},{2,26},{10... | collective-permute-start | bytes 442376 | tf_op jit(solution)/shard_map/ppermute | solution.py:40
  57.3 2.7 %collective-permute-start.11 = (bf16[5,32,768]{2,1,0:T(8,128)(2,1)S(1)}, bf16[5,32,768]{2,1,0:T(8,128)(2,1)S(1)}, u32[]{:S(2)}, u32[]{:S(2)}) collective-permute-start(bf16[5,32,768]{2,1,0:T(8,128)(2,1)S(1)} %slice.39), channel_id=1, source_target_pairs={{0,24},{8,0},{16,8},{24,16},{1,25},{9,1},{17,9},{25,17},{2,26},{10... | collective-permute-start | bytes 737288 | tf_op jit(solution)/shard_map/ppermute | solution.py:40
  68.3 2.4 %gather_fusion.2 = bf16[8,4,32,1536]{3,2,1,0:T(8,128)(2,1)} fusion(bf16[4,8,32,1536]{3,2,1,0:T(8,128)(2,1)S(1)} %pad_maximum_fusion, s32[1024]{0:T(1024)S(1)} %pad_clamp_fusion), kind=kCustom, calls=%fused_computation.2 | custom fusion | bytes 6291488 | tf_op jit(solution)/shard_map/jit(_take)/gather | solution.py:80
  70.7 2.2 %copy.9 = bf16[4,8,32,1536]{3,2,1,0:T(8,128)(2,1)S(1)} copy(bf16[4,8,32,1536]{3,2,0,1:T(8,128)(2,1)} %bitcast.105) | data formatting | bytes 6291456 | tf_op jit(solution)/shard_map/jit(_take)/gather | solution.py:80
  74.3 2.4 %maximum_select_fusion = bf16[4,2,128,1536]{3,2,1,0:T(8,128)(2,1)S(1)} fusion(bf16[4,1,128,1536]{3,2,1,0:T(8,128)(2,1)} %bitcast.7, bf16[4,1,128,1536]{3,2,1,0:T(8,128)(2,1)S(1)} %copy-done, pred[]{:T(512)S(6)} %eq.17), kind=kLoop, calls=%fused_computation.18 | loop fusion | flops 4718592 | bytes 6291457 | tf_op jit(solution)/shard_map/jit(_where)/select_n | solution.py:103
  76.8 3.8 %fusion.9 = bf16[4,4,32,1536]{3,2,1,0:T(8,128)(2,1)} fusion(bf16[1536,1536]{1,0:T(8,128)(2,1)S(1)} %bitcast.123, bf16[4,4,2,32,1536]{4,3,2,1,0:T(8,128)(2,1)S(1)} %bitcast.108, s32[]{:T(128)S(6)} %select_n.222), kind=kOutput, calls=%fused_computation.22 | convolution fusion | flops 2416705536 | bytes 7864324 | tf_op jit(solution)/shard_map/dot_general | solution.py:120
  80.6 7.7 %collective-permute-start.20 = (bf16[4,4,32,1536]{3,2,1,0:T(8,128)(2,1)}, bf16[4,4,32,1536]{3,2,1,0:T(8,128)(2,1)}, u32[]{:S(2)}, u32[]{:S(2)}) collective-permute-start(bf16[4,4,32,1536]{3,2,1,0:T(8,128)(2,1)} %fusion.9), channel_id=1, source_target_pairs={{0,1},{1,0},{2,3},{3,2},{4,5},{5,4},{6,7},{7,6},{8,9},{9,8},{10,11... | collective-permute-start | bytes 4718600 | tf_op jit(solution)/shard_map/ppermute | solution.py:122
  88.4 2.2 %fusion.1 = bf16[1024,1536]{1,0:T(8,128)(2,1)S(1)} fusion(bf16[1024,1536]{1,0:T(8,128)(2,1)S(1)} %bitcast.104), kind=kLoop, calls=%fused_computation.10 | loop fusion | flops 15728640 | bytes 6291456 | tf_op jit(solution)/shard_map/convert_element_type | solution.py:109
  92.4 5.5 %convert_add_fusion.1 = f32[4,4,32,1536]{3,2,1,0:T(8,128)S(1)} fusion(bf16[4,4,32,1536]{3,2,1,0:T(8,128)(2,1)} %collective-permute-done.20, bf16[1536,1536]{1,0:T(8,128)(2,1)} %param.6, bf16[4,4,2,32,1536]{4,3,2,1,0:T(8,128)(2,1)S(1)} %bitcast.109, s32[]{:T(128)S(6)} %select_n.221), kind=kOutput, calls=%fused_computation.21 | convolution fusion | flops 2417491968 | bytes 11010052 | tf_op jit(solution)/shard_map/dot_general | solution.py:123
  98.3 2.5 %collective-permute-start.25 = (bf16[128,768]{1,0:T(8,128)(2,1)S(1)}, bf16[128,768]{1,0:T(8,128)(2,1)S(1)}, u32[]{:S(2)}, u32[]{:S(2)}) collective-permute-start(bf16[128,768]{1,0:T(8,128)(2,1)S(1)} %get-tuple-element.10), channel_id=1, source_target_pairs={{0,6},{1,7},{2,0},{3,1},{4,2},{5,3},{6,4},{7,5},{8,14},{9,15},{10,... | collective-permute-start | bytes 589832 | tf_op jit(solution)/shard_map/ppermute | solution.py:144
  100.9 2.7 %collective-permute-start.22 = (bf16[128,1536]{1,0:T(8,128)(2,1)S(1)}, bf16[128,1536]{1,0:T(8,128)(2,1)S(1)}, u32[]{:S(2)}, u32[]{:S(2)}) collective-permute-start(bf16[128,1536]{1,0:T(8,128)(2,1)S(1)} %bitcast.120), channel_id=1, source_target_pairs={{0,6},{1,7},{2,0},{3,1},{4,2},{5,3},{6,4},{7,5},{8,14},{9,15},{10,... | collective-permute-start | bytes 1179656 | tf_op jit(solution)/shard_map/ppermute | solution.py:144
  103.6 6.9 %convolution_convert_fusion = bf16[1536,1536]{1,0:T(8,128)(2,1)} fusion(bf16[1024,1536]{1,0:T(8,128)(2,1)S(1)} %bitcast.107, bf16[1024,1536]{1,0:T(8,128)(2,1)S(1)} %copy-done.2), kind=kOutput, calls=%fused_computation.8 | convolution fusion | flops 4834197504 | bytes 11010048 | tf_op jit(solution)/shard_map/dot_general | solution.py:111
  110.5 2.7 %collective-permute-start.26 = (bf16[128,768]{1,0:T(8,128)(2,1)S(1)}, bf16[128,768]{1,0:T(8,128)(2,1)S(1)}, u32[]{:S(2)}, u32[]{:S(2)}) collective-permute-start(bf16[128,768]{1,0:T(8,128)(2,1)S(1)} %collective-permute-done.25), channel_id=1, source_target_pairs={{0,6},{1,7},{2,0},{3,1},{4,2},{5,3},{6,4},{7,5},{8,14},{9,15},{10,... | collective-permute-start | bytes 589832 | tf_op jit(solution)/shard_map/ppermute | solution.py:146
  113.2 4.5 %collective-permute-done.24 = bf16[128,768]{1,0:T(8,128)(2,1)S(1)} collective-permute-done((bf16[128,768]{1,0:T(8,128)(2,1)S(1)}, bf16[128,768]{1,0:T(8,128)(2,1)S(1)}, u32[]{:S(2)}, u32[]{:S(2)}) %collective-permute-start.24) | collective-permute-done | bytes 196640 | tf_op jit(solution)/shard_map/ppermute | solution.py:145
  117.8 1.4 %fusion.27 = bf16[128,1536]{1,0:T(8,128)(2,1)} fusion(bf16[128,1536]{1,0:T(8,128)(2,1)S(1)} %copy-done.4, f32[4,1,32,1536]{3,2,1,0:T(8,128)S(1)} %constant_dynamic-slice_fusion, bf16[128,1536]{1,0:T(8,128)(2,1)S(1)} %collective-permute-done.22, bf16[128,1536]{1,0:T(8,128)(2,1)S(1)} %collective-permute-done.21, ...), kind=kLoop, calls=%fused_computation.44 | loop fusion | flops 5701632 | bytes 2752512 | tf_op jit(solution)/shard_map/convert_element_type | solution.py:156
  (109 shorter events, 22.1 us)
Async XLA Ops:
  0.6 39.4 %copy-start.3 = (bf16[128,1536]{1,0:T(8,128)(2,1)S(1)}, bf16[128,1536]{1,0:T(8,128)(2,1)}, u32[]{:S(2)}) copy-start(bf16[128,1536]{1,0:T(8,128)(2,1)} %param.4) | copy-start | bytes 1179652
  0.6 14.5 %collective-permute-start.4 = (bf16[32,1536]{1,0:T(8,128)(2,1)}, bf16[32,1536]{1,0:T(8,128)(2,1)S(1)}, u32[]{:S(2)}, u32[]{:S(2)}) collective-permute-start(bf16[32,1536]{1,0:T(8,128)(2,1)} %param.5), channel_id=1, source_target_pairs={{0,224},{32,0},{64,32},{96,64},{128,96},{160,128},{192,160},{224,1... | collective-permute-start | bytes 294920 | tf_op jit(solution)/shard_map/ppermute | solution.py:66
  7.1 11.4 %collective-permute-start.6 = (bf16[32,1536]{1,0:T(8,128)(2,1)}, bf16[32,1536]{1,0:T(8,128)(2,1)S(1)}, u32[]{:S(2)}, u32[]{:S(2)}) collective-permute-start(bf16[32,1536]{1,0:T(8,128)(2,1)} %param.5), channel_id=1, source_target_pairs={{0,32},{32,64},{64,96},{96,128},{128,160},{160,192},{192,224},{224... | collective-permute-start | bytes 294920 | tf_op jit(solution)/shard_map/ppermute | solution.py:65
  7.1 30.2 %collective-permute-start = (bf16[128,1536]{1,0:T(8,128)(2,1)}, bf16[128,1536]{1,0:T(8,128)(2,1)S(1)}, u32[]{:S(2)}, u32[]{:S(2)}) collective-permute-start(bf16[128,1536]{1,0:T(8,128)(2,1)} %param.4), channel_id=1, source_target_pairs={{0,2},{1,3},{2,4},{3,5},{4,6},{5,7},{6,0},{7,1},{8,10},{9,11},{10,... | collective-permute-start | bytes 1179656 | tf_op jit(solution)/shard_map/ppermute | solution.py:98
  8.3 31.7 %collective-permute-start.1 = (bf16[128,1536]{1,0:T(8,128)(2,1)}, bf16[128,1536]{1,0:T(8,128)(2,1)S(1)}, u32[]{:S(2)}, u32[]{:S(2)}) collective-permute-start(bf16[128,1536]{1,0:T(8,128)(2,1)} %param.4), channel_id=1, source_target_pairs={{0,4},{1,5},{2,6},{3,7},{4,0},{5,1},{6,2},{7,3},{8,12},{9,13},{10,... | collective-permute-start | bytes 1179656 | tf_op jit(solution)/shard_map/ppermute | solution.py:98
  10.8 29.2 %collective-permute-start.2 = (bf16[128,1536]{1,0:T(8,128)(2,1)}, bf16[128,1536]{1,0:T(8,128)(2,1)}, u32[]{:S(2)}, u32[]{:S(2)}) collective-permute-start(bf16[128,1536]{1,0:T(8,128)(2,1)} %param.4), channel_id=1, source_target_pairs={{0,6},{1,7},{2,0},{3,1},{4,2},{5,3},{6,4},{7,5},{8,14},{9,15},{10,... | collective-permute-start | bytes 1179656 | tf_op jit(solution)/shard_map/ppermute | solution.py:98
  15.1 4.4 %collective-permute-start.5 = (bf16[32,1536]{1,0:T(8,128)(2,1)S(1)}, bf16[32,1536]{1,0:T(8,128)(2,1)S(1)}, u32[]{:S(2)}, u32[]{:S(2)}) collective-permute-start(bf16[32,1536]{1,0:T(8,128)(2,1)S(1)} %collective-permute-done.4), channel_id=1, source_target_pairs={{0,224},{32,0},{64,32},{96,64},{128,96},{160,128},{192,160},{224,1... | collective-permute-start | bytes 294920 | tf_op jit(solution)/shard_map/ppermute | solution.py:66
  18.5 5.0 %collective-permute-start.7 = (bf16[32,1536]{1,0:T(8,128)(2,1)S(1)}, bf16[32,1536]{1,0:T(8,128)(2,1)S(1)}, u32[]{:S(2)}, u32[]{:S(2)}) collective-permute-start(bf16[32,1536]{1,0:T(8,128)(2,1)S(1)} %collective-permute-done.6), channel_id=1, source_target_pairs={{0,32},{32,64},{64,96},{96,128},{128,160},{160,192},{192,224},{224... | collective-permute-start | bytes 294920 | tf_op jit(solution)/shard_map/ppermute | solution.py:65
  19.5 9.0 %collective-permute-start.12 = (bf16[32,1536]{1,0:T(8,128)(2,1)S(1)}, bf16[32,1536]{1,0:T(8,128)(2,1)S(1)}, u32[]{:S(2)}, u32[]{:S(2)}) collective-permute-start(bf16[32,1536]{1,0:T(8,128)(2,1)S(1)} %collective-permute-done.5), channel_id=1, source_target_pairs={{0,224},{32,0},{64,32},{96,64},{128,96},{160,128},{192,160},{224,1... | collective-permute-start | bytes 294920 | tf_op jit(solution)/shard_map/ppermute | solution.py:66
  23.5 5.0 %collective-permute-start.13 = (bf16[32,1536]{1,0:T(8,128)(2,1)S(1)}, bf16[32,1536]{1,0:T(8,128)(2,1)S(1)}, u32[]{:S(2)}, u32[]{:S(2)}) collective-permute-start(bf16[32,1536]{1,0:T(8,128)(2,1)S(1)} %collective-permute-done.7), channel_id=1, source_target_pairs={{0,32},{32,64},{64,96},{96,128},{128,160},{160,192},{192,224},{224... | collective-permute-start | bytes 294920 | tf_op jit(solution)/shard_map/ppermute | solution.py:65
  28.5 4.6 %collective-permute-start.14 = (bf16[32,768]{1,0:T(8,128)(2,1)S(1)}, bf16[32,768]{1,0:T(8,128)(2,1)S(1)}, u32[]{:S(2)}, u32[]{:S(2)}) collective-permute-start(bf16[32,768]{1,0:T(8,128)(2,1)S(1)} %slice.40), channel_id=1, source_target_pairs={{0,32},{32,64},{64,96},{96,128},{128,160},{160,192},{192,224},{224... | collective-permute-start | bytes 147464 | tf_op jit(solution)/shard_map/ppermute | solution.py:62
  28.5 7.3 %collective-permute-start.15 = (bf16[32,768]{1,0:T(8,128)(2,1)S(1)}, bf16[32,768]{1,0:T(8,128)(2,1)S(1)}, u32[]{:S(2)}, u32[]{:S(2)}) collective-permute-start(bf16[32,768]{1,0:T(8,128)(2,1)S(1)} %slice.41), channel_id=1, source_target_pairs={{0,224},{32,0},{64,32},{96,64},{128,96},{160,128},{192,160},{224,1... | collective-permute-start | bytes 147464 | tf_op jit(solution)/shard_map/ppermute | solution.py:63
  33.1 23.2 %collective-permute-start.8 = (bf16[5,32,1536]{2,1,0:T(8,128)(2,1)}, bf16[5,32,1536]{2,1,0:T(8,128)(2,1)}, u32[]{:S(2)}, u32[]{:S(2)}) collective-permute-start(bf16[5,32,1536]{2,1,0:T(8,128)(2,1)} %bitcast_dynamic-update-slice_fusion.12), channel_id=1, source_target_pairs={{0,24},{8,0},{16,8},{24,16},{1,25},{9,1},{17,9},{25,17},{2,26},{10... | collective-permute-start | bytes 1474568 | tf_op jit(solution)/shard_map/ppermute | solution.py:44
  35.8 19.4 %collective-permute-start.9 = (bf16[5,32,1536]{2,1,0:T(8,128)(2,1)}, bf16[5,32,1536]{2,1,0:T(8,128)(2,1)}, u32[]{:S(2)}, u32[]{:S(2)}) collective-permute-start(bf16[5,32,1536]{2,1,0:T(8,128)(2,1)} %bitcast_dynamic-update-slice_fusion.12), channel_id=1, source_target_pairs={{0,8},{8,16},{16,24},{24,0},{1,9},{9,17},{17,25},{25,1},{2,10},{10... | collective-permute-start | bytes 1474568 | tf_op jit(solution)/shard_map/ppermute | solution.py:43
  37.3 15.1 %collective-permute-start.16 = (bf16[3,32,1536]{2,1,0:T(8,128)(2,1)}, bf16[3,32,1536]{2,1,0:T(8,128)(2,1)S(1)}, u32[]{:S(2)}, u32[]{:S(2)}) collective-permute-start(bf16[3,32,1536]{2,1,0:T(8,128)(2,1)} %pad_maximum_fusion.2), channel_id=1, source_target_pairs={{0,24},{8,0},{16,8},{24,16},{1,25},{9,1},{17,9},{25,17},{2,26},{10... | collective-permute-start | bytes 884744 | tf_op jit(solution)/shard_map/ppermute | solution.py:44
  40.0 11.4 %collective-permute-start.17 = (bf16[3,32,1536]{2,1,0:T(8,128)(2,1)}, bf16[3,32,1536]{2,1,0:T(8,128)(2,1)}, u32[]{:S(2)}, u32[]{:S(2)}) collective-permute-start(bf16[3,32,1536]{2,1,0:T(8,128)(2,1)} %pad_maximum_fusion.2), channel_id=1, source_target_pairs={{0,8},{8,16},{16,24},{24,0},{1,9},{9,17},{17,25},{25,1},{2,10},{10... | collective-permute-start | bytes 884744 | tf_op jit(solution)/shard_map/ppermute | solution.py:43
  43.3 16.7 %copy-start.5 = (bf16[8,5,32,1536]{3,2,1,0:T(8,128)(2,1)S(1)}, bf16[8,5,32,1536]{3,2,1,0:T(8,128)(2,1)}, u32[]{:S(2)}) copy-start(bf16[8,5,32,1536]{3,2,1,0:T(8,128)(2,1)} %bitcast_dynamic-update-slice_fusion.4) | copy-start | bytes 11796484
  43.3 18.8 %copy-start.7 = (bf16[32,1536]{1,0:T(8,128)(2,1)S(1)}, bf16[32,1536]{1,0:T(8,128)(2,1)}, u32[]{:S(2)}) copy-start(bf16[32,1536]{1,0:T(8,128)(2,1)} %copy-done.6) | copy-start | bytes 294916
  43.3 18.8 %copy-start.9 = (bf16[32,1536]{1,0:T(8,128)(2,1)S(1)}, bf16[32,1536]{1,0:T(8,128)(2,1)}, u32[]{:S(2)}) copy-start(bf16[32,1536]{1,0:T(8,128)(2,1)} %copy-done.8) | copy-start | bytes 294916
  44.6 29.0 %collective-permute-start.3 = (bf16[4,128,1536]{2,1,0:T(8,128)(2,1)}, bf16[4,128,1536]{2,1,0:T(8,128)(2,1)}, u32[]{:S(2)}, u32[]{:S(2)}) collective-permute-start(bf16[4,128,1536]{2,1,0:T(8,128)(2,1)} %broadcast_select_fusion), channel_id=1, source_target_pairs={{0,1},{1,0},{2,3},{3,2},{4,5},{5,4},{6,7},{7,6},{8,9},{9,8},{10,11... | collective-permute-start | bytes 4718600 | tf_op jit(solution)/shard_map/ppermute | solution.py:102
  52.3 8.7 %collective-permute-start.18 = (bf16[3,32,768]{2,1,0:T(8,128)(2,1)S(1)}, bf16[3,32,768]{2,1,0:T(8,128)(2,1)S(1)}, u32[]{:S(2)}, u32[]{:S(2)}) collective-permute-start(bf16[3,32,768]{2,1,0:T(8,128)(2,1)S(1)} %slice.42), channel_id=1, source_target_pairs={{0,8},{8,16},{16,24},{24,0},{1,9},{9,17},{17,25},{25,1},{2,10},{10... | collective-permute-start | bytes 442376 | tf_op jit(solution)/shard_map/ppermute | solution.py:39
  52.5 8.6 %collective-permute-start.19 = (bf16[3,32,768]{2,1,0:T(8,128)(2,1)S(1)}, bf16[3,32,768]{2,1,0:T(8,128)(2,1)S(1)}, u32[]{:S(2)}, u32[]{:S(2)}) collective-permute-start(bf16[3,32,768]{2,1,0:T(8,128)(2,1)S(1)} %slice.43), channel_id=1, source_target_pairs={{0,24},{8,0},{16,8},{24,16},{1,25},{9,1},{17,9},{25,17},{2,26},{10... | collective-permute-start | bytes 442376 | tf_op jit(solution)/shard_map/ppermute | solution.py:40
  56.2 7.1 %collective-permute-start.10 = (bf16[5,32,768]{2,1,0:T(8,128)(2,1)S(1)}, bf16[5,32,768]{2,1,0:T(8,128)(2,1)S(1)}, u32[]{:S(2)}, u32[]{:S(2)}) collective-permute-start(bf16[5,32,768]{2,1,0:T(8,128)(2,1)S(1)} %slice.38), channel_id=1, source_target_pairs={{0,8},{8,16},{16,24},{24,0},{1,9},{9,17},{17,25},{25,1},{2,10},{10... | collective-permute-start | bytes 737288 | tf_op jit(solution)/shard_map/ppermute | solution.py:39
  57.3 6.2 %collective-permute-start.11 = (bf16[5,32,768]{2,1,0:T(8,128)(2,1)S(1)}, bf16[5,32,768]{2,1,0:T(8,128)(2,1)S(1)}, u32[]{:S(2)}, u32[]{:S(2)}) collective-permute-start(bf16[5,32,768]{2,1,0:T(8,128)(2,1)S(1)} %slice.39), channel_id=1, source_target_pairs={{0,24},{8,0},{16,8},{24,16},{1,25},{9,1},{17,9},{25,17},{2,26},{10... | collective-permute-start | bytes 737288 | tf_op jit(solution)/shard_map/ppermute | solution.py:40
  80.6 11.1 %collective-permute-start.20 = (bf16[4,4,32,1536]{3,2,1,0:T(8,128)(2,1)}, bf16[4,4,32,1536]{3,2,1,0:T(8,128)(2,1)}, u32[]{:S(2)}, u32[]{:S(2)}) collective-permute-start(bf16[4,4,32,1536]{3,2,1,0:T(8,128)(2,1)} %fusion.9), channel_id=1, source_target_pairs={{0,1},{1,0},{2,3},{3,2},{4,5},{5,4},{6,7},{7,6},{8,9},{9,8},{10,11... | collective-permute-start | bytes 4718600 | tf_op jit(solution)/shard_map/ppermute | solution.py:122
  98.1 12.4 %collective-permute-start.23 = (bf16[128,768]{1,0:T(8,128)(2,1)S(1)}, bf16[128,768]{1,0:T(8,128)(2,1)S(1)}, u32[]{:S(2)}, u32[]{:S(2)}) collective-permute-start(bf16[128,768]{1,0:T(8,128)(2,1)S(1)} %get-tuple-element.9), channel_id=1, source_target_pairs={{0,2},{1,3},{2,4},{3,5},{4,6},{5,7},{6,0},{7,1},{8,10},{9,11},{10,... | collective-permute-start | bytes 589832 | tf_op jit(solution)/shard_map/ppermute | solution.py:143
  98.3 12.1 %collective-permute-start.25 = (bf16[128,768]{1,0:T(8,128)(2,1)S(1)}, bf16[128,768]{1,0:T(8,128)(2,1)S(1)}, u32[]{:S(2)}, u32[]{:S(2)}) collective-permute-start(bf16[128,768]{1,0:T(8,128)(2,1)S(1)} %get-tuple-element.10), channel_id=1, source_target_pairs={{0,6},{1,7},{2,0},{3,1},{4,2},{5,3},{6,4},{7,5},{8,14},{9,15},{10,... | collective-permute-start | bytes 589832 | tf_op jit(solution)/shard_map/ppermute | solution.py:144
  100.9 16.9 %collective-permute-start.21 = (bf16[128,1536]{1,0:T(8,128)(2,1)S(1)}, bf16[128,1536]{1,0:T(8,128)(2,1)S(1)}, u32[]{:S(2)}, u32[]{:S(2)}) collective-permute-start(bf16[128,1536]{1,0:T(8,128)(2,1)S(1)} %bitcast.121), channel_id=1, source_target_pairs={{0,2},{1,3},{2,4},{3,5},{4,6},{5,7},{6,0},{7,1},{8,10},{9,11},{10,... | collective-permute-start | bytes 1179656 | tf_op jit(solution)/shard_map/ppermute | solution.py:143
  100.9 16.9 %collective-permute-start.22 = (bf16[128,1536]{1,0:T(8,128)(2,1)S(1)}, bf16[128,1536]{1,0:T(8,128)(2,1)S(1)}, u32[]{:S(2)}, u32[]{:S(2)}) collective-permute-start(bf16[128,1536]{1,0:T(8,128)(2,1)S(1)} %bitcast.120), channel_id=1, source_target_pairs={{0,6},{1,7},{2,0},{3,1},{4,2},{5,3},{6,4},{7,5},{8,14},{9,15},{10,... | collective-permute-start | bytes 1179656 | tf_op jit(solution)/shard_map/ppermute | solution.py:144
  103.5 14.2 %copy-start.4 = (bf16[128,1536]{1,0:T(8,128)(2,1)S(1)}, bf16[128,1536]{1,0:T(8,128)(2,1)}, u32[]{:S(2)}) copy-start(bf16[128,1536]{1,0:T(8,128)(2,1)} %param.4) | copy-start | bytes 1179652
  110.5 7.3 %collective-permute-start.24 = (bf16[128,768]{1,0:T(8,128)(2,1)S(1)}, bf16[128,768]{1,0:T(8,128)(2,1)S(1)}, u32[]{:S(2)}, u32[]{:S(2)}) collective-permute-start(bf16[128,768]{1,0:T(8,128)(2,1)S(1)} %collective-permute-done.23), channel_id=1, source_target_pairs={{0,2},{1,3},{2,4},{3,5},{4,6},{5,7},{6,0},{7,1},{8,10},{9,11},{10,... | collective-permute-start | bytes 589832 | tf_op jit(solution)/shard_map/ppermute | solution.py:145
  110.5 7.3 %collective-permute-start.26 = (bf16[128,768]{1,0:T(8,128)(2,1)S(1)}, bf16[128,768]{1,0:T(8,128)(2,1)S(1)}, u32[]{:S(2)}, u32[]{:S(2)}) collective-permute-start(bf16[128,768]{1,0:T(8,128)(2,1)S(1)} %collective-permute-done.25), channel_id=1, source_target_pairs={{0,6},{1,7},{2,0},{3,1},{4,2},{5,3},{6,4},{7,5},{8,14},{9,15},{10,... | collective-permute-start | bytes 589832 | tf_op jit(solution)/shard_map/ppermute | solution.py:146
  (8 other events, 52.9 us)

commit v12 on v9

--- a/solution.py
+++ b/solution.py
@@ -44,8 +44,13 @@
             bwd = lax.ppermute(bwd, axis, behind)
             by_off[-step % n] = fwd
             by_off[step] = bwd
-    stacked = jnp.stack([by_off[d] for d in range(n)], axis=0)
-    return jnp.roll(stacked, i, axis=0)
+    arrival = [0]
+    for step in range(1, n // 2 + 1):
+        arrival += [d for d in (-step % n, step) if d not in arrival]
+    out = jnp.zeros((n,) + block.shape, block.dtype)
+    for d in arrival:
+        out = lax.dynamic_update_slice_in_dim(out, by_off[d][None], (i + d) % n, axis=0)
+    return out
 
 
 def make_per_device(n_col, n_z, n_y):

time: 110 us -> 110 us (level)
  local copies, waits for them, and re-layouts: 14.6 us -> 16.6 us
  waiting for transfers between devices: 23.1 us -> 22 us
    ppermute x4, waiting for transfers between devices: 11 us -> 1 us  [ring_gather(): fwd = lax.ppermute(fwd, axis, ahead)]
    dynamic_update_slice x0 -> x10, local copies, waits for them, and re-layouts: none -> 9.1 us  [ring_gather(): lax.dynamic_update_slice_in_dim(out, by_off[d][None], (i + d) % n, axis=0)]
    unnamed x38 -> x14, local copies, waits for them, and re-layouts: 9.84 us -> 2.86 us
    ppermute x4, starting transfers between devices: 15.3 us -> 10.7 us  [ring_gather(): bwd = lax.ppermute(bwd, axis, behind)]
    ppermute x1, waiting for transfers between devices: 0.01 us -> 3.31 us  [per_device(): far_hi = lax.ppermute(dn_relay, COL, chip_shift(n_col, -1))]
    ppermute x2, waiting for transfers between devices: 0.01 us -> 3.23 us  [per_device(): lax.ppermute((dest(-1), far[:, cut:]), COL, chip_shift(n_col, -1))]
    ppermute x4, starting transfers between devices: 0.01 us -> 3.02 us  [ring_gather(): fwd = lax.ppermute(fwd, axis, ahead)]
    ppermute x2, waiting for transfers between devices: 0.02 us -> 2.12 us  [ring_gather(): from_ahead = lax.ppermute(bwd[..., half:], axis, behind)]
  transfers between devices with their start and end apart: 23 -> 23, of which waited for: 7 -> 10; matrix products, arithmetic and copies ran while one was open for 21% -> 23% of each run, Pallas kernels for 0% -> 0%
where the time goes in v12:
time: 110 us; the launch traced here: 109 us
  starting transfers between devices  47.3 us (43%)
  waiting for transfers between devices  22 us (20%)
  local copies, waits for them, and re-layouts  16.6 us (15%)
  matrix products  16.2 us (15%)
  other arithmetic  6.23 us (6%)
    ppermute x4, starting transfers between devices, ring_gather(): bwd = lax.ppermute(bwd, axis, behind)  10.7 us
    dynamic_update_slice x10, local copies, waits for them, and re-layouts, ring_gather(): lax.dynamic_update_slice_in_dim(out, by_off[d][None], (i + d) % n, axis=0)  9.1 us
    ppermute x1, starting transfers between devices, per_device(): lax.ppermute(p_theirs.astype(jnp.bfloat16), COL, core_swap(n_col))  8.61 us
    dot_general x1, matrix products, per_device(): lax.dot_general(hidden, grad_all, (((0,), (0,)), ((), ())), preferred_ele...  6.92 us
    ppermute x2, starting transfers between devices, ring_gather(): from_ahead = lax.ppermute(bwd[..., half:], axis, behind)  6.29 us
    ppermute x2, waiting for transfers between devices, ring_gather(): from_behind = lax.ppermute(fwd[..., :half], axis, ahead)  6.03 us
    ppermute x1, starting transfers between devices, per_device(): other_by_x = lax.ppermute(mine_by_x, COL, core_swap(n_col))  5.94 us
    dot_general x1, matrix products, per_device(): lax.dot_general(g_mine, weight, (((3,), (1,)), ((), ())), preferred_eleme...  5.49 us
  transfers between devices with their start and end apart: 23, of which 10 were waited for; matrix products, arithmetic and copies ran while one was open for 23% of the time, Pallas kernels for 0%

profile of v12, /device:TPU:1, one launch (start us, length us, event | category | flops | bytes accessed | tf_op | source)
XLA Modules:
  0.0 109.3 jit_solution(17109725602346870744)
XLA Ops:
  0.6 3.4 %collective-permute-start.2 = (bf16[128,1536]{1,0:T(8,128)(2,1)}, bf16[128,1536]{1,0:T(8,128)(2,1)S(1)}, u32[]{:S(2)}, u32[]{:S(2)}) collective-permute-start(bf16[128,1536]{1,0:T(8,128)(2,1)} %param.3), channel_id=1, source_target_pairs={{0,6},{1,7},{2,0},{3,1},{4,2},{5,3},{6,4},{7,5},{8,14},{9,15},{10,... | collective-permute-start | bytes 1179656 | tf_op jit(solution)/shard_map/ppermute | solution.py:71
  5.1 1.6 %collective-permute-start.4 = (bf16[32,1536]{1,0:T(8,128)(2,1)}, bf16[32,1536]{1,0:T(8,128)(2,1)S(1)}, u32[]{:S(2)}, u32[]{:S(2)}) collective-permute-start(bf16[32,1536]{1,0:T(8,128)(2,1)} %param.4), channel_id=1, source_target_pairs={{0,32},{32,64},{64,96},{96,128},{128,160},{160,192},{192,224},{224... | collective-permute-start | bytes 294920 | tf_op jit(solution)/shard_map/ppermute | solution.py:43
  6.8 3.9 %collective-permute-start.5 = (bf16[32,1536]{1,0:T(8,128)(2,1)}, bf16[32,1536]{1,0:T(8,128)(2,1)S(1)}, u32[]{:S(2)}, u32[]{:S(2)}) collective-permute-start(bf16[32,1536]{1,0:T(8,128)(2,1)} %param.4), channel_id=1, source_target_pairs={{0,224},{32,0},{64,32},{96,64},{128,96},{160,128},{192,160},{224,1... | collective-permute-start | bytes 294920 | tf_op jit(solution)/shard_map/ppermute | solution.py:44
  11.7 1.5 %bitcast_dynamic-update-slice_fusion.9 = bf16[8,32,1536]{2,1,0:T(8,128)(2,1)} fusion(bf16[8,32,1536]{2,1,0:T(8,128)(2,1)} %broadcast_in_dim.63, s32[]{:T(128)S(6)} %select_n.203, bf16[32,1536]{1,0:T(8,128)(2,1)} %param.4), kind=kLoop, calls=%fused_computation.61 | loop fusion | bytes 196612 | tf_op jit(solution)/shard_map/dynamic_update_slice | solution.py:52
  13.4 2.7 %collective-permute-start.7 = (bf16[32,1536]{1,0:T(8,128)(2,1)S(1)}, bf16[32,1536]{1,0:T(8,128)(2,1)S(1)}, u32[]{:S(2)}, u32[]{:S(2)}) collective-permute-start(bf16[32,1536]{1,0:T(8,128)(2,1)S(1)} %collective-permute-done.5), channel_id=1, source_target_pairs={{0,224},{32,0},{64,32},{96,64},{128,96},{160,128},{192,160},{224,1... | collective-permute-start | bytes 294920 | tf_op jit(solution)/shard_map/ppermute | solution.py:44
  18.3 2.7 %collective-permute-start.9 = (bf16[32,1536]{1,0:T(8,128)(2,1)S(1)}, bf16[32,1536]{1,0:T(8,128)(2,1)S(1)}, u32[]{:S(2)}, u32[]{:S(2)}) collective-permute-start(bf16[32,1536]{1,0:T(8,128)(2,1)S(1)} %collective-permute-done.7), channel_id=1, source_target_pairs={{0,224},{32,0},{64,32},{96,64},{128,96},{160,128},{192,160},{224,1... | collective-permute-start | bytes 294920 | tf_op jit(solution)/shard_map/ppermute | solution.py:44
  22.7 3.3 %collective-permute-start.11 = (bf16[32,768]{1,0:T(8,128)(2,1)S(1)}, bf16[32,768]{1,0:T(8,128)(2,1)S(1)}, u32[]{:S(2)}, u32[]{:S(2)}) collective-permute-start(bf16[32,768]{1,0:T(8,128)(2,1)S(1)} %slice.27), channel_id=1, source_target_pairs={{0,224},{32,0},{64,32},{96,64},{128,96},{160,128},{192,160},{224,1... | collective-permute-start | bytes 147464 | tf_op jit(solution)/shard_map/ppermute | solution.py:40
  27.4 2.9 %collective-permute-done.10 = bf16[32,768]{1,0:T(8,128)(2,1)S(1)} collective-permute-done((bf16[32,768]{1,0:T(8,128)(2,1)S(1)}, bf16[32,768]{1,0:T(8,128)(2,1)S(1)}, u32[]{:S(2)}, u32[]{:S(2)}) %collective-permute-start.10) | collective-permute-done | bytes 49184 | tf_op jit(solution)/shard_map/ppermute | solution.py:39
  31.5 1.3 %collective-permute-start.12 = (bf16[8,32,1536]{2,1,0:T(8,128)(2,1)}, bf16[8,32,1536]{2,1,0:T(8,128)(2,1)}, u32[]{:S(2)}, u32[]{:S(2)}) collective-permute-start(bf16[8,32,1536]{2,1,0:T(8,128)(2,1)} %fusion.33), channel_id=1, source_target_pairs={{0,8},{8,16},{16,24},{24,0},{1,9},{9,17},{17,25},{25,1},{2,10},{10... | collective-permute-start | bytes 2359304 | tf_op jit(solution)/shard_map/ppermute | solution.py:43
  32.8 1.4 %collective-permute-start.13 = (bf16[8,32,1536]{2,1,0:T(8,128)(2,1)}, bf16[8,32,1536]{2,1,0:T(8,128)(2,1)}, u32[]{:S(2)}, u32[]{:S(2)}) collective-permute-start(bf16[8,32,1536]{2,1,0:T(8,128)(2,1)} %fusion.33), channel_id=1, source_target_pairs={{0,24},{8,0},{16,8},{24,16},{1,25},{9,1},{17,9},{25,17},{2,26},{10... | collective-permute-start | bytes 2359304 | tf_op jit(solution)/shard_map/ppermute | solution.py:44
  34.6 1.2 %bitcast_dynamic-update-slice_fusion.2 = bf16[4,8,32,1536]{3,2,1,0:T(8,128)(2,1)S(1)} fusion(bf16[4,8,32,1536]{3,2,1,0:T(8,128)(2,1)S(1)} %broadcast_in_dim.62, s32[]{:T(128)S(6)} %select_n.219, bf16[8,32,1536]{2,1,0:T(8,128)(2,1)} %fusion.33), kind=kLoop, calls=%fused_computation.48 | loop fusion | bytes 1572868 | tf_op jit(solution)/shard_map/dynamic_update_slice | solution.py:52
  35.9 1.6 %copy-done = bf16[4,8,32,1536]{3,2,1,0:T(8,128)(2,1)} copy-done((bf16[4,8,32,1536]{3,2,1,0:T(8,128)(2,1)}, bf16[4,8,32,1536]{3,2,1,0:T(8,128)(2,1)S(1)}, u32[]{:S(2)}) %copy-start) | copy-done | bytes 3145752
  38.6 5.9 %collective-permute-start.3 = (bf16[4,128,1536]{2,1,0:T(8,128)(2,1)S(1)}, bf16[4,128,1536]{2,1,0:T(8,128)(2,1)S(1)}, u32[]{:S(2)}, u32[]{:S(2)}) collective-permute-start(bf16[4,128,1536]{2,1,0:T(8,128)(2,1)S(1)} %broadcast_select_fusion), channel_id=1, source_target_pairs={{0,1},{1,0},{2,3},{3,2},{4,5},{5,4},{6,7},{7,6},{8,9},{9,8},{10,11... | collective-permute-start | bytes 4718600 | tf_op jit(solution)/shard_map/ppermute | solution.py:75
  44.8 1.9 %collective-permute-done.13 = bf16[8,32,1536]{2,1,0:T(8,128)(2,1)} collective-permute-done((bf16[8,32,1536]{2,1,0:T(8,128)(2,1)}, bf16[8,32,1536]{2,1,0:T(8,128)(2,1)}, u32[]{:S(2)}, u32[]{:S(2)}) %collective-permute-start.13) | collective-permute-done | bytes 786464 | tf_op jit(solution)/shard_map/ppermute | solution.py:44
  47.6 3.0 %collective-permute-start.15 = (bf16[8,32,768]{2,1,0:T(8,128)(2,1)S(1)}, bf16[8,32,768]{2,1,0:T(8,128)(2,1)S(1)}, u32[]{:S(2)}, u32[]{:S(2)}) collective-permute-start(bf16[8,32,768]{2,1,0:T(8,128)(2,1)S(1)} %slice.29), channel_id=1, source_target_pairs={{0,24},{8,0},{16,8},{24,16},{1,25},{9,1},{17,9},{25,17},{2,26},{10... | collective-permute-start | bytes 1179656 | tf_op jit(solution)/shard_map/ppermute | solution.py:40
  50.6 1.2 %slice.28 = bf16[8,32,768]{2,1,0:T(8,128)(2,1)S(1)} slice(bf16[8,32,1536]{2,1,0:T(8,128)(2,1)} %collective-permute-done.12), slice={[0:8], [0:32], [0:768]} | slice | bytes 786432 | tf_op jit(solution)/shard_map/slice | solution.py:39
  51.9 1.3 %bitcast_dynamic-update-slice_fusion.1 = bf16[4,8,32,1536]{3,2,1,0:T(8,128)(2,1)S(1)} fusion(bf16[4,8,32,1536]{3,2,1,0:T(8,128)(2,1)S(1)} %copy-done.1, s32[]{:T(128)S(6)} %select_n.221, bf16[8,32,1536]{2,1,0:T(8,128)(2,1)} %collective-permute-done.12), kind=kLoop, calls=%fused_computation.47 | loop fusion | bytes 1572868 | tf_op jit(solution)/shard_map/dynamic_update_slice | solution.py:52
  53.2 1.2 %bitcast_dynamic-update-slice_fusion = bf16[4,8,32,1536]{3,2,1,0:T(8,128)(2,1)S(1)} fusion(bf16[4,8,32,1536]{3,2,1,0:T(8,128)(2,1)S(1)} %bitcast_dynamic-update-slice_fusion.1, s32[]{:T(128)S(6)} %select_n.223, bf16[8,32,1536]{2,1,0:T(8,128)(2,1)} %collective-permute-done.13), kind=kLoop, calls=%fused_computation.46 | loop fusion | bytes 1572868 | tf_op jit(solution)/shard_map/dynamic_update_slice | solution.py:52
  54.4 2.1 %collective-permute-done.15 = bf16[8,32,768]{2,1,0:T(8,128)(2,1)S(1)} collective-permute-done((bf16[8,32,768]{2,1,0:T(8,128)(2,1)S(1)}, bf16[8,32,768]{2,1,0:T(8,128)(2,1)S(1)}, u32[]{:S(2)}, u32[]{:S(2)}) %collective-permute-start.15) | collective-permute-done | bytes 393248 | tf_op jit(solution)/shard_map/ppermute | solution.py:40
  56.5 3.2 %collective-permute-done.14 = bf16[8,32,768]{2,1,0:T(8,128)(2,1)S(1)} collective-permute-done((bf16[8,32,768]{2,1,0:T(8,128)(2,1)S(1)}, bf16[8,32,768]{2,1,0:T(8,128)(2,1)S(1)}, u32[]{:S(2)}, u32[]{:S(2)}) %collective-permute-start.14) | collective-permute-done | bytes 393248 | tf_op jit(solution)/shard_map/ppermute | solution.py:39
  61.0 3.8 %fusion.9 = bf16[4,4,32,1536]{3,2,1,0:T(8,128)(2,1)} fusion(bf16[1536,1536]{1,0:T(8,128)(2,1)S(1)} %bitcast.97, bf16[4,4,2,32,1536]{4,3,2,1,0:T(8,128)(2,1)S(1)} %bitcast.85, s32[]{:T(128)S(6)} %select_n.227), kind=kOutput, calls=%fused_computation.18 | convolution fusion | flops 2416705536 | bytes 7864324 | tf_op jit(solution)/shard_map/dot_general | solution.py:93
  64.8 8.6 %collective-permute-start.16 = (bf16[4,4,32,1536]{3,2,1,0:T(8,128)(2,1)}, bf16[4,4,32,1536]{3,2,1,0:T(8,128)(2,1)}, u32[]{:S(2)}, u32[]{:S(2)}) collective-permute-start(bf16[4,4,32,1536]{3,2,1,0:T(8,128)(2,1)} %fusion.9), channel_id=1, source_target_pairs={{0,1},{1,0},{2,3},{3,2},{4,5},{5,4},{6,7},{7,6},{8,9},{9,8},{10,11... | collective-permute-start | bytes 4718600 | tf_op jit(solution)/shard_map/ppermute | solution.py:95
  73.4 2.2 %fusion.1 = bf16[1024,1536]{1,0:T(8,128)(2,1)S(1)} fusion(bf16[1024,1536]{1,0:T(8,128)(2,1)S(1)} %bitcast.82), kind=kLoop, calls=%fused_computation.8 | loop fusion | flops 15728640 | bytes 6291456 | tf_op jit(solution)/shard_map/convert_element_type | solution.py:82
  77.5 5.5 %convert_add_fusion.1 = f32[4,4,32,1536]{3,2,1,0:T(8,128)S(1)} fusion(bf16[4,4,32,1536]{3,2,1,0:T(8,128)(2,1)} %collective-permute-done.16, bf16[1536,1536]{1,0:T(8,128)(2,1)} %param.5, bf16[4,4,2,32,1536]{4,3,2,1,0:T(8,128)(2,1)S(1)} %bitcast.86, s32[]{:T(128)S(6)} %select_n.226), kind=kOutput, calls=%fused_computation.17 | convolution fusion | flops 2417491968 | bytes 11010052 | tf_op jit(solution)/shard_map/dot_general | solution.py:96
  83.1 2.1 %collective-permute-start.18 = (bf16[128,1536]{1,0:T(8,128)(2,1)S(1)}, bf16[128,1536]{1,0:T(8,128)(2,1)S(1)}, u32[]{:S(2)}, u32[]{:S(2)}) collective-permute-start(bf16[128,1536]{1,0:T(8,128)(2,1)S(1)} %bitcast.95), channel_id=1, source_target_pairs={{0,6},{1,7},{2,0},{3,1},{4,2},{5,3},{6,4},{7,5},{8,14},{9,15},{10,... | collective-permute-start | bytes 1179656 | tf_op jit(solution)/shard_map/ppermute | solution.py:117
  85.3 2.8 %collective-permute-start.21 = (bf16[128,768]{1,0:T(8,128)(2,1)S(1)}, bf16[128,768]{1,0:T(8,128)(2,1)S(1)}, u32[]{:S(2)}, u32[]{:S(2)}) collective-permute-start(bf16[128,768]{1,0:T(8,128)(2,1)S(1)} %get-tuple-element.10), channel_id=1, source_target_pairs={{0,6},{1,7},{2,0},{3,1},{4,2},{5,3},{6,4},{7,5},{8,14},{9,15},{10,... | collective-permute-start | bytes 589832 | tf_op jit(solution)/shard_map/ppermute | solution.py:117
  88.0 6.9 %convolution_convert_fusion = bf16[1536,1536]{1,0:T(8,128)(2,1)} fusion(bf16[1024,1536]{1,0:T(8,128)(2,1)S(1)} %bitcast.84, bf16[1024,1536]{1,0:T(8,128)(2,1)S(1)} %bitcast.87), kind=kOutput, calls=%fused_computation.6 | convolution fusion | flops 4834197504 | bytes 11010048 | tf_op jit(solution)/shard_map/dot_general | solution.py:84
  95.0 3.2 %collective-permute-done.21 = bf16[128,768]{1,0:T(8,128)(2,1)S(1)} collective-permute-done((bf16[128,768]{1,0:T(8,128)(2,1)S(1)}, bf16[128,768]{1,0:T(8,128)(2,1)S(1)}, u32[]{:S(2)}, u32[]{:S(2)}) %collective-permute-start.21) | collective-permute-done | bytes 196640 | tf_op jit(solution)/shard_map/ppermute | solution.py:117
  98.2 3.2 %collective-permute-start.22 = (bf16[128,768]{1,0:T(8,128)(2,1)S(1)}, bf16[128,768]{1,0:T(8,128)(2,1)S(1)}, u32[]{:S(2)}, u32[]{:S(2)}) collective-permute-start(bf16[128,768]{1,0:T(8,128)(2,1)S(1)} %collective-permute-done.21), channel_id=1, source_target_pairs={{0,6},{1,7},{2,0},{3,1},{4,2},{5,3},{6,4},{7,5},{8,14},{9,15},{10,... | collective-permute-start | bytes 589832 | tf_op jit(solution)/shard_map/ppermute | solution.py:119
  101.4 3.3 %collective-permute-done.22 = bf16[128,768]{1,0:T(8,128)(2,1)S(1)} collective-permute-done((bf16[128,768]{1,0:T(8,128)(2,1)S(1)}, bf16[128,768]{1,0:T(8,128)(2,1)S(1)}, u32[]{:S(2)}, u32[]{:S(2)}) %collective-permute-start.22) | collective-permute-done | bytes 196640 | tf_op jit(solution)/shard_map/ppermute | solution.py:119
  104.7 3.1 %collective-permute-done.20 = bf16[128,768]{1,0:T(8,128)(2,1)S(1)} collective-permute-done((bf16[128,768]{1,0:T(8,128)(2,1)S(1)}, bf16[128,768]{1,0:T(8,128)(2,1)S(1)}, u32[]{:S(2)}, u32[]{:S(2)}) %collective-permute-start.20) | collective-permute-done | bytes 196640 | tf_op jit(solution)/shard_map/ppermute | solution.py:118
  107.9 1.4 %fusion.27 = bf16[128,1536]{1,0:T(8,128)(2,1)} fusion(bf16[128,1536]{1,0:T(8,128)(2,1)S(1)} %copy-done.4, f32[4,1,32,1536]{3,2,1,0:T(8,128)S(1)} %constant_dynamic-slice_fusion, bf16[128,1536]{1,0:T(8,128)(2,1)S(1)} %collective-permute-done.18, bf16[128,1536]{1,0:T(8,128)(2,1)S(1)} %collective-permute-done.17, ...), kind=kLoop, calls=%fused_computation.40 | loop fusion | flops 5701632 | bytes 2752512 | tf_op jit(solution)/shard_map/convert_element_type | solution.py:129
  (66 shorter events, 14.9 us)
Async XLA Ops:
  0.6 35.2 %collective-permute-start.2 = (bf16[128,1536]{1,0:T(8,128)(2,1)}, bf16[128,1536]{1,0:T(8,128)(2,1)S(1)}, u32[]{:S(2)}, u32[]{:S(2)}) collective-permute-start(bf16[128,1536]{1,0:T(8,128)(2,1)} %param.3), channel_id=1, source_target_pairs={{0,6},{1,7},{2,0},{3,1},{4,2},{5,3},{6,4},{7,5},{8,14},{9,15},{10,... | collective-permute-start | bytes 1179656 | tf_op jit(solution)/shard_map/ppermute | solution.py:71
  4.0 31.9 %collective-permute-start.1 = (bf16[128,1536]{1,0:T(8,128)(2,1)}, bf16[128,1536]{1,0:T(8,128)(2,1)S(1)}, u32[]{:S(2)}, u32[]{:S(2)}) collective-permute-start(bf16[128,1536]{1,0:T(8,128)(2,1)} %param.3), channel_id=1, source_target_pairs={{0,4},{1,5},{2,6},{3,7},{4,0},{5,1},{6,2},{7,3},{8,12},{9,13},{10,... | collective-permute-start | bytes 1179656 | tf_op jit(solution)/shard_map/ppermute | solution.py:71
  4.5 31.3 %collective-permute-start = (bf16[128,1536]{1,0:T(8,128)(2,1)}, bf16[128,1536]{1,0:T(8,128)(2,1)S(1)}, u32[]{:S(2)}, u32[]{:S(2)}) collective-permute-start(bf16[128,1536]{1,0:T(8,128)(2,1)} %param.3), channel_id=1, source_target_pairs={{0,2},{1,3},{2,4},{3,5},{4,6},{5,7},{6,0},{7,1},{8,10},{9,11},{10,... | collective-permute-start | bytes 1179656 | tf_op jit(solution)/shard_map/ppermute | solution.py:71
  5.1 8.2 %collective-permute-start.4 = (bf16[32,1536]{1,0:T(8,128)(2,1)}, bf16[32,1536]{1,0:T(8,128)(2,1)S(1)}, u32[]{:S(2)}, u32[]{:S(2)}) collective-permute-start(bf16[32,1536]{1,0:T(8,128)(2,1)} %param.4), channel_id=1, source_target_pairs={{0,32},{32,64},{64,96},{96,128},{128,160},{160,192},{192,224},{224... | collective-permute-start | bytes 294920 | tf_op jit(solution)/shard_map/ppermute | solution.py:43
  6.8 6.6 %collective-permute-start.5 = (bf16[32,1536]{1,0:T(8,128)(2,1)}, bf16[32,1536]{1,0:T(8,128)(2,1)S(1)}, u32[]{:S(2)}, u32[]{:S(2)}) collective-permute-start(bf16[32,1536]{1,0:T(8,128)(2,1)} %param.4), channel_id=1, source_target_pairs={{0,224},{32,0},{64,32},{96,64},{128,96},{160,128},{192,160},{224,1... | collective-permute-start | bytes 294920 | tf_op jit(solution)/shard_map/ppermute | solution.py:44
  13.3 5.1 %collective-permute-start.6 = (bf16[32,1536]{1,0:T(8,128)(2,1)S(1)}, bf16[32,1536]{1,0:T(8,128)(2,1)S(1)}, u32[]{:S(2)}, u32[]{:S(2)}) collective-permute-start(bf16[32,1536]{1,0:T(8,128)(2,1)S(1)} %collective-permute-done.4), channel_id=1, source_target_pairs={{0,32},{32,64},{64,96},{96,128},{128,160},{160,192},{192,224},{224... | collective-permute-start | bytes 294920 | tf_op jit(solution)/shard_map/ppermute | solution.py:43
  13.4 5.0 %collective-permute-start.7 = (bf16[32,1536]{1,0:T(8,128)(2,1)S(1)}, bf16[32,1536]{1,0:T(8,128)(2,1)S(1)}, u32[]{:S(2)}, u32[]{:S(2)}) collective-permute-start(bf16[32,1536]{1,0:T(8,128)(2,1)S(1)} %collective-permute-done.5), channel_id=1, source_target_pairs={{0,224},{32,0},{64,32},{96,64},{128,96},{160,128},{192,160},{224,1... | collective-permute-start | bytes 294920 | tf_op jit(solution)/shard_map/ppermute | solution.py:44
  16.7 20.8 %copy-start.4 = (bf16[128,1536]{1,0:T(8,128)(2,1)S(1)}, bf16[128,1536]{1,0:T(8,128)(2,1)}, u32[]{:S(2)}) copy-start(bf16[128,1536]{1,0:T(8,128)(2,1)} %param.3) | copy-start | bytes 1179652
  18.3 7.7 %collective-permute-start.8 = (bf16[32,1536]{1,0:T(8,128)(2,1)S(1)}, bf16[32,1536]{1,0:T(8,128)(2,1)S(1)}, u32[]{:S(2)}, u32[]{:S(2)}) collective-permute-start(bf16[32,1536]{1,0:T(8,128)(2,1)S(1)} %collective-permute-done.6), channel_id=1, source_target_pairs={{0,32},{32,64},{64,96},{96,128},{128,160},{160,192},{192,224},{224... | collective-permute-start | bytes 294920 | tf_op jit(solution)/shard_map/ppermute | solution.py:43
  18.3 4.3 %collective-permute-start.9 = (bf16[32,1536]{1,0:T(8,128)(2,1)S(1)}, bf16[32,1536]{1,0:T(8,128)(2,1)S(1)}, u32[]{:S(2)}, u32[]{:S(2)}) collective-permute-start(bf16[32,1536]{1,0:T(8,128)(2,1)S(1)} %collective-permute-done.7), channel_id=1, source_target_pairs={{0,224},{32,0},{64,32},{96,64},{128,96},{160,128},{192,160},{224,1... | collective-permute-start | bytes 294920 | tf_op jit(solution)/shard_map/ppermute | solution.py:44
  22.7 4.7 %collective-permute-start.11 = (bf16[32,768]{1,0:T(8,128)(2,1)S(1)}, bf16[32,768]{1,0:T(8,128)(2,1)S(1)}, u32[]{:S(2)}, u32[]{:S(2)}) collective-permute-start(bf16[32,768]{1,0:T(8,128)(2,1)S(1)} %slice.27), channel_id=1, source_target_pairs={{0,224},{32,0},{64,32},{96,64},{128,96},{160,128},{192,160},{224,1... | collective-permute-start | bytes 147464 | tf_op jit(solution)/shard_map/ppermute | solution.py:40
  26.0 4.2 %collective-permute-start.10 = (bf16[32,768]{1,0:T(8,128)(2,1)S(1)}, bf16[32,768]{1,0:T(8,128)(2,1)S(1)}, u32[]{:S(2)}, u32[]{:S(2)}) collective-permute-start(bf16[32,768]{1,0:T(8,128)(2,1)S(1)} %slice.26), channel_id=1, source_target_pairs={{0,32},{32,64},{64,96},{96,128},{128,160},{160,192},{192,224},{224... | collective-permute-start | bytes 147464 | tf_op jit(solution)/shard_map/ppermute | solution.py:39
  31.5 19.1 %collective-permute-start.12 = (bf16[8,32,1536]{2,1,0:T(8,128)(2,1)}, bf16[8,32,1536]{2,1,0:T(8,128)(2,1)}, u32[]{:S(2)}, u32[]{:S(2)}) collective-permute-start(bf16[8,32,1536]{2,1,0:T(8,128)(2,1)} %fusion.33), channel_id=1, source_target_pairs={{0,8},{8,16},{16,24},{24,0},{1,9},{9,17},{17,25},{25,1},{2,10},{10... | collective-permute-start | bytes 2359304 | tf_op jit(solution)/shard_map/ppermute | solution.py:43
  32.8 13.8 %collective-permute-start.13 = (bf16[8,32,1536]{2,1,0:T(8,128)(2,1)}, bf16[8,32,1536]{2,1,0:T(8,128)(2,1)}, u32[]{:S(2)}, u32[]{:S(2)}) collective-permute-start(bf16[8,32,1536]{2,1,0:T(8,128)(2,1)} %fusion.33), channel_id=1, source_target_pairs={{0,24},{8,0},{16,8},{24,16},{1,25},{9,1},{17,9},{25,17},{2,26},{10... | collective-permute-start | bytes 2359304 | tf_op jit(solution)/shard_map/ppermute | solution.py:44
  35.8 1.7 %copy-start = (bf16[4,8,32,1536]{3,2,1,0:T(8,128)(2,1)}, bf16[4,8,32,1536]{3,2,1,0:T(8,128)(2,1)S(1)}, u32[]{:S(2)}) copy-start(bf16[4,8,32,1536]{3,2,1,0:T(8,128)(2,1)S(1)} %bitcast_dynamic-update-slice_fusion.2) | copy-start | bytes 9437188
  38.6 13.3 %copy-start.1 = (bf16[4,8,32,1536]{3,2,1,0:T(8,128)(2,1)S(1)}, bf16[4,8,32,1536]{3,2,1,0:T(8,128)(2,1)}, u32[]{:S(2)}) copy-start(bf16[4,8,32,1536]{3,2,1,0:T(8,128)(2,1)} %copy-done) | copy-start | bytes 9437188
  38.6 21.3 %collective-permute-start.3 = (bf16[4,128,1536]{2,1,0:T(8,128)(2,1)S(1)}, bf16[4,128,1536]{2,1,0:T(8,128)(2,1)S(1)}, u32[]{:S(2)}, u32[]{:S(2)}) collective-permute-start(bf16[4,128,1536]{2,1,0:T(8,128)(2,1)S(1)} %broadcast_select_fusion), channel_id=1, source_target_pairs={{0,1},{1,0},{2,3},{3,2},{4,5},{5,4},{6,7},{7,6},{8,9},{9,8},{10,11... | collective-permute-start | bytes 4718600 | tf_op jit(solution)/shard_map/ppermute | solution.py:75
  47.6 8.9 %collective-permute-start.15 = (bf16[8,32,768]{2,1,0:T(8,128)(2,1)S(1)}, bf16[8,32,768]{2,1,0:T(8,128)(2,1)S(1)}, u32[]{:S(2)}, u32[]{:S(2)}) collective-permute-start(bf16[8,32,768]{2,1,0:T(8,128)(2,1)S(1)} %slice.29), channel_id=1, source_target_pairs={{0,24},{8,0},{16,8},{24,16},{1,25},{9,1},{17,9},{25,17},{2,26},{10... | collective-permute-start | bytes 1179656 | tf_op jit(solution)/shard_map/ppermute | solution.py:40
  50.6 9.8 %slice-start = ((s8[4718592]{0:T(1024)(128)(4,1)}), s8[4194304]{0:T(1024)(128)(4,1)S(1)}, s32[]{:S(2)}) async-start(s8[4718592]{0:T(1024)(128)(4,1)} %bitcast.96), calls=%async_computation | async-start | bytes 8388608
  51.8 7.9 %collective-permute-start.14 = (bf16[8,32,768]{2,1,0:T(8,128)(2,1)S(1)}, bf16[8,32,768]{2,1,0:T(8,128)(2,1)S(1)}, u32[]{:S(2)}, u32[]{:S(2)}) collective-permute-start(bf16[8,32,768]{2,1,0:T(8,128)(2,1)S(1)} %slice.28), channel_id=1, source_target_pairs={{0,8},{8,16},{16,24},{24,0},{1,9},{9,17},{17,25},{25,1},{2,10},{10... | collective-permute-start | bytes 1179656 | tf_op jit(solution)/shard_map/ppermute | solution.py:39
  59.8 1.2 %slice-start.1 = ((s8[4718592]{0:T(1024)(128)(4,1)}), s8[524288]{0:T(1024)(128)(4,1)S(1)}, s32[]{:S(2)}) async-start(s8[4718592]{0:T(1024)(128)(4,1)} %bitcast.96), calls=%async_computation.1 | async-start | bytes 1048576
  59.9 4.9 %copy-start.2 = (bf16[4,8,32,1536]{3,2,1,0:T(8,128)(2,1)}, bf16[4,8,32,1536]{3,2,1,0:T(8,128)(2,1)S(1)}, u32[]{:S(2)}) copy-start(bf16[4,8,32,1536]{3,2,1,0:T(8,128)(2,1)S(1)} %fusion.31) | copy-start | bytes 9437188
  64.8 12.0 %collective-permute-start.16 = (bf16[4,4,32,1536]{3,2,1,0:T(8,128)(2,1)}, bf16[4,4,32,1536]{3,2,1,0:T(8,128)(2,1)}, u32[]{:S(2)}, u32[]{:S(2)}) collective-permute-start(bf16[4,4,32,1536]{3,2,1,0:T(8,128)(2,1)} %fusion.9), channel_id=1, source_target_pairs={{0,1},{1,0},{2,3},{3,2},{4,5},{5,4},{6,7},{7,6},{8,9},{9,8},{10,11... | collective-permute-start | bytes 4718600 | tf_op jit(solution)/shard_map/ppermute | solution.py:95
  75.6 1.9 %copy-start.3 = (bf16[4,8,32,1536]{3,2,1,0:T(8,128)(2,1)S(1)}, bf16[4,8,32,1536]{3,2,1,0:T(8,128)(2,1)}, u32[]{:S(2)}) copy-start(bf16[4,8,32,1536]{3,2,1,0:T(8,128)(2,1)} %copy-done.2) | copy-start | bytes 9437188
  83.1 18.3 %collective-permute-start.18 = (bf16[128,1536]{1,0:T(8,128)(2,1)S(1)}, bf16[128,1536]{1,0:T(8,128)(2,1)S(1)}, u32[]{:S(2)}, u32[]{:S(2)}) collective-permute-start(bf16[128,1536]{1,0:T(8,128)(2,1)S(1)} %bitcast.95), channel_id=1, source_target_pairs={{0,6},{1,7},{2,0},{3,1},{4,2},{5,3},{6,4},{7,5},{8,14},{9,15},{10,... | collective-permute-start | bytes 1179656 | tf_op jit(solution)/shard_map/ppermute | solution.py:117
  85.2 16.2 %collective-permute-start.17 = (bf16[128,1536]{1,0:T(8,128)(2,1)S(1)}, bf16[128,1536]{1,0:T(8,128)(2,1)S(1)}, u32[]{:S(2)}, u32[]{:S(2)}) collective-permute-start(bf16[128,1536]{1,0:T(8,128)(2,1)S(1)} %bitcast.94), channel_id=1, source_target_pairs={{0,2},{1,3},{2,4},{3,5},{4,6},{5,7},{6,0},{7,1},{8,10},{9,11},{10,... | collective-permute-start | bytes 1179656 | tf_op jit(solution)/shard_map/ppermute | solution.py:116
  85.3 12.9 %collective-permute-start.21 = (bf16[128,768]{1,0:T(8,128)(2,1)S(1)}, bf16[128,768]{1,0:T(8,128)(2,1)S(1)}, u32[]{:S(2)}, u32[]{:S(2)}) collective-permute-start(bf16[128,768]{1,0:T(8,128)(2,1)S(1)} %get-tuple-element.10), channel_id=1, source_target_pairs={{0,6},{1,7},{2,0},{3,1},{4,2},{5,3},{6,4},{7,5},{8,14},{9,15},{10,... | collective-permute-start | bytes 589832 | tf_op jit(solution)/shard_map/ppermute | solution.py:117
  88.0 13.3 %collective-permute-start.19 = (bf16[128,768]{1,0:T(8,128)(2,1)S(1)}, bf16[128,768]{1,0:T(8,128)(2,1)S(1)}, u32[]{:S(2)}, u32[]{:S(2)}) collective-permute-start(bf16[128,768]{1,0:T(8,128)(2,1)S(1)} %get-tuple-element.9), channel_id=1, source_target_pairs={{0,2},{1,3},{2,4},{3,5},{4,6},{5,7},{6,0},{7,1},{8,10},{9,11},{10,... | collective-permute-start | bytes 589832 | tf_op jit(solution)/shard_map/ppermute | solution.py:116
  98.2 6.5 %collective-permute-start.22 = (bf16[128,768]{1,0:T(8,128)(2,1)S(1)}, bf16[128,768]{1,0:T(8,128)(2,1)S(1)}, u32[]{:S(2)}, u32[]{:S(2)}) collective-permute-start(bf16[128,768]{1,0:T(8,128)(2,1)S(1)} %collective-permute-done.21), channel_id=1, source_target_pairs={{0,6},{1,7},{2,0},{3,1},{4,2},{5,3},{6,4},{7,5},{8,14},{9,15},{10,... | collective-permute-start | bytes 589832 | tf_op jit(solution)/shard_map/ppermute | solution.py:119
  101.3 6.5 %collective-permute-start.20 = (bf16[128,768]{1,0:T(8,128)(2,1)S(1)}, bf16[128,768]{1,0:T(8,128)(2,1)S(1)}, u32[]{:S(2)}, u32[]{:S(2)}) collective-permute-start(bf16[128,768]{1,0:T(8,128)(2,1)S(1)} %collective-permute-done.19), channel_id=1, source_target_pairs={{0,2},{1,3},{2,4},{3,5},{4,6},{5,7},{6,0},{7,1},{8,10},{9,11},{10,... | collective-permute-start | bytes 589832 | tf_op jit(solution)/shard_map/ppermute | solution.py:118

commit v13 on v12

--- a/solution.py
+++ b/solution.py
@@ -110,20 +110,9 @@
             pick = lambda c: lax.dynamic_index_in_dim(chip_sum, c, axis=0, keepdims=False)
         back = pick(x)
         dest = lambda s: pick((x + s) % n_x).astype(jnp.bfloat16)
-        if n_x == 4:
-            cut = back.shape[-1] // 2
-            far = dest(2)
-            up, up_relay = lax.ppermute((dest(1), far[:, :cut]), COL, chip_shift(n_col, 1))
-            dn, dn_relay = lax.ppermute((dest(-1), far[:, cut:]), COL, chip_shift(n_col, -1))
-            far_lo = lax.ppermute(up_relay, COL, chip_shift(n_col, 1))
-            far_hi = lax.ppermute(dn_relay, COL, chip_shift(n_col, -1))
-            far_got = jnp.concatenate([far_lo, far_hi], axis=-1)
-            for recv in (up, dn, far_got):
-                back = back + recv.astype(jnp.float32)
-        else:
-            for s in range(1, n_x):
-                recv = lax.ppermute(dest(s), COL, chip_shift(n_col, s))
-                back = back + recv.astype(jnp.float32)
+        for s in range(1, n_x):
+            recv = lax.ppermute(dest(s), COL, chip_shift(n_col, s))
+            back = back + recv.astype(jnp.float32)
 
         unused_value, own_slope = gelu_parts(saved_input.astype(jnp.float32))
         in_grad = (back * own_slope).astype(jnp.bfloat16)

time: 110 us -> 108 us (0.982)
  starting transfers between devices: 47.3 us -> 42.7 us
  waiting for transfers between devices: 22 us -> 25.1 us
    ppermute x6 -> x3, starting transfers between devices: 8.04 us -> 3.38 us  [per_device(): recv = lax.ppermute(dest(s), COL, chip_shift(n_col, s))]
    ppermute x6 -> x3, waiting for transfers between devices: 9.68 us -> 12.8 us  [per_device(): recv = lax.ppermute(dest(s), COL, chip_shift(n_col, s))]
  transfers between devices with their start and end apart: 23 -> 20, of which waited for: 10 -> 10; matrix products, arithmetic and copies ran while one was open for 23% -> 23% of each run, Pallas kernels for 0% -> 0%
where the time goes in v13:
time: 108 us
  starting transfers between devices  42.7 us (40%)
  waiting for transfers between devices  25.1 us (23%)
  local copies, waits for them, and re-layouts  16.5 us (15%)
  matrix products  16.2 us (15%)
  other arithmetic  6.19 us (6%)
    ppermute x3, waiting for transfers between devices, per_device(): recv = lax.ppermute(dest(s), COL, chip_shift(n_col, s))  12.8 us
    ppermute x4, starting transfers between devices, ring_gather(): bwd = lax.ppermute(bwd, axis, behind)  10.7 us
    dynamic_update_slice x10, local copies, waits for them, and re-layouts, ring_gather(): lax.dynamic_update_slice_in_dim(out, by_off[d][None], (i + d) % n, axis=0)  9.08 us
    ppermute x1, starting transfers between devices, per_device(): lax.ppermute(p_theirs.astype(jnp.bfloat16), COL, core_swap(n_col))  8.62 us
    dot_general x1, matrix products, per_device(): lax.dot_general(hidden, grad_all, (((0,), (0,)), ((), ())), preferred_ele...  6.92 us
    ppermute x2, starting transfers between devices, ring_gather(): from_ahead = lax.ppermute(bwd[..., half:], axis, behind)  6.3 us
    ppermute x2, waiting for transfers between devices, ring_gather(): from_behind = lax.ppermute(fwd[..., :half], axis, ahead)  6.01 us
    ppermute x1, starting transfers between devices, per_device(): other_by_x = lax.ppermute(mine_by_x, COL, core_swap(n_col))  5.96 us
  transfers between devices with their start and end apart: 20, of which 10 were waited for; matrix products, arithmetic and copies ran while one was open for 23% of the time, Pallas kernels for 0%

profile of v13, /device:TPU:1, one launch (start us, length us, event | category | flops | bytes accessed | tf_op | source)
XLA Modules:
  0.0 107.5 jit_solution(11490733571239120285)
XLA Ops:
  0.6 3.4 %collective-permute-start.2 = (bf16[128,1536]{1,0:T(8,128)(2,1)}, bf16[128,1536]{1,0:T(8,128)(2,1)S(1)}, u32[]{:S(2)}, u32[]{:S(2)}) collective-permute-start(bf16[128,1536]{1,0:T(8,128)(2,1)} %param.3), channel_id=1, source_target_pairs={{0,6},{1,7},{2,0},{3,1},{4,2},{5,3},{6,4},{7,5},{8,14},{9,15},{10,... | collective-permute-start | bytes 1179656 | tf_op jit(solution)/shard_map/ppermute | solution.py:71
  5.1 1.6 %collective-permute-start.4 = (bf16[32,1536]{1,0:T(8,128)(2,1)}, bf16[32,1536]{1,0:T(8,128)(2,1)S(1)}, u32[]{:S(2)}, u32[]{:S(2)}) collective-permute-start(bf16[32,1536]{1,0:T(8,128)(2,1)} %param.4), channel_id=1, source_target_pairs={{0,32},{32,64},{64,96},{96,128},{128,160},{160,192},{192,224},{224... | collective-permute-start | bytes 294920 | tf_op jit(solution)/shard_map/ppermute | solution.py:43
  6.8 3.9 %collective-permute-start.5 = (bf16[32,1536]{1,0:T(8,128)(2,1)}, bf16[32,1536]{1,0:T(8,128)(2,1)S(1)}, u32[]{:S(2)}, u32[]{:S(2)}) collective-permute-start(bf16[32,1536]{1,0:T(8,128)(2,1)} %param.4), channel_id=1, source_target_pairs={{0,224},{32,0},{64,32},{96,64},{128,96},{160,128},{192,160},{224,1... | collective-permute-start | bytes 294920 | tf_op jit(solution)/shard_map/ppermute | solution.py:44
  11.7 1.5 %bitcast_dynamic-update-slice_fusion.9 = bf16[8,32,1536]{2,1,0:T(8,128)(2,1)} fusion(bf16[8,32,1536]{2,1,0:T(8,128)(2,1)} %broadcast_in_dim.63, s32[]{:T(128)S(6)} %select_n.203, bf16[32,1536]{1,0:T(8,128)(2,1)} %param.4), kind=kLoop, calls=%fused_computation.61 | loop fusion | bytes 196612 | tf_op jit(solution)/shard_map/dynamic_update_slice | solution.py:52
  13.4 2.7 %collective-permute-start.7 = (bf16[32,1536]{1,0:T(8,128)(2,1)S(1)}, bf16[32,1536]{1,0:T(8,128)(2,1)S(1)}, u32[]{:S(2)}, u32[]{:S(2)}) collective-permute-start(bf16[32,1536]{1,0:T(8,128)(2,1)S(1)} %collective-permute-done.5), channel_id=1, source_target_pairs={{0,224},{32,0},{64,32},{96,64},{128,96},{160,128},{192,160},{224,1... | collective-permute-start | bytes 294920 | tf_op jit(solution)/shard_map/ppermute | solution.py:44
  17.3 1.0 collective-permute-done.6
  18.3 2.7 %collective-permute-start.9 = (bf16[32,1536]{1,0:T(8,128)(2,1)S(1)}, bf16[32,1536]{1,0:T(8,128)(2,1)S(1)}, u32[]{:S(2)}, u32[]{:S(2)}) collective-permute-start(bf16[32,1536]{1,0:T(8,128)(2,1)S(1)} %collective-permute-done.7), channel_id=1, source_target_pairs={{0,224},{32,0},{64,32},{96,64},{128,96},{160,128},{192,160},{224,1... | collective-permute-start | bytes 294920 | tf_op jit(solution)/shard_map/ppermute | solution.py:44
  22.7 3.3 %collective-permute-start.11 = (bf16[32,768]{1,0:T(8,128)(2,1)S(1)}, bf16[32,768]{1,0:T(8,128)(2,1)S(1)}, u32[]{:S(2)}, u32[]{:S(2)}) collective-permute-start(bf16[32,768]{1,0:T(8,128)(2,1)S(1)} %slice.19), channel_id=1, source_target_pairs={{0,224},{32,0},{64,32},{96,64},{128,96},{160,128},{192,160},{224,1... | collective-permute-start | bytes 147464 | tf_op jit(solution)/shard_map/ppermute | solution.py:40
  27.4 2.8 %collective-permute-done.10 = bf16[32,768]{1,0:T(8,128)(2,1)S(1)} collective-permute-done((bf16[32,768]{1,0:T(8,128)(2,1)S(1)}, bf16[32,768]{1,0:T(8,128)(2,1)S(1)}, u32[]{:S(2)}, u32[]{:S(2)}) %collective-permute-start.10) | collective-permute-done | bytes 49184 | tf_op jit(solution)/shard_map/ppermute | solution.py:39
  31.5 1.3 %collective-permute-start.12 = (bf16[8,32,1536]{2,1,0:T(8,128)(2,1)}, bf16[8,32,1536]{2,1,0:T(8,128)(2,1)}, u32[]{:S(2)}, u32[]{:S(2)}) collective-permute-start(bf16[8,32,1536]{2,1,0:T(8,128)(2,1)} %fusion.33), channel_id=1, source_target_pairs={{0,8},{8,16},{16,24},{24,0},{1,9},{9,17},{17,25},{25,1},{2,10},{10... | collective-permute-start | bytes 2359304 | tf_op jit(solution)/shard_map/ppermute | solution.py:43
  32.8 1.4 %collective-permute-start.13 = (bf16[8,32,1536]{2,1,0:T(8,128)(2,1)}, bf16[8,32,1536]{2,1,0:T(8,128)(2,1)}, u32[]{:S(2)}, u32[]{:S(2)}) collective-permute-start(bf16[8,32,1536]{2,1,0:T(8,128)(2,1)} %fusion.33), channel_id=1, source_target_pairs={{0,24},{8,0},{16,8},{24,16},{1,25},{9,1},{17,9},{25,17},{2,26},{10... | collective-permute-start | bytes 2359304 | tf_op jit(solution)/shard_map/ppermute | solution.py:44
  34.6 1.2 %bitcast_dynamic-update-slice_fusion.2 = bf16[4,8,32,1536]{3,2,1,0:T(8,128)(2,1)S(1)} fusion(bf16[4,8,32,1536]{3,2,1,0:T(8,128)(2,1)S(1)} %broadcast_in_dim.62, s32[]{:T(128)S(6)} %select_n.219, bf16[8,32,1536]{2,1,0:T(8,128)(2,1)} %fusion.33), kind=kLoop, calls=%fused_computation.48 | loop fusion | bytes 1572868 | tf_op jit(solution)/shard_map/dynamic_update_slice | solution.py:52
  35.8 1.6 %copy-done = bf16[4,8,32,1536]{3,2,1,0:T(8,128)(2,1)} copy-done((bf16[4,8,32,1536]{3,2,1,0:T(8,128)(2,1)}, bf16[4,8,32,1536]{3,2,1,0:T(8,128)(2,1)S(1)}, u32[]{:S(2)}) %copy-start) | copy-done | bytes 3145752
  38.5 6.0 %collective-permute-start.3 = (bf16[4,128,1536]{2,1,0:T(8,128)(2,1)S(1)}, bf16[4,128,1536]{2,1,0:T(8,128)(2,1)S(1)}, u32[]{:S(2)}, u32[]{:S(2)}) collective-permute-start(bf16[4,128,1536]{2,1,0:T(8,128)(2,1)S(1)} %broadcast_select_fusion), channel_id=1, source_target_pairs={{0,1},{1,0},{2,3},{3,2},{4,5},{5,4},{6,7},{7,6},{8,9},{9,8},{10,11... | collective-permute-start | bytes 4718600 | tf_op jit(solution)/shard_map/ppermute | solution.py:75
  44.7 1.8 %collective-permute-done.13 = bf16[8,32,1536]{2,1,0:T(8,128)(2,1)} collective-permute-done((bf16[8,32,1536]{2,1,0:T(8,128)(2,1)}, bf16[8,32,1536]{2,1,0:T(8,128)(2,1)}, u32[]{:S(2)}, u32[]{:S(2)}) %collective-permute-start.13) | collective-permute-done | bytes 786464 | tf_op jit(solution)/shard_map/ppermute | solution.py:44
  46.6 1.0 slice.21
  47.6 3.0 %collective-permute-start.15 = (bf16[8,32,768]{2,1,0:T(8,128)(2,1)S(1)}, bf16[8,32,768]{2,1,0:T(8,128)(2,1)S(1)}, u32[]{:S(2)}, u32[]{:S(2)}) collective-permute-start(bf16[8,32,768]{2,1,0:T(8,128)(2,1)S(1)} %slice.21), channel_id=1, source_target_pairs={{0,24},{8,0},{16,8},{24,16},{1,25},{9,1},{17,9},{25,17},{2,26},{10... | collective-permute-start | bytes 1179656 | tf_op jit(solution)/shard_map/ppermute | solution.py:40
  50.6 1.2 %slice.20 = bf16[8,32,768]{2,1,0:T(8,128)(2,1)S(1)} slice(bf16[8,32,1536]{2,1,0:T(8,128)(2,1)} %collective-permute-done.12), slice={[0:8], [0:32], [0:768]} | slice | bytes 786432 | tf_op jit(solution)/shard_map/slice | solution.py:39
  51.8 1.3 %bitcast_dynamic-update-slice_fusion.1 = bf16[4,8,32,1536]{3,2,1,0:T(8,128)(2,1)S(1)} fusion(bf16[4,8,32,1536]{3,2,1,0:T(8,128)(2,1)S(1)} %copy-done.1, s32[]{:T(128)S(6)} %select_n.221, bf16[8,32,1536]{2,1,0:T(8,128)(2,1)} %collective-permute-done.12), kind=kLoop, calls=%fused_computation.47 | loop fusion | bytes 1572868 | tf_op jit(solution)/shard_map/dynamic_update_slice | solution.py:52
  53.1 1.2 %bitcast_dynamic-update-slice_fusion = bf16[4,8,32,1536]{3,2,1,0:T(8,128)(2,1)S(1)} fusion(bf16[4,8,32,1536]{3,2,1,0:T(8,128)(2,1)S(1)} %bitcast_dynamic-update-slice_fusion.1, s32[]{:T(128)S(6)} %select_n.223, bf16[8,32,1536]{2,1,0:T(8,128)(2,1)} %collective-permute-done.13), kind=kLoop, calls=%fused_computation.46 | loop fusion | bytes 1572868 | tf_op jit(solution)/shard_map/dynamic_update_slice | solution.py:52
  54.3 2.1 %collective-permute-done.15 = bf16[8,32,768]{2,1,0:T(8,128)(2,1)S(1)} collective-permute-done((bf16[8,32,768]{2,1,0:T(8,128)(2,1)S(1)}, bf16[8,32,768]{2,1,0:T(8,128)(2,1)S(1)}, u32[]{:S(2)}, u32[]{:S(2)}) %collective-permute-start.15) | collective-permute-done | bytes 393248 | tf_op jit(solution)/shard_map/ppermute | solution.py:40
  56.5 3.2 %collective-permute-done.14 = bf16[8,32,768]{2,1,0:T(8,128)(2,1)S(1)} collective-permute-done((bf16[8,32,768]{2,1,0:T(8,128)(2,1)S(1)}, bf16[8,32,768]{2,1,0:T(8,128)(2,1)S(1)}, u32[]{:S(2)}, u32[]{:S(2)}) %collective-permute-start.14) | collective-permute-done | bytes 393248 | tf_op jit(solution)/shard_map/ppermute | solution.py:39
  60.9 3.7 %fusion.9 = bf16[4,4,32,1536]{3,2,1,0:T(8,128)(2,1)} fusion(bf16[1536,1536]{1,0:T(8,128)(2,1)S(1)} %bitcast.97, bf16[4,4,2,32,1536]{4,3,2,1,0:T(8,128)(2,1)S(1)} %bitcast.85, s32[]{:T(128)S(6)} %select_n.227), kind=kOutput, calls=%fused_computation.18 | convolution fusion | flops 2416705536 | bytes 7864324 | tf_op jit(solution)/shard_map/dot_general | solution.py:93
  64.7 8.6 %collective-permute-start.16 = (bf16[4,4,32,1536]{3,2,1,0:T(8,128)(2,1)}, bf16[4,4,32,1536]{3,2,1,0:T(8,128)(2,1)}, u32[]{:S(2)}, u32[]{:S(2)}) collective-permute-start(bf16[4,4,32,1536]{3,2,1,0:T(8,128)(2,1)} %fusion.9), channel_id=1, source_target_pairs={{0,1},{1,0},{2,3},{3,2},{4,5},{5,4},{6,7},{7,6},{8,9},{9,8},{10,11... | collective-permute-start | bytes 4718600 | tf_op jit(solution)/shard_map/ppermute | solution.py:95
  73.3 2.2 %fusion.1 = bf16[1024,1536]{1,0:T(8,128)(2,1)S(1)} fusion(bf16[1024,1536]{1,0:T(8,128)(2,1)S(1)} %bitcast.82), kind=kLoop, calls=%fused_computation.8 | loop fusion | flops 15728640 | bytes 6291456 | tf_op jit(solution)/shard_map/convert_element_type | solution.py:82
  77.3 5.5 %convert_add_fusion.1 = f32[4,4,32,1536]{3,2,1,0:T(8,128)S(1)} fusion(bf16[4,4,32,1536]{3,2,1,0:T(8,128)(2,1)} %collective-permute-done.16, bf16[1536,1536]{1,0:T(8,128)(2,1)} %param.5, bf16[4,4,2,32,1536]{4,3,2,1,0:T(8,128)(2,1)S(1)} %bitcast.86, s32[]{:T(128)S(6)} %select_n.226), kind=kOutput, calls=%fused_computation.17 | convolution fusion | flops 2417491968 | bytes 11010052 | tf_op jit(solution)/shard_map/dot_general | solution.py:96
  83.0 2.1 %collective-permute-start.19 = (bf16[128,1536]{1,0:T(8,128)(2,1)S(1)}, bf16[128,1536]{1,0:T(8,128)(2,1)S(1)}, u32[]{:S(2)}, u32[]{:S(2)}) collective-permute-start(bf16[128,1536]{1,0:T(8,128)(2,1)S(1)} %bitcast.95), channel_id=1, source_target_pairs={{0,6},{1,7},{2,0},{3,1},{4,2},{5,3},{6,4},{7,5},{8,14},{9,15},{10,... | collective-permute-start | bytes 1179656 | tf_op jit(solution)/shard_map/ppermute | solution.py:114
  85.1 1.2 %collective-permute-start.18 = (bf16[128,1536]{1,0:T(8,128)(2,1)S(1)}, bf16[128,1536]{1,0:T(8,128)(2,1)S(1)}, u32[]{:S(2)}, u32[]{:S(2)}) collective-permute-start(bf16[128,1536]{1,0:T(8,128)(2,1)S(1)} %bitcast.94), channel_id=1, source_target_pairs={{0,4},{1,5},{2,6},{3,7},{4,0},{5,1},{6,2},{7,3},{8,12},{9,13},{10,... | collective-permute-start | bytes 1179656 | tf_op jit(solution)/shard_map/ppermute | solution.py:114
  86.4 6.9 %convolution_convert_fusion = bf16[1536,1536]{1,0:T(8,128)(2,1)} fusion(bf16[1024,1536]{1,0:T(8,128)(2,1)S(1)} %bitcast.84, bf16[1024,1536]{1,0:T(8,128)(2,1)S(1)} %bitcast.87), kind=kOutput, calls=%fused_computation.6 | convolution fusion | flops 4834197504 | bytes 11010048 | tf_op jit(solution)/shard_map/dot_general | solution.py:84
  93.9 3.2 %collective-permute-done.18 = bf16[128,1536]{1,0:T(8,128)(2,1)S(1)} collective-permute-done((bf16[128,1536]{1,0:T(8,128)(2,1)S(1)}, bf16[128,1536]{1,0:T(8,128)(2,1)S(1)}, u32[]{:S(2)}, u32[]{:S(2)}) %collective-permute-start.18) | collective-permute-done | bytes 393248 | tf_op jit(solution)/shard_map/ppermute | solution.py:114
  97.1 9.0 %collective-permute-done.17 = bf16[128,1536]{1,0:T(8,128)(2,1)S(1)} collective-permute-done((bf16[128,1536]{1,0:T(8,128)(2,1)S(1)}, bf16[128,1536]{1,0:T(8,128)(2,1)S(1)}, u32[]{:S(2)}, u32[]{:S(2)}) %collective-permute-start.17) | collective-permute-done | bytes 393248 | tf_op jit(solution)/shard_map/ppermute | solution.py:114
  106.1 1.4 %fusion.27 = bf16[128,1536]{1,0:T(8,128)(2,1)} fusion(bf16[128,1536]{1,0:T(8,128)(2,1)S(1)} %copy-done.4, f32[4,1,32,1536]{3,2,1,0:T(8,128)S(1)} %constant_dynamic-slice_fusion, bf16[128,1536]{1,0:T(8,128)(2,1)S(1)} %collective-permute-done.19, bf16[128,1536]{1,0:T(8,128)(2,1)S(1)} %collective-permute-done.18, bf16[128,1536]{1,0:T(8,128)(2,1)S(1)} %collective-permute-done.17), kind=kLoop, calls=%fused_computation.40 | loop fusion | flops 5111808 | bytes 2752512 | tf_op jit(solution)/shard_map/convert_element_type | solution.py:118
  (59 shorter events, 13.4 us)
Async XLA Ops:
  0.6 35.2 %collective-permute-start.2 = (bf16[128,1536]{1,0:T(8,128)(2,1)}, bf16[128,1536]{1,0:T(8,128)(2,1)S(1)}, u32[]{:S(2)}, u32[]{:S(2)}) collective-permute-start(bf16[128,1536]{1,0:T(8,128)(2,1)} %param.3), channel_id=1, source_target_pairs={{0,6},{1,7},{2,0},{3,1},{4,2},{5,3},{6,4},{7,5},{8,14},{9,15},{10,... | collective-permute-start | bytes 1179656 | tf_op jit(solution)/shard_map/ppermute | solution.py:71
  4.0 31.8 %collective-permute-start.1 = (bf16[128,1536]{1,0:T(8,128)(2,1)}, bf16[128,1536]{1,0:T(8,128)(2,1)S(1)}, u32[]{:S(2)}, u32[]{:S(2)}) collective-permute-start(bf16[128,1536]{1,0:T(8,128)(2,1)} %param.3), channel_id=1, source_target_pairs={{0,4},{1,5},{2,6},{3,7},{4,0},{5,1},{6,2},{7,3},{8,12},{9,13},{10,... | collective-permute-start | bytes 1179656 | tf_op jit(solution)/shard_map/ppermute | solution.py:71
  4.5 31.3 %collective-permute-start = (bf16[128,1536]{1,0:T(8,128)(2,1)}, bf16[128,1536]{1,0:T(8,128)(2,1)S(1)}, u32[]{:S(2)}, u32[]{:S(2)}) collective-permute-start(bf16[128,1536]{1,0:T(8,128)(2,1)} %param.3), channel_id=1, source_target_pairs={{0,2},{1,3},{2,4},{3,5},{4,6},{5,7},{6,0},{7,1},{8,10},{9,11},{10,... | collective-permute-start | bytes 1179656 | tf_op jit(solution)/shard_map/ppermute | solution.py:71
  5.1 8.1 %collective-permute-start.4 = (bf16[32,1536]{1,0:T(8,128)(2,1)}, bf16[32,1536]{1,0:T(8,128)(2,1)S(1)}, u32[]{:S(2)}, u32[]{:S(2)}) collective-permute-start(bf16[32,1536]{1,0:T(8,128)(2,1)} %param.4), channel_id=1, source_target_pairs={{0,32},{32,64},{64,96},{96,128},{128,160},{160,192},{192,224},{224... | collective-permute-start | bytes 294920 | tf_op jit(solution)/shard_map/ppermute | solution.py:43
  6.8 6.6 %collective-permute-start.5 = (bf16[32,1536]{1,0:T(8,128)(2,1)}, bf16[32,1536]{1,0:T(8,128)(2,1)S(1)}, u32[]{:S(2)}, u32[]{:S(2)}) collective-permute-start(bf16[32,1536]{1,0:T(8,128)(2,1)} %param.4), channel_id=1, source_target_pairs={{0,224},{32,0},{64,32},{96,64},{128,96},{160,128},{192,160},{224,1... | collective-permute-start | bytes 294920 | tf_op jit(solution)/shard_map/ppermute | solution.py:44
  13.3 5.1 %collective-permute-start.6 = (bf16[32,1536]{1,0:T(8,128)(2,1)S(1)}, bf16[32,1536]{1,0:T(8,128)(2,1)S(1)}, u32[]{:S(2)}, u32[]{:S(2)}) collective-permute-start(bf16[32,1536]{1,0:T(8,128)(2,1)S(1)} %collective-permute-done.4), channel_id=1, source_target_pairs={{0,32},{32,64},{64,96},{96,128},{128,160},{160,192},{192,224},{224... | collective-permute-start | bytes 294920 | tf_op jit(solution)/shard_map/ppermute | solution.py:43
  13.4 5.0 %collective-permute-start.7 = (bf16[32,1536]{1,0:T(8,128)(2,1)S(1)}, bf16[32,1536]{1,0:T(8,128)(2,1)S(1)}, u32[]{:S(2)}, u32[]{:S(2)}) collective-permute-start(bf16[32,1536]{1,0:T(8,128)(2,1)S(1)} %collective-permute-done.5), channel_id=1, source_target_pairs={{0,224},{32,0},{64,32},{96,64},{128,96},{160,128},{192,160},{224,1... | collective-permute-start | bytes 294920 | tf_op jit(solution)/shard_map/ppermute | solution.py:44
  16.7 20.8 %copy-start.4 = (bf16[128,1536]{1,0:T(8,128)(2,1)S(1)}, bf16[128,1536]{1,0:T(8,128)(2,1)}, u32[]{:S(2)}) copy-start(bf16[128,1536]{1,0:T(8,128)(2,1)} %param.3) | copy-start | bytes 1179652
  18.3 7.7 %collective-permute-start.8 = (bf16[32,1536]{1,0:T(8,128)(2,1)S(1)}, bf16[32,1536]{1,0:T(8,128)(2,1)S(1)}, u32[]{:S(2)}, u32[]{:S(2)}) collective-permute-start(bf16[32,1536]{1,0:T(8,128)(2,1)S(1)} %collective-permute-done.6), channel_id=1, source_target_pairs={{0,32},{32,64},{64,96},{96,128},{128,160},{160,192},{192,224},{224... | collective-permute-start | bytes 294920 | tf_op jit(solution)/shard_map/ppermute | solution.py:43
  18.3 4.3 %collective-permute-start.9 = (bf16[32,1536]{1,0:T(8,128)(2,1)S(1)}, bf16[32,1536]{1,0:T(8,128)(2,1)S(1)}, u32[]{:S(2)}, u32[]{:S(2)}) collective-permute-start(bf16[32,1536]{1,0:T(8,128)(2,1)S(1)} %collective-permute-done.7), channel_id=1, source_target_pairs={{0,224},{32,0},{64,32},{96,64},{128,96},{160,128},{192,160},{224,1... | collective-permute-start | bytes 294920 | tf_op jit(solution)/shard_map/ppermute | solution.py:44
  22.7 4.7 %collective-permute-start.11 = (bf16[32,768]{1,0:T(8,128)(2,1)S(1)}, bf16[32,768]{1,0:T(8,128)(2,1)S(1)}, u32[]{:S(2)}, u32[]{:S(2)}) collective-permute-start(bf16[32,768]{1,0:T(8,128)(2,1)S(1)} %slice.19), channel_id=1, source_target_pairs={{0,224},{32,0},{64,32},{96,64},{128,96},{160,128},{192,160},{224,1... | collective-permute-start | bytes 147464 | tf_op jit(solution)/shard_map/ppermute | solution.py:40
  26.0 4.2 %collective-permute-start.10 = (bf16[32,768]{1,0:T(8,128)(2,1)S(1)}, bf16[32,768]{1,0:T(8,128)(2,1)S(1)}, u32[]{:S(2)}, u32[]{:S(2)}) collective-permute-start(bf16[32,768]{1,0:T(8,128)(2,1)S(1)} %slice.18), channel_id=1, source_target_pairs={{0,32},{32,64},{64,96},{96,128},{128,160},{160,192},{192,224},{224... | collective-permute-start | bytes 147464 | tf_op jit(solution)/shard_map/ppermute | solution.py:39
  31.5 19.1 %collective-permute-start.12 = (bf16[8,32,1536]{2,1,0:T(8,128)(2,1)}, bf16[8,32,1536]{2,1,0:T(8,128)(2,1)}, u32[]{:S(2)}, u32[]{:S(2)}) collective-permute-start(bf16[8,32,1536]{2,1,0:T(8,128)(2,1)} %fusion.33), channel_id=1, source_target_pairs={{0,8},{8,16},{16,24},{24,0},{1,9},{9,17},{17,25},{25,1},{2,10},{10... | collective-permute-start | bytes 2359304 | tf_op jit(solution)/shard_map/ppermute | solution.py:43
  32.8 13.8 %collective-permute-start.13 = (bf16[8,32,1536]{2,1,0:T(8,128)(2,1)}, bf16[8,32,1536]{2,1,0:T(8,128)(2,1)}, u32[]{:S(2)}, u32[]{:S(2)}) collective-permute-start(bf16[8,32,1536]{2,1,0:T(8,128)(2,1)} %fusion.33), channel_id=1, source_target_pairs={{0,24},{8,0},{16,8},{24,16},{1,25},{9,1},{17,9},{25,17},{2,26},{10... | collective-permute-start | bytes 2359304 | tf_op jit(solution)/shard_map/ppermute | solution.py:44
  35.8 1.7 %copy-start = (bf16[4,8,32,1536]{3,2,1,0:T(8,128)(2,1)}, bf16[4,8,32,1536]{3,2,1,0:T(8,128)(2,1)S(1)}, u32[]{:S(2)}) copy-start(bf16[4,8,32,1536]{3,2,1,0:T(8,128)(2,1)S(1)} %bitcast_dynamic-update-slice_fusion.2) | copy-start | bytes 9437188
  38.5 13.3 %copy-start.1 = (bf16[4,8,32,1536]{3,2,1,0:T(8,128)(2,1)S(1)}, bf16[4,8,32,1536]{3,2,1,0:T(8,128)(2,1)}, u32[]{:S(2)}) copy-start(bf16[4,8,32,1536]{3,2,1,0:T(8,128)(2,1)} %copy-done) | copy-start | bytes 9437188
  38.5 21.3 %collective-permute-start.3 = (bf16[4,128,1536]{2,1,0:T(8,128)(2,1)S(1)}, bf16[4,128,1536]{2,1,0:T(8,128)(2,1)S(1)}, u32[]{:S(2)}, u32[]{:S(2)}) collective-permute-start(bf16[4,128,1536]{2,1,0:T(8,128)(2,1)S(1)} %broadcast_select_fusion), channel_id=1, source_target_pairs={{0,1},{1,0},{2,3},{3,2},{4,5},{5,4},{6,7},{7,6},{8,9},{9,8},{10,11... | collective-permute-start | bytes 4718600 | tf_op jit(solution)/shard_map/ppermute | solution.py:75
  47.6 8.9 %collective-permute-start.15 = (bf16[8,32,768]{2,1,0:T(8,128)(2,1)S(1)}, bf16[8,32,768]{2,1,0:T(8,128)(2,1)S(1)}, u32[]{:S(2)}, u32[]{:S(2)}) collective-permute-start(bf16[8,32,768]{2,1,0:T(8,128)(2,1)S(1)} %slice.21), channel_id=1, source_target_pairs={{0,24},{8,0},{16,8},{24,16},{1,25},{9,1},{17,9},{25,17},{2,26},{10... | collective-permute-start | bytes 1179656 | tf_op jit(solution)/shard_map/ppermute | solution.py:40
  50.5 9.8 %slice-start = ((s8[4718592]{0:T(1024)(128)(4,1)}), s8[4194304]{0:T(1024)(128)(4,1)S(1)}, s32[]{:S(2)}) async-start(s8[4718592]{0:T(1024)(128)(4,1)} %bitcast.96), calls=%async_computation | async-start | bytes 8388608
  51.7 7.9 %collective-permute-start.14 = (bf16[8,32,768]{2,1,0:T(8,128)(2,1)S(1)}, bf16[8,32,768]{2,1,0:T(8,128)(2,1)S(1)}, u32[]{:S(2)}, u32[]{:S(2)}) collective-permute-start(bf16[8,32,768]{2,1,0:T(8,128)(2,1)S(1)} %slice.20), channel_id=1, source_target_pairs={{0,8},{8,16},{16,24},{24,0},{1,9},{9,17},{17,25},{25,1},{2,10},{10... | collective-permute-start | bytes 1179656 | tf_op jit(solution)/shard_map/ppermute | solution.py:39
  59.7 1.2 %slice-start.1 = ((s8[4718592]{0:T(1024)(128)(4,1)}), s8[524288]{0:T(1024)(128)(4,1)S(1)}, s32[]{:S(2)}) async-start(s8[4718592]{0:T(1024)(128)(4,1)} %bitcast.96), calls=%async_computation.1 | async-start | bytes 1048576
  59.8 4.8 %copy-start.2 = (bf16[4,8,32,1536]{3,2,1,0:T(8,128)(2,1)}, bf16[4,8,32,1536]{3,2,1,0:T(8,128)(2,1)S(1)}, u32[]{:S(2)}) copy-start(bf16[4,8,32,1536]{3,2,1,0:T(8,128)(2,1)S(1)} %fusion.31) | copy-start | bytes 9437188
  64.7 12.0 %collective-permute-start.16 = (bf16[4,4,32,1536]{3,2,1,0:T(8,128)(2,1)}, bf16[4,4,32,1536]{3,2,1,0:T(8,128)(2,1)}, u32[]{:S(2)}, u32[]{:S(2)}) collective-permute-start(bf16[4,4,32,1536]{3,2,1,0:T(8,128)(2,1)} %fusion.9), channel_id=1, source_target_pairs={{0,1},{1,0},{2,3},{3,2},{4,5},{5,4},{6,7},{7,6},{8,9},{9,8},{10,11... | collective-permute-start | bytes 4718600 | tf_op jit(solution)/shard_map/ppermute | solution.py:95
  75.4 1.9 %copy-start.3 = (bf16[4,8,32,1536]{3,2,1,0:T(8,128)(2,1)S(1)}, bf16[4,8,32,1536]{3,2,1,0:T(8,128)(2,1)}, u32[]{:S(2)}) copy-start(bf16[4,8,32,1536]{3,2,1,0:T(8,128)(2,1)} %copy-done.2) | copy-start | bytes 9437188
  83.0 10.9 %collective-permute-start.19 = (bf16[128,1536]{1,0:T(8,128)(2,1)S(1)}, bf16[128,1536]{1,0:T(8,128)(2,1)S(1)}, u32[]{:S(2)}, u32[]{:S(2)}) collective-permute-start(bf16[128,1536]{1,0:T(8,128)(2,1)S(1)} %bitcast.95), channel_id=1, source_target_pairs={{0,6},{1,7},{2,0},{3,1},{4,2},{5,3},{6,4},{7,5},{8,14},{9,15},{10,... | collective-permute-start | bytes 1179656 | tf_op jit(solution)/shard_map/ppermute | solution.py:114
  85.1 11.9 %collective-permute-start.18 = (bf16[128,1536]{1,0:T(8,128)(2,1)S(1)}, bf16[128,1536]{1,0:T(8,128)(2,1)S(1)}, u32[]{:S(2)}, u32[]{:S(2)}) collective-permute-start(bf16[128,1536]{1,0:T(8,128)(2,1)S(1)} %bitcast.94), channel_id=1, source_target_pairs={{0,4},{1,5},{2,6},{3,7},{4,0},{5,1},{6,2},{7,3},{8,12},{9,13},{10,... | collective-permute-start | bytes 1179656 | tf_op jit(solution)/shard_map/ppermute | solution.py:114
  86.4 19.7 %collective-permute-start.17 = (bf16[128,1536]{1,0:T(8,128)(2,1)S(1)}, bf16[128,1536]{1,0:T(8,128)(2,1)S(1)}, u32[]{:S(2)}, u32[]{:S(2)}) collective-permute-start(bf16[128,1536]{1,0:T(8,128)(2,1)S(1)} %bitcast.93), channel_id=1, source_target_pairs={{0,2},{1,3},{2,4},{3,5},{4,6},{5,7},{6,0},{7,1},{8,10},{9,11},{10,... | collective-permute-start | bytes 1179656 | tf_op jit(solution)/shard_map/ppermute | solution.py:114

commit v14 on v13

--- a/solution.py
+++ b/solution.py
@@ -110,7 +110,7 @@
             pick = lambda c: lax.dynamic_index_in_dim(chip_sum, c, axis=0, keepdims=False)
         back = pick(x)
         dest = lambda s: pick((x + s) % n_x).astype(jnp.bfloat16)
-        for s in range(1, n_x):
+        for s in sorted(range(1, n_x), key=lambda s: -min(s, n_x - s)):
             recv = lax.ppermute(dest(s), COL, chip_shift(n_col, s))
             back = back + recv.astype(jnp.float32)
 

time: 108 us -> 107 us (level)
  transfers between devices with their start and end apart: 20 -> 20, of which waited for: 10 -> 9; matrix products, arithmetic and copies ran while one was open for 23% -> 23% of each run, Pallas kernels for 0% -> 0%
where the time goes in v14:
time: 107 us
  starting transfers between devices  42.7 us (40%)
  waiting for transfers between devices  24.1 us (23%)
  local copies, waits for them, and re-layouts  16.5 us (15%)
  matrix products  16.1 us (15%)
  other arithmetic  6.19 us (6%)
    ppermute x3, waiting for transfers between devices, per_device(): recv = lax.ppermute(dest(s), COL, chip_shift(n_col, s))  11.8 us
    ppermute x4, starting transfers between devices, ring_gather(): bwd = lax.ppermute(bwd, axis, behind)  10.7 us
    dynamic_update_slice x10, local copies, waits for them, and re-layouts, ring_gather(): lax.dynamic_update_slice_in_dim(out, by_off[d][None], (i + d) % n, axis=0)  9.08 us
    ppermute x1, starting transfers between devices, per_device(): lax.ppermute(p_theirs.astype(jnp.bfloat16), COL, core_swap(n_col))  8.62 us
    dot_general x1, matrix products, per_device(): lax.dot_general(hidden, grad_all, (((0,), (0,)), ((), ())), preferred_ele...  6.91 us
    ppermute x2, starting transfers between devices, ring_gather(): from_ahead = lax.ppermute(bwd[..., half:], axis, behind)  6.3 us
    ppermute x2, waiting for transfers between devices, ring_gather(): from_behind = lax.ppermute(fwd[..., :half], axis, ahead)  6.01 us
    ppermute x1, starting transfers between devices, per_device(): other_by_x = lax.ppermute(mine_by_x, COL, core_swap(n_col))  5.96 us
  transfers between devices with their start and end apart: 20, of which 9 were waited for; matrix products, arithmetic and copies ran while one was open for 23% of the time, Pallas kernels for 0%

profile of v14, /device:TPU:1, one launch (start us, length us, event | category | flops | bytes accessed | tf_op | source)
XLA Modules:
  0.0 106.6 jit_solution(9066511465866143658)
XLA Ops:
  0.6 3.4 %collective-permute-start.2 = (bf16[128,1536]{1,0:T(8,128)(2,1)}, bf16[128,1536]{1,0:T(8,128)(2,1)S(1)}, u32[]{:S(2)}, u32[]{:S(2)}) collective-permute-start(bf16[128,1536]{1,0:T(8,128)(2,1)} %param.3), channel_id=1, source_target_pairs={{0,6},{1,7},{2,0},{3,1},{4,2},{5,3},{6,4},{7,5},{8,14},{9,15},{10,... | collective-permute-start | bytes 1179656 | tf_op jit(solution)/shard_map/ppermute | solution.py:71
  5.1 1.6 %collective-permute-start.4 = (bf16[32,1536]{1,0:T(8,128)(2,1)}, bf16[32,1536]{1,0:T(8,128)(2,1)S(1)}, u32[]{:S(2)}, u32[]{:S(2)}) collective-permute-start(bf16[32,1536]{1,0:T(8,128)(2,1)} %param.4), channel_id=1, source_target_pairs={{0,32},{32,64},{64,96},{96,128},{128,160},{160,192},{192,224},{224... | collective-permute-start | bytes 294920 | tf_op jit(solution)/shard_map/ppermute | solution.py:43
  6.8 3.9 %collective-permute-start.5 = (bf16[32,1536]{1,0:T(8,128)(2,1)}, bf16[32,1536]{1,0:T(8,128)(2,1)S(1)}, u32[]{:S(2)}, u32[]{:S(2)}) collective-permute-start(bf16[32,1536]{1,0:T(8,128)(2,1)} %param.4), channel_id=1, source_target_pairs={{0,224},{32,0},{64,32},{96,64},{128,96},{160,128},{192,160},{224,1... | collective-permute-start | bytes 294920 | tf_op jit(solution)/shard_map/ppermute | solution.py:44
  11.7 1.5 %bitcast_dynamic-update-slice_fusion.9 = bf16[8,32,1536]{2,1,0:T(8,128)(2,1)} fusion(bf16[8,32,1536]{2,1,0:T(8,128)(2,1)} %broadcast_in_dim.63, s32[]{:T(128)S(6)} %select_n.203, bf16[32,1536]{1,0:T(8,128)(2,1)} %param.4), kind=kLoop, calls=%fused_computation.61 | loop fusion | bytes 196612 | tf_op jit(solution)/shard_map/dynamic_update_slice | solution.py:52
  13.4 2.7 %collective-permute-start.7 = (bf16[32,1536]{1,0:T(8,128)(2,1)S(1)}, bf16[32,1536]{1,0:T(8,128)(2,1)S(1)}, u32[]{:S(2)}, u32[]{:S(2)}) collective-permute-start(bf16[32,1536]{1,0:T(8,128)(2,1)S(1)} %collective-permute-done.5), channel_id=1, source_target_pairs={{0,224},{32,0},{64,32},{96,64},{128,96},{160,128},{192,160},{224,1... | collective-permute-start | bytes 294920 | tf_op jit(solution)/shard_map/ppermute | solution.py:44
  17.3 1.0 collective-permute-done.6
  18.3 2.7 %collective-permute-start.9 = (bf16[32,1536]{1,0:T(8,128)(2,1)S(1)}, bf16[32,1536]{1,0:T(8,128)(2,1)S(1)}, u32[]{:S(2)}, u32[]{:S(2)}) collective-permute-start(bf16[32,1536]{1,0:T(8,128)(2,1)S(1)} %collective-permute-done.7), channel_id=1, source_target_pairs={{0,224},{32,0},{64,32},{96,64},{128,96},{160,128},{192,160},{224,1... | collective-permute-start | bytes 294920 | tf_op jit(solution)/shard_map/ppermute | solution.py:44
  22.7 3.3 %collective-permute-start.11 = (bf16[32,768]{1,0:T(8,128)(2,1)S(1)}, bf16[32,768]{1,0:T(8,128)(2,1)S(1)}, u32[]{:S(2)}, u32[]{:S(2)}) collective-permute-start(bf16[32,768]{1,0:T(8,128)(2,1)S(1)} %slice.19), channel_id=1, source_target_pairs={{0,224},{32,0},{64,32},{96,64},{128,96},{160,128},{192,160},{224,1... | collective-permute-start | bytes 147464 | tf_op jit(solution)/shard_map/ppermute | solution.py:40
  27.4 2.8 %collective-permute-done.10 = bf16[32,768]{1,0:T(8,128)(2,1)S(1)} collective-permute-done((bf16[32,768]{1,0:T(8,128)(2,1)S(1)}, bf16[32,768]{1,0:T(8,128)(2,1)S(1)}, u32[]{:S(2)}, u32[]{:S(2)}) %collective-permute-start.10) | collective-permute-done | bytes 49184 | tf_op jit(solution)/shard_map/ppermute | solution.py:39
  31.5 1.3 %collective-permute-start.12 = (bf16[8,32,1536]{2,1,0:T(8,128)(2,1)}, bf16[8,32,1536]{2,1,0:T(8,128)(2,1)}, u32[]{:S(2)}, u32[]{:S(2)}) collective-permute-start(bf16[8,32,1536]{2,1,0:T(8,128)(2,1)} %fusion.33), channel_id=1, source_target_pairs={{0,8},{8,16},{16,24},{24,0},{1,9},{9,17},{17,25},{25,1},{2,10},{10... | collective-permute-start | bytes 2359304 | tf_op jit(solution)/shard_map/ppermute | solution.py:43
  32.8 1.4 %collective-permute-start.13 = (bf16[8,32,1536]{2,1,0:T(8,128)(2,1)}, bf16[8,32,1536]{2,1,0:T(8,128)(2,1)}, u32[]{:S(2)}, u32[]{:S(2)}) collective-permute-start(bf16[8,32,1536]{2,1,0:T(8,128)(2,1)} %fusion.33), channel_id=1, source_target_pairs={{0,24},{8,0},{16,8},{24,16},{1,25},{9,1},{17,9},{25,17},{2,26},{10... | collective-permute-start | bytes 2359304 | tf_op jit(solution)/shard_map/ppermute | solution.py:44
  34.6 1.2 %bitcast_dynamic-update-slice_fusion.2 = bf16[4,8,32,1536]{3,2,1,0:T(8,128)(2,1)S(1)} fusion(bf16[4,8,32,1536]{3,2,1,0:T(8,128)(2,1)S(1)} %broadcast_in_dim.62, s32[]{:T(128)S(6)} %select_n.219, bf16[8,32,1536]{2,1,0:T(8,128)(2,1)} %fusion.33), kind=kLoop, calls=%fused_computation.48 | loop fusion | bytes 1572868 | tf_op jit(solution)/shard_map/dynamic_update_slice | solution.py:52
  35.8 1.6 %copy-done = bf16[4,8,32,1536]{3,2,1,0:T(8,128)(2,1)} copy-done((bf16[4,8,32,1536]{3,2,1,0:T(8,128)(2,1)}, bf16[4,8,32,1536]{3,2,1,0:T(8,128)(2,1)S(1)}, u32[]{:S(2)}) %copy-start) | copy-done | bytes 3145752
  38.5 6.0 %collective-permute-start.3 = (bf16[4,128,1536]{2,1,0:T(8,128)(2,1)S(1)}, bf16[4,128,1536]{2,1,0:T(8,128)(2,1)S(1)}, u32[]{:S(2)}, u32[]{:S(2)}) collective-permute-start(bf16[4,128,1536]{2,1,0:T(8,128)(2,1)S(1)} %broadcast_select_fusion), channel_id=1, source_target_pairs={{0,1},{1,0},{2,3},{3,2},{4,5},{5,4},{6,7},{7,6},{8,9},{9,8},{10,11... | collective-permute-start | bytes 4718600 | tf_op jit(solution)/shard_map/ppermute | solution.py:75
  44.7 1.8 %collective-permute-done.13 = bf16[8,32,1536]{2,1,0:T(8,128)(2,1)} collective-permute-done((bf16[8,32,1536]{2,1,0:T(8,128)(2,1)}, bf16[8,32,1536]{2,1,0:T(8,128)(2,1)}, u32[]{:S(2)}, u32[]{:S(2)}) %collective-permute-start.13) | collective-permute-done | bytes 786464 | tf_op jit(solution)/shard_map/ppermute | solution.py:44
  46.6 1.0 slice.21
  47.6 3.0 %collective-permute-start.15 = (bf16[8,32,768]{2,1,0:T(8,128)(2,1)S(1)}, bf16[8,32,768]{2,1,0:T(8,128)(2,1)S(1)}, u32[]{:S(2)}, u32[]{:S(2)}) collective-permute-start(bf16[8,32,768]{2,1,0:T(8,128)(2,1)S(1)} %slice.21), channel_id=1, source_target_pairs={{0,24},{8,0},{16,8},{24,16},{1,25},{9,1},{17,9},{25,17},{2,26},{10... | collective-permute-start | bytes 1179656 | tf_op jit(solution)/shard_map/ppermute | solution.py:40
  50.6 1.2 %slice.20 = bf16[8,32,768]{2,1,0:T(8,128)(2,1)S(1)} slice(bf16[8,32,1536]{2,1,0:T(8,128)(2,1)} %collective-permute-done.12), slice={[0:8], [0:32], [0:768]} | slice | bytes 786432 | tf_op jit(solution)/shard_map/slice | solution.py:39
  51.8 1.3 %bitcast_dynamic-update-slice_fusion.1 = bf16[4,8,32,1536]{3,2,1,0:T(8,128)(2,1)S(1)} fusion(bf16[4,8,32,1536]{3,2,1,0:T(8,128)(2,1)S(1)} %copy-done.1, s32[]{:T(128)S(6)} %select_n.221, bf16[8,32,1536]{2,1,0:T(8,128)(2,1)} %collective-permute-done.12), kind=kLoop, calls=%fused_computation.47 | loop fusion | bytes 1572868 | tf_op jit(solution)/shard_map/dynamic_update_slice | solution.py:52
  53.1 1.2 %bitcast_dynamic-update-slice_fusion = bf16[4,8,32,1536]{3,2,1,0:T(8,128)(2,1)S(1)} fusion(bf16[4,8,32,1536]{3,2,1,0:T(8,128)(2,1)S(1)} %bitcast_dynamic-update-slice_fusion.1, s32[]{:T(128)S(6)} %select_n.223, bf16[8,32,1536]{2,1,0:T(8,128)(2,1)} %collective-permute-done.13), kind=kLoop, calls=%fused_computation.46 | loop fusion | bytes 1572868 | tf_op jit(solution)/shard_map/dynamic_update_slice | solution.py:52
  54.3 2.1 %collective-permute-done.15 = bf16[8,32,768]{2,1,0:T(8,128)(2,1)S(1)} collective-permute-done((bf16[8,32,768]{2,1,0:T(8,128)(2,1)S(1)}, bf16[8,32,768]{2,1,0:T(8,128)(2,1)S(1)}, u32[]{:S(2)}, u32[]{:S(2)}) %collective-permute-start.15) | collective-permute-done | bytes 393248 | tf_op jit(solution)/shard_map/ppermute | solution.py:40
  56.5 3.2 %collective-permute-done.14 = bf16[8,32,768]{2,1,0:T(8,128)(2,1)S(1)} collective-permute-done((bf16[8,32,768]{2,1,0:T(8,128)(2,1)S(1)}, bf16[8,32,768]{2,1,0:T(8,128)(2,1)S(1)}, u32[]{:S(2)}, u32[]{:S(2)}) %collective-permute-start.14) | collective-permute-done | bytes 393248 | tf_op jit(solution)/shard_map/ppermute | solution.py:39
  60.9 3.7 %fusion.9 = bf16[4,4,32,1536]{3,2,1,0:T(8,128)(2,1)} fusion(bf16[1536,1536]{1,0:T(8,128)(2,1)S(1)} %bitcast.97, bf16[4,4,2,32,1536]{4,3,2,1,0:T(8,128)(2,1)S(1)} %bitcast.85, s32[]{:T(128)S(6)} %select_n.227), kind=kOutput, calls=%fused_computation.18 | convolution fusion | flops 2416705536 | bytes 7864324 | tf_op jit(solution)/shard_map/dot_general | solution.py:93
  64.7 8.6 %collective-permute-start.16 = (bf16[4,4,32,1536]{3,2,1,0:T(8,128)(2,1)}, bf16[4,4,32,1536]{3,2,1,0:T(8,128)(2,1)}, u32[]{:S(2)}, u32[]{:S(2)}) collective-permute-start(bf16[4,4,32,1536]{3,2,1,0:T(8,128)(2,1)} %fusion.9), channel_id=1, source_target_pairs={{0,1},{1,0},{2,3},{3,2},{4,5},{5,4},{6,7},{7,6},{8,9},{9,8},{10,11... | collective-permute-start | bytes 4718600 | tf_op jit(solution)/shard_map/ppermute | solution.py:95
  73.3 2.2 %fusion.1 = bf16[1024,1536]{1,0:T(8,128)(2,1)S(1)} fusion(bf16[1024,1536]{1,0:T(8,128)(2,1)S(1)} %bitcast.82), kind=kLoop, calls=%fused_computation.8 | loop fusion | flops 15728640 | bytes 6291456 | tf_op jit(solution)/shard_map/convert_element_type | solution.py:82
  75.7 1.0 collective-permute-done.16
  77.3 5.5 %convert_add_fusion.1 = f32[4,4,32,1536]{3,2,1,0:T(8,128)S(1)} fusion(bf16[4,4,32,1536]{3,2,1,0:T(8,128)(2,1)} %collective-permute-done.16, bf16[1536,1536]{1,0:T(8,128)(2,1)} %param.5, bf16[4,4,2,32,1536]{4,3,2,1,0:T(8,128)(2,1)S(1)} %bitcast.86, s32[]{:T(128)S(6)} %select_n.226), kind=kOutput, calls=%fused_computation.17 | convolution fusion | flops 2417491968 | bytes 11010052 | tf_op jit(solution)/shard_map/dot_general | solution.py:96
  83.0 2.1 %collective-permute-start.19 = (bf16[128,1536]{1,0:T(8,128)(2,1)S(1)}, bf16[128,1536]{1,0:T(8,128)(2,1)S(1)}, u32[]{:S(2)}, u32[]{:S(2)}) collective-permute-start(bf16[128,1536]{1,0:T(8,128)(2,1)S(1)} %bitcast.95), channel_id=1, source_target_pairs={{0,6},{1,7},{2,0},{3,1},{4,2},{5,3},{6,4},{7,5},{8,14},{9,15},{10,... | collective-permute-start | bytes 1179656 | tf_op jit(solution)/shard_map/ppermute | solution.py:114
  85.1 1.3 %collective-permute-start.17 = (bf16[128,1536]{1,0:T(8,128)(2,1)S(1)}, bf16[128,1536]{1,0:T(8,128)(2,1)S(1)}, u32[]{:S(2)}, u32[]{:S(2)}) collective-permute-start(bf16[128,1536]{1,0:T(8,128)(2,1)S(1)} %bitcast.93), channel_id=1, source_target_pairs={{0,4},{1,5},{2,6},{3,7},{4,0},{5,1},{6,2},{7,3},{8,12},{9,13},{10,... | collective-permute-start | bytes 1179656 | tf_op jit(solution)/shard_map/ppermute | solution.py:114
  86.4 6.9 %convolution_convert_fusion = bf16[1536,1536]{1,0:T(8,128)(2,1)} fusion(bf16[1024,1536]{1,0:T(8,128)(2,1)S(1)} %bitcast.84, bf16[1024,1536]{1,0:T(8,128)(2,1)S(1)} %bitcast.87), kind=kOutput, calls=%fused_computation.6 | convolution fusion | flops 4834197504 | bytes 11010048 | tf_op jit(solution)/shard_map/dot_general | solution.py:84
  93.9 11.3 %collective-permute-done.18 = bf16[128,1536]{1,0:T(8,128)(2,1)S(1)} collective-permute-done((bf16[128,1536]{1,0:T(8,128)(2,1)S(1)}, bf16[128,1536]{1,0:T(8,128)(2,1)S(1)}, u32[]{:S(2)}, u32[]{:S(2)}) %collective-permute-start.18) | collective-permute-done | bytes 393248 | tf_op jit(solution)/shard_map/ppermute | solution.py:114
  105.2 1.4 %fusion.27 = bf16[128,1536]{1,0:T(8,128)(2,1)} fusion(bf16[128,1536]{1,0:T(8,128)(2,1)S(1)} %copy-done.4, f32[4,1,32,1536]{3,2,1,0:T(8,128)S(1)} %constant_dynamic-slice_fusion, bf16[128,1536]{1,0:T(8,128)(2,1)S(1)} %collective-permute-done.19, bf16[128,1536]{1,0:T(8,128)(2,1)S(1)} %collective-permute-done.18, bf16[128,1536]{1,0:T(8,128)(2,1)S(1)} %collective-permute-done.17), kind=kLoop, calls=%fused_computation.40 | loop fusion | flops 5111808 | bytes 2752512 | tf_op jit(solution)/shard_map/convert_element_type | solution.py:118
  (59 shorter events, 12.3 us)
Async XLA Ops:
  0.6 35.2 %collective-permute-start.2 = (bf16[128,1536]{1,0:T(8,128)(2,1)}, bf16[128,1536]{1,0:T(8,128)(2,1)S(1)}, u32[]{:S(2)}, u32[]{:S(2)}) collective-permute-start(bf16[128,1536]{1,0:T(8,128)(2,1)} %param.3), channel_id=1, source_target_pairs={{0,6},{1,7},{2,0},{3,1},{4,2},{5,3},{6,4},{7,5},{8,14},{9,15},{10,... | collective-permute-start | bytes 1179656 | tf_op jit(solution)/shard_map/ppermute | solution.py:71
  4.0 31.8 %collective-permute-start.1 = (bf16[128,1536]{1,0:T(8,128)(2,1)}, bf16[128,1536]{1,0:T(8,128)(2,1)S(1)}, u32[]{:S(2)}, u32[]{:S(2)}) collective-permute-start(bf16[128,1536]{1,0:T(8,128)(2,1)} %param.3), channel_id=1, source_target_pairs={{0,4},{1,5},{2,6},{3,7},{4,0},{5,1},{6,2},{7,3},{8,12},{9,13},{10,... | collective-permute-start | bytes 1179656 | tf_op jit(solution)/shard_map/ppermute | solution.py:71
  4.5 31.3 %collective-permute-start = (bf16[128,1536]{1,0:T(8,128)(2,1)}, bf16[128,1536]{1,0:T(8,128)(2,1)S(1)}, u32[]{:S(2)}, u32[]{:S(2)}) collective-permute-start(bf16[128,1536]{1,0:T(8,128)(2,1)} %param.3), channel_id=1, source_target_pairs={{0,2},{1,3},{2,4},{3,5},{4,6},{5,7},{6,0},{7,1},{8,10},{9,11},{10,... | collective-permute-start | bytes 1179656 | tf_op jit(solution)/shard_map/ppermute | solution.py:71
  5.1 8.1 %collective-permute-start.4 = (bf16[32,1536]{1,0:T(8,128)(2,1)}, bf16[32,1536]{1,0:T(8,128)(2,1)S(1)}, u32[]{:S(2)}, u32[]{:S(2)}) collective-permute-start(bf16[32,1536]{1,0:T(8,128)(2,1)} %param.4), channel_id=1, source_target_pairs={{0,32},{32,64},{64,96},{96,128},{128,160},{160,192},{192,224},{224... | collective-permute-start | bytes 294920 | tf_op jit(solution)/shard_map/ppermute | solution.py:43
  6.8 6.6 %collective-permute-start.5 = (bf16[32,1536]{1,0:T(8,128)(2,1)}, bf16[32,1536]{1,0:T(8,128)(2,1)S(1)}, u32[]{:S(2)}, u32[]{:S(2)}) collective-permute-start(bf16[32,1536]{1,0:T(8,128)(2,1)} %param.4), channel_id=1, source_target_pairs={{0,224},{32,0},{64,32},{96,64},{128,96},{160,128},{192,160},{224,1... | collective-permute-start | bytes 294920 | tf_op jit(solution)/shard_map/ppermute | solution.py:44
  13.3 5.1 %collective-permute-start.6 = (bf16[32,1536]{1,0:T(8,128)(2,1)S(1)}, bf16[32,1536]{1,0:T(8,128)(2,1)S(1)}, u32[]{:S(2)}, u32[]{:S(2)}) collective-permute-start(bf16[32,1536]{1,0:T(8,128)(2,1)S(1)} %collective-permute-done.4), channel_id=1, source_target_pairs={{0,32},{32,64},{64,96},{96,128},{128,160},{160,192},{192,224},{224... | collective-permute-start | bytes 294920 | tf_op jit(solution)/shard_map/ppermute | solution.py:43
  13.4 5.0 %collective-permute-start.7 = (bf16[32,1536]{1,0:T(8,128)(2,1)S(1)}, bf16[32,1536]{1,0:T(8,128)(2,1)S(1)}, u32[]{:S(2)}, u32[]{:S(2)}) collective-permute-start(bf16[32,1536]{1,0:T(8,128)(2,1)S(1)} %collective-permute-done.5), channel_id=1, source_target_pairs={{0,224},{32,0},{64,32},{96,64},{128,96},{160,128},{192,160},{224,1... | collective-permute-start | bytes 294920 | tf_op jit(solution)/shard_map/ppermute | solution.py:44
  16.7 20.8 %copy-start.4 = (bf16[128,1536]{1,0:T(8,128)(2,1)S(1)}, bf16[128,1536]{1,0:T(8,128)(2,1)}, u32[]{:S(2)}) copy-start(bf16[128,1536]{1,0:T(8,128)(2,1)} %param.3) | copy-start | bytes 1179652
  18.3 7.7 %collective-permute-start.8 = (bf16[32,1536]{1,0:T(8,128)(2,1)S(1)}, bf16[32,1536]{1,0:T(8,128)(2,1)S(1)}, u32[]{:S(2)}, u32[]{:S(2)}) collective-permute-start(bf16[32,1536]{1,0:T(8,128)(2,1)S(1)} %collective-permute-done.6), channel_id=1, source_target_pairs={{0,32},{32,64},{64,96},{96,128},{128,160},{160,192},{192,224},{224... | collective-permute-start | bytes 294920 | tf_op jit(solution)/shard_map/ppermute | solution.py:43
  18.3 4.3 %collective-permute-start.9 = (bf16[32,1536]{1,0:T(8,128)(2,1)S(1)}, bf16[32,1536]{1,0:T(8,128)(2,1)S(1)}, u32[]{:S(2)}, u32[]{:S(2)}) collective-permute-start(bf16[32,1536]{1,0:T(8,128)(2,1)S(1)} %collective-permute-done.7), channel_id=1, source_target_pairs={{0,224},{32,0},{64,32},{96,64},{128,96},{160,128},{192,160},{224,1... | collective-permute-start | bytes 294920 | tf_op jit(solution)/shard_map/ppermute | solution.py:44
  22.7 4.7 %collective-permute-start.11 = (bf16[32,768]{1,0:T(8,128)(2,1)S(1)}, bf16[32,768]{1,0:T(8,128)(2,1)S(1)}, u32[]{:S(2)}, u32[]{:S(2)}) collective-permute-start(bf16[32,768]{1,0:T(8,128)(2,1)S(1)} %slice.19), channel_id=1, source_target_pairs={{0,224},{32,0},{64,32},{96,64},{128,96},{160,128},{192,160},{224,1... | collective-permute-start | bytes 147464 | tf_op jit(solution)/shard_map/ppermute | solution.py:40
  26.0 4.2 %collective-permute-start.10 = (bf16[32,768]{1,0:T(8,128)(2,1)S(1)}, bf16[32,768]{1,0:T(8,128)(2,1)S(1)}, u32[]{:S(2)}, u32[]{:S(2)}) collective-permute-start(bf16[32,768]{1,0:T(8,128)(2,1)S(1)} %slice.18), channel_id=1, source_target_pairs={{0,32},{32,64},{64,96},{96,128},{128,160},{160,192},{192,224},{224... | collective-permute-start | bytes 147464 | tf_op jit(solution)/shard_map/ppermute | solution.py:39
  31.5 19.1 %collective-permute-start.12 = (bf16[8,32,1536]{2,1,0:T(8,128)(2,1)}, bf16[8,32,1536]{2,1,0:T(8,128)(2,1)}, u32[]{:S(2)}, u32[]{:S(2)}) collective-permute-start(bf16[8,32,1536]{2,1,0:T(8,128)(2,1)} %fusion.33), channel_id=1, source_target_pairs={{0,8},{8,16},{16,24},{24,0},{1,9},{9,17},{17,25},{25,1},{2,10},{10... | collective-permute-start | bytes 2359304 | tf_op jit(solution)/shard_map/ppermute | solution.py:43
  32.8 13.8 %collective-permute-start.13 = (bf16[8,32,1536]{2,1,0:T(8,128)(2,1)}, bf16[8,32,1536]{2,1,0:T(8,128)(2,1)}, u32[]{:S(2)}, u32[]{:S(2)}) collective-permute-start(bf16[8,32,1536]{2,1,0:T(8,128)(2,1)} %fusion.33), channel_id=1, source_target_pairs={{0,24},{8,0},{16,8},{24,16},{1,25},{9,1},{17,9},{25,17},{2,26},{10... | collective-permute-start | bytes 2359304 | tf_op jit(solution)/shard_map/ppermute | solution.py:44
  35.8 1.7 %copy-start = (bf16[4,8,32,1536]{3,2,1,0:T(8,128)(2,1)}, bf16[4,8,32,1536]{3,2,1,0:T(8,128)(2,1)S(1)}, u32[]{:S(2)}) copy-start(bf16[4,8,32,1536]{3,2,1,0:T(8,128)(2,1)S(1)} %bitcast_dynamic-update-slice_fusion.2) | copy-start | bytes 9437188
  38.5 13.3 %copy-start.1 = (bf16[4,8,32,1536]{3,2,1,0:T(8,128)(2,1)S(1)}, bf16[4,8,32,1536]{3,2,1,0:T(8,128)(2,1)}, u32[]{:S(2)}) copy-start(bf16[4,8,32,1536]{3,2,1,0:T(8,128)(2,1)} %copy-done) | copy-start | bytes 9437188
  38.5 21.3 %collective-permute-start.3 = (bf16[4,128,1536]{2,1,0:T(8,128)(2,1)S(1)}, bf16[4,128,1536]{2,1,0:T(8,128)(2,1)S(1)}, u32[]{:S(2)}, u32[]{:S(2)}) collective-permute-start(bf16[4,128,1536]{2,1,0:T(8,128)(2,1)S(1)} %broadcast_select_fusion), channel_id=1, source_target_pairs={{0,1},{1,0},{2,3},{3,2},{4,5},{5,4},{6,7},{7,6},{8,9},{9,8},{10,11... | collective-permute-start | bytes 4718600 | tf_op jit(solution)/shard_map/ppermute | solution.py:75
  47.6 8.9 %collective-permute-start.15 = (bf16[8,32,768]{2,1,0:T(8,128)(2,1)S(1)}, bf16[8,32,768]{2,1,0:T(8,128)(2,1)S(1)}, u32[]{:S(2)}, u32[]{:S(2)}) collective-permute-start(bf16[8,32,768]{2,1,0:T(8,128)(2,1)S(1)} %slice.21), channel_id=1, source_target_pairs={{0,24},{8,0},{16,8},{24,16},{1,25},{9,1},{17,9},{25,17},{2,26},{10... | collective-permute-start | bytes 1179656 | tf_op jit(solution)/shard_map/ppermute | solution.py:40
  50.5 9.8 %slice-start = ((s8[4718592]{0:T(1024)(128)(4,1)}), s8[4194304]{0:T(1024)(128)(4,1)S(1)}, s32[]{:S(2)}) async-start(s8[4718592]{0:T(1024)(128)(4,1)} %bitcast.96), calls=%async_computation | async-start | bytes 8388608
  51.7 7.9 %collective-permute-start.14 = (bf16[8,32,768]{2,1,0:T(8,128)(2,1)S(1)}, bf16[8,32,768]{2,1,0:T(8,128)(2,1)S(1)}, u32[]{:S(2)}, u32[]{:S(2)}) collective-permute-start(bf16[8,32,768]{2,1,0:T(8,128)(2,1)S(1)} %slice.20), channel_id=1, source_target_pairs={{0,8},{8,16},{16,24},{24,0},{1,9},{9,17},{17,25},{25,1},{2,10},{10... | collective-permute-start | bytes 1179656 | tf_op jit(solution)/shard_map/ppermute | solution.py:39
  59.7 1.2 %slice-start.1 = ((s8[4718592]{0:T(1024)(128)(4,1)}), s8[524288]{0:T(1024)(128)(4,1)S(1)}, s32[]{:S(2)}) async-start(s8[4718592]{0:T(1024)(128)(4,1)} %bitcast.96), calls=%async_computation.1 | async-start | bytes 1048576
  59.8 4.8 %copy-start.2 = (bf16[4,8,32,1536]{3,2,1,0:T(8,128)(2,1)}, bf16[4,8,32,1536]{3,2,1,0:T(8,128)(2,1)S(1)}, u32[]{:S(2)}) copy-start(bf16[4,8,32,1536]{3,2,1,0:T(8,128)(2,1)S(1)} %fusion.31) | copy-start | bytes 9437188
  64.7 12.0 %collective-permute-start.16 = (bf16[4,4,32,1536]{3,2,1,0:T(8,128)(2,1)}, bf16[4,4,32,1536]{3,2,1,0:T(8,128)(2,1)}, u32[]{:S(2)}, u32[]{:S(2)}) collective-permute-start(bf16[4,4,32,1536]{3,2,1,0:T(8,128)(2,1)} %fusion.9), channel_id=1, source_target_pairs={{0,1},{1,0},{2,3},{3,2},{4,5},{5,4},{6,7},{7,6},{8,9},{9,8},{10,11... | collective-permute-start | bytes 4718600 | tf_op jit(solution)/shard_map/ppermute | solution.py:95
  75.4 1.9 %copy-start.3 = (bf16[4,8,32,1536]{3,2,1,0:T(8,128)(2,1)S(1)}, bf16[4,8,32,1536]{3,2,1,0:T(8,128)(2,1)}, u32[]{:S(2)}) copy-start(bf16[4,8,32,1536]{3,2,1,0:T(8,128)(2,1)} %copy-done.2) | copy-start | bytes 9437188
  83.0 10.9 %collective-permute-start.19 = (bf16[128,1536]{1,0:T(8,128)(2,1)S(1)}, bf16[128,1536]{1,0:T(8,128)(2,1)S(1)}, u32[]{:S(2)}, u32[]{:S(2)}) collective-permute-start(bf16[128,1536]{1,0:T(8,128)(2,1)S(1)} %bitcast.95), channel_id=1, source_target_pairs={{0,6},{1,7},{2,0},{3,1},{4,2},{5,3},{6,4},{7,5},{8,14},{9,15},{10,... | collective-permute-start | bytes 1179656 | tf_op jit(solution)/shard_map/ppermute | solution.py:114
  85.1 20.0 %collective-permute-start.18 = (bf16[128,1536]{1,0:T(8,128)(2,1)S(1)}, bf16[128,1536]{1,0:T(8,128)(2,1)S(1)}, u32[]{:S(2)}, u32[]{:S(2)}) collective-permute-start(bf16[128,1536]{1,0:T(8,128)(2,1)S(1)} %bitcast.94), channel_id=1, source_target_pairs={{0,2},{1,3},{2,4},{3,5},{4,6},{5,7},{6,0},{7,1},{8,10},{9,11},{10,... | collective-permute-start | bytes 1179656 | tf_op jit(solution)/shard_map/ppermute | solution.py:114
  85.1 20.0 %collective-permute-start.17 = (bf16[128,1536]{1,0:T(8,128)(2,1)S(1)}, bf16[128,1536]{1,0:T(8,128)(2,1)S(1)}, u32[]{:S(2)}, u32[]{:S(2)}) collective-permute-start(bf16[128,1536]{1,0:T(8,128)(2,1)S(1)} %bitcast.93), channel_id=1, source_target_pairs={{0,4},{1,5},{2,6},{3,7},{4,0},{5,1},{6,2},{7,3},{8,12},{9,13},{10,... | collective-permute-start | bytes 1179656 | tf_op jit(solution)/shard_map/ppermute | solution.py:114
